TPU v7x, 512 devices: a whole 4x8x8 slice. The times are simulated.
512 devices in a mesh: seq: 8 (over z_lo, core), ctx: 64 (over z_hi, y, x).
Axes of the slice: x: 4, y: 8, z: 8 (z_hi: 2, z_lo: 4; z = z_hi * 4 + z_lo), core: 2. Of those that a mesh axis runs over, the one named last changes fastest.
Arguments:
- tokens: bfloat16 [8, 8192, 2048], P('seq', 'ctx'), may hold values from -80 to 80
- qkv_weight: bfloat16 [2048, 1536], P(None, 'seq'), may hold values from -0.125 to 0.125
- doc_lengths: int32 [8, 36], P('seq'), may hold values from 1 to 1024, 8192 in all within a row
- span_order: int32 [8, 128], P('seq'), may hold values from 0 to 127, as said below
Outputs:
- attended: bfloat16 [8, 8192, 1024], P('seq', 'ctx')
Inputs may be any that keep to these rules, and one draw needn't show every extreme that they name: `doc_lengths`: each row sums to 8192; its largest entry is exactly 1024. `span_order`: in each row, slots 2 i and 2 i + 1 hold spans i and 127 - i, in an order drawn for each pair.
All inputs are finite; a program needn't handle non-finite values.
Results may differ from a plain program's by a relative error of at most 0.012.
The roundings to bfloat16 on the way count: a program that leaves them out, or rounds other values in their place, can miss the bound.
Values may be sent and summed in bfloat16 or wider, within the bound.
No kernel may reach another device: no remote copies, remote signals or barrier semaphores. Data moves between devices by JAX's collectives and lax.ppermute only.
A program may use at most 192 MiB of HBM per device.

v0:
```python
import jax
import jax.numpy as jnp
from jax import lax
from jax.sharding import PartitionSpec as P

QUERY_HEADS = 16
KEY_VALUE_HEADS = 4
HEAD_SIZE = 64
QUERY_PER_KV = 4
SPAN = 64
DOC_MOST = 1024
WINDOW = DOC_MOST // SPAN


def apply_rotary(value_rows, token_positions):
    token_count = value_rows.shape[0]
    heads = value_rows.reshape(token_count, -1, HEAD_SIZE)
    half = HEAD_SIZE // 2
    freq = 500000.0 ** (-jnp.arange(half, dtype=jnp.float32) * 2.0 / HEAD_SIZE)
    angle = token_positions.astype(jnp.float32)[:, None] * freq[None, :]
    cosine = jnp.cos(angle)[:, None, :]
    sine = jnp.sin(angle)[:, None, :]
    first = heads[..., :half]
    second = heads[..., half:]
    turned = jnp.concatenate(
        [first * cosine - second * sine, second * cosine + first * sine], axis=-1
    )
    return turned.reshape(token_count, -1)


def positions(order_row):
    offsets = jnp.arange(SPAN, dtype=jnp.int32)
    return (order_row[:, None] * SPAN + offsets[None, :]).reshape(-1)


def documents(lengths_row, token_positions):
    ends = jnp.cumsum(lengths_row)
    return jnp.sum((ends[None, :] <= token_positions[..., None]).astype(jnp.int32), axis=-1)


def moved(value, count, pairs):
    pairs = [(s, d) for s, d in pairs if 0 <= s < count and 0 <= d < count]
    if not pairs:
        return jnp.zeros_like(value)
    return lax.ppermute(value, "ctx", pairs)


def body(tokens, qkv_weight, doc_lengths, span_order):
    rows = tokens[0]
    token_count = rows.shape[0]
    query_key_value = jnp.dot(
        rows,
        lax.all_gather(qkv_weight, "seq", axis=1, tiled=True),
        preferred_element_type=jnp.float32,
    ).astype(jnp.bfloat16)
    lengths_row = doc_lengths[0]
    order_row = span_order[0]
    places_all = positions(order_row)
    my_index = lax.axis_index("ctx")
    devices = lax.axis_size("ctx")
    first_row = my_index * token_count
    token_positions = lax.dynamic_slice_in_dim(places_all, first_row, token_count)
    query_rows = apply_rotary(
        query_key_value[:, : QUERY_HEADS * HEAD_SIZE].astype(jnp.float32), token_positions
    ).astype(jnp.bfloat16)
    key_rows = apply_rotary(
        query_key_value[
            :, QUERY_HEADS * HEAD_SIZE : (QUERY_HEADS + KEY_VALUE_HEADS) * HEAD_SIZE
        ].astype(jnp.float32),
        token_positions,
    ).astype(jnp.bfloat16)
    value_rows = query_key_value[:, (QUERY_HEADS + KEY_VALUE_HEADS) * HEAD_SIZE :]
    key_cols = key_rows.shape[1]
    stacked = jnp.concatenate([key_rows, value_rows], axis=1)

    early_first = order_row[2 * my_index] < devices
    offset = jnp.where(early_first, 0, SPAN).astype(jnp.int32)
    early_rows = lax.dynamic_slice_in_dim(stacked, offset, SPAN, 0)
    late_rows = lax.dynamic_slice_in_dim(stacked, SPAN - offset, SPAN, 0)
    early_queries = lax.dynamic_slice_in_dim(query_rows, offset, SPAN, 0)
    late_queries = lax.dynamic_slice_in_dim(query_rows, SPAN - offset, SPAN, 0)

    count = devices
    up = early_rows[None]
    down = jnp.stack([early_rows, late_rows])[None]
    reach = 1
    while reach < WINDOW:
        up = jnp.concatenate(
            [up, moved(up, count, [(d, d + reach) for d in range(count)])], axis=0
        )
        down = jnp.concatenate(
            [down, moved(down, count, [(d, d - reach) for d in range(count)])], axis=0
        )
        reach *= 2
    up = jnp.concatenate(
        [up, moved(early_rows[None], count, [(d, d + WINDOW) for d in range(count)])], axis=0
    )
    down = jnp.concatenate(
        [down, moved(down[:1], count, [(d, d - WINDOW) for d in range(count)])], axis=0
    )
    early_keys = up.reshape(-1, up.shape[-1])
    around = jnp.concatenate([up[::-1], down[1:, 0]], axis=0)
    steps = jnp.arange(WINDOW + 1, dtype=jnp.int32)
    mirror = jnp.clip(2 * count - 1 - 2 * my_index - steps + WINDOW, 0, 2 * WINDOW)
    late_keys = jnp.where(
        (my_index + steps <= count - 1)[:, None, None], down[:, 1], jnp.take(around, mirror, axis=0)
    ).reshape(-1, up.shape[-1])
    key_blocks = jnp.stack([early_keys, late_keys])

    steps = jnp.arange(WINDOW + 1, dtype=jnp.int32)
    query_spans = jnp.stack([my_index, 2 * devices - 1 - my_index])
    key_spans = query_spans[:, None] - steps[None, :]
    ramp = jnp.arange(SPAN, dtype=jnp.int32)
    key_places = (key_spans[:, :, None] * SPAN + ramp).reshape(2, -1)
    key_ok = jnp.repeat(key_spans >= 0, SPAN, axis=1)
    query_places = query_spans[:, None] * SPAN + ramp[None, :]
    key_docs = documents(lengths_row, key_places)
    query_docs = documents(lengths_row, query_places)
    live = (
        (query_docs[:, :, None] == key_docs[:, None, :])
        & (key_places[:, None, :] <= query_places[:, :, None])
        & key_ok[:, None, :]
    )

    queries = jnp.stack([early_queries, late_queries]).reshape(
        2, SPAN, KEY_VALUE_HEADS, QUERY_PER_KV, HEAD_SIZE
    )
    keys = key_blocks[:, :, :key_cols].reshape(2, -1, KEY_VALUE_HEADS, HEAD_SIZE)
    values = key_blocks[:, :, key_cols:].reshape(2, -1, KEY_VALUE_HEADS, HEAD_SIZE)
    scores = (
        jnp.einsum("sqhgd,skhd->shgqk", queries, keys, preferred_element_type=jnp.float32)
        * 0.125
    )
    live = live[:, None, None]
    scores = jnp.where(live, scores, -1e30)
    top = jnp.max(scores, axis=-1, keepdims=True)
    weights = jnp.where(live, jnp.exp(scores - top), 0.0)
    total = jnp.sum(weights, axis=-1)
    summed = jnp.einsum(
        "shgqk,skhd->shgqd",
        weights.astype(jnp.bfloat16),
        values,
        preferred_element_type=jnp.float32,
    )
    outputs = summed / total[..., None]
    outputs = jnp.transpose(outputs, (0, 3, 1, 2, 4)).reshape(2, SPAN, QUERY_HEADS * HEAD_SIZE)
    outputs = outputs.astype(jnp.bfloat16)
    ordered = jnp.where(early_first, outputs, outputs[::-1]).reshape(
        token_count, QUERY_HEADS * HEAD_SIZE
    )
    return ordered[None]


def solution(mesh):
    placed = (P("seq", "ctx", None), P(None, "seq"), P("seq", None), P("seq", None))
    return jax.shard_map(
        body, mesh=mesh, in_specs=placed, out_specs=P("seq", "ctx", None), check_vma=False
    )
```

profile of v0, /device:TPU:62, one launch (start us, length us, event | category | flops | bytes accessed | tf_op | source)
XLA Modules:
  0.0 265.6 jit_solution(11324576805438696198)
XLA Ops:
  6.5 0.7 all-gather.2.cloned.1.call-update
  7.3 1.3 fusion.38
  10.5 0.8 copy.17
  12.4 0.9 and_and_fusion
  13.3 77.4 %all-gather.2.cloned.1.call-done = bf16[2048,1536]{0,1:T(8,128)(2,1)} async-done(((bf16[2048,192]{0,1:T(8,128)(2,1)}), bf16[2048,1536]{0,1:T(8,128)(2,1)}) %all-gather.2.cloned.1.call-update) | async-done | bytes 6291472 | tf_op jit(solution)/shard_map/all_gather | solution.py:53
  90.7 5.0 %convolution_convert_fusion = bf16[128,1536]{1,0:T(8,128)(2,1)S(1)} fusion(bf16[2048,1536]{0,1:T(8,128)(2,1)} %all-gather.2.cloned.1.call-done, bf16[1,128,2048]{2,1,0:T(8,128)(2,1)S(1)} %copy-done), kind=kOutput, calls=%fused_computation.10 | convolution fusion | flops 805502976 | bytes 7208960 | tf_op jit(solution)/shard_map/dot_general | solution.py:51
  96.0 5.1 %collective-permute-start = (bf16[1,64,512]{2,1,0:T(8,128)(2,1)S(1)}, bf16[1,64,512]{2,1,0:T(8,128)(2,1)S(1)}, u32[]{:S(2)}, u32[]{:S(2)}) collective-permute-start(bf16[1,64,512]{2,1,0:T(8,128)(2,1)S(1)} %get-tuple-element.8), channel_id=1, source_target_pairs={{0,1},{1,2},{2,3},{3,4},{4,5},{5,6},{6,7},{7,8},{8,9},{9,10},{10,1... | collective-permute-start | bytes 196616 | tf_op jit(solution)/shard_map/ppermute | solution.py:45
  101.2 1.9 collective-permute-done
  103.0 0.7 pad_maximum_fusion.15
  103.7 1.9 collective-permute-start.5
  106.3 14.0 %collective-permute-done.5 = bf16[1,2,64,512]{3,2,0,1:T(8,128)(2,1)S(1)} collective-permute-done((bf16[1,2,64,512]{3,2,0,1:T(8,128)(2,1)S(1)}, bf16[1,2,64,512]{3,2,0,1:T(8,128)(2,1)S(1)}, u32[]{:S(2)}, u32[]{:S(2)}) %collective-permute-start.5) | collective-permute-done | bytes 131104 | tf_op jit(solution)/shard_map/ppermute | solution.py:45
  120.3 0.7 pad_maximum_fusion.12
  121.0 1.9 collective-permute-start.6
  123.7 0.7 broadcast_in_dim.81
  124.4 1.9 collective-permute-start.4
  126.5 12.3 %collective-permute-start.1 = (bf16[2,64,512]{2,1,0:T(8,128)(2,1)}, bf16[2,64,512]{2,1,0:T(8,128)(2,1)S(1)}, u32[]{:S(2)}, u32[]{:S(2)}) collective-permute-start(bf16[2,64,512]{2,1,0:T(8,128)(2,1)} %get-tuple-element.29), channel_id=1, source_target_pairs={{0,2},{1,3},{2,4},{3,5},{4,6},{5,7},{6,8},{7,9},{8,10},{9,11},{10,... | collective-permute-start | bytes 393224 | tf_op jit(solution)/shard_map/ppermute | solution.py:45
  138.9 5.6 %collective-permute-done.6 = bf16[2,2,64,512]{3,2,0,1:T(8,128)(2,1)S(1)} collective-permute-done((bf16[2,2,64,512]{3,2,0,1:T(8,128)(2,1)}, bf16[2,2,64,512]{3,2,0,1:T(8,128)(2,1)S(1)}, u32[]{:S(2)}, u32[]{:S(2)}) %collective-permute-start.6) | collective-permute-done | bytes 262176 | tf_op jit(solution)/shard_map/ppermute | solution.py:45
  144.5 0.9 pad_maximum_fusion.4
  145.3 1.9 collective-permute-start.7
  147.2 0.8 subtract_convert_fusion
  148.1 0.7 pad_maximum_fusion.11
  148.8 9.9 %collective-permute-start.2 = (bf16[4,64,512]{2,1,0:T(8,128)(2,1)}, bf16[4,64,512]{2,1,0:T(8,128)(2,1)}, u32[]{:S(2)}, u32[]{:S(2)}) collective-permute-start(bf16[4,64,512]{2,1,0:T(8,128)(2,1)} %pad_maximum_fusion.11), channel_id=1, source_target_pairs={{0,4},{1,5},{2,6},{3,7},{4,8},{5,9},{6,10},{7,11},{8,12},{9,13},{1... | collective-permute-start | bytes 786440 | tf_op jit(solution)/shard_map/ppermute | solution.py:45
  159.0 0.9 copy.25
  159.8 0.9 copy.24
  161.4 1.9 collective-permute-start.9
  163.3 9.0 %collective-permute-done.7 = bf16[4,2,64,512]{3,2,0,1:T(8,128)(2,1)S(1)} collective-permute-done((bf16[4,2,64,512]{3,2,0,1:T(8,128)(2,1)}, bf16[4,2,64,512]{3,2,0,1:T(8,128)(2,1)S(1)}, u32[]{:S(2)}, u32[]{:S(2)}) %collective-permute-start.7) | collective-permute-done | bytes 524320 | tf_op jit(solution)/shard_map/ppermute | solution.py:45
  172.3 1.2 pad_maximum_fusion.2
  173.4 1.9 collective-permute-start.8
  175.4 1.0 pad_maximum_fusion.3
  176.4 10.8 %collective-permute-start.3 = (bf16[8,64,512]{2,1,0:T(8,128)(2,1)S(1)}, bf16[8,64,512]{2,1,0:T(8,128)(2,1)S(1)}, u32[]{:S(2)}, u32[]{:S(2)}) collective-permute-start(bf16[8,64,512]{2,1,0:T(8,128)(2,1)S(1)} %pad_maximum_fusion.3), channel_id=1, source_target_pairs={{0,8},{1,9},{2,10},{3,11},{4,12},{5,13},{6,14},{7,15},{8,16},{9,17... | collective-permute-start | bytes 1572872 | tf_op jit(solution)/shard_map/ppermute | solution.py:45
  187.3 0.7 constant_dynamic-update-slice_fusion.10
  188.0 1.0 constant_dynamic-update-slice_fusion.2
  188.9 0.9 constant_dynamic-update-slice_fusion.9
  189.8 14.5 %collective-permute-done.3 = bf16[8,64,512]{2,1,0:T(8,128)(2,1)S(1)} collective-permute-done((bf16[8,64,512]{2,1,0:T(8,128)(2,1)S(1)}, bf16[8,64,512]{2,1,0:T(8,128)(2,1)S(1)}, u32[]{:S(2)}, u32[]{:S(2)}) %collective-permute-start.3) | collective-permute-done | bytes 524320 | tf_op jit(solution)/shard_map/ppermute | solution.py:45
  204.3 0.8 constant_dynamic-update-slice_fusion
  205.2 1.2 rev.6
  206.4 1.1 constant_dynamic-update-slice_fusion.8
  207.4 25.4 %collective-permute-done.8 = bf16[8,2,64,512]{3,2,0,1:T(8,128)(2,1)} collective-permute-done((bf16[8,2,64,512]{3,2,0,1:T(8,128)(2,1)}, bf16[8,2,64,512]{3,2,0,1:T(8,128)(2,1)}, u32[]{:S(2)}, u32[]{:S(2)}) %collective-permute-start.8) | collective-permute-done | bytes 1048608 | tf_op jit(solution)/shard_map/ppermute | solution.py:45
  232.8 2.8 %constant_dynamic-update-slice_fusion.7 = (bf16[17,2,64,512]{3,2,0,1:T(8,128)(2,1)}, bf16[16,2,64,512]{3,2,0,1:T(8,128)(2,1)}) fusion(bf16[17,2,64,512]{3,2,0,1:T(8,128)(2,1)} %get-tuple-element.15, bf16[8,2,64,512]{3,2,0,1:T(8,128)(2,1)} %collective-permute-done.8, bf16[16,2,64,512]{3,2,0,1:T(8,128)(2,1)} %get-tuple-element.16), kind=kLoop, calls=%fused_computation.64 | loop fusion | bytes 3145728
  235.7 1.7 constant_dynamic-update-slice_fusion.6
  237.3 2.5 slice.51
  240.2 1.8 gather_fusion
  242.0 2.2 fusion.19
  244.4 1.4 copy.26
  245.8 0.7 copy.20
  246.6 6.3 %fusion.39 = (f32[2,4,4,64]{3,2,1,0:T(4,128)}, bf16[2,4,4,64,1088]{4,3,2,1,0:T(8,128)(2,1)}) fusion(pred[2,64,1088]{2,1,0:T(8,128)(4,1)S(1)} %copy-done.9, bf16[2,1088,4,64,1]{1,3,4,2,0:T(8,128)(2,1)S(1)} %bitcast.70, bf16[1,64,4,4,64]{4,1,3,2,0:T(8,128)(2,1)S(1)} %copy-done.6, bf16[1,64,4,4,64]{4,1,3,2,0:T(8,128)(2,1)S(1)} %copy-done.7), kind=kOutput, calls=%fused_computation.100 | convolution fusion | flops 299107392 | bytes 5980160 | tf_op jit(solution)/shard_map/sub | solution.py:137
  252.8 3.7 %fusion.15 = bf16[2,64,4,4,64]{4,1,3,2,0:T(8,128)(2,1)S(1)} fusion(bf16[2,1088,4,64,1]{1,3,4,2,0:T(8,128)(2,1)S(1)} %bitcast.69, bf16[2,4,4,64,1088]{4,3,2,1,0:T(8,128)(2,1)} %get-tuple-element.34, f32[2,64,4,4]{1,3,2,0:T(4,128)} %bitcast.76), kind=kOutput, calls=%fused_computation.17 | convolution fusion | flops 285474816 | bytes 5840896 | tf_op jit(solution)/shard_map/shgqk,skhd->shgqd/dot_general | solution.py:139
  257.3 1.4 reverse_select_fusion
  (77 shorter events, 6.4 us)
Async XLA Ops:
  6.5 84.2 %copy-start = (bf16[1,128,2048]{2,1,0:T(8,128)(2,1)S(1)}, bf16[1,128,2048]{2,1,0:T(8,128)(2,1)}, u32[]{:S(2)}) copy-start(bf16[1,128,2048]{2,1,0:T(8,128)(2,1)} %param.4) | copy-start | bytes 1572868
  6.5 84.2 %all-gather.2.cloned.1.call-start = ((), (), s32[]{:S(2)}) async-start(), calls=%async_computation | async-start | bytes 7077888 | tf_op jit(solution)/shard_map/all_gather | solution.py:53
  12.4 83.4 %copy-start.8 = (f32[128,32]{0,1:T(8,128)}, f32[128,32]{0,1:T(8,128)S(1)}, u32[]{:S(2)}) copy-start(f32[128,32]{0,1:T(8,128)S(1)} %get-tuple-element.32) | copy-start | bytes 49156
  96.0 7.0 %collective-permute-start = (bf16[1,64,512]{2,1,0:T(8,128)(2,1)S(1)}, bf16[1,64,512]{2,1,0:T(8,128)(2,1)S(1)}, u32[]{:S(2)}, u32[]{:S(2)}) collective-permute-start(bf16[1,64,512]{2,1,0:T(8,128)(2,1)S(1)} %get-tuple-element.8), channel_id=1, source_target_pairs={{0,1},{1,2},{2,3},{3,4},{4,5},{5,6},{6,7},{7,8},{8,9},{9,10},{10,1... | collective-permute-start | bytes 196616 | tf_op jit(solution)/shard_map/ppermute | solution.py:45
  103.7 16.6 %collective-permute-start.5 = (bf16[1,2,64,512]{3,2,0,1:T(8,128)(2,1)S(1)}, bf16[1,2,64,512]{3,2,0,1:T(8,128)(2,1)S(1)}, u32[]{:S(2)}, u32[]{:S(2)}) collective-permute-start(bf16[1,2,64,512]{3,2,0,1:T(8,128)(2,1)S(1)} %get-tuple-element.30), channel_id=1, source_target_pairs={{1,0},{2,1},{3,2},{4,3},{5,4},{6,5},{7,6},{8,7},{9,8},{10,9},{11,1... | collective-permute-start | bytes 393224 | tf_op jit(solution)/shard_map/ppermute | solution.py:45
  121.0 23.5 %collective-permute-start.6 = (bf16[2,2,64,512]{3,2,0,1:T(8,128)(2,1)}, bf16[2,2,64,512]{3,2,0,1:T(8,128)(2,1)S(1)}, u32[]{:S(2)}, u32[]{:S(2)}) collective-permute-start(bf16[2,2,64,512]{3,2,0,1:T(8,128)(2,1)} %pad_maximum_fusion.12), channel_id=1, source_target_pairs={{2,0},{3,1},{4,2},{5,3},{6,4},{7,5},{8,6},{9,7},{10,8},{11,9},{12,... | collective-permute-start | bytes 786440 | tf_op jit(solution)/shard_map/ppermute | solution.py:45
  124.4 79.9 %collective-permute-start.4 = (bf16[1,64,512]{2,1,0:T(8,128)(2,1)S(1)}, bf16[1,64,512]{2,1,0:T(8,128)(2,1)}, u32[]{:S(2)}, u32[]{:S(2)}) collective-permute-start(bf16[1,64,512]{2,1,0:T(8,128)(2,1)S(1)} %get-tuple-element.8), channel_id=1, source_target_pairs={{0,16},{1,17},{2,18},{3,19},{4,20},{5,21},{6,22},{7,23},{8,24},{9,... | collective-permute-start | bytes 196616 | tf_op jit(solution)/shard_map/ppermute | solution.py:45
  126.5 21.5 %collective-permute-start.1 = (bf16[2,64,512]{2,1,0:T(8,128)(2,1)}, bf16[2,64,512]{2,1,0:T(8,128)(2,1)S(1)}, u32[]{:S(2)}, u32[]{:S(2)}) collective-permute-start(bf16[2,64,512]{2,1,0:T(8,128)(2,1)} %get-tuple-element.29), channel_id=1, source_target_pairs={{0,2},{1,3},{2,4},{3,5},{4,6},{5,7},{6,8},{7,9},{8,10},{9,11},{10,... | collective-permute-start | bytes 393224 | tf_op jit(solution)/shard_map/ppermute | solution.py:45
  145.3 26.9 %collective-permute-start.7 = (bf16[4,2,64,512]{3,2,0,1:T(8,128)(2,1)}, bf16[4,2,64,512]{3,2,0,1:T(8,128)(2,1)S(1)}, u32[]{:S(2)}, u32[]{:S(2)}) collective-permute-start(bf16[4,2,64,512]{3,2,0,1:T(8,128)(2,1)} %pad_maximum_fusion.4), channel_id=1, source_target_pairs={{4,0},{5,1},{6,2},{7,3},{8,4},{9,5},{10,6},{11,7},{12,8},{13,9},{1... | collective-permute-start | bytes 1572872 | tf_op jit(solution)/shard_map/ppermute | solution.py:45
  148.8 26.6 %collective-permute-start.2 = (bf16[4,64,512]{2,1,0:T(8,128)(2,1)}, bf16[4,64,512]{2,1,0:T(8,128)(2,1)}, u32[]{:S(2)}, u32[]{:S(2)}) collective-permute-start(bf16[4,64,512]{2,1,0:T(8,128)(2,1)} %pad_maximum_fusion.11), channel_id=1, source_target_pairs={{0,4},{1,5},{2,6},{3,7},{4,8},{5,9},{6,10},{7,11},{8,12},{9,13},{1... | collective-permute-start | bytes 786440 | tf_op jit(solution)/shard_map/ppermute | solution.py:45
  161.4 74.3 %collective-permute-start.9 = (bf16[1,2,64,512]{3,2,0,1:T(8,128)(2,1)S(1)}, bf16[1,2,64,512]{3,2,0,1:T(8,128)(2,1)}, u32[]{:S(2)}, u32[]{:S(2)}) collective-permute-start(bf16[1,2,64,512]{3,2,0,1:T(8,128)(2,1)S(1)} %get-tuple-element.30), channel_id=1, source_target_pairs={{16,0},{17,1},{18,2},{19,3},{20,4},{21,5},{22,6},{23,7},{24,8},{25... | collective-permute-start | bytes 393224 | tf_op jit(solution)/shard_map/ppermute | solution.py:45
  173.4 59.4 %collective-permute-start.8 = (bf16[8,2,64,512]{3,2,0,1:T(8,128)(2,1)}, bf16[8,2,64,512]{3,2,0,1:T(8,128)(2,1)}, u32[]{:S(2)}, u32[]{:S(2)}) collective-permute-start(bf16[8,2,64,512]{3,2,0,1:T(8,128)(2,1)} %pad_maximum_fusion.2), channel_id=1, source_target_pairs={{8,0},{9,1},{10,2},{11,3},{12,4},{13,5},{14,6},{15,7},{16,8},{17,9... | collective-permute-start | bytes 3145736 | tf_op jit(solution)/shard_map/ppermute | solution.py:45
  176.4 27.9 %collective-permute-start.3 = (bf16[8,64,512]{2,1,0:T(8,128)(2,1)S(1)}, bf16[8,64,512]{2,1,0:T(8,128)(2,1)S(1)}, u32[]{:S(2)}, u32[]{:S(2)}) collective-permute-start(bf16[8,64,512]{2,1,0:T(8,128)(2,1)S(1)} %pad_maximum_fusion.3), channel_id=1, source_target_pairs={{0,8},{1,9},{2,10},{3,11},{4,12},{5,13},{6,14},{7,15},{8,16},{9,17... | collective-permute-start | bytes 1572872 | tf_op jit(solution)/shard_map/ppermute | solution.py:45
  205.2 30.5 %copy-start.1 = (bf16[17,64,512]{2,1,0:T(8,128)(2,1)}, bf16[17,64,512]{2,1,0:T(8,128)(2,1)S(1)}, u32[]{:S(2)}) copy-start(bf16[17,64,512]{2,1,0:T(8,128)(2,1)S(1)} %constant_dynamic-update-slice_fusion) | copy-start | bytes 3342340
  237.3 2.5 copy-start.5
  237.3 2.6 copy-start.3
  240.1 1.9 copy-start.10
  240.1 1.9 copy-start.11
  242.0 2.2 copy-start.2
  244.4 2.2 copy-start.6
  244.4 2.2 copy-start.7
  244.4 2.2 copy-start.9
  246.5 6.3 %copy-start.4 = (bf16[2,1088,256]{1,2,0:T(8,128)(2,1)S(1)}, bf16[2,1088,256]{1,2,0:T(8,128)(2,1)}, u32[]{:S(2)}) copy-start(bf16[2,1088,256]{1,2,0:T(8,128)(2,1)} %copy.26) | copy-start | bytes 3342340
Sparse Core Ops, SparseCore 0:
  9.4 81.2 all-gather.1
where the time goes:
time: 266 us
  waiting for transfers between devices  148 us (56%)
  starting transfers between devices  49.7 us (19%)
  local copies, waits for them, and re-layouts  22.5 us (8%)
  other arithmetic  15.3 us (6%)
  matrix products  15 us (6%)
  between operations  14.6 us (5%)
    all_gather x1, waiting for transfers between devices, body(): lax.all_gather(qkv_weight, 'seq', axis=1, tiled=True)  77.4 us
    ppermute x10, waiting for transfers between devices, moved(): return lax.ppermute(value, 'ctx', pairs)  70.3 us
    ppermute x10, starting transfers between devices, moved(): return lax.ppermute(value, 'ctx', pairs)  49.7 us
    unnamed x32, local copies, waits for them, and re-layouts  6.51 us
    sub x1, matrix products, body(): weights = jnp.where(live, jnp.exp(scores - top), 0.0)  6.27 us
  transfers between devices with their start and end apart: 11, of which 7 were waited for; matrix products, arithmetic and copies ran while one was open for 9% of the time, Pallas kernels for 0%

commit v1 on v0

--- a/solution.py
+++ b/solution.py
@@ -81,8 +81,10 @@
     late_queries = lax.dynamic_slice_in_dim(query_rows, SPAN - offset, SPAN, 0)
 
     count = devices
+    region = range(count - WINDOW // 2, count)
     up = early_rows[None]
-    down = jnp.stack([early_rows, late_rows])[None]
+    down = late_rows[None]
+    mirror = early_rows[None]
     reach = 1
     while reach < WINDOW:
         up = jnp.concatenate(
@@ -91,20 +93,33 @@
         down = jnp.concatenate(
             [down, moved(down, count, [(d, d - reach) for d in range(count)])], axis=0
         )
+        if reach < WINDOW // 2:
+            mirror = jnp.concatenate(
+                [mirror, moved(mirror, count, [(d, d - reach) for d in region if d - reach in region])],
+                axis=0,
+            )
         reach *= 2
     up = jnp.concatenate(
         [up, moved(early_rows[None], count, [(d, d + WINDOW) for d in range(count)])], axis=0
     )
     down = jnp.concatenate(
-        [down, moved(down[:1], count, [(d, d - WINDOW) for d in range(count)])], axis=0
+        [down, moved(late_rows[None], count, [(d, d - WINDOW) for d in range(count)])], axis=0
     )
+    crossed = moved(mirror, count, [(d, 2 * count - 1 - WINDOW - d) for d in region])
+    inside = my_index >= count - WINDOW // 2
+    mirror = jnp.where(inside, mirror, crossed)
+    base = jnp.where(inside, my_index, 2 * count - 1 - WINDOW - my_index)
+    around = jnp.concatenate([up, mirror, down], axis=0)
+    steps = jnp.arange(WINDOW + 1, dtype=jnp.int32)
+    target = 2 * count - 1 - my_index - steps
+    pick = jnp.where(
+        my_index + steps <= count - 1,
+        up.shape[0] + mirror.shape[0] + steps,
+        jnp.where(target >= base, up.shape[0] + target - base, my_index - target),
+    )
+    pick = jnp.clip(pick, 0, around.shape[0] - 1)
     early_keys = up.reshape(-1, up.shape[-1])
-    around = jnp.concatenate([up[::-1], down[1:, 0]], axis=0)
-    steps = jnp.arange(WINDOW + 1, dtype=jnp.int32)
-    mirror = jnp.clip(2 * count - 1 - 2 * my_index - steps + WINDOW, 0, 2 * WINDOW)
-    late_keys = jnp.where(
-        (my_index + steps <= count - 1)[:, None, None], down[:, 1], jnp.take(around, mirror, axis=0)
-    ).reshape(-1, up.shape[-1])
+    late_keys = jnp.take(around, pick, axis=0).reshape(-1, up.shape[-1])
     key_blocks = jnp.stack([early_keys, late_keys])
 
     steps = jnp.arange(WINDOW + 1, dtype=jnp.int32)

time: 266 us -> 288 us (1.083)
  waiting for transfers between devices: 148 us -> 178 us
  local copies, waits for them, and re-layouts: 22.5 us -> 16.4 us
  other arithmetic: 15.3 us -> 11.7 us
    ppermute x10 -> x14, waiting for transfers between devices: 70.3 us -> 97.8 us  [moved(): return lax.ppermute(value, 'ctx', pairs)]
    ppermute x10 -> x14, starting transfers between devices: 49.7 us -> 51 us  [moved(): return lax.ppermute(value, 'ctx', pairs)]
    unnamed x32 -> x19, local copies, waits for them, and re-layouts: 6.51 us -> 7.53 us
  transfers between devices with their start and end apart: 11 -> 15, of which waited for: 7 -> 9; matrix products, arithmetic and copies ran while one was open for 9% -> 5% of each run, Pallas kernels for 0% -> 0%
where the time goes in v1:
time: 288 us; the launch traced here: 287 us
  waiting for transfers between devices  178 us (62%)
  starting transfers between devices  51 us (18%)
  local copies, waits for them, and re-layouts  16.4 us (6%)
  matrix products  15.4 us (5%)
  between operations  14.5 us (5%)
  other arithmetic  11.7 us (4%)
    ppermute x14, waiting for transfers between devices, moved(): return lax.ppermute(value, 'ctx', pairs)  97.8 us
    all_gather x1, waiting for transfers between devices, body(): lax.all_gather(qkv_weight, 'seq', axis=1, tiled=True)  79.9 us
    ppermute x14, starting transfers between devices, moved(): return lax.ppermute(value, 'ctx', pairs)  51 us
    unnamed x19, local copies, waits for them, and re-layouts  7.53 us
    sub x1, matrix products, body(): weights = jnp.where(live, jnp.exp(scores - top), 0.0)  6.67 us
  transfers between devices with their start and end apart: 15, of which 9 were waited for; matrix products, arithmetic and copies ran while one was open for 5% of the time, Pallas kernels for 0%

profile of v1, /device:TPU:62, one launch (start us, length us, event | category | flops | bytes accessed | tf_op | source)
XLA Modules:
  0.0 287.3 jit_solution(10059558451414486897)
XLA Ops:
  6.5 0.7 all-gather.2.cloned.1.call-update
  7.3 1.3 fusion.45
  8.6 0.7 multiply_bitcast_fusion
  10.7 79.9 %all-gather.2.cloned.1.call-done = bf16[2048,1536]{0,1:T(8,128)(2,1)} async-done(((bf16[2048,192]{0,1:T(8,128)(2,1)}), bf16[2048,1536]{0,1:T(8,128)(2,1)}) %all-gather.2.cloned.1.call-update) | async-done | bytes 6291472 | tf_op jit(solution)/shard_map/all_gather | solution.py:53
  90.7 5.0 %convolution_convert_fusion = bf16[128,1536]{1,0:T(8,128)(2,1)S(1)} fusion(bf16[2048,1536]{0,1:T(8,128)(2,1)} %all-gather.2.cloned.1.call-done, bf16[1,128,2048]{2,1,0:T(8,128)(2,1)S(1)} %copy-done), kind=kOutput, calls=%fused_computation.10 | convolution fusion | flops 805502976 | bytes 7208960 | tf_op jit(solution)/shard_map/dot_general | solution.py:51
  96.0 5.1 %collective-permute-start = (bf16[1,64,512]{2,1,0:T(8,128)(2,1)S(1)}, bf16[1,64,512]{2,1,0:T(8,128)(2,1)S(1)}, u32[]{:S(2)}, u32[]{:S(2)}) collective-permute-start(bf16[1,64,512]{2,1,0:T(8,128)(2,1)S(1)} %get-tuple-element.8), channel_id=1, source_target_pairs={{0,1},{1,2},{2,3},{3,4},{4,5},{5,6},{6,7},{7,8},{8,9},{9,10},{10,1... | collective-permute-start | bytes 196616 | tf_op jit(solution)/shard_map/ppermute | solution.py:45
  101.1 0.7 collective-permute-start.5
  101.8 1.2 collective-permute-done
  103.0 5.2 %collective-permute-start.1 = (bf16[2,64,512]{2,1,0:T(8,128)(2,1)S(1)}, bf16[2,64,512]{2,1,0:T(8,128)(2,1)S(1)}, u32[]{:S(2)}, u32[]{:S(2)}) collective-permute-start(bf16[2,64,512]{2,1,0:T(8,128)(2,1)S(1)} %get-tuple-element.36), channel_id=1, source_target_pairs={{0,2},{1,3},{2,4},{3,5},{4,6},{5,7},{6,8},{7,9},{8,10},{9,11},{10,... | collective-permute-start | bytes 393224 | tf_op jit(solution)/shard_map/ppermute | solution.py:45
  108.2 0.7 collective-permute-start.6
  109.0 2.4 collective-permute-done.1
  111.4 0.7 fusion.27
  112.1 4.3 %collective-permute-start.2 = (bf16[4,64,512]{2,1,0:T(8,128)(2,1)}, bf16[4,64,512]{2,1,0:T(8,128)(2,1)S(1)}, u32[]{:S(2)}, u32[]{:S(2)}) collective-permute-start(bf16[4,64,512]{2,1,0:T(8,128)(2,1)} %get-tuple-element.34), channel_id=1, source_target_pairs={{0,4},{1,5},{2,6},{3,7},{4,8},{5,9},{6,10},{7,11},{8,12},{9,13},{1... | collective-permute-start | bytes 786440 | tf_op jit(solution)/shard_map/ppermute | solution.py:45
  116.4 0.7 collective-permute-start.7
  118.0 4.0 %collective-permute-done.2 = bf16[4,64,512]{2,1,0:T(8,128)(2,1)S(1)} collective-permute-done((bf16[4,64,512]{2,1,0:T(8,128)(2,1)}, bf16[4,64,512]{2,1,0:T(8,128)(2,1)S(1)}, u32[]{:S(2)}, u32[]{:S(2)}) %collective-permute-start.2) | collective-permute-done | bytes 262176 | tf_op jit(solution)/shard_map/ppermute | solution.py:45
  122.0 1.1 fusion.22
  123.1 3.8 %collective-permute-start.3 = (bf16[8,64,512]{2,1,0:T(8,128)(2,1)}, bf16[8,64,512]{2,1,0:T(8,128)(2,1)}, u32[]{:S(2)}, u32[]{:S(2)}) collective-permute-start(bf16[8,64,512]{2,1,0:T(8,128)(2,1)} %get-tuple-element.32), channel_id=1, source_target_pairs={{0,8},{1,9},{2,10},{3,11},{4,12},{5,13},{6,14},{7,15},{8,16},{9,17... | collective-permute-start | bytes 1572872 | tf_op jit(solution)/shard_map/ppermute | solution.py:45
  126.9 0.9 and_and_fusion
  127.7 12.3 %collective-permute-start.4 = (bf16[1,64,512]{2,1,0:T(8,128)(2,1)S(1)}, bf16[1,64,512]{2,1,0:T(8,128)(2,1)S(1)}, u32[]{:S(2)}, u32[]{:S(2)}) collective-permute-start(bf16[1,64,512]{2,1,0:T(8,128)(2,1)S(1)} %get-tuple-element.8), channel_id=1, source_target_pairs={{0,16},{1,17},{2,18},{3,19},{4,20},{5,21},{6,22},{7,23},{8,24},{9,... | collective-permute-start | bytes 196616 | tf_op jit(solution)/shard_map/ppermute | solution.py:45
  140.7 0.7 collective-permute-start.8
  141.4 0.6 constant_dynamic-update-slice_fusion.4
  142.1 0.7 constant_dynamic-update-slice_fusion.3
  142.7 0.7 constant_dynamic-update-slice_fusion.2
  143.5 5.9 %collective-permute-done.3 = bf16[8,64,512]{2,1,0:T(8,128)(2,1)} collective-permute-done((bf16[8,64,512]{2,1,0:T(8,128)(2,1)}, bf16[8,64,512]{2,1,0:T(8,128)(2,1)}, u32[]{:S(2)}, u32[]{:S(2)}) %collective-permute-start.3) | collective-permute-done | bytes 524320 | tf_op jit(solution)/shard_map/ppermute | solution.py:45
  149.3 1.9 constant_dynamic-update-slice_fusion.1
  151.9 1.1 select_dynamic-update-slice_fusion
  153.0 0.6 constant_dynamic-update-slice_fusion.11
  153.7 9.9 %collective-permute-start.9 = (bf16[1,64,512]{2,1,0:T(8,128)(2,1)S(1)}, bf16[1,64,512]{2,1,0:T(8,128)(2,1)S(1)}, u32[]{:S(2)}, u32[]{:S(2)}) collective-permute-start(bf16[1,64,512]{2,1,0:T(8,128)(2,1)S(1)} %get-tuple-element.10), channel_id=1, source_target_pairs={{1,0},{2,1},{3,2},{4,3},{5,4},{6,5},{7,6},{8,7},{9,8},{10,9},{11,1... | collective-permute-start | bytes 196616 | tf_op jit(solution)/shard_map/ppermute | solution.py:45
  163.6 30.1 %collective-permute-done.9 = bf16[1,64,512]{2,1,0:T(8,128)(2,1)S(1)} collective-permute-done((bf16[1,64,512]{2,1,0:T(8,128)(2,1)S(1)}, bf16[1,64,512]{2,1,0:T(8,128)(2,1)S(1)}, u32[]{:S(2)}, u32[]{:S(2)}) %collective-permute-start.9) | collective-permute-done | bytes 65568 | tf_op jit(solution)/shard_map/ppermute | solution.py:45
  193.7 1.9 collective-permute-start.10
  195.8 14.9 %collective-permute-done.10 = bf16[2,64,512]{2,1,0:T(8,128)(2,1)S(1)} collective-permute-done((bf16[2,64,512]{2,1,0:T(8,128)(2,1)S(1)}, bf16[2,64,512]{2,1,0:T(8,128)(2,1)S(1)}, u32[]{:S(2)}, u32[]{:S(2)}) %collective-permute-start.10) | collective-permute-done | bytes 131104 | tf_op jit(solution)/shard_map/ppermute | solution.py:45
  210.7 1.9 collective-permute-start.11
  213.0 14.1 %collective-permute-done.11 = bf16[4,64,512]{2,1,0:T(8,128)(2,1)S(1)} collective-permute-done((bf16[4,64,512]{2,1,0:T(8,128)(2,1)S(1)}, bf16[4,64,512]{2,1,0:T(8,128)(2,1)S(1)}, u32[]{:S(2)}, u32[]{:S(2)}) %collective-permute-start.11) | collective-permute-done | bytes 262176 | tf_op jit(solution)/shard_map/ppermute | solution.py:45
  227.0 0.8 pad_maximum_fusion.3
  227.9 1.9 collective-permute-start.12
  230.2 0.9 copy.25
  231.1 1.9 collective-permute-start.13
  233.6 0.7 constant_dynamic-update-slice_fusion.9
  234.3 0.7 constant_dynamic-update-slice_fusion.8
  235.0 25.2 %collective-permute-done.12 = bf16[8,64,512]{2,1,0:T(8,128)(2,1)S(1)} collective-permute-done((bf16[8,64,512]{2,1,0:T(8,128)(2,1)}, bf16[8,64,512]{2,1,0:T(8,128)(2,1)S(1)}, u32[]{:S(2)}, u32[]{:S(2)}) %collective-permute-start.12) | collective-permute-done | bytes 524320 | tf_op jit(solution)/shard_map/ppermute | solution.py:45
  260.2 0.9 constant_dynamic-update-slice_fusion.7
  261.7 2.4 gather_fusion
  264.3 1.4 fusion.18
  265.7 1.4 copy.27
  267.2 0.7 copy.21
  267.9 6.7 %fusion.46 = (f32[2,4,4,64]{3,2,1,0:T(4,128)S(1)}, bf16[2,4,4,64,1088]{4,3,2,1,0:T(8,128)(2,1)}) fusion(pred[2,64,1088]{2,1,0:T(8,128)(4,1)} %and_and_fusion, bf16[2,1088,4,64,1]{1,3,4,2,0:T(8,128)(2,1)S(1)} %bitcast.61, bf16[1,64,4,4,64]{4,1,3,2,0:T(8,128)(2,1)S(1)} %copy.26, bf16[1,64,4,4,64]{4,1,3,2,0:T(8,128)(2,1)S(1)} %copy-done.3), kind=kOutput, calls=%fused_computation.111 | convolution fusion | flops 299107392 | bytes 5980160 | tf_op jit(solution)/shard_map/sub | solution.py:152
  274.6 3.7 %fusion.15 = bf16[2,64,4,4,64]{4,1,3,2,0:T(8,128)(2,1)S(1)} fusion(bf16[2,1088,4,64,1]{1,3,4,2,0:T(8,128)(2,1)S(1)} %bitcast.60, bf16[2,4,4,64,1088]{4,3,2,1,0:T(8,128)(2,1)} %get-tuple-element.40, f32[2,64,4,4]{1,3,2,0:T(4,128)S(1)} %bitcast.67), kind=kOutput, calls=%fused_computation.16 | convolution fusion | flops 285474816 | bytes 5840896 | tf_op jit(solution)/shard_map/shgqk,skhd->shgqd/dot_general | solution.py:154
  279.0 1.4 reverse_select_fusion
  (65 shorter events, 6.5 us)
Async XLA Ops:
  6.5 84.1 %copy-start = (bf16[1,128,2048]{2,1,0:T(8,128)(2,1)S(1)}, bf16[1,128,2048]{2,1,0:T(8,128)(2,1)}, u32[]{:S(2)}) copy-start(bf16[1,128,2048]{2,1,0:T(8,128)(2,1)} %param.4) | copy-start | bytes 1572868
  6.5 84.1 %all-gather.2.cloned.1.call-start = ((), (), s32[]{:S(2)}) async-start(), calls=%async_computation | async-start | bytes 7077888 | tf_op jit(solution)/shard_map/all_gather | solution.py:53
  95.6 21.5 %copy-start.4 = (s32[1,36]{1,0:T(1,128)S(1)}, s32[1,36]{1,0:T(1,128)}, u32[]{:S(2)}) copy-start(s32[1,36]{1,0:T(1,128)} %param.6) | copy-start | bytes 436
  96.0 7.0 %collective-permute-start = (bf16[1,64,512]{2,1,0:T(8,128)(2,1)S(1)}, bf16[1,64,512]{2,1,0:T(8,128)(2,1)S(1)}, u32[]{:S(2)}, u32[]{:S(2)}) collective-permute-start(bf16[1,64,512]{2,1,0:T(8,128)(2,1)S(1)} %get-tuple-element.8), channel_id=1, source_target_pairs={{0,1},{1,2},{2,3},{3,4},{4,5},{5,6},{6,7},{7,8},{8,9},{9,10},{10,1... | collective-permute-start | bytes 196616 | tf_op jit(solution)/shard_map/ppermute | solution.py:45
  101.1 1.9 collective-permute-start.5
  103.0 8.4 %collective-permute-start.1 = (bf16[2,64,512]{2,1,0:T(8,128)(2,1)S(1)}, bf16[2,64,512]{2,1,0:T(8,128)(2,1)S(1)}, u32[]{:S(2)}, u32[]{:S(2)}) collective-permute-start(bf16[2,64,512]{2,1,0:T(8,128)(2,1)S(1)} %get-tuple-element.36), channel_id=1, source_target_pairs={{0,2},{1,3},{2,4},{3,5},{4,6},{5,7},{6,8},{7,9},{8,10},{9,11},{10,... | collective-permute-start | bytes 393224 | tf_op jit(solution)/shard_map/ppermute | solution.py:45
  108.2 3.2 %collective-permute-start.6 = (bf16[2,64,512]{2,1,0:T(8,128)(2,1)S(1)}, bf16[2,64,512]{2,1,0:T(8,128)(2,1)S(1)}, u32[]{:S(2)}, u32[]{:S(2)}) collective-permute-start(bf16[2,64,512]{2,1,0:T(8,128)(2,1)S(1)} %get-tuple-element.35), channel_id=1, source_target_pairs={{58,56},{59,57},{60,58},{61,59},{62,60},{63,61},{122,120},{123,121... | collective-permute-start | bytes 393224 | tf_op jit(solution)/shard_map/ppermute | solution.py:45
  112.1 9.9 %collective-permute-start.2 = (bf16[4,64,512]{2,1,0:T(8,128)(2,1)}, bf16[4,64,512]{2,1,0:T(8,128)(2,1)S(1)}, u32[]{:S(2)}, u32[]{:S(2)}) collective-permute-start(bf16[4,64,512]{2,1,0:T(8,128)(2,1)} %get-tuple-element.34), channel_id=1, source_target_pairs={{0,4},{1,5},{2,6},{3,7},{4,8},{5,9},{6,10},{7,11},{8,12},{9,13},{1... | collective-permute-start | bytes 786440 | tf_op jit(solution)/shard_map/ppermute | solution.py:45
  116.4 5.6 %collective-permute-start.7 = (bf16[4,64,512]{2,1,0:T(8,128)(2,1)S(1)}, bf16[4,64,512]{2,1,0:T(8,128)(2,1)S(1)}, u32[]{:S(2)}, u32[]{:S(2)}) collective-permute-start(bf16[4,64,512]{2,1,0:T(8,128)(2,1)S(1)} %get-tuple-element.33), channel_id=1, source_target_pairs={{60,56},{61,57},{62,58},{63,59},{124,120},{125,121},{126,122},{127... | collective-permute-start | bytes 786440 | tf_op jit(solution)/shard_map/ppermute | solution.py:45
  123.1 26.2 %collective-permute-start.3 = (bf16[8,64,512]{2,1,0:T(8,128)(2,1)}, bf16[8,64,512]{2,1,0:T(8,128)(2,1)}, u32[]{:S(2)}, u32[]{:S(2)}) collective-permute-start(bf16[8,64,512]{2,1,0:T(8,128)(2,1)} %get-tuple-element.32), channel_id=1, source_target_pairs={{0,8},{1,9},{2,10},{3,11},{4,12},{5,13},{6,14},{7,15},{8,16},{9,17... | collective-permute-start | bytes 1572872 | tf_op jit(solution)/shard_map/ppermute | solution.py:45
  127.7 23.6 %collective-permute-start.4 = (bf16[1,64,512]{2,1,0:T(8,128)(2,1)S(1)}, bf16[1,64,512]{2,1,0:T(8,128)(2,1)S(1)}, u32[]{:S(2)}, u32[]{:S(2)}) collective-permute-start(bf16[1,64,512]{2,1,0:T(8,128)(2,1)S(1)} %get-tuple-element.8), channel_id=1, source_target_pairs={{0,16},{1,17},{2,18},{3,19},{4,20},{5,21},{6,22},{7,23},{8,24},{9,... | collective-permute-start | bytes 196616 | tf_op jit(solution)/shard_map/ppermute | solution.py:45
  140.7 11.2 %collective-permute-start.8 = (bf16[8,64,512]{2,1,0:T(8,128)(2,1)}, bf16[8,64,512]{2,1,0:T(8,128)(2,1)S(1)}, u32[]{:S(2)}, u32[]{:S(2)}) collective-permute-start(bf16[8,64,512]{2,1,0:T(8,128)(2,1)} %get-tuple-element.31), channel_id=1, source_target_pairs={{56,55},{57,54},{58,53},{59,52},{60,51},{61,50},{62,49},{63,48},{1... | collective-permute-start | bytes 1572872 | tf_op jit(solution)/shard_map/ppermute | solution.py:45
  151.9 75.9 %copy-start.1 = (bf16[17,64,512]{2,1,0:T(8,128)(2,1)}, bf16[17,64,512]{2,1,0:T(8,128)(2,1)S(1)}, u32[]{:S(2)}) copy-start(bf16[17,64,512]{2,1,0:T(8,128)(2,1)S(1)} %get-tuple-element.27) | copy-start | bytes 3342340
  153.7 40.0 %collective-permute-start.9 = (bf16[1,64,512]{2,1,0:T(8,128)(2,1)S(1)}, bf16[1,64,512]{2,1,0:T(8,128)(2,1)S(1)}, u32[]{:S(2)}, u32[]{:S(2)}) collective-permute-start(bf16[1,64,512]{2,1,0:T(8,128)(2,1)S(1)} %get-tuple-element.10), channel_id=1, source_target_pairs={{1,0},{2,1},{3,2},{4,3},{5,4},{6,5},{7,6},{8,7},{9,8},{10,9},{11,1... | collective-permute-start | bytes 196616 | tf_op jit(solution)/shard_map/ppermute | solution.py:45
  193.7 17.0 %collective-permute-start.10 = (bf16[2,64,512]{2,1,0:T(8,128)(2,1)S(1)}, bf16[2,64,512]{2,1,0:T(8,128)(2,1)S(1)}, u32[]{:S(2)}, u32[]{:S(2)}) collective-permute-start(bf16[2,64,512]{2,1,0:T(8,128)(2,1)S(1)} %pad_maximum_fusion.16), channel_id=1, source_target_pairs={{2,0},{3,1},{4,2},{5,3},{6,4},{7,5},{8,6},{9,7},{10,8},{11,9},{12,... | collective-permute-start | bytes 393224 | tf_op jit(solution)/shard_map/ppermute | solution.py:45
  210.7 16.3 %collective-permute-start.11 = (bf16[4,64,512]{2,1,0:T(8,128)(2,1)S(1)}, bf16[4,64,512]{2,1,0:T(8,128)(2,1)S(1)}, u32[]{:S(2)}, u32[]{:S(2)}) collective-permute-start(bf16[4,64,512]{2,1,0:T(8,128)(2,1)S(1)} %pad_maximum_fusion.12), channel_id=1, source_target_pairs={{4,0},{5,1},{6,2},{7,3},{8,4},{9,5},{10,6},{11,7},{12,8},{13,9},{1... | collective-permute-start | bytes 786440 | tf_op jit(solution)/shard_map/ppermute | solution.py:45
  227.9 32.3 %collective-permute-start.12 = (bf16[8,64,512]{2,1,0:T(8,128)(2,1)}, bf16[8,64,512]{2,1,0:T(8,128)(2,1)S(1)}, u32[]{:S(2)}, u32[]{:S(2)}) collective-permute-start(bf16[8,64,512]{2,1,0:T(8,128)(2,1)} %pad_maximum_fusion.3), channel_id=1, source_target_pairs={{8,0},{9,1},{10,2},{11,3},{12,4},{13,5},{14,6},{15,7},{16,8},{17,9... | collective-permute-start | bytes 1572872 | tf_op jit(solution)/shard_map/ppermute | solution.py:45
  231.1 30.0 %collective-permute-start.13 = (bf16[1,64,512]{2,1,0:T(8,128)(2,1)S(1)}, bf16[1,64,512]{2,1,0:T(8,128)(2,1)S(1)}, u32[]{:S(2)}, u32[]{:S(2)}) collective-permute-start(bf16[1,64,512]{2,1,0:T(8,128)(2,1)S(1)} %get-tuple-element.10), channel_id=1, source_target_pairs={{16,0},{17,1},{18,2},{19,3},{20,4},{21,5},{22,6},{23,7},{24,8},{25... | collective-permute-start | bytes 196616 | tf_op jit(solution)/shard_map/ppermute | solution.py:45
  265.7 2.1 copy-start.3
  267.9 6.7 %copy-start.2 = (bf16[2,1088,256]{1,2,0:T(8,128)(2,1)S(1)}, bf16[2,1088,256]{1,2,0:T(8,128)(2,1)}, u32[]{:S(2)}) copy-start(bf16[2,1088,256]{1,2,0:T(8,128)(2,1)} %copy.27) | copy-start | bytes 3342340
Sparse Core Ops, SparseCore 0:
  9.4 81.1 all-gather.1

commit v2 on v0

--- a/solution.py
+++ b/solution.py
@@ -88,16 +88,24 @@
         up = jnp.concatenate(
             [up, moved(up, count, [(d, d + reach) for d in range(count)])], axis=0
         )
-        down = jnp.concatenate(
-            [down, moved(down, count, [(d, d - reach) for d in range(count)])], axis=0
-        )
+        if 2 * reach < WINDOW:
+            got = moved(down, count, [(d, d - reach) for d in range(count)])
+        else:
+            tail = range(count - reach, count)
+            got = jnp.stack(
+                [
+                    moved(down[:, 0], count, [(d, d - reach) for d in tail]),
+                    moved(down[:, 1], count, [(d, d - reach) for d in range(count)]),
+                ],
+                axis=1,
+            )
+        down = jnp.concatenate([down, got], axis=0)
         reach *= 2
     up = jnp.concatenate(
         [up, moved(early_rows[None], count, [(d, d + WINDOW) for d in range(count)])], axis=0
     )
-    down = jnp.concatenate(
-        [down, moved(down[:1], count, [(d, d - WINDOW) for d in range(count)])], axis=0
-    )
+    far = moved(late_rows[None], count, [(d, d - WINDOW) for d in range(count)])
+    down = jnp.concatenate([down, jnp.stack([jnp.zeros_like(far), far], axis=1)], axis=0)
     early_keys = up.reshape(-1, up.shape[-1])
     around = jnp.concatenate([up[::-1], down[1:, 0]], axis=0)
     steps = jnp.arange(WINDOW + 1, dtype=jnp.int32)

time: 266 us -> 240 us (0.902)
  the two profiles are of different devices: /device:TPU:62 before, /device:TPU:56 now
where the time goes in v2:
time: 240 us; the launch traced here: 239 us
  waiting for transfers between devices  125 us (52%)
  starting transfers between devices  52.5 us (22%)
  local copies, waits for them, and re-layouts  19.1 us (8%)
  matrix products  14.9 us (6%)
  between operations  14.5 us (6%)
  other arithmetic  12.3 us (5%)
    all_gather x1, waiting for transfers between devices, body(): lax.all_gather(qkv_weight, 'seq', axis=1, tiled=True)  76.2 us
    ppermute x11, starting transfers between devices, moved(): return lax.ppermute(value, 'ctx', pairs)  52.5 us
    ppermute x11, waiting for transfers between devices, moved(): return lax.ppermute(value, 'ctx', pairs)  48.4 us
    sub x1, matrix products, body(): weights = jnp.where(live, jnp.exp(scores - top), 0.0)  6.26 us
    dot_general x1, matrix products, body(): jnp.dot(rows, lax.all_gather(qkv_weight, 'seq', axis=1, tiled=True), pref...  4.97 us
  transfers between devices with their start and end apart: 12, of which 4 were waited for; matrix products, arithmetic and copies ran while one was open for 8% of the time, Pallas kernels for 0%

profile of v2, /device:TPU:56, one launch (start us, length us, event | category | flops | bytes accessed | tf_op | source)
XLA Modules:
  0.0 238.5 jit_solution(5053498593622495443)
XLA Ops:
  6.5 0.7 all-gather.2.cloned.1.call-update
  7.3 1.3 fusion.42
  8.5 0.7 multiply_bitcast_fusion
  10.1 0.7 broadcast_in_dim.86
  10.9 0.7 broadcast_in_dim.82
  11.9 0.8 copy.30
  13.2 0.6 pad_clamp_fusion
  14.0 0.2 fusion.24
  14.4 0.2 and_and_fusion
  14.6 76.2 %all-gather.2.cloned.1.call-done = bf16[2048,1536]{0,1:T(8,128)(2,1)} async-done(((bf16[2048,192]{0,1:T(8,128)(2,1)}), bf16[2048,1536]{0,1:T(8,128)(2,1)}) %all-gather.2.cloned.1.call-update) | async-done | bytes 6291472 | tf_op jit(solution)/shard_map/all_gather | solution.py:53
  90.8 5.0 %convolution_convert_fusion = bf16[128,1536]{1,0:T(8,128)(2,1)S(1)} fusion(bf16[2048,1536]{0,1:T(8,128)(2,1)} %all-gather.2.cloned.1.call-done, bf16[1,128,2048]{2,1,0:T(8,128)(2,1)S(1)} %copy-done), kind=kOutput, calls=%fused_computation.10 | convolution fusion | flops 805502976 | bytes 7208960 | tf_op jit(solution)/shard_map/dot_general | solution.py:51
  96.1 3.4 %collective-permute-start = (bf16[1,64,512]{2,1,0:T(8,128)(2,1)S(1)}, bf16[1,64,512]{2,1,0:T(8,128)(2,1)S(1)}, u32[]{:S(2)}, u32[]{:S(2)}) collective-permute-start(bf16[1,64,512]{2,1,0:T(8,128)(2,1)S(1)} %get-tuple-element.8), channel_id=1, source_target_pairs={{0,1},{1,2},{2,3},{3,4},{4,5},{5,6},{6,7},{7,8},{8,9},{9,10},{10,1... | collective-permute-start | bytes 196616 | tf_op jit(solution)/shard_map/ppermute | solution.py:45
  99.5 7.9 %collective-permute-start.4 = (bf16[1,64,512]{2,1,0:T(8,128)(2,1)S(1)}, bf16[1,64,512]{2,1,0:T(8,128)(2,1)}, u32[]{:S(2)}, u32[]{:S(2)}) collective-permute-start(bf16[1,64,512]{2,1,0:T(8,128)(2,1)S(1)} %get-tuple-element.8), channel_id=1, source_target_pairs={{0,16},{1,17},{2,18},{3,19},{4,20},{5,21},{6,22},{7,23},{8,24},{9,... | collective-permute-start | bytes 196616 | tf_op jit(solution)/shard_map/ppermute | solution.py:45
  107.5 2.4 %collective-permute-start.10 = (bf16[1,64,512]{2,1,0:T(8,128)(2,1)S(1)}, bf16[1,64,512]{2,1,0:T(8,128)(2,1)}, u32[]{:S(2)}, u32[]{:S(2)}) collective-permute-start(bf16[1,64,512]{2,1,0:T(8,128)(2,1)S(1)} %fusion.28), channel_id=1, source_target_pairs={{16,0},{17,1},{18,2},{19,3},{20,4},{21,5},{22,6},{23,7},{24,8},{25... | collective-permute-start | bytes 196616 | tf_op jit(solution)/shard_map/ppermute | solution.py:45
  109.9 0.2 copy.44
  110.1 0.7 constant_dynamic-update-slice_fusion.7
  110.8 4.6 %collective-permute-start.5 = (bf16[1,2,64,512]{3,2,0,1:T(8,128)(2,1)S(1)}, bf16[1,2,64,512]{3,2,0,1:T(8,128)(2,1)S(1)}, u32[]{:S(2)}, u32[]{:S(2)}) collective-permute-start(bf16[1,2,64,512]{3,2,0,1:T(8,128)(2,1)S(1)} %get-tuple-element.30), channel_id=1, source_target_pairs={{1,0},{2,1},{3,2},{4,3},{5,4},{6,5},{7,6},{8,7},{9,8},{10,9},{11,1... | collective-permute-start | bytes 393224 | tf_op jit(solution)/shard_map/ppermute | solution.py:45
  115.5 2.8 %collective-permute-start.1 = (bf16[2,64,512]{2,1,0:T(8,128)(2,1)S(1)}, bf16[2,64,512]{2,1,0:T(8,128)(2,1)S(1)}, u32[]{:S(2)}, u32[]{:S(2)}) collective-permute-start(bf16[2,64,512]{2,1,0:T(8,128)(2,1)S(1)} %get-tuple-element.33), channel_id=1, source_target_pairs={{0,2},{1,3},{2,4},{3,5},{4,6},{5,7},{6,8},{7,9},{8,10},{9,11},{10,... | collective-permute-start | bytes 393224 | tf_op jit(solution)/shard_map/ppermute | solution.py:45
  118.3 0.7 pad_maximum_fusion.13
  119.0 5.5 %collective-permute-start.6 = (bf16[2,2,64,512]{3,2,1,0:T(8,128)(2,1)}, bf16[2,2,64,512]{3,2,1,0:T(8,128)(2,1)S(1)}, u32[]{:S(2)}, u32[]{:S(2)}) collective-permute-start(bf16[2,2,64,512]{3,2,1,0:T(8,128)(2,1)} %pad_maximum_fusion.13), channel_id=1, source_target_pairs={{2,0},{3,1},{4,2},{5,3},{6,4},{7,5},{8,6},{9,7},{10,8},{11,9},{12,... | collective-permute-start | bytes 786440 | tf_op jit(solution)/shard_map/ppermute | solution.py:45
  124.5 0.2 constant_dynamic-slice_fusion.1
  124.9 0.9 copy.47
  125.8 17.2 %collective-permute-start.2 = (bf16[4,64,512]{2,1,0:T(8,128)(2,1)S(1)}, bf16[4,64,512]{2,1,0:T(8,128)(2,1)S(1)}, u32[]{:S(2)}, u32[]{:S(2)}) collective-permute-start(bf16[4,64,512]{2,1,0:T(8,128)(2,1)S(1)} %pad_maximum_fusion.12), channel_id=1, source_target_pairs={{0,4},{1,5},{2,6},{3,7},{4,8},{5,9},{6,10},{7,11},{8,12},{9,13},{1... | collective-permute-start | bytes 786440 | tf_op jit(solution)/shard_map/ppermute | solution.py:45
  143.1 1.9 collective-permute-start.7
  145.0 0.7 constant_dynamic-update-slice_fusion.6
  145.7 3.2 %collective-permute-done.2 = bf16[4,64,512]{2,1,0:T(8,128)(2,1)S(1)} collective-permute-done((bf16[4,64,512]{2,1,0:T(8,128)(2,1)S(1)}, bf16[4,64,512]{2,1,0:T(8,128)(2,1)S(1)}, u32[]{:S(2)}, u32[]{:S(2)}) %collective-permute-start.2) | collective-permute-done | bytes 262176 | tf_op jit(solution)/shard_map/ppermute | solution.py:45
  148.9 3.4 %collective-permute-start.3 = (bf16[8,64,512]{2,1,0:T(8,128)(2,1)S(1)}, bf16[8,64,512]{2,1,0:T(8,128)(2,1)S(1)}, u32[]{:S(2)}, u32[]{:S(2)}) collective-permute-start(bf16[8,64,512]{2,1,0:T(8,128)(2,1)S(1)} %pad_maximum_fusion.4), channel_id=1, source_target_pairs={{0,8},{1,9},{2,10},{3,11},{4,12},{5,13},{6,14},{7,15},{8,16},{9,17... | collective-permute-start | bytes 1572872 | tf_op jit(solution)/shard_map/ppermute | solution.py:45
  152.4 0.8 copy_dynamic-update-slice_fusion.3
  153.2 19.3 %collective-permute-done.7 = bf16[4,2,64,512]{3,2,1,0:T(8,128)(2,1)S(1)} collective-permute-done((bf16[4,2,64,512]{3,2,1,0:T(8,128)(2,1)S(1)}, bf16[4,2,64,512]{3,2,1,0:T(8,128)(2,1)S(1)}, u32[]{:S(2)}, u32[]{:S(2)}) %collective-permute-start.7) | collective-permute-done | bytes 524320 | tf_op jit(solution)/shard_map/ppermute | solution.py:45
  172.6 1.1 slice_bitcast_fusion.2
  173.7 1.9 collective-permute-start.9
  175.6 1.5 collective-permute-start.8
  177.2 0.8 constant_dynamic-update-slice_fusion
  178.0 1.2 rev.6
  179.2 1.1 copy_dynamic-update-slice_fusion.1
  180.3 25.9 %collective-permute-done.9 = bf16[8,64,512]{2,1,0:T(8,128)(2,1)S(1)} collective-permute-done((bf16[8,64,512]{2,1,0:T(8,128)(2,1)}, bf16[8,64,512]{2,1,0:T(8,128)(2,1)S(1)}, u32[]{:S(2)}, u32[]{:S(2)}) %collective-permute-start.9) | collective-permute-done | bytes 524320 | tf_op jit(solution)/shard_map/ppermute | solution.py:45
  206.2 2.6 %fusion.21 = (bf16[17,2,64,512]{3,2,0,1:T(8,128)(2,1)}, bf16[16,2,64,512]{3,2,0,1:T(8,128)(2,1)}) fusion(bf16[17,2,64,512]{3,2,0,1:T(8,128)(2,1)} %get-tuple-element.17, bf16[8,1,64,512]{3,2,0,1:T(8,128)(2,1)S(1)} %bitcast.93, bf16[8,1,64,512]{3,2,0,1:T(8,128)(2,1)} %bitcast.18, bf16[16,2,64,512]{3,2,0,1:T(8,128)(2,1)} %get-tuple-element.18), kind=kLoop, calls=%fused_computation.26 | loop fusion | flops 2097152 | bytes 3145728
  208.8 1.6 pad_dynamic-update-slice_fusion.1
  210.4 2.5 %slice.61 = bf16[17,1,64,512]{3,2,0,1:T(8,128)(2,1)} slice(bf16[17,2,64,512]{3,2,0,1:T(8,128)(2,1)} %get-tuple-element.31), slice={[0:17], [1:2], [0:64], [0:512]} | slice | bytes 2228224 | tf_op jit(solution)/shard_map/slice | solution.py:114
  213.2 1.9 gather_fusion
  215.0 2.2 fusion.19
  217.4 1.4 copy.49
  218.8 0.7 copy.43
  219.5 6.3 %fusion.43 = (f32[2,4,4,64]{3,2,1,0:T(4,128)}, bf16[2,4,4,64,1088]{4,3,2,1,0:T(8,128)(2,1)}) fusion(pred[2,64,1088]{2,1,0:T(8,128)(4,1)S(1)} %and_and_fusion, bf16[2,1088,4,64,1]{1,3,4,2,0:T(8,128)(2,1)S(1)} %bitcast.89, bf16[1,64,4,4,64]{4,1,3,2,0:T(8,128)(2,1)S(1)} %copy.48, bf16[1,64,4,4,64]{4,1,3,2,0:T(8,128)(2,1)S(1)} %copy-done.6), kind=kOutput, calls=%fused_computation.105 | convolution fusion | flops 299107392 | bytes 5980160 | tf_op jit(solution)/shard_map/sub | solution.py:145
  225.8 3.7 %fusion.15 = bf16[2,64,4,4,64]{4,1,3,2,0:T(8,128)(2,1)S(1)} fusion(bf16[2,1088,4,64,1]{1,3,4,2,0:T(8,128)(2,1)S(1)} %bitcast.88, bf16[2,4,4,64,1088]{4,3,2,1,0:T(8,128)(2,1)} %get-tuple-element.37, f32[2,64,4,4]{1,3,2,0:T(4,128)} %bitcast.96), kind=kOutput, calls=%fused_computation.17 | convolution fusion | flops 285474816 | bytes 5840896 | tf_op jit(solution)/shard_map/shgqk,skhd->shgqd/dot_general | solution.py:147
  229.5 0.4 copy.50
  229.9 0.3 convert_element_type.40
  230.3 1.4 reverse_select_fusion
  (74 shorter events, 3.0 us)
Async XLA Ops:
  6.5 84.2 %copy-start = (bf16[1,128,2048]{2,1,0:T(8,128)(2,1)S(1)}, bf16[1,128,2048]{2,1,0:T(8,128)(2,1)}, u32[]{:S(2)}) copy-start(bf16[1,128,2048]{2,1,0:T(8,128)(2,1)} %param.4) | copy-start | bytes 1572868
  6.5 84.2 %all-gather.2.cloned.1.call-start = ((), (), s32[]{:S(2)}) async-start(), calls=%async_computation | async-start | bytes 7077888 | tf_op jit(solution)/shard_map/all_gather | solution.py:53
  96.1 14.7 %collective-permute-start = (bf16[1,64,512]{2,1,0:T(8,128)(2,1)S(1)}, bf16[1,64,512]{2,1,0:T(8,128)(2,1)S(1)}, u32[]{:S(2)}, u32[]{:S(2)}) collective-permute-start(bf16[1,64,512]{2,1,0:T(8,128)(2,1)S(1)} %get-tuple-element.8), channel_id=1, source_target_pairs={{0,1},{1,2},{2,3},{3,4},{4,5},{5,6},{6,7},{7,8},{8,9},{9,10},{10,1... | collective-permute-start | bytes 196616 | tf_op jit(solution)/shard_map/ppermute | solution.py:45
  99.5 77.7 %collective-permute-start.4 = (bf16[1,64,512]{2,1,0:T(8,128)(2,1)S(1)}, bf16[1,64,512]{2,1,0:T(8,128)(2,1)}, u32[]{:S(2)}, u32[]{:S(2)}) collective-permute-start(bf16[1,64,512]{2,1,0:T(8,128)(2,1)S(1)} %get-tuple-element.8), channel_id=1, source_target_pairs={{0,16},{1,17},{2,18},{3,19},{4,20},{5,21},{6,22},{7,23},{8,24},{9,... | collective-permute-start | bytes 196616 | tf_op jit(solution)/shard_map/ppermute | solution.py:45
  107.5 101.3 %collective-permute-start.10 = (bf16[1,64,512]{2,1,0:T(8,128)(2,1)S(1)}, bf16[1,64,512]{2,1,0:T(8,128)(2,1)}, u32[]{:S(2)}, u32[]{:S(2)}) collective-permute-start(bf16[1,64,512]{2,1,0:T(8,128)(2,1)S(1)} %fusion.28), channel_id=1, source_target_pairs={{16,0},{17,1},{18,2},{19,3},{20,4},{21,5},{22,6},{23,7},{24,8},{25... | collective-permute-start | bytes 196616 | tf_op jit(solution)/shard_map/ppermute | solution.py:45
  110.8 7.5 %collective-permute-start.5 = (bf16[1,2,64,512]{3,2,0,1:T(8,128)(2,1)S(1)}, bf16[1,2,64,512]{3,2,0,1:T(8,128)(2,1)S(1)}, u32[]{:S(2)}, u32[]{:S(2)}) collective-permute-start(bf16[1,2,64,512]{3,2,0,1:T(8,128)(2,1)S(1)} %get-tuple-element.30), channel_id=1, source_target_pairs={{1,0},{2,1},{3,2},{4,3},{5,4},{6,5},{7,6},{8,7},{9,8},{10,9},{11,1... | collective-permute-start | bytes 393224 | tf_op jit(solution)/shard_map/ppermute | solution.py:45
  115.5 10.3 %collective-permute-start.1 = (bf16[2,64,512]{2,1,0:T(8,128)(2,1)S(1)}, bf16[2,64,512]{2,1,0:T(8,128)(2,1)S(1)}, u32[]{:S(2)}, u32[]{:S(2)}) collective-permute-start(bf16[2,64,512]{2,1,0:T(8,128)(2,1)S(1)} %get-tuple-element.33), channel_id=1, source_target_pairs={{0,2},{1,3},{2,4},{3,5},{4,6},{5,7},{6,8},{7,9},{8,10},{9,11},{10,... | collective-permute-start | bytes 393224 | tf_op jit(solution)/shard_map/ppermute | solution.py:45
  119.0 24.0 %collective-permute-start.6 = (bf16[2,2,64,512]{3,2,1,0:T(8,128)(2,1)}, bf16[2,2,64,512]{3,2,1,0:T(8,128)(2,1)S(1)}, u32[]{:S(2)}, u32[]{:S(2)}) collective-permute-start(bf16[2,2,64,512]{3,2,1,0:T(8,128)(2,1)} %pad_maximum_fusion.13), channel_id=1, source_target_pairs={{2,0},{3,1},{4,2},{5,3},{6,4},{7,5},{8,6},{9,7},{10,8},{11,9},{12,... | collective-permute-start | bytes 786440 | tf_op jit(solution)/shard_map/ppermute | solution.py:45
  125.8 23.1 %collective-permute-start.2 = (bf16[4,64,512]{2,1,0:T(8,128)(2,1)S(1)}, bf16[4,64,512]{2,1,0:T(8,128)(2,1)S(1)}, u32[]{:S(2)}, u32[]{:S(2)}) collective-permute-start(bf16[4,64,512]{2,1,0:T(8,128)(2,1)S(1)} %pad_maximum_fusion.12), channel_id=1, source_target_pairs={{0,4},{1,5},{2,6},{3,7},{4,8},{5,9},{6,10},{7,11},{8,12},{9,13},{1... | collective-permute-start | bytes 786440 | tf_op jit(solution)/shard_map/ppermute | solution.py:45
  143.1 29.4 %collective-permute-start.7 = (bf16[4,2,64,512]{3,2,1,0:T(8,128)(2,1)S(1)}, bf16[4,2,64,512]{3,2,1,0:T(8,128)(2,1)S(1)}, u32[]{:S(2)}, u32[]{:S(2)}) collective-permute-start(bf16[4,2,64,512]{3,2,1,0:T(8,128)(2,1)S(1)} %pad_maximum_fusion.5), channel_id=1, source_target_pairs={{4,0},{5,1},{6,2},{7,3},{8,4},{9,5},{10,6},{11,7},{12,8},{13,9},{1... | collective-permute-start | bytes 1572872 | tf_op jit(solution)/shard_map/ppermute | solution.py:45
  148.9 28.2 %collective-permute-start.3 = (bf16[8,64,512]{2,1,0:T(8,128)(2,1)S(1)}, bf16[8,64,512]{2,1,0:T(8,128)(2,1)S(1)}, u32[]{:S(2)}, u32[]{:S(2)}) collective-permute-start(bf16[8,64,512]{2,1,0:T(8,128)(2,1)S(1)} %pad_maximum_fusion.4), channel_id=1, source_target_pairs={{0,8},{1,9},{2,10},{3,11},{4,12},{5,13},{6,14},{7,15},{8,16},{9,17... | collective-permute-start | bytes 1572872 | tf_op jit(solution)/shard_map/ppermute | solution.py:45
  173.7 32.5 %collective-permute-start.9 = (bf16[8,64,512]{2,1,0:T(8,128)(2,1)}, bf16[8,64,512]{2,1,0:T(8,128)(2,1)S(1)}, u32[]{:S(2)}, u32[]{:S(2)}) collective-permute-start(bf16[8,64,512]{2,1,0:T(8,128)(2,1)} %get-tuple-element.14), channel_id=1, source_target_pairs={{8,0},{9,1},{10,2},{11,3},{12,4},{13,5},{14,6},{15,7},{16,8},{17,9... | collective-permute-start | bytes 1572872 | tf_op jit(solution)/shard_map/ppermute | solution.py:45
  175.6 30.6 %collective-permute-start.8 = (bf16[8,64,512]{2,1,0:T(8,128)(2,1)}, bf16[8,64,512]{2,1,0:T(8,128)(2,1)}, u32[]{:S(2)}, u32[]{:S(2)}) collective-permute-start(bf16[8,64,512]{2,1,0:T(8,128)(2,1)} %get-tuple-element.13), channel_id=1, source_target_pairs={{56,48},{57,49},{58,50},{59,51},{60,52},{61,53},{62,54},{63,55},{1... | collective-permute-start | bytes 1572872 | tf_op jit(solution)/shard_map/ppermute | solution.py:45
  178.0 30.8 %copy-start.1 = (bf16[17,64,512]{2,1,0:T(8,128)(2,1)}, bf16[17,64,512]{2,1,0:T(8,128)(2,1)S(1)}, u32[]{:S(2)}) copy-start(bf16[17,64,512]{2,1,0:T(8,128)(2,1)S(1)} %constant_dynamic-update-slice_fusion) | copy-start | bytes 3342340
  210.4 2.5 %copy-start.5 = (bf16[16,2,64,512]{3,2,0,1:T(8,128)(2,1)S(1)}, bf16[16,2,64,512]{3,2,0,1:T(8,128)(2,1)}, u32[]{:S(2)}) copy-start(bf16[16,2,64,512]{3,2,0,1:T(8,128)(2,1)} %get-tuple-element.32) | copy-start | bytes 6291460
  210.4 2.6 %copy-start.3 = (bf16[17,64,512]{2,1,0:T(8,128)(2,1)S(1)}, bf16[17,64,512]{2,1,0:T(8,128)(2,1)}, u32[]{:S(2)}) copy-start(bf16[17,64,512]{2,1,0:T(8,128)(2,1)} %rev.6) | copy-start | bytes 3342340
  213.2 1.9 copy-start.7
  213.2 1.9 copy-start.8
  215.0 2.2 copy-start.2
  217.4 2.1 copy-start.6
  219.5 6.3 %copy-start.4 = (bf16[2,1088,256]{1,2,0:T(8,128)(2,1)S(1)}, bf16[2,1088,256]{1,2,0:T(8,128)(2,1)}, u32[]{:S(2)}) copy-start(bf16[2,1088,256]{1,2,0:T(8,128)(2,1)} %copy.49) | copy-start | bytes 3342340
Sparse Core Ops, SparseCore 0:
  9.4 81.3 all-gather.1

commit v3 on v2

--- a/solution.py
+++ b/solution.py
@@ -45,14 +45,63 @@
     return lax.ppermute(value, "ctx", pairs)
 
 
+def chip_of(index, lanes):
+    line, core = divmod(index // lanes, 2)
+    half, rest = divmod(index % lanes, lanes // 2)
+    return line, core, half, rest
+
+
+def device_of(line, core, half, rest, lanes, lines):
+    return (2 * line + core) * lanes + half * (lanes // 2) + rest
+
+
+def project(rows, weight):
+    lines = lax.axis_size("seq") // 2
+    lanes = lax.axis_size("ctx")
+    total = 2 * lines * lanes
+    both = ("seq", "ctx")
+
+    def pairs_for(offset):
+        found = []
+        for dest in range(total):
+            line, core, half, rest = chip_of(dest, lanes)
+            level = half * lines + line + offset(core)
+            level %= 2 * lines
+            found.append((device_of(level % lines, core, level // lines, rest, lanes, lines), dest))
+        return found
+
+    def mate_pairs():
+        found = []
+        for dest in range(total):
+            line, core, half, rest = chip_of(dest, lanes)
+            found.append((device_of(line, 1 - core, half, rest, lanes, lines), dest))
+        return found
+
+    step = [lambda core: 0]
+    for shift in range(1, lines):
+        if 2 * shift == lines:
+            step.append(lambda core, s=shift: s if core == 0 else -s)
+        elif 2 * shift < lines:
+            step.append(lambda core, s=shift: s)
+        else:
+            step.append(lambda core, s=shift: s - lines)
+    mine = [weight] + [lax.ppermute(weight, both, pairs_for(f)) for f in step[1:]]
+    mine = jnp.stack(mine)
+    mate = lax.ppermute(mine, both, mate_pairs())
+    blocks = jnp.concatenate([mine, mate], axis=0)
+    seq_index = lax.axis_index("seq")
+    line, core = seq_index // 2, seq_index % 2
+    wanted = jnp.arange(2 * lines, dtype=jnp.int32)
+    slot = (wanted // 2 - line) % lines + lines * (wanted % 2 != core).astype(jnp.int32)
+    ordered = jnp.take(blocks, slot, axis=0)
+    full = jnp.transpose(ordered, (1, 0, 2)).reshape(weight.shape[0], -1)
+    return jnp.dot(rows, full, preferred_element_type=jnp.float32).astype(jnp.bfloat16)
+
+
 def body(tokens, qkv_weight, doc_lengths, span_order):
     rows = tokens[0]
     token_count = rows.shape[0]
-    query_key_value = jnp.dot(
-        rows,
-        lax.all_gather(qkv_weight, "seq", axis=1, tiled=True),
-        preferred_element_type=jnp.float32,
-    ).astype(jnp.bfloat16)
+    query_key_value = project(rows, qkv_weight)
     lengths_row = doc_lengths[0]
     order_row = span_order[0]
     places_all = positions(order_row)

time: 240 us -> 211 us (0.88)
  waiting for transfers between devices: 125 us -> 72 us
  starting transfers between devices: 52.5 us -> 75.7 us
  between operations: 14.5 us -> 1.23 us
  local copies, waits for them, and re-layouts: 19.1 us -> 30.2 us
  other arithmetic: 12.3 us -> 18.1 us
  matrix products: 14.9 us -> 12.2 us
    all_gather x1 -> x0, waiting for transfers between devices: 76.2 us -> none  [body(): lax.all_gather(qkv_weight, 'seq', axis=1, tiled=True)]
    ppermute x0 -> x4, waiting for transfers between devices: none -> 23.2 us  [the longest x3 23 us: project(): lax.ppermute(weight, both, pairs_for(f))]
    ppermute x0 -> x4, starting transfers between devices: none -> 21.5 us  [the longest x3 16.9 us: project(): lax.ppermute(weight, both, pairs_for(f))]
    gather x0 -> x1, local copies, waits for them, and re-layouts: none -> 6.35 us  [project(): ordered = jnp.take(blocks, slot, axis=0)]
    unnamed x25 -> x24, local copies, waits for them, and re-layouts: 2.72 us -> 6.49 us
    select_n x0 -> x2, other arithmetic: none -> 3.47 us  [project(): ordered = jnp.take(blocks, slot, axis=0)]
    dot_general x1, matrix products: 4.97 us -> 1.84 us  [project(): jnp.dot(rows, full, preferred_element_type=jnp.float32).astype(jnp.bfloat16)]
  transfers between devices with their start and end apart: 12 -> 15, of which waited for: 4 -> 6; matrix products, arithmetic and copies ran while one was open for 8% -> 10% of each run, Pallas kernels for 0% -> 0%
where the time goes in v3:
time: 211 us; the launch traced here: 210 us
  starting transfers between devices  75.7 us (36%)
  waiting for transfers between devices  72 us (34%)
  local copies, waits for them, and re-layouts  30.2 us (14%)
  other arithmetic  18.1 us (9%)
  matrix products  12.2 us (6%)
    ppermute x11, starting transfers between devices, moved(): return lax.ppermute(value, 'ctx', pairs)  54.2 us
    ppermute x11, waiting for transfers between devices, moved(): return lax.ppermute(value, 'ctx', pairs)  48.8 us
    ppermute x3, waiting for transfers between devices, project(): lax.ppermute(weight, both, pairs_for(f))  23 us
    ppermute x3, starting transfers between devices, project(): lax.ppermute(weight, both, pairs_for(f))  16.9 us
    sub x1, matrix products, body(): weights = jnp.where(live, jnp.exp(scores - top), 0.0)  6.64 us
    unnamed x24, local copies, waits for them, and re-layouts  6.49 us
    gather x1, local copies, waits for them, and re-layouts, project(): ordered = jnp.take(blocks, slot, axis=0)  6.35 us
    ppermute x1, starting transfers between devices, project(): mate = lax.ppermute(mine, both, mate_pairs())  4.6 us
  transfers between devices with their start and end apart: 15, of which 6 were waited for; matrix products, arithmetic and copies ran while one was open for 10% of the time, Pallas kernels for 0%

profile of v3, /device:TPU:56, one launch (start us, length us, event | category | flops | bytes accessed | tf_op | source)
XLA Modules:
  0.0 209.5 jit_solution(2852386669196155595)
XLA Ops:
  0.0 11.1 %collective-permute-start = (bf16[2048,192]{0,1:T(8,128)(2,1)}, bf16[2048,192]{0,1:T(8,128)(2,1)S(1)}, u32[]{:S(2)}, u32[]{:S(2)}) collective-permute-start(bf16[2048,192]{0,1:T(8,128)(2,1)} %param.5), channel_id=1, source_target_pairs={{128,0},{129,1},{130,2},{131,3},{132,4},{133,5},{134,6},{135,7},{1... | collective-permute-start | bytes 2359304 | tf_op jit(solution)/shard_map/ppermute | solution.py:88
  11.1 2.5 %collective-permute-start.1 = (bf16[2048,192]{0,1:T(8,128)(2,1)}, bf16[2048,192]{0,1:T(8,128)(2,1)S(1)}, u32[]{:S(2)}, u32[]{:S(2)}) collective-permute-start(bf16[2048,192]{0,1:T(8,128)(2,1)} %param.5), channel_id=1, source_target_pairs={{256,0},{257,1},{258,2},{259,3},{260,4},{261,5},{262,6},{263,7},{2... | collective-permute-start | bytes 2359304 | tf_op jit(solution)/shard_map/ppermute | solution.py:88
  13.5 3.4 %collective-permute-start.2 = (bf16[2048,192]{0,1:T(8,128)(2,1)}, bf16[2048,192]{0,1:T(8,128)(2,1)S(1)}, u32[]{:S(2)}, u32[]{:S(2)}) collective-permute-start(bf16[2048,192]{0,1:T(8,128)(2,1)} %param.5), channel_id=1, source_target_pairs={{416,0},{417,1},{418,2},{419,3},{420,4},{421,5},{422,6},{423,7},{4... | collective-permute-start | bytes 2359304 | tf_op jit(solution)/shard_map/ppermute | solution.py:88
  17.9 1.3 fusion.47
  20.6 0.8 copy.46
  22.0 14.6 %collective-permute-done = bf16[2048,192]{0,1:T(8,128)(2,1)S(1)} collective-permute-done((bf16[2048,192]{0,1:T(8,128)(2,1)}, bf16[2048,192]{0,1:T(8,128)(2,1)S(1)}, u32[]{:S(2)}, u32[]{:S(2)}) %collective-permute-start) | collective-permute-done | bytes 786464 | tf_op jit(solution)/shard_map/ppermute | solution.py:88
  36.6 8.4 %collective-permute-done.1 = bf16[2048,192]{0,1:T(8,128)(2,1)S(1)} collective-permute-done((bf16[2048,192]{0,1:T(8,128)(2,1)}, bf16[2048,192]{0,1:T(8,128)(2,1)S(1)}, u32[]{:S(2)}, u32[]{:S(2)}) %collective-permute-start.1) | collective-permute-done | bytes 786464 | tf_op jit(solution)/shard_map/ppermute | solution.py:88
  45.0 1.5 pad_maximum_fusion
  46.5 4.6 %collective-permute-start.3 = (bf16[4,2048,192]{1,2,0:T(8,128)(2,1)S(1)}, bf16[4,2048,192]{1,2,0:T(8,128)(2,1)S(1)}, u32[]{:S(2)}, u32[]{:S(2)}) collective-permute-start(bf16[4,2048,192]{1,2,0:T(8,128)(2,1)S(1)} %pad_maximum_fusion), channel_id=1, source_target_pairs={{64,0},{65,1},{66,2},{67,3},{68,4},{69,5},{70,6},{71,7},{72,8},{73... | collective-permute-start | bytes 9437192 | tf_op jit(solution)/shard_map/ppermute | solution.py:90
  51.6 0.9 and_and_fusion
  52.4 0.9 constant_dynamic-update-slice_fusion.4
  53.4 1.0 constant_dynamic-update-slice_fusion.3
  54.3 0.9 constant_dynamic-update-slice_fusion.2
  55.3 0.9 constant_dynamic-update-slice_fusion.1
  56.4 2.1 %constant_dynamic-update-slice_fusion = bf16[8,2048,192]{1,2,0:T(8,128)(2,1)} fusion(bf16[8,2048,192]{1,2,0:T(8,128)(2,1)} %constant_dynamic-update-slice_fusion.1, bf16[4,2048,192]{1,2,0:T(8,128)(2,1)S(1)} %collective-permute-done.3), kind=kLoop, calls=%fused_computation.68 | loop fusion | bytes 6291456 | tf_op jit(solution)/shard_map/concatenate | solution.py:91
  58.5 6.3 %gather_fusion = bf16[8,2048,192]{1,2,0:T(8,128)(2,1)} fusion(bf16[8,2048,192]{1,2,0:T(8,128)(2,1)} %constant_dynamic-update-slice_fusion, s32[1024]{0:T(1024)S(1)} %pad_clamp_fusion.1), kind=kCustom, calls=%fused_computation | custom fusion | bytes 12582944 | tf_op jit(solution)/shard_map/jit(_take)/gather | solution.py:96
  64.9 3.5 %broadcast_select_fusion = bf16[8,2048,192]{1,2,0:T(8,128)(2,1)S(1)} fusion(bf16[8,2048,192]{1,2,0:T(8,128)(2,1)} %gather_fusion, pred[8]{0:T(512)(128)(4,1)S(1)} %compare_and_fusion.1), kind=kLoop, calls=%fused_computation.6 | loop fusion | flops 3145728 | bytes 12582920 | tf_op jit(solution)/shard_map/jit(_take)/select_n | solution.py:96
  68.3 1.8 fusion.7
  70.5 3.4 %collective-permute-start.4 = (bf16[1,64,512]{2,1,0:T(8,128)(2,1)S(1)}, bf16[1,64,512]{2,1,0:T(8,128)(2,1)S(1)}, u32[]{:S(2)}, u32[]{:S(2)}) collective-permute-start(bf16[1,64,512]{2,1,0:T(8,128)(2,1)S(1)} %bitcast.104), channel_id=1, source_target_pairs={{0,1},{1,2},{2,3},{3,4},{4,5},{5,6},{6,7},{7,8},{8,9},{9,10},{10,1... | collective-permute-start | bytes 196616 | tf_op jit(solution)/shard_map/ppermute | solution.py:45
  73.9 7.9 %collective-permute-start.8 = (bf16[1,64,512]{2,1,0:T(8,128)(2,1)S(1)}, bf16[1,64,512]{2,1,0:T(8,128)(2,1)}, u32[]{:S(2)}, u32[]{:S(2)}) collective-permute-start(bf16[1,64,512]{2,1,0:T(8,128)(2,1)S(1)} %bitcast.105), channel_id=1, source_target_pairs={{0,16},{1,17},{2,18},{3,19},{4,20},{5,21},{6,22},{7,23},{8,24},{9,... | collective-permute-start | bytes 196616 | tf_op jit(solution)/shard_map/ppermute | solution.py:45
  82.0 2.4 %collective-permute-start.14 = (bf16[1,64,512]{2,1,0:T(8,128)(2,1)S(1)}, bf16[1,64,512]{2,1,0:T(8,128)(2,1)}, u32[]{:S(2)}, u32[]{:S(2)}) collective-permute-start(bf16[1,64,512]{2,1,0:T(8,128)(2,1)S(1)} %bitcast.118), channel_id=1, source_target_pairs={{16,0},{17,1},{18,2},{19,3},{20,4},{21,5},{22,6},{23,7},{24,8},{25... | collective-permute-start | bytes 196616 | tf_op jit(solution)/shard_map/ppermute | solution.py:45
  85.8 4.5 %collective-permute-start.9 = (bf16[1,2,64,512]{3,2,0,1:T(8,128)(2,1)S(1)}, bf16[1,2,64,512]{3,2,0,1:T(8,128)(2,1)S(1)}, u32[]{:S(2)}, u32[]{:S(2)}) collective-permute-start(bf16[1,2,64,512]{3,2,0,1:T(8,128)(2,1)S(1)} %get-tuple-element.28), channel_id=1, source_target_pairs={{1,0},{2,1},{3,2},{4,3},{5,4},{6,5},{7,6},{8,7},{9,8},{10,9},{11,1... | collective-permute-start | bytes 393224 | tf_op jit(solution)/shard_map/ppermute | solution.py:45
  90.5 2.8 %collective-permute-start.5 = (bf16[2,64,512]{2,1,0:T(8,128)(2,1)}, bf16[2,64,512]{2,1,0:T(8,128)(2,1)S(1)}, u32[]{:S(2)}, u32[]{:S(2)}) collective-permute-start(bf16[2,64,512]{2,1,0:T(8,128)(2,1)} %get-tuple-element.33), channel_id=1, source_target_pairs={{0,2},{1,3},{2,4},{3,5},{4,6},{5,7},{6,8},{7,9},{8,10},{9,11},{10,... | collective-permute-start | bytes 393224 | tf_op jit(solution)/shard_map/ppermute | solution.py:45
  94.0 5.4 %collective-permute-start.10 = (bf16[2,2,64,512]{3,2,1,0:T(8,128)(2,1)}, bf16[2,2,64,512]{3,2,1,0:T(8,128)(2,1)S(1)}, u32[]{:S(2)}, u32[]{:S(2)}) collective-permute-start(bf16[2,2,64,512]{3,2,1,0:T(8,128)(2,1)} %pad_maximum_fusion.14), channel_id=1, source_target_pairs={{2,0},{3,1},{4,2},{5,3},{6,4},{7,5},{8,6},{9,7},{10,8},{11,9},{12,... | collective-permute-start | bytes 786440 | tf_op jit(solution)/shard_map/ppermute | solution.py:45
  100.1 18.6 %collective-permute-start.6 = (bf16[4,64,512]{2,1,0:T(8,128)(2,1)S(1)}, bf16[4,64,512]{2,1,0:T(8,128)(2,1)S(1)}, u32[]{:S(2)}, u32[]{:S(2)}) collective-permute-start(bf16[4,64,512]{2,1,0:T(8,128)(2,1)S(1)} %pad_maximum_fusion.13), channel_id=1, source_target_pairs={{0,4},{1,5},{2,6},{3,7},{4,8},{5,9},{6,10},{7,11},{8,12},{9,13},{1... | collective-permute-start | bytes 786440 | tf_op jit(solution)/shard_map/ppermute | solution.py:45
  118.8 1.9 collective-permute-start.11
  120.7 0.7 constant_dynamic-update-slice_fusion.11
  121.5 1.9 collective-permute-done.6
  123.5 3.8 %collective-permute-start.7 = (bf16[8,64,512]{2,1,0:T(8,128)(2,1)S(1)}, bf16[8,64,512]{2,1,0:T(8,128)(2,1)S(1)}, u32[]{:S(2)}, u32[]{:S(2)}) collective-permute-start(bf16[8,64,512]{2,1,0:T(8,128)(2,1)S(1)} %pad_maximum_fusion.5), channel_id=1, source_target_pairs={{0,8},{1,9},{2,10},{3,11},{4,12},{5,13},{6,14},{7,15},{8,16},{9,17... | collective-permute-start | bytes 1572872 | tf_op jit(solution)/shard_map/ppermute | solution.py:45
  127.3 0.8 copy_dynamic-update-slice_fusion.3
  128.1 19.8 %collective-permute-done.11 = bf16[4,2,64,512]{3,2,1,0:T(8,128)(2,1)S(1)} collective-permute-done((bf16[4,2,64,512]{3,2,1,0:T(8,128)(2,1)S(1)}, bf16[4,2,64,512]{3,2,1,0:T(8,128)(2,1)S(1)}, u32[]{:S(2)}, u32[]{:S(2)}) %collective-permute-start.11) | collective-permute-done | bytes 524320 | tf_op jit(solution)/shard_map/ppermute | solution.py:45
  148.0 1.1 slice_bitcast_fusion.2
  149.0 1.9 collective-permute-start.13
  150.9 1.5 collective-permute-start.12
  152.5 0.8 constant_dynamic-update-slice_fusion.5
  153.4 1.2 rev.6
  154.6 1.1 copy_dynamic-update-slice_fusion.1
  155.6 27.1 %collective-permute-done.13 = bf16[8,64,512]{2,1,0:T(8,128)(2,1)S(1)} collective-permute-done((bf16[8,64,512]{2,1,0:T(8,128)(2,1)}, bf16[8,64,512]{2,1,0:T(8,128)(2,1)S(1)}, u32[]{:S(2)}, u32[]{:S(2)}) %collective-permute-start.13) | collective-permute-done | bytes 524320 | tf_op jit(solution)/shard_map/ppermute | solution.py:45
  182.7 2.6 %fusion.22 = (bf16[17,2,64,512]{3,2,0,1:T(8,128)(2,1)}, bf16[16,2,64,512]{3,2,0,1:T(8,128)(2,1)}) fusion(bf16[17,2,64,512]{3,2,0,1:T(8,128)(2,1)} %get-tuple-element.15, bf16[8,1,64,512]{3,2,0,1:T(8,128)(2,1)S(1)} %bitcast.121, bf16[8,1,64,512]{3,2,0,1:T(8,128)(2,1)} %bitcast.27, bf16[16,2,64,512]{3,2,0,1:T(8,128)(2,1)} %get-tuple-element.16), kind=kLoop, calls=%fused_computation.30 | loop fusion | flops 2097152 | bytes 3145728
  185.3 1.6 pad_dynamic-update-slice_fusion.1
  186.9 2.4 %slice.63 = bf16[17,1,64,512]{3,2,0,1:T(8,128)(2,1)} slice(bf16[17,2,64,512]{3,2,0,1:T(8,128)(2,1)} %get-tuple-element.31), slice={[0:17], [1:2], [0:64], [0:512]} | slice | bytes 2228224 | tf_op jit(solution)/shard_map/slice | solution.py:163
  189.3 1.3 slice_bitcast_fusion
  190.8 1.7 gather_fusion.1
  192.5 2.2 %fusion.20 = bf16[1,1088,512]{2,1,0:T(8,128)(2,1)S(1)} fusion(bf16[17,1,64,512]{3,2,0,1:T(8,128)(2,1)} %slice.63, pred[1088]{0:T(1024)(128)(4,1)S(1)} %broadcast_in_dim.98, pred[1088]{0:T(1024)(128)(4,1)S(1)} %broadcast_in_dim.94, bf16[1,1088,512]{2,1,0:T(8,128)(2,1)} %bitcast.98), kind=kLoop, calls=%fused_computation.25 | loop fusion | flops 1114112 | bytes 3344512 | tf_op jit(solution)/shard_map/jit(_where)/select_n | solution.py:162
  194.8 1.4 copy.64
  197.0 6.6 %fusion.48 = (f32[2,4,4,64]{3,2,1,0:T(4,128)S(1)}, bf16[2,4,4,64,1088]{4,3,2,1,0:T(8,128)(2,1)}) fusion(pred[2,64,1088]{2,1,0:T(8,128)(4,1)} %and_and_fusion, bf16[2,1088,4,64,1]{1,3,4,2,0:T(8,128)(2,1)S(1)} %bitcast.114, bf16[1,64,4,4,64]{4,1,3,2,0:T(8,128)(2,1)S(1)} %copy.63, bf16[1,64,4,4,64]{4,1,3,2,0:T(8,128)(2,1)S(1)} %copy.62), kind=kOutput, calls=%fused_computation.139 | convolution fusion | flops 299107392 | bytes 5980160 | tf_op jit(solution)/shard_map/sub | solution.py:194
  203.6 3.7 %fusion.16 = bf16[2,64,4,4,64]{4,1,3,2,0:T(8,128)(2,1)S(1)} fusion(bf16[2,1088,4,64,1]{1,3,4,2,0:T(8,128)(2,1)S(1)} %bitcast.113, bf16[2,4,4,64,1088]{4,3,2,1,0:T(8,128)(2,1)} %get-tuple-element.37, f32[2,64,4,4]{1,3,2,0:T(4,128)S(1)} %bitcast.125), kind=kOutput, calls=%fused_computation.21 | convolution fusion | flops 285474816 | bytes 5840896 | tf_op jit(solution)/shard_map/shgqk,skhd->shgqd/dot_general | solution.py:196
  208.1 1.4 reverse_select_fusion
  (85 shorter events, 8.2 us)
Async XLA Ops:
  0.0 68.3 %copy-start = (bf16[1,128,2048]{2,1,0:T(8,128)(2,1)S(1)}, bf16[1,128,2048]{2,1,0:T(8,128)(2,1)}, u32[]{:S(2)}) copy-start(bf16[1,128,2048]{2,1,0:T(8,128)(2,1)} %param.4) | copy-start | bytes 1572868
  0.0 36.6 %collective-permute-start = (bf16[2048,192]{0,1:T(8,128)(2,1)}, bf16[2048,192]{0,1:T(8,128)(2,1)S(1)}, u32[]{:S(2)}, u32[]{:S(2)}) collective-permute-start(bf16[2048,192]{0,1:T(8,128)(2,1)} %param.5), channel_id=1, source_target_pairs={{128,0},{129,1},{130,2},{131,3},{132,4},{133,5},{134,6},{135,7},{1... | collective-permute-start | bytes 2359304 | tf_op jit(solution)/shard_map/ppermute | solution.py:88
  11.1 33.9 %collective-permute-start.1 = (bf16[2048,192]{0,1:T(8,128)(2,1)}, bf16[2048,192]{0,1:T(8,128)(2,1)S(1)}, u32[]{:S(2)}, u32[]{:S(2)}) collective-permute-start(bf16[2048,192]{0,1:T(8,128)(2,1)} %param.5), channel_id=1, source_target_pairs={{256,0},{257,1},{258,2},{259,3},{260,4},{261,5},{262,6},{263,7},{2... | collective-permute-start | bytes 2359304 | tf_op jit(solution)/shard_map/ppermute | solution.py:88
  13.5 31.5 %collective-permute-start.2 = (bf16[2048,192]{0,1:T(8,128)(2,1)}, bf16[2048,192]{0,1:T(8,128)(2,1)S(1)}, u32[]{:S(2)}, u32[]{:S(2)}) collective-permute-start(bf16[2048,192]{0,1:T(8,128)(2,1)} %param.5), channel_id=1, source_target_pairs={{416,0},{417,1},{418,2},{419,3},{420,4},{421,5},{422,6},{423,7},{4... | collective-permute-start | bytes 2359304 | tf_op jit(solution)/shard_map/ppermute | solution.py:88
  45.0 7.4 %copy-start.4 = (bf16[2048,192]{0,1:T(8,128)(2,1)S(1)}, bf16[2048,192]{0,1:T(8,128)(2,1)}, u32[]{:S(2)}) copy-start(bf16[2048,192]{0,1:T(8,128)(2,1)} %param.5) | copy-start | bytes 2359300
  46.5 9.9 %collective-permute-start.3 = (bf16[4,2048,192]{1,2,0:T(8,128)(2,1)S(1)}, bf16[4,2048,192]{1,2,0:T(8,128)(2,1)S(1)}, u32[]{:S(2)}, u32[]{:S(2)}) collective-permute-start(bf16[4,2048,192]{1,2,0:T(8,128)(2,1)S(1)} %pad_maximum_fusion), channel_id=1, source_target_pairs={{64,0},{65,1},{66,2},{67,3},{68,4},{69,5},{70,6},{71,7},{72,8},{73... | collective-permute-start | bytes 9437192 | tf_op jit(solution)/shard_map/ppermute | solution.py:90
  70.5 14.6 %collective-permute-start.4 = (bf16[1,64,512]{2,1,0:T(8,128)(2,1)S(1)}, bf16[1,64,512]{2,1,0:T(8,128)(2,1)S(1)}, u32[]{:S(2)}, u32[]{:S(2)}) collective-permute-start(bf16[1,64,512]{2,1,0:T(8,128)(2,1)S(1)} %bitcast.104), channel_id=1, source_target_pairs={{0,1},{1,2},{2,3},{3,4},{4,5},{5,6},{6,7},{7,8},{8,9},{9,10},{10,1... | collective-permute-start | bytes 196616 | tf_op jit(solution)/shard_map/ppermute | solution.py:45
  73.9 78.6 %collective-permute-start.8 = (bf16[1,64,512]{2,1,0:T(8,128)(2,1)S(1)}, bf16[1,64,512]{2,1,0:T(8,128)(2,1)}, u32[]{:S(2)}, u32[]{:S(2)}) collective-permute-start(bf16[1,64,512]{2,1,0:T(8,128)(2,1)S(1)} %bitcast.105), channel_id=1, source_target_pairs={{0,16},{1,17},{2,18},{3,19},{4,20},{5,21},{6,22},{7,23},{8,24},{9,... | collective-permute-start | bytes 196616 | tf_op jit(solution)/shard_map/ppermute | solution.py:45
  82.0 103.3 %collective-permute-start.14 = (bf16[1,64,512]{2,1,0:T(8,128)(2,1)S(1)}, bf16[1,64,512]{2,1,0:T(8,128)(2,1)}, u32[]{:S(2)}, u32[]{:S(2)}) collective-permute-start(bf16[1,64,512]{2,1,0:T(8,128)(2,1)S(1)} %bitcast.118), channel_id=1, source_target_pairs={{16,0},{17,1},{18,2},{19,3},{20,4},{21,5},{22,6},{23,7},{24,8},{25... | collective-permute-start | bytes 196616 | tf_op jit(solution)/shard_map/ppermute | solution.py:45
  85.8 7.5 %collective-permute-start.9 = (bf16[1,2,64,512]{3,2,0,1:T(8,128)(2,1)S(1)}, bf16[1,2,64,512]{3,2,0,1:T(8,128)(2,1)S(1)}, u32[]{:S(2)}, u32[]{:S(2)}) collective-permute-start(bf16[1,2,64,512]{3,2,0,1:T(8,128)(2,1)S(1)} %get-tuple-element.28), channel_id=1, source_target_pairs={{1,0},{2,1},{3,2},{4,3},{5,4},{6,5},{7,6},{8,7},{9,8},{10,9},{11,1... | collective-permute-start | bytes 393224 | tf_op jit(solution)/shard_map/ppermute | solution.py:45
  90.5 9.6 %collective-permute-start.5 = (bf16[2,64,512]{2,1,0:T(8,128)(2,1)}, bf16[2,64,512]{2,1,0:T(8,128)(2,1)S(1)}, u32[]{:S(2)}, u32[]{:S(2)}) collective-permute-start(bf16[2,64,512]{2,1,0:T(8,128)(2,1)} %get-tuple-element.33), channel_id=1, source_target_pairs={{0,2},{1,3},{2,4},{3,5},{4,6},{5,7},{6,8},{7,9},{8,10},{9,11},{10,... | collective-permute-start | bytes 393224 | tf_op jit(solution)/shard_map/ppermute | solution.py:45
  94.0 24.7 %collective-permute-start.10 = (bf16[2,2,64,512]{3,2,1,0:T(8,128)(2,1)}, bf16[2,2,64,512]{3,2,1,0:T(8,128)(2,1)S(1)}, u32[]{:S(2)}, u32[]{:S(2)}) collective-permute-start(bf16[2,2,64,512]{3,2,1,0:T(8,128)(2,1)} %pad_maximum_fusion.14), channel_id=1, source_target_pairs={{2,0},{3,1},{4,2},{5,3},{6,4},{7,5},{8,6},{9,7},{10,8},{11,9},{12,... | collective-permute-start | bytes 786440 | tf_op jit(solution)/shard_map/ppermute | solution.py:45
  100.1 23.3 %collective-permute-start.6 = (bf16[4,64,512]{2,1,0:T(8,128)(2,1)S(1)}, bf16[4,64,512]{2,1,0:T(8,128)(2,1)S(1)}, u32[]{:S(2)}, u32[]{:S(2)}) collective-permute-start(bf16[4,64,512]{2,1,0:T(8,128)(2,1)S(1)} %pad_maximum_fusion.13), channel_id=1, source_target_pairs={{0,4},{1,5},{2,6},{3,7},{4,8},{5,9},{6,10},{7,11},{8,12},{9,13},{1... | collective-permute-start | bytes 786440 | tf_op jit(solution)/shard_map/ppermute | solution.py:45
  118.8 29.0 %collective-permute-start.11 = (bf16[4,2,64,512]{3,2,1,0:T(8,128)(2,1)S(1)}, bf16[4,2,64,512]{3,2,1,0:T(8,128)(2,1)S(1)}, u32[]{:S(2)}, u32[]{:S(2)}) collective-permute-start(bf16[4,2,64,512]{3,2,1,0:T(8,128)(2,1)S(1)} %pad_maximum_fusion.6), channel_id=1, source_target_pairs={{4,0},{5,1},{6,2},{7,3},{8,4},{9,5},{10,6},{11,7},{12,8},{13,9},{1... | collective-permute-start | bytes 1572872 | tf_op jit(solution)/shard_map/ppermute | solution.py:45
  123.5 29.0 %collective-permute-start.7 = (bf16[8,64,512]{2,1,0:T(8,128)(2,1)S(1)}, bf16[8,64,512]{2,1,0:T(8,128)(2,1)S(1)}, u32[]{:S(2)}, u32[]{:S(2)}) collective-permute-start(bf16[8,64,512]{2,1,0:T(8,128)(2,1)S(1)} %pad_maximum_fusion.5), channel_id=1, source_target_pairs={{0,8},{1,9},{2,10},{3,11},{4,12},{5,13},{6,14},{7,15},{8,16},{9,17... | collective-permute-start | bytes 1572872 | tf_op jit(solution)/shard_map/ppermute | solution.py:45
  149.0 33.7 %collective-permute-start.13 = (bf16[8,64,512]{2,1,0:T(8,128)(2,1)}, bf16[8,64,512]{2,1,0:T(8,128)(2,1)S(1)}, u32[]{:S(2)}, u32[]{:S(2)}) collective-permute-start(bf16[8,64,512]{2,1,0:T(8,128)(2,1)} %get-tuple-element.12), channel_id=1, source_target_pairs={{8,0},{9,1},{10,2},{11,3},{12,4},{13,5},{14,6},{15,7},{16,8},{17,9... | collective-permute-start | bytes 1572872 | tf_op jit(solution)/shard_map/ppermute | solution.py:45
  150.9 31.8 %collective-permute-start.12 = (bf16[8,64,512]{2,1,0:T(8,128)(2,1)}, bf16[8,64,512]{2,1,0:T(8,128)(2,1)}, u32[]{:S(2)}, u32[]{:S(2)}) collective-permute-start(bf16[8,64,512]{2,1,0:T(8,128)(2,1)} %get-tuple-element.11), channel_id=1, source_target_pairs={{56,48},{57,49},{58,50},{59,51},{60,52},{61,53},{62,54},{63,55},{1... | collective-permute-start | bytes 1572872 | tf_op jit(solution)/shard_map/ppermute | solution.py:45
  153.4 31.9 %copy-start.1 = (bf16[17,64,512]{2,1,0:T(8,128)(2,1)}, bf16[17,64,512]{2,1,0:T(8,128)(2,1)S(1)}, u32[]{:S(2)}) copy-start(bf16[17,64,512]{2,1,0:T(8,128)(2,1)S(1)} %constant_dynamic-update-slice_fusion.5) | copy-start | bytes 3342340
  186.9 3.7 %copy-start.3 = (bf16[17,64,512]{2,1,0:T(8,128)(2,1)S(1)}, bf16[17,64,512]{2,1,0:T(8,128)(2,1)}, u32[]{:S(2)}) copy-start(bf16[17,64,512]{2,1,0:T(8,128)(2,1)} %rev.6) | copy-start | bytes 3342340
  192.5 2.2 %copy-start.2 = (bf16[17,64,512]{2,1,0:T(8,128)(2,1)S(1)}, bf16[17,64,512]{2,1,0:T(8,128)(2,1)}, u32[]{:S(2)}) copy-start(bf16[17,64,512]{2,1,0:T(8,128)(2,1)} %copy-done.1) | copy-start | bytes 3342340
  197.0 6.7 %copy-start.5 = (bf16[2,1088,256]{1,2,0:T(8,128)(2,1)S(1)}, bf16[2,1088,256]{1,2,0:T(8,128)(2,1)}, u32[]{:S(2)}) copy-start(bf16[2,1088,256]{1,2,0:T(8,128)(2,1)} %copy.64) | copy-start | bytes 3342340

commit v4 on v3

--- a/solution.py
+++ b/solution.py
@@ -86,16 +86,18 @@
         else:
             step.append(lambda core, s=shift: s - lines)
     mine = [weight] + [lax.ppermute(weight, both, pairs_for(f)) for f in step[1:]]
-    mine = jnp.stack(mine)
-    mate = lax.ppermute(mine, both, mate_pairs())
-    blocks = jnp.concatenate([mine, mate], axis=0)
+    mate = lax.ppermute(jnp.stack(mine), both, mate_pairs())
+    parts = [jnp.dot(rows, block, preferred_element_type=jnp.float32) for block in mine]
+    parts += [
+        jnp.dot(rows, mate[index], preferred_element_type=jnp.float32) for index in range(len(mine))
+    ]
+    parts = jnp.stack(parts).astype(jnp.bfloat16)
     seq_index = lax.axis_index("seq")
     line, core = seq_index // 2, seq_index % 2
     wanted = jnp.arange(2 * lines, dtype=jnp.int32)
     slot = (wanted // 2 - line) % lines + lines * (wanted % 2 != core).astype(jnp.int32)
-    ordered = jnp.take(blocks, slot, axis=0)
-    full = jnp.transpose(ordered, (1, 0, 2)).reshape(weight.shape[0], -1)
-    return jnp.dot(rows, full, preferred_element_type=jnp.float32).astype(jnp.bfloat16)
+    ordered = jnp.take(parts, slot, axis=0)
+    return jnp.transpose(ordered, (1, 0, 2)).reshape(rows.shape[0], -1)
 
 
 def body(tokens, qkv_weight, doc_lengths, span_order):
@@ -156,12 +158,16 @@
     far = moved(late_rows[None], count, [(d, d - WINDOW) for d in range(count)])
     down = jnp.concatenate([down, jnp.stack([jnp.zeros_like(far), far], axis=1)], axis=0)
     early_keys = up.reshape(-1, up.shape[-1])
-    around = jnp.concatenate([up[::-1], down[1:, 0]], axis=0)
+    around = jnp.concatenate([up, down[:, 0], down[:, 1]], axis=0)
     steps = jnp.arange(WINDOW + 1, dtype=jnp.int32)
-    mirror = jnp.clip(2 * count - 1 - 2 * my_index - steps + WINDOW, 0, 2 * WINDOW)
-    late_keys = jnp.where(
-        (my_index + steps <= count - 1)[:, None, None], down[:, 1], jnp.take(around, mirror, axis=0)
-    ).reshape(-1, up.shape[-1])
+    source = 2 * count - 1 - my_index - steps
+    pick = jnp.where(
+        my_index + steps <= count - 1,
+        2 * (WINDOW + 1) + steps,
+        jnp.where(source <= my_index, my_index - source, WINDOW + 1 + source - my_index),
+    )
+    pick = jnp.clip(pick, 0, around.shape[0] - 1)
+    late_keys = jnp.take(around, pick, axis=0).reshape(-1, up.shape[-1])
     key_blocks = jnp.stack([early_keys, late_keys])
 
     steps = jnp.arange(WINDOW + 1, dtype=jnp.int32)

time: 211 us -> 198 us (0.938)
  local copies, waits for them, and re-layouts: 30.2 us -> 22.7 us
  other arithmetic: 18.1 us -> 11.1 us
  waiting for transfers between devices: 72 us -> 76.7 us
  starting transfers between devices: 75.7 us -> 72.1 us
    select_n x4, other arithmetic: 5.65 us -> 0.35 us  [the longest x2 0.22 us: body(): late_keys = jnp.take(around, pick, axis=0).reshape(-1, up.shape[-1])]
    gather x2, local copies, waits for them, and re-layouts: 8.07 us -> 3.19 us  [the longest x1 2.56 us: body(): late_keys = jnp.take(around, pick, axis=0).reshape(-1, up.shape[-1])]
    ppermute x11, starting transfers between devices: 54.2 us -> 50.6 us  [moved(): return lax.ppermute(value, 'ctx', pairs)]
    another operation x2, local copies, waits for them, and re-layouts: 0.35 us -> 3.61 us  [body(): jnp.stack([early_queries, late_queries])]
    slice x1 -> x0, local copies, waits for them, and re-layouts: 2.42 us -> none  [body(): down[:, 1]]
    unnamed x2, other arithmetic: 3.25 us -> 0.92 us
    ppermute x11, waiting for transfers between devices: 48.8 us -> 51 us  [moved(): return lax.ppermute(value, 'ctx', pairs)]
    unnamed x24 -> x23, local copies, waits for them, and re-layouts: 6.49 us -> 6.22 us
  transfers between devices with their start and end apart: 15 -> 15, of which waited for: 6 -> 6; matrix products, arithmetic and copies ran while one was open for 10% -> 11% of each run, Pallas kernels for 0% -> 0%
where the time goes in v4:
time: 198 us; the launch traced here: 197 us
  waiting for transfers between devices  76.7 us (39%)
  starting transfers between devices  72.1 us (36%)
  local copies, waits for them, and re-layouts  22.7 us (11%)
  matrix products  13 us (7%)
  other arithmetic  11.1 us (6%)
    ppermute x11, waiting for transfers between devices, moved(): return lax.ppermute(value, 'ctx', pairs)  51 us
    ppermute x11, starting transfers between devices, moved(): return lax.ppermute(value, 'ctx', pairs)  50.6 us
    ppermute x3, waiting for transfers between devices, project(): lax.ppermute(weight, both, pairs_for(f))  23.6 us
    ppermute x3, starting transfers between devices, project(): lax.ppermute(weight, both, pairs_for(f))  16.9 us
    sub x1, matrix products, body(): weights = jnp.where(live, jnp.exp(scores - top), 0.0)  6.23 us
    unnamed x23, local copies, waits for them, and re-layouts  6.22 us
    ppermute x1, starting transfers between devices, project(): mate = lax.ppermute(jnp.stack(mine), both, mate_pairs())  4.6 us
  transfers between devices with their start and end apart: 15, of which 6 were waited for; matrix products, arithmetic and copies ran while one was open for 11% of the time, Pallas kernels for 0%

profile of v4, /device:TPU:56, one launch (start us, length us, event | category | flops | bytes accessed | tf_op | source)
XLA Modules:
  0.0 196.8 jit_solution(3835402072261659273)
XLA Ops:
  0.0 11.1 %collective-permute-start = (bf16[2048,192]{0,1:T(8,128)(2,1)}, bf16[2048,192]{0,1:T(8,128)(2,1)S(1)}, u32[]{:S(2)}, u32[]{:S(2)}) collective-permute-start(bf16[2048,192]{0,1:T(8,128)(2,1)} %param.5), channel_id=1, source_target_pairs={{128,0},{129,1},{130,2},{131,3},{132,4},{133,5},{134,6},{135,7},{1... | collective-permute-start | bytes 2359304 | tf_op jit(solution)/shard_map/ppermute | solution.py:88
  11.1 2.5 %collective-permute-start.1 = (bf16[2048,192]{0,1:T(8,128)(2,1)}, bf16[2048,192]{0,1:T(8,128)(2,1)S(1)}, u32[]{:S(2)}, u32[]{:S(2)}) collective-permute-start(bf16[2048,192]{0,1:T(8,128)(2,1)} %param.5), channel_id=1, source_target_pairs={{256,0},{257,1},{258,2},{259,3},{260,4},{261,5},{262,6},{263,7},{2... | collective-permute-start | bytes 2359304 | tf_op jit(solution)/shard_map/ppermute | solution.py:88
  13.5 3.4 %collective-permute-start.2 = (bf16[2048,192]{0,1:T(8,128)(2,1)}, bf16[2048,192]{0,1:T(8,128)(2,1)S(1)}, u32[]{:S(2)}, u32[]{:S(2)}) collective-permute-start(bf16[2048,192]{0,1:T(8,128)(2,1)} %param.5), channel_id=1, source_target_pairs={{416,0},{417,1},{418,2},{419,3},{420,4},{421,5},{422,6},{423,7},{4... | collective-permute-start | bytes 2359304 | tf_op jit(solution)/shard_map/ppermute | solution.py:88
  17.7 1.3 fusion.69
  20.2 0.8 copy.41
  21.5 15.1 %collective-permute-done = bf16[2048,192]{0,1:T(8,128)(2,1)S(1)} collective-permute-done((bf16[2048,192]{0,1:T(8,128)(2,1)}, bf16[2048,192]{0,1:T(8,128)(2,1)S(1)}, u32[]{:S(2)}, u32[]{:S(2)}) %collective-permute-start) | collective-permute-done | bytes 786464 | tf_op jit(solution)/shard_map/ppermute | solution.py:88
  36.6 8.4 %collective-permute-done.1 = bf16[2048,192]{0,1:T(8,128)(2,1)S(1)} collective-permute-done((bf16[2048,192]{0,1:T(8,128)(2,1)}, bf16[2048,192]{0,1:T(8,128)(2,1)S(1)}, u32[]{:S(2)}, u32[]{:S(2)}) %collective-permute-start.1) | collective-permute-done | bytes 786464 | tf_op jit(solution)/shard_map/ppermute | solution.py:88
  45.0 1.5 pad_maximum_fusion
  46.5 4.6 %collective-permute-start.3 = (bf16[4,2048,192]{1,2,0:T(8,128)(2,1)S(1)}, bf16[4,2048,192]{1,2,0:T(8,128)(2,1)S(1)}, u32[]{:S(2)}, u32[]{:S(2)}) collective-permute-start(bf16[4,2048,192]{1,2,0:T(8,128)(2,1)S(1)} %pad_maximum_fusion), channel_id=1, source_target_pairs={{64,0},{65,1},{66,2},{67,3},{68,4},{69,5},{70,6},{71,7},{72,8},{73... | collective-permute-start | bytes 9437192 | tf_op jit(solution)/shard_map/ppermute | solution.py:89
  52.3 0.9 and_and_fusion
  54.3 2.1 %collective-permute-done.3 = bf16[4,2048,192]{1,2,0:T(8,128)(2,1)S(1)} collective-permute-done((bf16[4,2048,192]{1,2,0:T(8,128)(2,1)S(1)}, bf16[4,2048,192]{1,2,0:T(8,128)(2,1)S(1)}, u32[]{:S(2)}, u32[]{:S(2)}) %collective-permute-start.3) | collective-permute-done | bytes 3145760 | tf_op jit(solution)/shard_map/ppermute | solution.py:89
  59.1 0.7 constant_dynamic-update-slice_fusion.5
  59.7 3.4 %collective-permute-start.4 = (bf16[1,64,512]{2,1,0:T(8,128)(2,1)S(1)}, bf16[1,64,512]{2,1,0:T(8,128)(2,1)S(1)}, u32[]{:S(2)}, u32[]{:S(2)}) collective-permute-start(bf16[1,64,512]{2,1,0:T(8,128)(2,1)S(1)} %bitcast.164), channel_id=1, source_target_pairs={{0,1},{1,2},{2,3},{3,4},{4,5},{5,6},{6,7},{7,8},{8,9},{9,10},{10,1... | collective-permute-start | bytes 196616 | tf_op jit(solution)/shard_map/ppermute | solution.py:45
  63.1 7.9 %collective-permute-start.8 = (bf16[1,64,512]{2,1,0:T(8,128)(2,1)S(1)}, bf16[1,64,512]{2,1,0:T(8,128)(2,1)}, u32[]{:S(2)}, u32[]{:S(2)}) collective-permute-start(bf16[1,64,512]{2,1,0:T(8,128)(2,1)S(1)} %bitcast.165), channel_id=1, source_target_pairs={{0,16},{1,17},{2,18},{3,19},{4,20},{5,21},{6,22},{7,23},{8,24},{9,... | collective-permute-start | bytes 196616 | tf_op jit(solution)/shard_map/ppermute | solution.py:45
  71.1 0.7 copy.43
  71.8 2.4 %collective-permute-start.14 = (bf16[1,64,512]{2,1,0:T(8,128)(2,1)}, bf16[1,64,512]{2,1,0:T(8,128)(2,1)}, u32[]{:S(2)}, u32[]{:S(2)}) collective-permute-start(bf16[1,64,512]{2,1,0:T(8,128)(2,1)} %bitcast.35), channel_id=1, source_target_pairs={{16,0},{17,1},{18,2},{19,3},{20,4},{21,5},{22,6},{23,7},{24,8},{25... | collective-permute-start | bytes 196616 | tf_op jit(solution)/shard_map/ppermute | solution.py:45
  74.3 0.8 bitcast_dynamic-update-slice_fusion
  75.1 1.5 fusion.49
  76.7 4.5 %collective-permute-start.9 = (bf16[1,2,64,512]{3,2,1,0:T(8,128)(2,1)S(1)}, bf16[1,2,64,512]{3,2,1,0:T(8,128)(2,1)S(1)}, u32[]{:S(2)}, u32[]{:S(2)}) collective-permute-start(bf16[1,2,64,512]{3,2,1,0:T(8,128)(2,1)S(1)} %get-tuple-element.33), channel_id=1, source_target_pairs={{1,0},{2,1},{3,2},{4,3},{5,4},{6,5},{7,6},{8,7},{9,8},{10,9},{11,1... | collective-permute-start | bytes 393224 | tf_op jit(solution)/shard_map/ppermute | solution.py:45
  81.3 2.8 %collective-permute-start.5 = (bf16[2,64,512]{2,1,0:T(8,128)(2,1)}, bf16[2,64,512]{2,1,0:T(8,128)(2,1)S(1)}, u32[]{:S(2)}, u32[]{:S(2)}) collective-permute-start(bf16[2,64,512]{2,1,0:T(8,128)(2,1)} %get-tuple-element.34), channel_id=1, source_target_pairs={{0,2},{1,3},{2,4},{3,5},{4,6},{5,7},{6,8},{7,9},{8,10},{9,11},{10,... | collective-permute-start | bytes 393224 | tf_op jit(solution)/shard_map/ppermute | solution.py:45
  84.2 0.7 pad_maximum_fusion.12
  84.9 5.4 %collective-permute-start.10 = (bf16[2,2,64,512]{3,2,1,0:T(8,128)(2,1)}, bf16[2,2,64,512]{3,2,1,0:T(8,128)(2,1)S(1)}, u32[]{:S(2)}, u32[]{:S(2)}) collective-permute-start(bf16[2,2,64,512]{3,2,1,0:T(8,128)(2,1)} %pad_maximum_fusion.12), channel_id=1, source_target_pairs={{2,0},{3,1},{4,2},{5,3},{6,4},{7,5},{8,6},{9,7},{10,8},{11,9},{12,... | collective-permute-start | bytes 786440 | tf_op jit(solution)/shard_map/ppermute | solution.py:45
  90.3 1.0 constant_dynamic-slice_fusion.1
  91.3 1.8 copy.53
  93.1 1.8 copy.52
  94.9 0.7 constant_dynamic-update-slice_fusion.4
  95.6 16.9 %collective-permute-start.6 = (bf16[4,64,512]{2,1,0:T(8,128)(2,1)S(1)}, bf16[4,64,512]{2,1,0:T(8,128)(2,1)S(1)}, u32[]{:S(2)}, u32[]{:S(2)}) collective-permute-start(bf16[4,64,512]{2,1,0:T(8,128)(2,1)S(1)} %pad_maximum_fusion.11), channel_id=1, source_target_pairs={{0,4},{1,5},{2,6},{3,7},{4,8},{5,9},{6,10},{7,11},{8,12},{9,13},{1... | collective-permute-start | bytes 786440 | tf_op jit(solution)/shard_map/ppermute | solution.py:45
  112.6 1.9 collective-permute-start.11
  114.6 0.7 constant_dynamic-update-slice_fusion.3
  115.3 3.3 %collective-permute-done.6 = bf16[4,64,512]{2,1,0:T(8,128)(2,1)S(1)} collective-permute-done((bf16[4,64,512]{2,1,0:T(8,128)(2,1)S(1)}, bf16[4,64,512]{2,1,0:T(8,128)(2,1)S(1)}, u32[]{:S(2)}, u32[]{:S(2)}) %collective-permute-start.6) | collective-permute-done | bytes 262176 | tf_op jit(solution)/shard_map/ppermute | solution.py:45
  118.6 2.5 %collective-permute-start.7 = (bf16[8,64,512]{2,1,0:T(8,128)(2,1)S(1)}, bf16[8,64,512]{2,1,0:T(8,128)(2,1)S(1)}, u32[]{:S(2)}, u32[]{:S(2)}) collective-permute-start(bf16[8,64,512]{2,1,0:T(8,128)(2,1)S(1)} %pad_maximum_fusion.3), channel_id=1, source_target_pairs={{0,8},{1,9},{2,10},{3,11},{4,12},{5,13},{6,14},{7,15},{8,16},{9,17... | collective-permute-start | bytes 1572872 | tf_op jit(solution)/shard_map/ppermute | solution.py:45
  121.1 22.2 %collective-permute-done.11 = bf16[4,2,64,512]{3,2,1,0:T(8,128)(2,1)S(1)} collective-permute-done((bf16[4,2,64,512]{3,2,1,0:T(8,128)(2,1)S(1)}, bf16[4,2,64,512]{3,2,1,0:T(8,128)(2,1)S(1)}, u32[]{:S(2)}, u32[]{:S(2)}) %collective-permute-start.11) | collective-permute-done | bytes 524320 | tf_op jit(solution)/shard_map/ppermute | solution.py:45
  143.5 1.9 collective-permute-start.13
  145.4 0.9 collective-permute-start.12
  146.3 0.8 constant_dynamic-update-slice_fusion.2
  147.2 1.1 constant_dynamic-update-slice_fusion.1
  148.3 1.5 constant_dynamic-update-slice_fusion
  149.8 25.5 %collective-permute-done.13 = bf16[8,64,512]{2,1,0:T(8,128)(2,1)S(1)} collective-permute-done((bf16[8,64,512]{2,1,0:T(8,128)(2,1)S(1)}, bf16[8,64,512]{2,1,0:T(8,128)(2,1)S(1)}, u32[]{:S(2)}, u32[]{:S(2)}) %collective-permute-start.13) | collective-permute-done | bytes 524320 | tf_op jit(solution)/shard_map/ppermute | solution.py:45
  175.4 0.8 pad_dynamic-update-slice_fusion
  176.3 1.1 fusion.36
  177.4 1.1 fusion.35
  178.5 2.6 %gather_fusion.1 = bf16[17,64,512]{2,1,0:T(8,128)(2,1)S(1)} fusion(bf16[51,64,512]{2,1,0:T(8,128)(2,1)} %fusion.35, s32[1024]{0:T(1024)S(1)} %pad_clamp_fusion), kind=kCustom, calls=%fused_computation.1 | custom fusion | bytes 2228292 | tf_op jit(solution)/shard_map/jit(_take)/gather | solution.py:170
  181.3 1.0 copy-done.2
  182.5 1.4 copy.54
  183.9 0.7 copy.49
  184.7 6.2 %fusion.70 = (f32[2,4,4,64]{3,2,1,0:T(4,128)}, bf16[2,4,4,64,1088]{4,3,2,1,0:T(8,128)(2,1)}) fusion(pred[2,64,1088]{2,1,0:T(8,128)(4,1)S(1)} %copy-done.6, bf16[2,1088,4,64,1]{1,3,4,2,0:T(8,128)(2,1)S(1)} %bitcast.174, bf16[1,64,4,4,64]{4,1,3,2,0:T(8,128)(2,1)S(1)} %copy-done.4, bf16[1,64,4,4,64]{4,1,3,2,0:T(8,128)(2,1)S(1)} %copy-done.5), kind=kOutput, calls=%fused_computation.172 | convolution fusion | flops 299107392 | bytes 5980160 | tf_op jit(solution)/shard_map/sub | solution.py:200
  190.9 3.7 %fusion.15 = bf16[2,64,4,4,64]{4,1,3,2,0:T(8,128)(2,1)S(1)} fusion(bf16[2,1088,4,64,1]{1,3,4,2,0:T(8,128)(2,1)S(1)} %bitcast.173, bf16[2,4,4,64,1088]{4,3,2,1,0:T(8,128)(2,1)} %get-tuple-element.38, f32[2,64,4,4]{1,3,2,0:T(4,128)} %bitcast.183), kind=kOutput, calls=%fused_computation.17 | convolution fusion | flops 285474816 | bytes 5840896 | tf_op jit(solution)/shard_map/shgqk,skhd->shgqd/dot_general | solution.py:202
  195.4 1.4 reverse_select_fusion
  (84 shorter events, 8.4 us)
Async XLA Ops:
  0.0 51.9 %copy-start = (bf16[1,128,2048]{2,1,0:T(8,128)(2,1)S(1)}, bf16[1,128,2048]{2,1,0:T(8,128)(2,1)}, u32[]{:S(2)}) copy-start(bf16[1,128,2048]{2,1,0:T(8,128)(2,1)} %param.4) | copy-start | bytes 1572868
  0.0 36.6 %collective-permute-start = (bf16[2048,192]{0,1:T(8,128)(2,1)}, bf16[2048,192]{0,1:T(8,128)(2,1)S(1)}, u32[]{:S(2)}, u32[]{:S(2)}) collective-permute-start(bf16[2048,192]{0,1:T(8,128)(2,1)} %param.5), channel_id=1, source_target_pairs={{128,0},{129,1},{130,2},{131,3},{132,4},{133,5},{134,6},{135,7},{1... | collective-permute-start | bytes 2359304 | tf_op jit(solution)/shard_map/ppermute | solution.py:88
  11.1 33.9 %collective-permute-start.1 = (bf16[2048,192]{0,1:T(8,128)(2,1)}, bf16[2048,192]{0,1:T(8,128)(2,1)S(1)}, u32[]{:S(2)}, u32[]{:S(2)}) collective-permute-start(bf16[2048,192]{0,1:T(8,128)(2,1)} %param.5), channel_id=1, source_target_pairs={{256,0},{257,1},{258,2},{259,3},{260,4},{261,5},{262,6},{263,7},{2... | collective-permute-start | bytes 2359304 | tf_op jit(solution)/shard_map/ppermute | solution.py:88
  13.5 31.5 %collective-permute-start.2 = (bf16[2048,192]{0,1:T(8,128)(2,1)}, bf16[2048,192]{0,1:T(8,128)(2,1)S(1)}, u32[]{:S(2)}, u32[]{:S(2)}) collective-permute-start(bf16[2048,192]{0,1:T(8,128)(2,1)} %param.5), channel_id=1, source_target_pairs={{416,0},{417,1},{418,2},{419,3},{420,4},{421,5},{422,6},{423,7},{4... | collective-permute-start | bytes 2359304 | tf_op jit(solution)/shard_map/ppermute | solution.py:88
  45.0 6.9 %copy-start.1 = (bf16[2048,192]{0,1:T(8,128)(2,1)S(1)}, bf16[2048,192]{0,1:T(8,128)(2,1)}, u32[]{:S(2)}) copy-start(bf16[2048,192]{0,1:T(8,128)(2,1)} %param.5) | copy-start | bytes 2359300
  46.5 9.9 %collective-permute-start.3 = (bf16[4,2048,192]{1,2,0:T(8,128)(2,1)S(1)}, bf16[4,2048,192]{1,2,0:T(8,128)(2,1)S(1)}, u32[]{:S(2)}, u32[]{:S(2)}) collective-permute-start(bf16[4,2048,192]{1,2,0:T(8,128)(2,1)S(1)} %pad_maximum_fusion), channel_id=1, source_target_pairs={{64,0},{65,1},{66,2},{67,3},{68,4},{69,5},{70,6},{71,7},{72,8},{73... | collective-permute-start | bytes 9437192 | tf_op jit(solution)/shard_map/ppermute | solution.py:89
  59.7 15.4 %collective-permute-start.4 = (bf16[1,64,512]{2,1,0:T(8,128)(2,1)S(1)}, bf16[1,64,512]{2,1,0:T(8,128)(2,1)S(1)}, u32[]{:S(2)}, u32[]{:S(2)}) collective-permute-start(bf16[1,64,512]{2,1,0:T(8,128)(2,1)S(1)} %bitcast.164), channel_id=1, source_target_pairs={{0,1},{1,2},{2,3},{3,4},{4,5},{5,6},{6,7},{7,8},{8,9},{9,10},{10,1... | collective-permute-start | bytes 196616 | tf_op jit(solution)/shard_map/ppermute | solution.py:45
  63.1 85.2 %collective-permute-start.8 = (bf16[1,64,512]{2,1,0:T(8,128)(2,1)S(1)}, bf16[1,64,512]{2,1,0:T(8,128)(2,1)}, u32[]{:S(2)}, u32[]{:S(2)}) collective-permute-start(bf16[1,64,512]{2,1,0:T(8,128)(2,1)S(1)} %bitcast.165), channel_id=1, source_target_pairs={{0,16},{1,17},{2,18},{3,19},{4,20},{5,21},{6,22},{7,23},{8,24},{9,... | collective-permute-start | bytes 196616 | tf_op jit(solution)/shard_map/ppermute | solution.py:45
  71.8 103.6 %collective-permute-start.14 = (bf16[1,64,512]{2,1,0:T(8,128)(2,1)}, bf16[1,64,512]{2,1,0:T(8,128)(2,1)}, u32[]{:S(2)}, u32[]{:S(2)}) collective-permute-start(bf16[1,64,512]{2,1,0:T(8,128)(2,1)} %bitcast.35), channel_id=1, source_target_pairs={{16,0},{17,1},{18,2},{19,3},{20,4},{21,5},{22,6},{23,7},{24,8},{25... | collective-permute-start | bytes 196616 | tf_op jit(solution)/shard_map/ppermute | solution.py:45
  76.7 7.5 %collective-permute-start.9 = (bf16[1,2,64,512]{3,2,1,0:T(8,128)(2,1)S(1)}, bf16[1,2,64,512]{3,2,1,0:T(8,128)(2,1)S(1)}, u32[]{:S(2)}, u32[]{:S(2)}) collective-permute-start(bf16[1,2,64,512]{3,2,1,0:T(8,128)(2,1)S(1)} %get-tuple-element.33), channel_id=1, source_target_pairs={{1,0},{2,1},{3,2},{4,3},{5,4},{6,5},{7,6},{8,7},{9,8},{10,9},{11,1... | collective-permute-start | bytes 393224 | tf_op jit(solution)/shard_map/ppermute | solution.py:45
  81.3 14.3 %collective-permute-start.5 = (bf16[2,64,512]{2,1,0:T(8,128)(2,1)}, bf16[2,64,512]{2,1,0:T(8,128)(2,1)S(1)}, u32[]{:S(2)}, u32[]{:S(2)}) collective-permute-start(bf16[2,64,512]{2,1,0:T(8,128)(2,1)} %get-tuple-element.34), channel_id=1, source_target_pairs={{0,2},{1,3},{2,4},{3,5},{4,6},{5,7},{6,8},{7,9},{8,10},{9,11},{10,... | collective-permute-start | bytes 393224 | tf_op jit(solution)/shard_map/ppermute | solution.py:45
  84.9 27.7 %collective-permute-start.10 = (bf16[2,2,64,512]{3,2,1,0:T(8,128)(2,1)}, bf16[2,2,64,512]{3,2,1,0:T(8,128)(2,1)S(1)}, u32[]{:S(2)}, u32[]{:S(2)}) collective-permute-start(bf16[2,2,64,512]{3,2,1,0:T(8,128)(2,1)} %pad_maximum_fusion.12), channel_id=1, source_target_pairs={{2,0},{3,1},{4,2},{5,3},{6,4},{7,5},{8,6},{9,7},{10,8},{11,9},{12,... | collective-permute-start | bytes 786440 | tf_op jit(solution)/shard_map/ppermute | solution.py:45
  95.6 22.9 %collective-permute-start.6 = (bf16[4,64,512]{2,1,0:T(8,128)(2,1)S(1)}, bf16[4,64,512]{2,1,0:T(8,128)(2,1)S(1)}, u32[]{:S(2)}, u32[]{:S(2)}) collective-permute-start(bf16[4,64,512]{2,1,0:T(8,128)(2,1)S(1)} %pad_maximum_fusion.11), channel_id=1, source_target_pairs={{0,4},{1,5},{2,6},{3,7},{4,8},{5,9},{6,10},{7,11},{8,12},{9,13},{1... | collective-permute-start | bytes 786440 | tf_op jit(solution)/shard_map/ppermute | solution.py:45
  112.6 30.7 %collective-permute-start.11 = (bf16[4,2,64,512]{3,2,1,0:T(8,128)(2,1)S(1)}, bf16[4,2,64,512]{3,2,1,0:T(8,128)(2,1)S(1)}, u32[]{:S(2)}, u32[]{:S(2)}) collective-permute-start(bf16[4,2,64,512]{3,2,1,0:T(8,128)(2,1)S(1)} %pad_maximum_fusion.4), channel_id=1, source_target_pairs={{4,0},{5,1},{6,2},{7,3},{8,4},{9,5},{10,6},{11,7},{12,8},{13,9},{1... | collective-permute-start | bytes 1572872 | tf_op jit(solution)/shard_map/ppermute | solution.py:45
  118.6 28.5 %collective-permute-start.7 = (bf16[8,64,512]{2,1,0:T(8,128)(2,1)S(1)}, bf16[8,64,512]{2,1,0:T(8,128)(2,1)S(1)}, u32[]{:S(2)}, u32[]{:S(2)}) collective-permute-start(bf16[8,64,512]{2,1,0:T(8,128)(2,1)S(1)} %pad_maximum_fusion.3), channel_id=1, source_target_pairs={{0,8},{1,9},{2,10},{3,11},{4,12},{5,13},{6,14},{7,15},{8,16},{9,17... | collective-permute-start | bytes 1572872 | tf_op jit(solution)/shard_map/ppermute | solution.py:45
  143.5 31.8 %collective-permute-start.13 = (bf16[8,64,512]{2,1,0:T(8,128)(2,1)S(1)}, bf16[8,64,512]{2,1,0:T(8,128)(2,1)S(1)}, u32[]{:S(2)}, u32[]{:S(2)}) collective-permute-start(bf16[8,64,512]{2,1,0:T(8,128)(2,1)S(1)} %get-tuple-element.10), channel_id=1, source_target_pairs={{8,0},{9,1},{10,2},{11,3},{12,4},{13,5},{14,6},{15,7},{16,8},{17,9... | collective-permute-start | bytes 1572872 | tf_op jit(solution)/shard_map/ppermute | solution.py:45
  145.4 29.9 %collective-permute-start.12 = (bf16[8,64,512]{2,1,0:T(8,128)(2,1)S(1)}, bf16[8,64,512]{2,1,0:T(8,128)(2,1)S(1)}, u32[]{:S(2)}, u32[]{:S(2)}) collective-permute-start(bf16[8,64,512]{2,1,0:T(8,128)(2,1)S(1)} %get-tuple-element.9), channel_id=1, source_target_pairs={{56,48},{57,49},{58,50},{59,51},{60,52},{61,53},{62,54},{63,55},{1... | collective-permute-start | bytes 1572872 | tf_op jit(solution)/shard_map/ppermute | solution.py:45
  181.1 1.2 copy-start.2
  182.5 2.2 %copy-start.4 = (bf16[1,64,4,4,64]{4,1,3,2,0:T(8,128)(2,1)S(1)}, bf16[1,64,4,4,64]{4,1,3,2,0:T(8,128)(2,1)}, u32[]{:S(2)}) copy-start(bf16[1,64,4,4,64]{4,1,3,2,0:T(8,128)(2,1)} %copy.53) | copy-start | bytes 393220
  182.5 2.2 %copy-start.5 = (bf16[1,64,4,4,64]{4,1,3,2,0:T(8,128)(2,1)S(1)}, bf16[1,64,4,4,64]{4,1,3,2,0:T(8,128)(2,1)}, u32[]{:S(2)}) copy-start(bf16[1,64,4,4,64]{4,1,3,2,0:T(8,128)(2,1)} %copy.52) | copy-start | bytes 393220
  182.5 2.2 %copy-start.6 = (pred[2,64,1088]{2,1,0:T(8,128)(4,1)S(1)}, pred[2,64,1088]{2,1,0:T(8,128)(4,1)}, u32[]{:S(2)}) copy-start(pred[2,64,1088]{2,1,0:T(8,128)(4,1)} %and_and_fusion) | copy-start | bytes 417796
  184.7 6.2 %copy-start.3 = (bf16[2,1088,256]{1,2,0:T(8,128)(2,1)S(1)}, bf16[2,1088,256]{1,2,0:T(8,128)(2,1)}, u32[]{:S(2)}) copy-start(bf16[2,1088,256]{1,2,0:T(8,128)(2,1)} %copy.54) | copy-start | bytes 3342340

commit v5 on v4

--- a/solution.py
+++ b/solution.py
@@ -2,6 +2,8 @@
 import jax.numpy as jnp
 from jax import lax
 from jax.sharding import PartitionSpec as P
+from jax.experimental import pallas as pl
+from jax.experimental.pallas import tpu as pltpu
 
 QUERY_HEADS = 16
 KEY_VALUE_HEADS = 4
@@ -185,33 +187,54 @@
         & key_ok[:, None, :]
     )
 
-    queries = jnp.stack([early_queries, late_queries]).reshape(
-        2, SPAN, KEY_VALUE_HEADS, QUERY_PER_KV, HEAD_SIZE
-    )
-    keys = key_blocks[:, :, :key_cols].reshape(2, -1, KEY_VALUE_HEADS, HEAD_SIZE)
-    values = key_blocks[:, :, key_cols:].reshape(2, -1, KEY_VALUE_HEADS, HEAD_SIZE)
-    scores = (
-        jnp.einsum("sqhgd,skhd->shgqk", queries, keys, preferred_element_type=jnp.float32)
-        * 0.125
-    )
-    live = live[:, None, None]
-    scores = jnp.where(live, scores, -1e30)
-    top = jnp.max(scores, axis=-1, keepdims=True)
-    weights = jnp.where(live, jnp.exp(scores - top), 0.0)
-    total = jnp.sum(weights, axis=-1)
-    summed = jnp.einsum(
-        "shgqk,skhd->shgqd",
-        weights.astype(jnp.bfloat16),
-        values,
-        preferred_element_type=jnp.float32,
-    )
-    outputs = summed / total[..., None]
-    outputs = jnp.transpose(outputs, (0, 3, 1, 2, 4)).reshape(2, SPAN, QUERY_HEADS * HEAD_SIZE)
-    outputs = outputs.astype(jnp.bfloat16)
-    ordered = jnp.where(early_first, outputs, outputs[::-1]).reshape(
-        token_count, QUERY_HEADS * HEAD_SIZE
-    )
-    return ordered[None]
+    key_docs = jnp.where(key_ok, key_docs, -1)
+    return attend(
+        offset.reshape(1),
+        query_rows,
+        early_keys,
+        late_keys,
+        query_places[:, :, None],
+        query_docs[:, :, None],
+        key_places[:, None, :],
+        key_docs[:, None, :],
+    )[None]
+
+
+def attend_kernel(offset_ref, q_ref, early_ref, late_ref, qpos_ref, qdoc_ref, kpos_ref, kdoc_ref, o_ref):
+    offset = pl.multiple_of(offset_ref[0], SPAN)
+    for span, kv_ref in ((0, early_ref), (1, late_ref)):
+        row = offset if span == 0 else SPAN - offset
+        row = pl.multiple_of(row, SPAN)
+        live = (qdoc_ref[span] == kdoc_ref[span]) & (kpos_ref[span] <= qpos_ref[span])
+        for group in range(KEY_VALUE_HEADS):
+            key = kv_ref[:, group * HEAD_SIZE : (group + 1) * HEAD_SIZE]
+            base = KEY_VALUE_HEADS * HEAD_SIZE + group * HEAD_SIZE
+            value = kv_ref[:, base : base + HEAD_SIZE]
+            for member in range(QUERY_PER_KV):
+                head = group * QUERY_PER_KV + member
+                cols = slice(head * HEAD_SIZE, (head + 1) * HEAD_SIZE)
+                query = q_ref[pl.ds(row, SPAN), cols]
+                scores = lax.dot_general(
+                    query, key, (((1,), (1,)), ((), ())), preferred_element_type=jnp.float32
+                ) * 0.125
+                scores = jnp.where(live, scores, -1e30)
+                top = jnp.max(scores, axis=1, keepdims=True)
+                weights = jnp.where(live, jnp.exp(scores - top), 0.0)
+                total = jnp.sum(weights, axis=1, keepdims=True)
+                summed = jnp.dot(
+                    weights.astype(jnp.bfloat16), value, preferred_element_type=jnp.float32
+                )
+                o_ref[pl.ds(row, SPAN), cols] = (summed / total).astype(o_ref.dtype)
+
+
+def attend(offset, query_rows, early_keys, late_keys, qpos, qdoc, kpos, kdoc):
+    vmem = pl.BlockSpec(memory_space=pltpu.VMEM)
+    return pl.pallas_call(
+        attend_kernel,
+        out_shape=jax.ShapeDtypeStruct(query_rows.shape, query_rows.dtype),
+        in_specs=[pl.BlockSpec(memory_space=pltpu.SMEM)] + [vmem] * 7,
+        out_specs=vmem,
+    )(offset, query_rows, early_keys, late_keys, qpos, qdoc, kpos, kdoc)
 
 
 def solution(mesh):

time: 198 us -> 195 us (0.985)
  Pallas kernels: 0 us -> 14.3 us
  matrix products: 13 us -> 3.08 us
  local copies, waits for them, and re-layouts: 22.7 us -> 16.8 us
    pallas_call x0 -> x1, Pallas kernels: none -> 14.3 us  [attend(): pl.pallas_call(attend_kernel, out_shape=jax.ShapeDtypeStruct(query_rows.s...]
    sub x1 -> x0, matrix products: 6.23 us -> none  [body(): weights = jnp.where(live, jnp.exp(scores - top), 0.0)]
    dot_general x1 -> x0, matrix products: 3.71 us -> none  [body(): jnp.einsum('shgqk,skhd->shgqd', weights.astype(jnp.bfloat16), values, pre...]
    another operation x3 -> x1, local copies, waits for them, and re-layouts: 4.36 us -> 0.75 us  [the longest x2 3.61 us: body(): jnp.stack([early_queries, late_queries])]
    slice x2 -> x0, local copies, waits for them, and re-layouts: 2.13 us -> none  [the longest x1 1.43 us: body(): key_blocks[:, :, key_cols:].reshape(2, -1, KEY_VALUE_HEADS, HEAD_SIZE)]
    unnamed x23 -> x14, local copies, waits for them, and re-layouts: 6.22 us -> 6.71 us
where the time goes in v5:
time: 195 us; the launch traced here: 194 us
  waiting for transfers between devices  75 us (38%)
  starting transfers between devices  72.1 us (37%)
  local copies, waits for them, and re-layouts  16.8 us (9%)
  Pallas kernels  14.3 us (7%)
  other arithmetic  11.8 us (6%)
  matrix products  3.08 us (2%)
    ppermute x11, starting transfers between devices, moved(): return lax.ppermute(value, 'ctx', pairs)  50.6 us
    ppermute x11, waiting for transfers between devices, moved(): return lax.ppermute(value, 'ctx', pairs)  50.6 us
    ppermute x3, waiting for transfers between devices, project(): lax.ppermute(weight, both, pairs_for(f))  22.6 us
    ppermute x3, starting transfers between devices, project(): lax.ppermute(weight, both, pairs_for(f))  16.9 us
    pallas_call x1, Pallas kernels, attend(): pl.pallas_call(attend_kernel, out_shape=jax.ShapeDtypeStruct(query_rows.s...  14.3 us
    unnamed x14, local copies, waits for them, and re-layouts  6.71 us
    ppermute x1, starting transfers between devices, project(): mate = lax.ppermute(jnp.stack(mine), both, mate_pairs())  4.6 us
  transfers between devices with their start and end apart: 15, of which 6 were waited for; matrix products, arithmetic and copies ran while one was open for 11% of the time, Pallas kernels for 0%

profile of v5, /device:TPU:56, one launch (start us, length us, event | category | flops | bytes accessed | tf_op | source)
XLA Modules:
  0.0 194.2 jit_solution(9696423301103080323)
XLA Ops:
  0.0 11.1 %collective-permute-start = (bf16[2048,192]{0,1:T(8,128)(2,1)}, bf16[2048,192]{0,1:T(8,128)(2,1)S(1)}, u32[]{:S(2)}, u32[]{:S(2)}) collective-permute-start(bf16[2048,192]{0,1:T(8,128)(2,1)} %param.5), channel_id=1, source_target_pairs={{128,0},{129,1},{130,2},{131,3},{132,4},{133,5},{134,6},{135,7},{1... | collective-permute-start | bytes 2359304 | tf_op jit(solution)/shard_map/ppermute | solution.py:90
  11.1 2.5 %collective-permute-start.1 = (bf16[2048,192]{0,1:T(8,128)(2,1)}, bf16[2048,192]{0,1:T(8,128)(2,1)S(1)}, u32[]{:S(2)}, u32[]{:S(2)}) collective-permute-start(bf16[2048,192]{0,1:T(8,128)(2,1)} %param.5), channel_id=1, source_target_pairs={{256,0},{257,1},{258,2},{259,3},{260,4},{261,5},{262,6},{263,7},{2... | collective-permute-start | bytes 2359304 | tf_op jit(solution)/shard_map/ppermute | solution.py:90
  13.5 3.4 %collective-permute-start.2 = (bf16[2048,192]{0,1:T(8,128)(2,1)}, bf16[2048,192]{0,1:T(8,128)(2,1)S(1)}, u32[]{:S(2)}, u32[]{:S(2)}) collective-permute-start(bf16[2048,192]{0,1:T(8,128)(2,1)} %param.5), channel_id=1, source_target_pairs={{416,0},{417,1},{418,2},{419,3},{420,4},{421,5},{422,6},{423,7},{4... | collective-permute-start | bytes 2359304 | tf_op jit(solution)/shard_map/ppermute | solution.py:90
  17.3 0.7 multiply_bitcast_fusion
  18.0 1.2 fusion.45
  20.2 0.8 copy.73
  21.3 0.7 copy.78.qdoc_ref
  22.4 14.2 %collective-permute-done = bf16[2048,192]{0,1:T(8,128)(2,1)S(1)} collective-permute-done((bf16[2048,192]{0,1:T(8,128)(2,1)}, bf16[2048,192]{0,1:T(8,128)(2,1)S(1)}, u32[]{:S(2)}, u32[]{:S(2)}) %collective-permute-start) | collective-permute-done | bytes 786464 | tf_op jit(solution)/shard_map/ppermute | solution.py:90
  36.6 8.4 %collective-permute-done.1 = bf16[2048,192]{0,1:T(8,128)(2,1)S(1)} collective-permute-done((bf16[2048,192]{0,1:T(8,128)(2,1)}, bf16[2048,192]{0,1:T(8,128)(2,1)S(1)}, u32[]{:S(2)}, u32[]{:S(2)}) %collective-permute-start.1) | collective-permute-done | bytes 786464 | tf_op jit(solution)/shard_map/ppermute | solution.py:90
  45.0 1.5 pad_maximum_fusion
  46.5 4.6 %collective-permute-start.3 = (bf16[4,2048,192]{1,2,0:T(8,128)(2,1)S(1)}, bf16[4,2048,192]{1,2,0:T(8,128)(2,1)S(1)}, u32[]{:S(2)}, u32[]{:S(2)}) collective-permute-start(bf16[4,2048,192]{1,2,0:T(8,128)(2,1)S(1)} %pad_maximum_fusion), channel_id=1, source_target_pairs={{64,0},{65,1},{66,2},{67,3},{68,4},{69,5},{70,6},{71,7},{72,8},{73... | collective-permute-start | bytes 9437192 | tf_op jit(solution)/shard_map/ppermute | solution.py:91
  51.7 0.7 iota_add_fusion.qpos_ref
  52.8 0.6 reshape_select_fusion
  54.6 1.8 collective-permute-done.3
  56.8 0.4 fusion.11
  58.0 0.6 gather_fusion
  59.1 3.4 %collective-permute-start.4 = (bf16[1,64,512]{2,1,0:T(8,128)(2,1)S(1)}, bf16[1,64,512]{2,1,0:T(8,128)(2,1)S(1)}, u32[]{:S(2)}, u32[]{:S(2)}) collective-permute-start(bf16[1,64,512]{2,1,0:T(8,128)(2,1)S(1)} %bitcast.138), channel_id=1, source_target_pairs={{0,1},{1,2},{2,3},{3,4},{4,5},{5,6},{6,7},{7,8},{8,9},{9,10},{10,1... | collective-permute-start | bytes 196616 | tf_op jit(solution)/shard_map/ppermute | solution.py:47
  62.5 0.7 constant_dynamic-update-slice_fusion.13
  63.2 7.9 %collective-permute-start.8 = (bf16[1,64,512]{2,1,0:T(8,128)(2,1)S(1)}, bf16[1,64,512]{2,1,0:T(8,128)(2,1)}, u32[]{:S(2)}, u32[]{:S(2)}) collective-permute-start(bf16[1,64,512]{2,1,0:T(8,128)(2,1)S(1)} %bitcast.139), channel_id=1, source_target_pairs={{0,16},{1,17},{2,18},{3,19},{4,20},{5,21},{6,22},{7,23},{8,24},{9,... | collective-permute-start | bytes 196616 | tf_op jit(solution)/shard_map/ppermute | solution.py:47
  71.1 0.7 copy.64
  71.9 2.4 %collective-permute-start.14 = (bf16[1,64,512]{2,1,0:T(8,128)(2,1)}, bf16[1,64,512]{2,1,0:T(8,128)(2,1)}, u32[]{:S(2)}, u32[]{:S(2)}) collective-permute-start(bf16[1,64,512]{2,1,0:T(8,128)(2,1)} %bitcast.36), channel_id=1, source_target_pairs={{16,0},{17,1},{18,2},{19,3},{20,4},{21,5},{22,6},{23,7},{24,8},{25... | collective-permute-start | bytes 196616 | tf_op jit(solution)/shard_map/ppermute | solution.py:47
  74.3 1.6 fusion.30
  75.9 4.5 %collective-permute-start.9 = (bf16[1,2,64,512]{3,2,0,1:T(8,128)(2,1)S(1)}, bf16[1,2,64,512]{3,2,0,1:T(8,128)(2,1)S(1)}, u32[]{:S(2)}, u32[]{:S(2)}) collective-permute-start(bf16[1,2,64,512]{3,2,0,1:T(8,128)(2,1)S(1)} %get-tuple-element.20), channel_id=1, source_target_pairs={{1,0},{2,1},{3,2},{4,3},{5,4},{6,5},{7,6},{8,7},{9,8},{10,9},{11,1... | collective-permute-start | bytes 393224 | tf_op jit(solution)/shard_map/ppermute | solution.py:47
  80.5 0.8 constant_dynamic-update-slice_fusion.7
  81.4 2.8 %collective-permute-start.5 = (bf16[2,64,512]{2,1,0:T(8,128)(2,1)}, bf16[2,64,512]{2,1,0:T(8,128)(2,1)S(1)}, u32[]{:S(2)}, u32[]{:S(2)}) collective-permute-start(bf16[2,64,512]{2,1,0:T(8,128)(2,1)} %get-tuple-element.25), channel_id=1, source_target_pairs={{0,2},{1,3},{2,4},{3,5},{4,6},{5,7},{6,8},{7,9},{8,10},{9,11},{10,... | collective-permute-start | bytes 393224 | tf_op jit(solution)/shard_map/ppermute | solution.py:47
  84.2 0.8 pad_maximum_fusion.6
  84.9 5.4 %collective-permute-start.10 = (bf16[2,2,64,512]{3,2,1,0:T(8,128)(2,1)}, bf16[2,2,64,512]{3,2,1,0:T(8,128)(2,1)S(1)}, u32[]{:S(2)}, u32[]{:S(2)}) collective-permute-start(bf16[2,2,64,512]{3,2,1,0:T(8,128)(2,1)} %pad_maximum_fusion.6), channel_id=1, source_target_pairs={{2,0},{3,1},{4,2},{5,3},{6,4},{7,5},{8,6},{9,7},{10,8},{11,9},{12,... | collective-permute-start | bytes 786440 | tf_op jit(solution)/shard_map/ppermute | solution.py:47
  90.4 0.7 pad_maximum_fusion.4
  91.1 1.8 copy.77.q_ref
  92.9 0.7 constant_dynamic-update-slice_fusion.12
  93.6 16.9 %collective-permute-start.6 = (bf16[4,64,512]{2,1,0:T(8,128)(2,1)S(1)}, bf16[4,64,512]{2,1,0:T(8,128)(2,1)S(1)}, u32[]{:S(2)}, u32[]{:S(2)}) collective-permute-start(bf16[4,64,512]{2,1,0:T(8,128)(2,1)S(1)} %pad_maximum_fusion.5), channel_id=1, source_target_pairs={{0,4},{1,5},{2,6},{3,7},{4,8},{5,9},{6,10},{7,11},{8,12},{9,13},{1... | collective-permute-start | bytes 786440 | tf_op jit(solution)/shard_map/ppermute | solution.py:47
  110.6 1.9 collective-permute-start.11
  112.5 0.7 constant_dynamic-update-slice_fusion.11
  113.3 3.3 %collective-permute-done.6 = bf16[4,64,512]{2,1,0:T(8,128)(2,1)S(1)} collective-permute-done((bf16[4,64,512]{2,1,0:T(8,128)(2,1)S(1)}, bf16[4,64,512]{2,1,0:T(8,128)(2,1)S(1)}, u32[]{:S(2)}, u32[]{:S(2)}) %collective-permute-start.6) | collective-permute-done | bytes 262176 | tf_op jit(solution)/shard_map/ppermute | solution.py:47
  116.6 2.5 %collective-permute-start.7 = (bf16[8,64,512]{2,1,0:T(8,128)(2,1)S(1)}, bf16[8,64,512]{2,1,0:T(8,128)(2,1)S(1)}, u32[]{:S(2)}, u32[]{:S(2)}) collective-permute-start(bf16[8,64,512]{2,1,0:T(8,128)(2,1)S(1)} %pad_maximum_fusion.2), channel_id=1, source_target_pairs={{0,8},{1,9},{2,10},{3,11},{4,12},{5,13},{6,14},{7,15},{8,16},{9,17... | collective-permute-start | bytes 1572872 | tf_op jit(solution)/shard_map/ppermute | solution.py:47
  119.1 22.2 %collective-permute-done.11 = bf16[4,2,64,512]{3,2,1,0:T(8,128)(2,1)S(1)} collective-permute-done((bf16[4,2,64,512]{3,2,1,0:T(8,128)(2,1)S(1)}, bf16[4,2,64,512]{3,2,1,0:T(8,128)(2,1)S(1)}, u32[]{:S(2)}, u32[]{:S(2)}) %collective-permute-start.11) | collective-permute-done | bytes 524320 | tf_op jit(solution)/shard_map/ppermute | solution.py:47
  141.5 1.9 collective-permute-start.13
  143.4 0.9 collective-permute-start.12
  144.3 0.8 constant_dynamic-update-slice_fusion.10
  145.2 1.1 constant_dynamic-update-slice_fusion.9
  146.3 1.5 constant_dynamic-update-slice_fusion.8
  147.8 25.1 %collective-permute-done.13 = bf16[8,64,512]{2,1,0:T(8,128)(2,1)S(1)} collective-permute-done((bf16[8,64,512]{2,1,0:T(8,128)(2,1)S(1)}, bf16[8,64,512]{2,1,0:T(8,128)(2,1)S(1)}, u32[]{:S(2)}, u32[]{:S(2)}) %collective-permute-start.13) | collective-permute-done | bytes 524320 | tf_op jit(solution)/shard_map/ppermute | solution.py:47
  173.0 0.8 pad_dynamic-update-slice_fusion
  173.9 1.1 fusion.17
  174.9 1.1 fusion.16
  176.1 2.6 %gather_fusion.1 = bf16[17,64,512]{2,1,0:T(8,128)(2,1)S(1)} fusion(bf16[51,64,512]{2,1,0:T(8,128)(2,1)} %fusion.16, s32[1024]{0:T(1024)S(1)} %pad_clamp_fusion), kind=kCustom, calls=%fused_computation.1 | custom fusion | bytes 2228292 | tf_op jit(solution)/shard_map/jit(_take)/gather | solution.py:172
  178.6 1.2 bitcast_select_fusion.late_ref
  179.9 14.3 %shard_map.46 = bf16[128,1024]{1,0:T(8,128)(2,1)} custom-call(s32[1]{0:T(128)} %bitcast.offset_ref, bf16[128,1024]{1,0:T(8,128)(2,1)} %copy.77.q_ref, bf16[1088,512]{1,0:T(8,128)(2,1)} %bitcast.149, bf16[1088,512]{1,0:T(8,128)(2,1)} %bitcast_select_fusion.late_ref, s32[2,64,1]{2,1,0:T(8,128)} %iota_add_fusion.qpos_ref, s32[2,64,1]{2,1,0:T(8,128)} %copy.78.qdoc_ref, ...), custom_call_target="tpu_custom_call" | custom-call | tf_op jit(solution)/shard_map/pallas_call | solution.py:232
  (68 shorter events, 5.6 us)
Async XLA Ops:
  0.0 52.4 %copy-start = (bf16[1,128,2048]{2,1,0:T(8,128)(2,1)S(1)}, bf16[1,128,2048]{2,1,0:T(8,128)(2,1)}, u32[]{:S(2)}) copy-start(bf16[1,128,2048]{2,1,0:T(8,128)(2,1)} %param.4) | copy-start | bytes 1572868
  0.0 36.6 %collective-permute-start = (bf16[2048,192]{0,1:T(8,128)(2,1)}, bf16[2048,192]{0,1:T(8,128)(2,1)S(1)}, u32[]{:S(2)}, u32[]{:S(2)}) collective-permute-start(bf16[2048,192]{0,1:T(8,128)(2,1)} %param.5), channel_id=1, source_target_pairs={{128,0},{129,1},{130,2},{131,3},{132,4},{133,5},{134,6},{135,7},{1... | collective-permute-start | bytes 2359304 | tf_op jit(solution)/shard_map/ppermute | solution.py:90
  11.1 33.9 %collective-permute-start.1 = (bf16[2048,192]{0,1:T(8,128)(2,1)}, bf16[2048,192]{0,1:T(8,128)(2,1)S(1)}, u32[]{:S(2)}, u32[]{:S(2)}) collective-permute-start(bf16[2048,192]{0,1:T(8,128)(2,1)} %param.5), channel_id=1, source_target_pairs={{256,0},{257,1},{258,2},{259,3},{260,4},{261,5},{262,6},{263,7},{2... | collective-permute-start | bytes 2359304 | tf_op jit(solution)/shard_map/ppermute | solution.py:90
  13.5 31.5 %collective-permute-start.2 = (bf16[2048,192]{0,1:T(8,128)(2,1)}, bf16[2048,192]{0,1:T(8,128)(2,1)S(1)}, u32[]{:S(2)}, u32[]{:S(2)}) collective-permute-start(bf16[2048,192]{0,1:T(8,128)(2,1)} %param.5), channel_id=1, source_target_pairs={{416,0},{417,1},{418,2},{419,3},{420,4},{421,5},{422,6},{423,7},{4... | collective-permute-start | bytes 2359304 | tf_op jit(solution)/shard_map/ppermute | solution.py:90
  45.0 7.4 %copy-start.1 = (bf16[2048,192]{0,1:T(8,128)(2,1)S(1)}, bf16[2048,192]{0,1:T(8,128)(2,1)}, u32[]{:S(2)}) copy-start(bf16[2048,192]{0,1:T(8,128)(2,1)} %param.5) | copy-start | bytes 2359300
  46.5 9.9 %collective-permute-start.3 = (bf16[4,2048,192]{1,2,0:T(8,128)(2,1)S(1)}, bf16[4,2048,192]{1,2,0:T(8,128)(2,1)S(1)}, u32[]{:S(2)}, u32[]{:S(2)}) collective-permute-start(bf16[4,2048,192]{1,2,0:T(8,128)(2,1)S(1)} %pad_maximum_fusion), channel_id=1, source_target_pairs={{64,0},{65,1},{66,2},{67,3},{68,4},{69,5},{70,6},{71,7},{72,8},{73... | collective-permute-start | bytes 9437192 | tf_op jit(solution)/shard_map/ppermute | solution.py:91
  59.1 15.3 %collective-permute-start.4 = (bf16[1,64,512]{2,1,0:T(8,128)(2,1)S(1)}, bf16[1,64,512]{2,1,0:T(8,128)(2,1)S(1)}, u32[]{:S(2)}, u32[]{:S(2)}) collective-permute-start(bf16[1,64,512]{2,1,0:T(8,128)(2,1)S(1)} %bitcast.138), channel_id=1, source_target_pairs={{0,1},{1,2},{2,3},{3,4},{4,5},{5,6},{6,7},{7,8},{8,9},{9,10},{10,1... | collective-permute-start | bytes 196616 | tf_op jit(solution)/shard_map/ppermute | solution.py:47
  63.2 83.1 %collective-permute-start.8 = (bf16[1,64,512]{2,1,0:T(8,128)(2,1)S(1)}, bf16[1,64,512]{2,1,0:T(8,128)(2,1)}, u32[]{:S(2)}, u32[]{:S(2)}) collective-permute-start(bf16[1,64,512]{2,1,0:T(8,128)(2,1)S(1)} %bitcast.139), channel_id=1, source_target_pairs={{0,16},{1,17},{2,18},{3,19},{4,20},{5,21},{6,22},{7,23},{8,24},{9,... | collective-permute-start | bytes 196616 | tf_op jit(solution)/shard_map/ppermute | solution.py:47
  71.9 101.1 %collective-permute-start.14 = (bf16[1,64,512]{2,1,0:T(8,128)(2,1)}, bf16[1,64,512]{2,1,0:T(8,128)(2,1)}, u32[]{:S(2)}, u32[]{:S(2)}) collective-permute-start(bf16[1,64,512]{2,1,0:T(8,128)(2,1)} %bitcast.36), channel_id=1, source_target_pairs={{16,0},{17,1},{18,2},{19,3},{20,4},{21,5},{22,6},{23,7},{24,8},{25... | collective-permute-start | bytes 196616 | tf_op jit(solution)/shard_map/ppermute | solution.py:47
  75.9 8.3 %collective-permute-start.9 = (bf16[1,2,64,512]{3,2,0,1:T(8,128)(2,1)S(1)}, bf16[1,2,64,512]{3,2,0,1:T(8,128)(2,1)S(1)}, u32[]{:S(2)}, u32[]{:S(2)}) collective-permute-start(bf16[1,2,64,512]{3,2,0,1:T(8,128)(2,1)S(1)} %get-tuple-element.20), channel_id=1, source_target_pairs={{1,0},{2,1},{3,2},{4,3},{5,4},{6,5},{7,6},{8,7},{9,8},{10,9},{11,1... | collective-permute-start | bytes 393224 | tf_op jit(solution)/shard_map/ppermute | solution.py:47
  81.4 12.2 %collective-permute-start.5 = (bf16[2,64,512]{2,1,0:T(8,128)(2,1)}, bf16[2,64,512]{2,1,0:T(8,128)(2,1)S(1)}, u32[]{:S(2)}, u32[]{:S(2)}) collective-permute-start(bf16[2,64,512]{2,1,0:T(8,128)(2,1)} %get-tuple-element.25), channel_id=1, source_target_pairs={{0,2},{1,3},{2,4},{3,5},{4,6},{5,7},{6,8},{7,9},{8,10},{9,11},{10,... | collective-permute-start | bytes 393224 | tf_op jit(solution)/shard_map/ppermute | solution.py:47
  84.9 25.6 %collective-permute-start.10 = (bf16[2,2,64,512]{3,2,1,0:T(8,128)(2,1)}, bf16[2,2,64,512]{3,2,1,0:T(8,128)(2,1)S(1)}, u32[]{:S(2)}, u32[]{:S(2)}) collective-permute-start(bf16[2,2,64,512]{3,2,1,0:T(8,128)(2,1)} %pad_maximum_fusion.6), channel_id=1, source_target_pairs={{2,0},{3,1},{4,2},{5,3},{6,4},{7,5},{8,6},{9,7},{10,8},{11,9},{12,... | collective-permute-start | bytes 786440 | tf_op jit(solution)/shard_map/ppermute | solution.py:47
  93.6 22.9 %collective-permute-start.6 = (bf16[4,64,512]{2,1,0:T(8,128)(2,1)S(1)}, bf16[4,64,512]{2,1,0:T(8,128)(2,1)S(1)}, u32[]{:S(2)}, u32[]{:S(2)}) collective-permute-start(bf16[4,64,512]{2,1,0:T(8,128)(2,1)S(1)} %pad_maximum_fusion.5), channel_id=1, source_target_pairs={{0,4},{1,5},{2,6},{3,7},{4,8},{5,9},{6,10},{7,11},{8,12},{9,13},{1... | collective-permute-start | bytes 786440 | tf_op jit(solution)/shard_map/ppermute | solution.py:47
  110.6 30.7 %collective-permute-start.11 = (bf16[4,2,64,512]{3,2,1,0:T(8,128)(2,1)S(1)}, bf16[4,2,64,512]{3,2,1,0:T(8,128)(2,1)S(1)}, u32[]{:S(2)}, u32[]{:S(2)}) collective-permute-start(bf16[4,2,64,512]{3,2,1,0:T(8,128)(2,1)S(1)} %pad_maximum_fusion.3), channel_id=1, source_target_pairs={{4,0},{5,1},{6,2},{7,3},{8,4},{9,5},{10,6},{11,7},{12,8},{13,9},{1... | collective-permute-start | bytes 1572872 | tf_op jit(solution)/shard_map/ppermute | solution.py:47
  116.6 28.5 %collective-permute-start.7 = (bf16[8,64,512]{2,1,0:T(8,128)(2,1)S(1)}, bf16[8,64,512]{2,1,0:T(8,128)(2,1)S(1)}, u32[]{:S(2)}, u32[]{:S(2)}) collective-permute-start(bf16[8,64,512]{2,1,0:T(8,128)(2,1)S(1)} %pad_maximum_fusion.2), channel_id=1, source_target_pairs={{0,8},{1,9},{2,10},{3,11},{4,12},{5,13},{6,14},{7,15},{8,16},{9,17... | collective-permute-start | bytes 1572872 | tf_op jit(solution)/shard_map/ppermute | solution.py:47
  141.5 31.4 %collective-permute-start.13 = (bf16[8,64,512]{2,1,0:T(8,128)(2,1)S(1)}, bf16[8,64,512]{2,1,0:T(8,128)(2,1)S(1)}, u32[]{:S(2)}, u32[]{:S(2)}) collective-permute-start(bf16[8,64,512]{2,1,0:T(8,128)(2,1)S(1)} %get-tuple-element.8), channel_id=1, source_target_pairs={{8,0},{9,1},{10,2},{11,3},{12,4},{13,5},{14,6},{15,7},{16,8},{17,9... | collective-permute-start | bytes 1572872 | tf_op jit(solution)/shard_map/ppermute | solution.py:47
  143.4 29.5 %collective-permute-start.12 = (bf16[8,64,512]{2,1,0:T(8,128)(2,1)S(1)}, bf16[8,64,512]{2,1,0:T(8,128)(2,1)S(1)}, u32[]{:S(2)}, u32[]{:S(2)}) collective-permute-start(bf16[8,64,512]{2,1,0:T(8,128)(2,1)S(1)} %get-tuple-element.7), channel_id=1, source_target_pairs={{56,48},{57,49},{58,50},{59,51},{60,52},{61,53},{62,54},{63,55},{1... | collective-permute-start | bytes 1572872 | tf_op jit(solution)/shard_map/ppermute | solution.py:47

commit v6 on v5

--- a/solution.py
+++ b/solution.py
@@ -188,8 +188,18 @@
     )
 
     key_docs = jnp.where(key_ok, key_docs, -1)
+    pad = CHUNK - key_places.shape[1] % CHUNK
+    key_places = jnp.pad(key_places, ((0, 0), (0, pad)))
+    key_docs = jnp.pad(key_docs, ((0, 0), (0, pad)), constant_values=-1)
+    early_keys = jnp.pad(early_keys, ((0, pad), (0, 0)))
+    late_keys = jnp.pad(late_keys, ((0, pad), (0, 0)))
+    ends = jnp.cumsum(lengths_row)
+    first = query_spans * SPAN
+    opening = jnp.max(jnp.where(ends[None, :] <= first[:, None], ends[None, :], 0), axis=1)
+    reach_back = query_spans - opening // SPAN
+    chunks = jnp.clip(reach_back // (CHUNK // SPAN) + 1, 1, key_places.shape[1] // CHUNK)
     return attend(
-        offset.reshape(1),
+        jnp.concatenate([offset.reshape(1), chunks.astype(jnp.int32)]),
         query_rows,
         early_keys,
         late_keys,
@@ -200,42 +210,80 @@
     )[None]
 
 
-def attend_kernel(offset_ref, q_ref, early_ref, late_ref, qpos_ref, qdoc_ref, kpos_ref, kdoc_ref, o_ref):
-    offset = pl.multiple_of(offset_ref[0], SPAN)
+CHUNK = 128
+
+
+def attend_kernel(meta_ref, q_ref, early_ref, late_ref, qpos_ref, qdoc_ref, kpos_ref, kdoc_ref, o_ref):
+    offset = pl.multiple_of(meta_ref[0], SPAN)
+    rows = QUERY_PER_KV * SPAN
     for span, kv_ref in ((0, early_ref), (1, late_ref)):
         row = offset if span == 0 else SPAN - offset
         row = pl.multiple_of(row, SPAN)
-        live = (qdoc_ref[span] == kdoc_ref[span]) & (kpos_ref[span] <= qpos_ref[span])
+        count = meta_ref[1 + span]
+        qpos = qpos_ref[span]
+        qdoc = qdoc_ref[span]
+
+        def live_of(start):
+            kpos = kpos_ref[span, :, pl.ds(start, CHUNK)]
+            kdoc = kdoc_ref[span, :, pl.ds(start, CHUNK)]
+            live = (qdoc == kdoc) & (kpos <= qpos)
+            return jnp.concatenate([live] * QUERY_PER_KV, axis=0)
+
         for group in range(KEY_VALUE_HEADS):
-            key = kv_ref[:, group * HEAD_SIZE : (group + 1) * HEAD_SIZE]
+            heads = range(group * QUERY_PER_KV, (group + 1) * QUERY_PER_KV)
+            query = jnp.concatenate(
+                [q_ref[pl.ds(row, SPAN), head * HEAD_SIZE : (head + 1) * HEAD_SIZE] for head in heads],
+                axis=0,
+            )
+            key_cols = slice(group * HEAD_SIZE, (group + 1) * HEAD_SIZE)
             base = KEY_VALUE_HEADS * HEAD_SIZE + group * HEAD_SIZE
-            value = kv_ref[:, base : base + HEAD_SIZE]
-            for member in range(QUERY_PER_KV):
-                head = group * QUERY_PER_KV + member
-                cols = slice(head * HEAD_SIZE, (head + 1) * HEAD_SIZE)
-                query = q_ref[pl.ds(row, SPAN), cols]
+
+            def scores_of(index):
+                start = pl.multiple_of(index * CHUNK, CHUNK)
+                key = kv_ref[pl.ds(start, CHUNK), key_cols]
                 scores = lax.dot_general(
                     query, key, (((1,), (1,)), ((), ())), preferred_element_type=jnp.float32
                 ) * 0.125
-                scores = jnp.where(live, scores, -1e30)
-                top = jnp.max(scores, axis=1, keepdims=True)
-                weights = jnp.where(live, jnp.exp(scores - top), 0.0)
-                total = jnp.sum(weights, axis=1, keepdims=True)
-                summed = jnp.dot(
+                return jnp.where(live_of(start), scores, -1e30), start
+
+            def find_top(index, top):
+                scores, _ = scores_of(index)
+                return jnp.maximum(top, jnp.max(scores, axis=1, keepdims=True))
+
+            top = lax.fori_loop(0, count, find_top, jnp.full((rows, 1), -1e30, jnp.float32))
+
+            def gather(index, carry):
+                total, summed = carry
+                scores, start = scores_of(index)
+                weights = jnp.exp(scores - top)
+                value = kv_ref[pl.ds(start, CHUNK), base : base + HEAD_SIZE]
+                total = total + jnp.sum(weights, axis=1, keepdims=True)
+                summed = summed + jnp.dot(
                     weights.astype(jnp.bfloat16), value, preferred_element_type=jnp.float32
                 )
-                o_ref[pl.ds(row, SPAN), cols] = (summed / total).astype(o_ref.dtype)
-
-
-def attend(offset, query_rows, early_keys, late_keys, qpos, qdoc, kpos, kdoc):
+                return total, summed
+
+            total, summed = lax.fori_loop(
+                0,
+                count,
+                gather,
+                (jnp.zeros((rows, 1), jnp.float32), jnp.zeros((rows, HEAD_SIZE), jnp.float32)),
+            )
+            result = (summed / total).astype(o_ref.dtype)
+            for member, head in enumerate(heads):
+                o_ref[pl.ds(row, SPAN), head * HEAD_SIZE : (head + 1) * HEAD_SIZE] = result[
+                    member * SPAN : (member + 1) * SPAN
+                ]
+
+
+def attend(meta, query_rows, early_keys, late_keys, qpos, qdoc, kpos, kdoc):
     vmem = pl.BlockSpec(memory_space=pltpu.VMEM)
     return pl.pallas_call(
         attend_kernel,
         out_shape=jax.ShapeDtypeStruct(query_rows.shape, query_rows.dtype),
         in_specs=[pl.BlockSpec(memory_space=pltpu.SMEM)] + [vmem] * 7,
         out_specs=vmem,
-    )(offset, query_rows, early_keys, late_keys, qpos, qdoc, kpos, kdoc)
-
+    )(meta, query_rows, early_keys, late_keys, qpos, qdoc, kpos, kdoc)
 
 def solution(mesh):
     placed = (P("seq", "ctx", None), P(None, "seq"), P("seq", None), P("seq", None))

time: 195 us -> 219 us (1.12)
  the two profiles are of different devices: /device:TPU:56 before, /device:TPU:62 now
where the time goes in v6:
time: 219 us; the launch traced here: 218 us
  waiting for transfers between devices  83.7 us (38%)
  starting transfers between devices  57.9 us (26%)
  Pallas kernels  34.7 us (16%)
  local copies, waits for them, and re-layouts  20.7 us (9%)
  other arithmetic  12.7 us (6%)
  matrix products  7.65 us (3%)
    ppermute x11, waiting for transfers between devices, moved(): return lax.ppermute(value, 'ctx', pairs)  60.5 us
    ppermute x11, starting transfers between devices, moved(): return lax.ppermute(value, 'ctx', pairs)  36.4 us
    pallas_call x1, Pallas kernels, attend(): pl.pallas_call(attend_kernel, out_shape=jax.ShapeDtypeStruct(query_rows.s...  34.7 us
    ppermute x3, waiting for transfers between devices, project(): lax.ppermute(weight, both, pairs_for(f))  21.7 us
    ppermute x3, starting transfers between devices, project(): lax.ppermute(weight, both, pairs_for(f))  16.9 us
    unnamed x20, local copies, waits for them, and re-layouts  7.19 us
    dot_general x4, matrix products, project(): jnp.dot(rows, mate[index], preferred_element_type=jnp.float32)  6.07 us
    ppermute x1, starting transfers between devices, project(): mate = lax.ppermute(jnp.stack(mine), both, mate_pairs())  4.59 us
  transfers between devices with their start and end apart: 15, of which 7 were waited for; matrix products, arithmetic and copies ran while one was open for 10% of the time, Pallas kernels for 0%

profile of v6, /device:TPU:62, one launch (start us, length us, event | category | flops | bytes accessed | tf_op | source)
XLA Modules:
  0.0 218.4 jit_solution(11009549219616291567)
XLA Ops:
  0.0 11.1 %collective-permute-start = (bf16[2048,192]{0,1:T(8,128)(2,1)}, bf16[2048,192]{0,1:T(8,128)(2,1)S(1)}, u32[]{:S(2)}, u32[]{:S(2)}) collective-permute-start(bf16[2048,192]{0,1:T(8,128)(2,1)} %param.5), channel_id=1, source_target_pairs={{128,0},{129,1},{130,2},{131,3},{132,4},{133,5},{134,6},{135,7},{1... | collective-permute-start | bytes 2359304 | tf_op jit(solution)/shard_map/ppermute | solution.py:90
  11.1 2.5 %collective-permute-start.1 = (bf16[2048,192]{0,1:T(8,128)(2,1)}, bf16[2048,192]{0,1:T(8,128)(2,1)S(1)}, u32[]{:S(2)}, u32[]{:S(2)}) collective-permute-start(bf16[2048,192]{0,1:T(8,128)(2,1)} %param.5), channel_id=1, source_target_pairs={{256,0},{257,1},{258,2},{259,3},{260,4},{261,5},{262,6},{263,7},{2... | collective-permute-start | bytes 2359304 | tf_op jit(solution)/shard_map/ppermute | solution.py:90
  13.5 3.4 %collective-permute-start.2 = (bf16[2048,192]{0,1:T(8,128)(2,1)}, bf16[2048,192]{0,1:T(8,128)(2,1)S(1)}, u32[]{:S(2)}, u32[]{:S(2)}) collective-permute-start(bf16[2048,192]{0,1:T(8,128)(2,1)} %param.5), channel_id=1, source_target_pairs={{416,0},{417,1},{418,2},{419,3},{420,4},{421,5},{422,6},{423,7},{4... | collective-permute-start | bytes 2359304 | tf_op jit(solution)/shard_map/ppermute | solution.py:90
  16.9 0.8 copy.44
  18.5 1.3 fusion.46
  21.2 0.7 copy.56.qdoc_ref
  23.3 13.3 %collective-permute-done = bf16[2048,192]{0,1:T(8,128)(2,1)S(1)} collective-permute-done((bf16[2048,192]{0,1:T(8,128)(2,1)}, bf16[2048,192]{0,1:T(8,128)(2,1)S(1)}, u32[]{:S(2)}, u32[]{:S(2)}) %collective-permute-start) | collective-permute-done | bytes 786464 | tf_op jit(solution)/shard_map/ppermute | solution.py:90
  36.6 8.4 %collective-permute-done.1 = bf16[2048,192]{0,1:T(8,128)(2,1)S(1)} collective-permute-done((bf16[2048,192]{0,1:T(8,128)(2,1)}, bf16[2048,192]{0,1:T(8,128)(2,1)S(1)}, u32[]{:S(2)}, u32[]{:S(2)}) %collective-permute-start.1) | collective-permute-done | bytes 786464 | tf_op jit(solution)/shard_map/ppermute | solution.py:90
  45.0 0.9 copy-done.2
  46.0 3.1 %pad_maximum_fusion = bf16[4,2048,192]{1,2,0:T(8,128)(2,1)} fusion(bf16[1,2048,192]{1,2,0:T(8,128)(2,1)} %bitcast.137, bf16[1,2048,192]{1,2,0:T(8,128)(2,1)S(1)} %bitcast.136, bf16[1,2048,192]{1,2,0:T(8,128)(2,1)S(1)} %bitcast.135, bf16[1,2048,192]{1,2,0:T(8,128)(2,1)} %bitcast.134), kind=kLoop, calls=%fused_computation.2 | loop fusion | flops 4718592 | bytes 6291456 | tf_op jit(solution)/shard_map/stack | solution.py:91
  49.0 4.6 %collective-permute-start.3 = (bf16[4,2048,192]{1,2,0:T(8,128)(2,1)}, bf16[4,2048,192]{1,2,0:T(8,128)(2,1)}, u32[]{:S(2)}, u32[]{:S(2)}) collective-permute-start(bf16[4,2048,192]{1,2,0:T(8,128)(2,1)} %pad_maximum_fusion), channel_id=1, source_target_pairs={{64,0},{65,1},{66,2},{67,3},{68,4},{69,5},{70,6},{71,7},{72,8},{73... | collective-permute-start | bytes 9437192 | tf_op jit(solution)/shard_map/ppermute | solution.py:91
  57.8 1.5 collective-permute-done.3
  59.3 1.5 fusion.9
  60.8 1.5 fusion.11
  62.3 1.5 fusion.13
  63.8 1.5 fusion.15
  66.4 4.8 %collective-permute-start.4 = (bf16[1,64,512]{2,1,0:T(8,128)(2,1)S(1)}, bf16[1,64,512]{2,1,0:T(8,128)(2,1)S(1)}, u32[]{:S(2)}, u32[]{:S(2)}) collective-permute-start(bf16[1,64,512]{2,1,0:T(8,128)(2,1)S(1)} %bitcast.138), channel_id=1, source_target_pairs={{0,1},{1,2},{2,3},{3,4},{4,5},{5,6},{6,7},{7,8},{8,9},{9,10},{10,1... | collective-permute-start | bytes 196616 | tf_op jit(solution)/shard_map/ppermute | solution.py:47
  71.9 7.7 %collective-permute-start.8 = (bf16[1,64,512]{2,1,0:T(8,128)(2,1)S(1)}, bf16[1,64,512]{2,1,0:T(8,128)(2,1)}, u32[]{:S(2)}, u32[]{:S(2)}) collective-permute-start(bf16[1,64,512]{2,1,0:T(8,128)(2,1)S(1)} %bitcast.139), channel_id=1, source_target_pairs={{0,16},{1,17},{2,18},{3,19},{4,20},{5,21},{6,22},{7,23},{8,24},{9,... | collective-permute-start | bytes 196616 | tf_op jit(solution)/shard_map/ppermute | solution.py:47
  79.7 0.7 copy.46
  80.4 2.6 %collective-permute-start.14 = (bf16[1,64,512]{2,1,0:T(8,128)(2,1)}, bf16[1,64,512]{2,1,0:T(8,128)(2,1)}, u32[]{:S(2)}, u32[]{:S(2)}) collective-permute-start(bf16[1,64,512]{2,1,0:T(8,128)(2,1)} %bitcast.39), channel_id=1, source_target_pairs={{16,0},{17,1},{18,2},{19,3},{20,4},{21,5},{22,6},{23,7},{24,8},{25... | collective-permute-start | bytes 196616 | tf_op jit(solution)/shard_map/ppermute | solution.py:47
  83.1 1.6 fusion.30
  84.6 1.9 collective-permute-start.9
  86.6 0.8 constant_dynamic-update-slice_fusion.7
  87.5 9.0 %collective-permute-start.5 = (bf16[2,64,512]{2,1,0:T(8,128)(2,1)}, bf16[2,64,512]{2,1,0:T(8,128)(2,1)S(1)}, u32[]{:S(2)}, u32[]{:S(2)}) collective-permute-start(bf16[2,64,512]{2,1,0:T(8,128)(2,1)} %get-tuple-element.25), channel_id=1, source_target_pairs={{0,2},{1,3},{2,4},{3,5},{4,6},{5,7},{6,8},{7,9},{8,10},{9,11},{10,... | collective-permute-start | bytes 393224 | tf_op jit(solution)/shard_map/ppermute | solution.py:47
  96.5 5.2 %collective-permute-done.9 = bf16[1,2,64,512]{3,2,0,1:T(8,128)(2,1)S(1)} collective-permute-done((bf16[1,2,64,512]{3,2,0,1:T(8,128)(2,1)S(1)}, bf16[1,2,64,512]{3,2,0,1:T(8,128)(2,1)S(1)}, u32[]{:S(2)}, u32[]{:S(2)}) %collective-permute-start.9) | collective-permute-done | bytes 131104 | tf_op jit(solution)/shard_map/ppermute | solution.py:47
  101.7 0.7 pad_maximum_fusion.6
  102.5 1.9 collective-permute-start.10
  104.4 0.7 pad_maximum_fusion.4
  105.1 1.8 copy.55.q_ref
  107.6 1.9 collective-permute-start.6
  109.5 13.6 %collective-permute-done.10 = bf16[2,2,64,512]{3,2,1,0:T(8,128)(2,1)S(1)} collective-permute-done((bf16[2,2,64,512]{3,2,1,0:T(8,128)(2,1)}, bf16[2,2,64,512]{3,2,1,0:T(8,128)(2,1)S(1)}, u32[]{:S(2)}, u32[]{:S(2)}) %collective-permute-start.10) | collective-permute-done | bytes 262176 | tf_op jit(solution)/shard_map/ppermute | solution.py:47
  123.2 1.9 collective-permute-start.11
  125.1 0.7 constant_dynamic-update-slice_fusion.11
  125.9 1.9 collective-permute-start.7
  127.9 21.0 %collective-permute-done.11 = bf16[4,2,64,512]{3,2,1,0:T(8,128)(2,1)S(1)} collective-permute-done((bf16[4,2,64,512]{3,2,1,0:T(8,128)(2,1)S(1)}, bf16[4,2,64,512]{3,2,1,0:T(8,128)(2,1)S(1)}, u32[]{:S(2)}, u32[]{:S(2)}) %collective-permute-start.11) | collective-permute-done | bytes 524320 | tf_op jit(solution)/shard_map/ppermute | solution.py:47
  149.1 1.9 collective-permute-start.13
  151.0 0.7 collective-permute-start.12
  151.7 0.7 constant_dynamic-update-slice_fusion.10
  152.5 0.9 constant_dynamic-update-slice_fusion.9
  153.3 1.5 constant_dynamic-update-slice_fusion.8
  154.8 1.1 pad.15.early_ref
  155.9 20.7 %collective-permute-done.13 = bf16[8,64,512]{2,1,0:T(8,128)(2,1)S(1)} collective-permute-done((bf16[8,64,512]{2,1,0:T(8,128)(2,1)S(1)}, bf16[8,64,512]{2,1,0:T(8,128)(2,1)S(1)}, u32[]{:S(2)}, u32[]{:S(2)}) %collective-permute-start.13) | collective-permute-done | bytes 524320 | tf_op jit(solution)/shard_map/ppermute | solution.py:47
  176.7 0.8 pad_dynamic-update-slice_fusion
  177.6 1.1 fusion.17
  178.6 1.1 fusion.16
  179.8 2.6 %gather_fusion.1 = bf16[17,64,512]{2,1,0:T(8,128)(2,1)S(1)} fusion(bf16[51,64,512]{2,1,0:T(8,128)(2,1)} %fusion.16, s32[1024]{0:T(1024)S(1)} %pad_clamp_fusion), kind=kCustom, calls=%fused_computation.1 | custom fusion | bytes 2228292 | tf_op jit(solution)/shard_map/jit(_take)/gather | solution.py:172
  182.6 1.1 pad.16.late_ref
  183.7 34.7 %shard_map.46 = bf16[128,1024]{1,0:T(8,128)(2,1)} custom-call(s32[3]{0:T(128)} %pad_add_fusion.1.meta_ref, bf16[128,1024]{1,0:T(8,128)(2,1)} %copy.55.q_ref, bf16[1152,512]{1,0:T(8,128)(2,1)} %pad.15.early_ref, bf16[1152,512]{1,0:T(8,128)(2,1)} %pad.16.late_ref, s32[2,64,1]{2,1,0:T(8,128)} %iota_add_fusion.qpos_ref, s32[2,64,1]{2,1,0:T(8,128)} %copy.56.qdoc_ref, ...), custom_call_target="tpu_custom_call" | custom-call | tf_op jit(solution)/shard_map/pallas_call | solution.py:281
  (82 shorter events, 10.1 us)
Async XLA Ops:
  0.0 56.1 %copy-start = (bf16[1,128,2048]{2,1,0:T(8,128)(2,1)S(1)}, bf16[1,128,2048]{2,1,0:T(8,128)(2,1)}, u32[]{:S(2)}) copy-start(bf16[1,128,2048]{2,1,0:T(8,128)(2,1)} %param.4) | copy-start | bytes 1572868
  0.0 36.6 %collective-permute-start = (bf16[2048,192]{0,1:T(8,128)(2,1)}, bf16[2048,192]{0,1:T(8,128)(2,1)S(1)}, u32[]{:S(2)}, u32[]{:S(2)}) collective-permute-start(bf16[2048,192]{0,1:T(8,128)(2,1)} %param.5), channel_id=1, source_target_pairs={{128,0},{129,1},{130,2},{131,3},{132,4},{133,5},{134,6},{135,7},{1... | collective-permute-start | bytes 2359304 | tf_op jit(solution)/shard_map/ppermute | solution.py:90
  11.1 33.9 %collective-permute-start.1 = (bf16[2048,192]{0,1:T(8,128)(2,1)}, bf16[2048,192]{0,1:T(8,128)(2,1)S(1)}, u32[]{:S(2)}, u32[]{:S(2)}) collective-permute-start(bf16[2048,192]{0,1:T(8,128)(2,1)} %param.5), channel_id=1, source_target_pairs={{256,0},{257,1},{258,2},{259,3},{260,4},{261,5},{262,6},{263,7},{2... | collective-permute-start | bytes 2359304 | tf_op jit(solution)/shard_map/ppermute | solution.py:90
  13.5 31.5 %collective-permute-start.2 = (bf16[2048,192]{0,1:T(8,128)(2,1)}, bf16[2048,192]{0,1:T(8,128)(2,1)S(1)}, u32[]{:S(2)}, u32[]{:S(2)}) collective-permute-start(bf16[2048,192]{0,1:T(8,128)(2,1)} %param.5), channel_id=1, source_target_pairs={{416,0},{417,1},{418,2},{419,3},{420,4},{421,5},{422,6},{423,7},{4... | collective-permute-start | bytes 2359304 | tf_op jit(solution)/shard_map/ppermute | solution.py:90
  45.0 0.9 copy-start.2
  46.0 10.2 %copy-start.1 = (bf16[2048,192]{0,1:T(8,128)(2,1)S(1)}, bf16[2048,192]{0,1:T(8,128)(2,1)}, u32[]{:S(2)}) copy-start(bf16[2048,192]{0,1:T(8,128)(2,1)} %param.5) | copy-start | bytes 2359300
  49.0 10.2 %collective-permute-start.3 = (bf16[4,2048,192]{1,2,0:T(8,128)(2,1)}, bf16[4,2048,192]{1,2,0:T(8,128)(2,1)}, u32[]{:S(2)}, u32[]{:S(2)}) collective-permute-start(bf16[4,2048,192]{1,2,0:T(8,128)(2,1)} %pad_maximum_fusion), channel_id=1, source_target_pairs={{64,0},{65,1},{66,2},{67,3},{68,4},{69,5},{70,6},{71,7},{72,8},{73... | collective-permute-start | bytes 9437192 | tf_op jit(solution)/shard_map/ppermute | solution.py:91
  54.3 3.0 %copy-start.3 = (bf16[2048,192]{0,1:T(8,128)(2,1)S(1)}, bf16[2048,192]{0,1:T(8,128)(2,1)}, u32[]{:S(2)}) copy-start(bf16[2048,192]{0,1:T(8,128)(2,1)} %copy-done.2) | copy-start | bytes 2359300
  66.4 16.6 %collective-permute-start.4 = (bf16[1,64,512]{2,1,0:T(8,128)(2,1)S(1)}, bf16[1,64,512]{2,1,0:T(8,128)(2,1)S(1)}, u32[]{:S(2)}, u32[]{:S(2)}) collective-permute-start(bf16[1,64,512]{2,1,0:T(8,128)(2,1)S(1)} %bitcast.138), channel_id=1, source_target_pairs={{0,1},{1,2},{2,3},{3,4},{4,5},{5,6},{6,7},{7,8},{8,9},{9,10},{10,1... | collective-permute-start | bytes 196616 | tf_op jit(solution)/shard_map/ppermute | solution.py:47
  71.9 81.4 %collective-permute-start.8 = (bf16[1,64,512]{2,1,0:T(8,128)(2,1)S(1)}, bf16[1,64,512]{2,1,0:T(8,128)(2,1)}, u32[]{:S(2)}, u32[]{:S(2)}) collective-permute-start(bf16[1,64,512]{2,1,0:T(8,128)(2,1)S(1)} %bitcast.139), channel_id=1, source_target_pairs={{0,16},{1,17},{2,18},{3,19},{4,20},{5,21},{6,22},{7,23},{8,24},{9,... | collective-permute-start | bytes 196616 | tf_op jit(solution)/shard_map/ppermute | solution.py:47
  80.4 96.2 %collective-permute-start.14 = (bf16[1,64,512]{2,1,0:T(8,128)(2,1)}, bf16[1,64,512]{2,1,0:T(8,128)(2,1)}, u32[]{:S(2)}, u32[]{:S(2)}) collective-permute-start(bf16[1,64,512]{2,1,0:T(8,128)(2,1)} %bitcast.39), channel_id=1, source_target_pairs={{16,0},{17,1},{18,2},{19,3},{20,4},{21,5},{22,6},{23,7},{24,8},{25... | collective-permute-start | bytes 196616 | tf_op jit(solution)/shard_map/ppermute | solution.py:47
  84.6 17.1 %collective-permute-start.9 = (bf16[1,2,64,512]{3,2,0,1:T(8,128)(2,1)S(1)}, bf16[1,2,64,512]{3,2,0,1:T(8,128)(2,1)S(1)}, u32[]{:S(2)}, u32[]{:S(2)}) collective-permute-start(bf16[1,2,64,512]{3,2,0,1:T(8,128)(2,1)S(1)} %get-tuple-element.20), channel_id=1, source_target_pairs={{1,0},{2,1},{3,2},{4,3},{5,4},{6,5},{7,6},{8,7},{9,8},{10,9},{11,1... | collective-permute-start | bytes 393224 | tf_op jit(solution)/shard_map/ppermute | solution.py:47
  87.5 20.1 %collective-permute-start.5 = (bf16[2,64,512]{2,1,0:T(8,128)(2,1)}, bf16[2,64,512]{2,1,0:T(8,128)(2,1)S(1)}, u32[]{:S(2)}, u32[]{:S(2)}) collective-permute-start(bf16[2,64,512]{2,1,0:T(8,128)(2,1)} %get-tuple-element.25), channel_id=1, source_target_pairs={{0,2},{1,3},{2,4},{3,5},{4,6},{5,7},{6,8},{7,9},{8,10},{9,11},{10,... | collective-permute-start | bytes 393224 | tf_op jit(solution)/shard_map/ppermute | solution.py:47
  102.5 20.7 %collective-permute-start.10 = (bf16[2,2,64,512]{3,2,1,0:T(8,128)(2,1)}, bf16[2,2,64,512]{3,2,1,0:T(8,128)(2,1)S(1)}, u32[]{:S(2)}, u32[]{:S(2)}) collective-permute-start(bf16[2,2,64,512]{3,2,1,0:T(8,128)(2,1)} %pad_maximum_fusion.6), channel_id=1, source_target_pairs={{2,0},{3,1},{4,2},{5,3},{6,4},{7,5},{8,6},{9,7},{10,8},{11,9},{12,... | collective-permute-start | bytes 786440 | tf_op jit(solution)/shard_map/ppermute | solution.py:47
  107.6 18.3 %collective-permute-start.6 = (bf16[4,64,512]{2,1,0:T(8,128)(2,1)S(1)}, bf16[4,64,512]{2,1,0:T(8,128)(2,1)S(1)}, u32[]{:S(2)}, u32[]{:S(2)}) collective-permute-start(bf16[4,64,512]{2,1,0:T(8,128)(2,1)S(1)} %pad_maximum_fusion.5), channel_id=1, source_target_pairs={{0,4},{1,5},{2,6},{3,7},{4,8},{5,9},{6,10},{7,11},{8,12},{9,13},{1... | collective-permute-start | bytes 786440 | tf_op jit(solution)/shard_map/ppermute | solution.py:47
  123.2 25.7 %collective-permute-start.11 = (bf16[4,2,64,512]{3,2,1,0:T(8,128)(2,1)S(1)}, bf16[4,2,64,512]{3,2,1,0:T(8,128)(2,1)S(1)}, u32[]{:S(2)}, u32[]{:S(2)}) collective-permute-start(bf16[4,2,64,512]{3,2,1,0:T(8,128)(2,1)S(1)} %pad_maximum_fusion.3), channel_id=1, source_target_pairs={{4,0},{5,1},{6,2},{7,3},{8,4},{9,5},{10,6},{11,7},{12,8},{13,9},{1... | collective-permute-start | bytes 1572872 | tf_op jit(solution)/shard_map/ppermute | solution.py:47
  125.9 26.5 %collective-permute-start.7 = (bf16[8,64,512]{2,1,0:T(8,128)(2,1)S(1)}, bf16[8,64,512]{2,1,0:T(8,128)(2,1)S(1)}, u32[]{:S(2)}, u32[]{:S(2)}) collective-permute-start(bf16[8,64,512]{2,1,0:T(8,128)(2,1)S(1)} %pad_maximum_fusion.2), channel_id=1, source_target_pairs={{0,8},{1,9},{2,10},{3,11},{4,12},{5,13},{6,14},{7,15},{8,16},{9,17... | collective-permute-start | bytes 1572872 | tf_op jit(solution)/shard_map/ppermute | solution.py:47
  127.9 23.8 %copy-start.4 = (bf16[17,64,512]{2,1,0:T(8,128)(2,1)S(1)}, bf16[17,64,512]{2,1,0:T(8,128)(2,1)}, u32[]{:S(2)}) copy-start(bf16[17,64,512]{2,1,0:T(8,128)(2,1)} %get-tuple-element.24) | copy-start | bytes 3342340
  149.1 27.5 %collective-permute-start.13 = (bf16[8,64,512]{2,1,0:T(8,128)(2,1)S(1)}, bf16[8,64,512]{2,1,0:T(8,128)(2,1)S(1)}, u32[]{:S(2)}, u32[]{:S(2)}) collective-permute-start(bf16[8,64,512]{2,1,0:T(8,128)(2,1)S(1)} %get-tuple-element.8), channel_id=1, source_target_pairs={{8,0},{9,1},{10,2},{11,3},{12,4},{13,5},{14,6},{15,7},{16,8},{17,9... | collective-permute-start | bytes 1572872 | tf_op jit(solution)/shard_map/ppermute | solution.py:47
  151.0 25.6 %collective-permute-start.12 = (bf16[8,64,512]{2,1,0:T(8,128)(2,1)S(1)}, bf16[8,64,512]{2,1,0:T(8,128)(2,1)S(1)}, u32[]{:S(2)}, u32[]{:S(2)}) collective-permute-start(bf16[8,64,512]{2,1,0:T(8,128)(2,1)S(1)} %get-tuple-element.7), channel_id=1, source_target_pairs={{56,48},{57,49},{58,50},{59,51},{60,52},{61,53},{62,54},{63,55},{1... | collective-permute-start | bytes 1572872 | tf_op jit(solution)/shard_map/ppermute | solution.py:47

commit v7 on v5

--- a/solution.py
+++ b/solution.py
@@ -137,7 +137,12 @@
     up = early_rows[None]
     down = jnp.stack([early_rows, late_rows])[None]
     reach = 1
+    lone_early, lone_late = early_rows[None], late_rows[None]
     while reach < WINDOW:
+        if 2 * reach == WINDOW:
+            lone_early, lone_late, up, down = lax.optimization_barrier(
+                (lone_early, lone_late, up, down)
+            )
         up = jnp.concatenate(
             [up, moved(up, count, [(d, d + reach) for d in range(count)])], axis=0
         )
@@ -155,9 +160,9 @@
         down = jnp.concatenate([down, got], axis=0)
         reach *= 2
     up = jnp.concatenate(
-        [up, moved(early_rows[None], count, [(d, d + WINDOW) for d in range(count)])], axis=0
-    )
-    far = moved(late_rows[None], count, [(d, d - WINDOW) for d in range(count)])
+        [up, moved(lone_early, count, [(d, d + WINDOW) for d in range(count)])], axis=0
+    )
+    far = moved(lone_late, count, [(d, d - WINDOW) for d in range(count)])
     down = jnp.concatenate([down, jnp.stack([jnp.zeros_like(far), far], axis=1)], axis=0)
     early_keys = up.reshape(-1, up.shape[-1])
     around = jnp.concatenate([up, down[:, 0], down[:, 1]], axis=0)

time: 195 us -> 203 us (1.041)
  the two profiles are of different devices: /device:TPU:56 before, /device:TPU:236 now
where the time goes in v7:
time: 203 us; the launch traced here: 202 us
  starting transfers between devices  98.2 us (48%)
  waiting for transfers between devices  54.9 us (27%)
  Pallas kernels  14.3 us (7%)
  local copies, waits for them, and re-layouts  13.7 us (7%)
  other arithmetic  11.8 us (6%)
  matrix products  7.65 us (4%)
    ppermute x11, starting transfers between devices, moved(): return lax.ppermute(value, 'ctx', pairs)  80.1 us
    ppermute x11, waiting for transfers between devices, moved(): return lax.ppermute(value, 'ctx', pairs)  27.1 us
    ppermute x3, waiting for transfers between devices, project(): lax.ppermute(weight, both, pairs_for(f))  26.5 us
    pallas_call x1, Pallas kernels, attend(): pl.pallas_call(attend_kernel, out_shape=jax.ShapeDtypeStruct(query_rows.s...  14.3 us
    ppermute x3, starting transfers between devices, project(): lax.ppermute(weight, both, pairs_for(f))  9.46 us
    ppermute x1, starting transfers between devices, project(): mate = lax.ppermute(jnp.stack(mine), both, mate_pairs())  8.62 us
    dot_general x4, matrix products, project(): jnp.dot(rows, mate[index], preferred_element_type=jnp.float32)  6.08 us
    unnamed x24, local copies, waits for them, and re-layouts  4.36 us
  transfers between devices with their start and end apart: 15, of which 10 were waited for; matrix products, arithmetic and copies ran while one was open for 6% of the time, Pallas kernels for 0%

profile of v7, /device:TPU:236, one launch (start us, length us, event | category | flops | bytes accessed | tf_op | source)
XLA Modules:
  0.0 201.8 jit_solution(10952875216429194029)
XLA Ops:
  0.0 2.0 %collective-permute-start = (bf16[2048,192]{0,1:T(8,128)(2,1)}, bf16[2048,192]{0,1:T(8,128)(2,1)S(1)}, u32[]{:S(2)}, u32[]{:S(2)}) collective-permute-start(bf16[2048,192]{0,1:T(8,128)(2,1)} %param.5), channel_id=1, source_target_pairs={{128,0},{129,1},{130,2},{131,3},{132,4},{133,5},{134,6},{135,7},{1... | collective-permute-start | bytes 2359304 | tf_op jit(solution)/shard_map/ppermute | solution.py:90
  2.1 1.9 collective-permute-start.1
  4.0 5.5 %collective-permute-start.2 = (bf16[2048,192]{0,1:T(8,128)(2,1)}, bf16[2048,192]{0,1:T(8,128)(2,1)S(1)}, u32[]{:S(2)}, u32[]{:S(2)}) collective-permute-start(bf16[2048,192]{0,1:T(8,128)(2,1)} %param.5), channel_id=1, source_target_pairs={{416,0},{417,1},{418,2},{419,3},{420,4},{421,5},{422,6},{423,7},{4... | collective-permute-start | bytes 2359304 | tf_op jit(solution)/shard_map/ppermute | solution.py:90
  9.6 13.8 %collective-permute-done = bf16[2048,192]{0,1:T(8,128)(2,1)S(1)} collective-permute-done((bf16[2048,192]{0,1:T(8,128)(2,1)}, bf16[2048,192]{0,1:T(8,128)(2,1)S(1)}, u32[]{:S(2)}, u32[]{:S(2)}) %collective-permute-start) | collective-permute-done | bytes 786464 | tf_op jit(solution)/shard_map/ppermute | solution.py:90
  23.4 10.6 %collective-permute-done.1 = bf16[2048,192]{0,1:T(8,128)(2,1)S(1)} collective-permute-done((bf16[2048,192]{0,1:T(8,128)(2,1)}, bf16[2048,192]{0,1:T(8,128)(2,1)S(1)}, u32[]{:S(2)}, u32[]{:S(2)}) %collective-permute-start.1) | collective-permute-done | bytes 786464 | tf_op jit(solution)/shard_map/ppermute | solution.py:90
  34.0 2.1 %collective-permute-done.2 = bf16[2048,192]{0,1:T(8,128)(2,1)S(1)} collective-permute-done((bf16[2048,192]{0,1:T(8,128)(2,1)}, bf16[2048,192]{0,1:T(8,128)(2,1)S(1)}, u32[]{:S(2)}, u32[]{:S(2)}) %collective-permute-start.2) | collective-permute-done | bytes 786464 | tf_op jit(solution)/shard_map/ppermute | solution.py:90
  36.0 0.9 copy-done.2
  37.0 3.1 %pad_maximum_fusion = bf16[4,2048,192]{1,2,0:T(8,128)(2,1)} fusion(bf16[1,2048,192]{1,2,0:T(8,128)(2,1)} %bitcast.127, bf16[1,2048,192]{1,2,0:T(8,128)(2,1)S(1)} %bitcast.126, bf16[1,2048,192]{1,2,0:T(8,128)(2,1)S(1)} %bitcast.125, bf16[1,2048,192]{1,2,0:T(8,128)(2,1)} %bitcast.124), kind=kLoop, calls=%fused_computation.4 | loop fusion | flops 4718592 | bytes 6291456 | tf_op jit(solution)/shard_map/stack | solution.py:91
  40.1 8.6 %collective-permute-start.3 = (bf16[4,2048,192]{1,2,0:T(8,128)(2,1)}, bf16[4,2048,192]{1,2,0:T(8,128)(2,1)}, u32[]{:S(2)}, u32[]{:S(2)}) collective-permute-start(bf16[4,2048,192]{1,2,0:T(8,128)(2,1)} %pad_maximum_fusion), channel_id=1, source_target_pairs={{64,0},{65,1},{66,2},{67,3},{68,4},{69,5},{70,6},{71,7},{72,8},{73... | collective-permute-start | bytes 9437192 | tf_op jit(solution)/shard_map/ppermute | solution.py:91
  53.0 1.3 collective-permute-done.3
  54.3 1.5 fusion.11
  55.8 1.5 fusion.13
  57.4 1.5 fusion.15
  58.9 1.5 fusion.17
  60.4 0.6 gather_fusion
  61.5 3.1 %collective-permute-start.4 = (bf16[1,64,512]{2,1,0:T(8,128)(2,1)S(1)}, bf16[1,64,512]{2,1,0:T(8,128)(2,1)S(1)}, u32[]{:S(2)}, u32[]{:S(2)}) collective-permute-start(bf16[1,64,512]{2,1,0:T(8,128)(2,1)S(1)} %bitcast.132), channel_id=1, source_target_pairs={{0,1},{1,2},{2,3},{3,4},{4,5},{5,6},{6,7},{7,8},{8,9},{9,10},{10,1... | collective-permute-start | bytes 196616 | tf_op jit(solution)/shard_map/ppermute | solution.py:47
  65.0 2.8 %collective-permute-done.4 = bf16[1,64,512]{2,1,0:T(8,128)(2,1)S(1)} collective-permute-done((bf16[1,64,512]{2,1,0:T(8,128)(2,1)S(1)}, bf16[1,64,512]{2,1,0:T(8,128)(2,1)S(1)}, u32[]{:S(2)}, u32[]{:S(2)}) %collective-permute-start.4) | collective-permute-done | bytes 65568 | tf_op jit(solution)/shard_map/ppermute | solution.py:47
  67.8 2.4 %collective-permute-start.7 = (bf16[1,2,64,512]{3,2,1,0:T(8,128)(2,1)S(1)}, bf16[1,2,64,512]{3,2,1,0:T(8,128)(2,1)S(1)}, u32[]{:S(2)}, u32[]{:S(2)}) collective-permute-start(bf16[1,2,64,512]{3,2,1,0:T(8,128)(2,1)S(1)} %get-tuple-element.25), channel_id=1, source_target_pairs={{1,0},{2,1},{3,2},{4,3},{5,4},{6,5},{7,6},{8,7},{9,8},{10,9},{11,1... | collective-permute-start | bytes 393224 | tf_op jit(solution)/shard_map/ppermute | solution.py:47
  70.9 3.8 %collective-permute-done.7 = bf16[1,2,64,512]{3,2,1,0:T(8,128)(2,1)S(1)} collective-permute-done((bf16[1,2,64,512]{3,2,1,0:T(8,128)(2,1)S(1)}, bf16[1,2,64,512]{3,2,1,0:T(8,128)(2,1)S(1)}, u32[]{:S(2)}, u32[]{:S(2)}) %collective-permute-start.7) | collective-permute-done | bytes 131104 | tf_op jit(solution)/shard_map/ppermute | solution.py:47
  74.7 4.5 %collective-permute-start.8 = (bf16[2,2,64,512]{3,2,1,0:T(8,128)(2,1)S(1)}, bf16[2,2,64,512]{3,2,1,0:T(8,128)(2,1)S(1)}, u32[]{:S(2)}, u32[]{:S(2)}) collective-permute-start(bf16[2,2,64,512]{3,2,1,0:T(8,128)(2,1)S(1)} %pad_maximum_fusion.7), channel_id=1, source_target_pairs={{2,0},{3,1},{4,2},{5,3},{6,4},{7,5},{8,6},{9,7},{10,8},{11,9},{12,... | collective-permute-start | bytes 786440 | tf_op jit(solution)/shard_map/ppermute | solution.py:47
  79.3 0.7 fusion.32
  80.0 3.7 %collective-permute-start.5 = (bf16[2,64,512]{2,1,0:T(8,128)(2,1)S(1)}, bf16[2,64,512]{2,1,0:T(8,128)(2,1)S(1)}, u32[]{:S(2)}, u32[]{:S(2)}) collective-permute-start(bf16[2,64,512]{2,1,0:T(8,128)(2,1)S(1)} %get-tuple-element.26), channel_id=1, source_target_pairs={{0,2},{1,3},{2,4},{3,5},{4,6},{5,7},{6,8},{7,9},{8,10},{9,11},{10,... | collective-permute-start | bytes 393224 | tf_op jit(solution)/shard_map/ppermute | solution.py:47
  83.7 1.9 collective-permute-done.8
  85.7 3.5 %collective-permute-start.9 = (bf16[4,2,64,512]{3,2,1,0:T(8,128)(2,1)S(1)}, bf16[4,2,64,512]{3,2,1,0:T(8,128)(2,1)S(1)}, u32[]{:S(2)}, u32[]{:S(2)}) collective-permute-start(bf16[4,2,64,512]{3,2,1,0:T(8,128)(2,1)S(1)} %pad_maximum_fusion.4), channel_id=1, source_target_pairs={{4,0},{5,1},{6,2},{7,3},{8,4},{9,5},{10,6},{11,7},{12,8},{13,9},{1... | collective-permute-start | bytes 1572872 | tf_op jit(solution)/shard_map/ppermute | solution.py:47
  89.3 2.3 %collective-permute-start.6 = (bf16[4,64,512]{2,1,0:T(8,128)(2,1)S(1)}, bf16[4,64,512]{2,1,0:T(8,128)(2,1)S(1)}, u32[]{:S(2)}, u32[]{:S(2)}) collective-permute-start(bf16[4,64,512]{2,1,0:T(8,128)(2,1)S(1)} %pad_maximum_fusion.6), channel_id=1, source_target_pairs={{0,4},{1,5},{2,6},{3,7},{4,8},{5,9},{6,10},{7,11},{8,12},{9,13},{1... | collective-permute-start | bytes 786440 | tf_op jit(solution)/shard_map/ppermute | solution.py:47
  92.2 0.7 iota_add_fusion.qpos_ref
  92.9 4.7 %collective-permute-done.6 = bf16[4,64,512]{2,1,0:T(8,128)(2,1)S(1)} collective-permute-done((bf16[4,64,512]{2,1,0:T(8,128)(2,1)S(1)}, bf16[4,64,512]{2,1,0:T(8,128)(2,1)S(1)}, u32[]{:S(2)}, u32[]{:S(2)}) %collective-permute-start.6) | collective-permute-done | bytes 262176 | tf_op jit(solution)/shard_map/ppermute | solution.py:47
  97.7 1.1 collective-permute-done.9
  98.9 1.1 slice_bitcast_fusion.11
  100.0 6.6 %collective-permute-start.13 = (bf16[8,64,512]{2,1,0:T(8,128)(2,1)}, bf16[8,64,512]{2,1,0:T(8,128)(2,1)S(1)}, u32[]{:S(2)}, u32[]{:S(2)}) collective-permute-start(bf16[8,64,512]{2,1,0:T(8,128)(2,1)} %get-tuple-element.16), channel_id=1, source_target_pairs={{8,0},{9,1},{10,2},{11,3},{12,4},{13,5},{14,6},{15,7},{16,8},{17,9... | collective-permute-start | bytes 1572872 | tf_op jit(solution)/shard_map/ppermute | solution.py:47
  106.6 1.5 collective-permute-start.12
  108.2 0.7 broadcast_in_dim.71
  108.8 1.4 copy.53.qdoc_ref
  110.4 40.0 %collective-permute-start.10 = (bf16[8,64,512]{2,1,0:T(8,128)(2,1)S(1)}, bf16[8,64,512]{2,1,0:T(8,128)(2,1)S(1)}, u32[]{:S(2)}, u32[]{:S(2)}) collective-permute-start(bf16[8,64,512]{2,1,0:T(8,128)(2,1)S(1)} %pad_maximum_fusion.3), channel_id=1, source_target_pairs={{0,8},{1,9},{2,10},{3,11},{4,12},{5,13},{6,14},{7,15},{8,16},{9,17... | collective-permute-start | bytes 1572872 | tf_op jit(solution)/shard_map/ppermute | solution.py:47
  150.5 0.9 copy.52.q_ref
  151.3 10.3 %collective-permute-start.11 = (bf16[1,64,512]{2,1,0:T(8,128)(2,1)S(1)}, bf16[1,64,512]{2,1,0:T(8,128)(2,1)S(1)}, u32[]{:S(2)}, u32[]{:S(2)}) collective-permute-start(bf16[1,64,512]{2,1,0:T(8,128)(2,1)S(1)} %bitcast.136), channel_id=1, source_target_pairs={{0,16},{1,17},{2,18},{3,19},{4,20},{5,21},{6,22},{7,23},{8,24},{9,... | collective-permute-start | bytes 196616 | tf_op jit(solution)/shard_map/ppermute | solution.py:47
  161.6 2.1 %collective-permute-start.14 = (bf16[1,64,512]{2,1,0:T(8,128)(2,1)}, bf16[1,64,512]{2,1,0:T(8,128)(2,1)S(1)}, u32[]{:S(2)}, u32[]{:S(2)}) collective-permute-start(bf16[1,64,512]{2,1,0:T(8,128)(2,1)} %bitcast.139), channel_id=1, source_target_pairs={{16,0},{17,1},{18,2},{19,3},{20,4},{21,5},{22,6},{23,7},{24,8},{25... | collective-permute-start | bytes 196616 | tf_op jit(solution)/shard_map/ppermute | solution.py:47
  163.7 0.9 constant_dynamic-update-slice_fusion.2
  164.6 12.8 %collective-permute-done.14 = bf16[1,64,512]{2,1,0:T(8,128)(2,1)S(1)} collective-permute-done((bf16[1,64,512]{2,1,0:T(8,128)(2,1)}, bf16[1,64,512]{2,1,0:T(8,128)(2,1)S(1)}, u32[]{:S(2)}, u32[]{:S(2)}) %collective-permute-start.14) | collective-permute-done | bytes 65568 | tf_op jit(solution)/shard_map/ppermute | solution.py:47
  177.4 1.2 fusion.1
  178.7 0.9 constant_dynamic-update-slice_fusion.1
  179.5 0.6 constant_dynamic-update-slice_fusion
  180.1 1.1 fusion.19
  181.2 1.1 fusion.18
  182.3 2.7 %gather_fusion.1 = bf16[17,64,512]{2,1,0:T(8,128)(2,1)S(1)} fusion(bf16[51,64,512]{2,1,0:T(8,128)(2,1)} %fusion.18, s32[1024]{0:T(1024)} %pad_clamp_fusion), kind=kCustom, calls=%fused_computation.1 | custom fusion | bytes 2228292 | tf_op jit(solution)/shard_map/jit(_take)/gather | solution.py:177
  185.0 1.2 bitcast_select_fusion.late_ref
  186.2 1.2 pad_maximum_fusion.1
  187.4 14.3 %shard_map.46 = bf16[128,1024]{1,0:T(8,128)(2,1)} custom-call(s32[1]{0:T(128)} %bitcast.offset_ref, bf16[128,1024]{1,0:T(8,128)(2,1)} %copy.52.q_ref, bf16[1088,512]{1,0:T(8,128)(2,1)} %bitcast.123, bf16[1088,512]{1,0:T(8,128)(2,1)} %bitcast_select_fusion.late_ref, s32[2,64,1]{2,1,0:T(8,128)} %iota_add_fusion.qpos_ref, s32[2,64,1]{2,1,0:T(8,128)} %copy.53.qdoc_ref, ...), custom_call_target="tpu_custom_call" | custom-call | tf_op jit(solution)/shard_map/pallas_call | solution.py:237
  (77 shorter events, 6.2 us)
Async XLA Ops:
  0.0 51.3 %copy-start = (bf16[1,128,2048]{2,1,0:T(8,128)(2,1)S(1)}, bf16[1,128,2048]{2,1,0:T(8,128)(2,1)}, u32[]{:S(2)}) copy-start(bf16[1,128,2048]{2,1,0:T(8,128)(2,1)} %param.4) | copy-start | bytes 1572868
  0.0 23.4 %collective-permute-start = (bf16[2048,192]{0,1:T(8,128)(2,1)}, bf16[2048,192]{0,1:T(8,128)(2,1)S(1)}, u32[]{:S(2)}, u32[]{:S(2)}) collective-permute-start(bf16[2048,192]{0,1:T(8,128)(2,1)} %param.5), channel_id=1, source_target_pairs={{128,0},{129,1},{130,2},{131,3},{132,4},{133,5},{134,6},{135,7},{1... | collective-permute-start | bytes 2359304 | tf_op jit(solution)/shard_map/ppermute | solution.py:90
  2.1 31.9 %collective-permute-start.1 = (bf16[2048,192]{0,1:T(8,128)(2,1)}, bf16[2048,192]{0,1:T(8,128)(2,1)S(1)}, u32[]{:S(2)}, u32[]{:S(2)}) collective-permute-start(bf16[2048,192]{0,1:T(8,128)(2,1)} %param.5), channel_id=1, source_target_pairs={{256,0},{257,1},{258,2},{259,3},{260,4},{261,5},{262,6},{263,7},{2... | collective-permute-start | bytes 2359304 | tf_op jit(solution)/shard_map/ppermute | solution.py:90
  4.0 32.1 %collective-permute-start.2 = (bf16[2048,192]{0,1:T(8,128)(2,1)}, bf16[2048,192]{0,1:T(8,128)(2,1)S(1)}, u32[]{:S(2)}, u32[]{:S(2)}) collective-permute-start(bf16[2048,192]{0,1:T(8,128)(2,1)} %param.5), channel_id=1, source_target_pairs={{416,0},{417,1},{418,2},{419,3},{420,4},{421,5},{422,6},{423,7},{4... | collective-permute-start | bytes 2359304 | tf_op jit(solution)/shard_map/ppermute | solution.py:90
  36.0 0.9 copy-start.2
  36.9 12.1 %copy-start.9 = (s32[1,128]{1,0:T(1,128)S(1)}, s32[1,128]{1,0:T(1,128)}, u32[]{:S(2)}) copy-start(s32[1,128]{1,0:T(1,128)} %param.7) | copy-start | bytes 1540
  36.9 13.5 %copy-start.8 = (s32[1,36]{1,0:T(1,128)S(1)}, s32[1,36]{1,0:T(1,128)}, u32[]{:S(2)}) copy-start(s32[1,36]{1,0:T(1,128)} %param.6) | copy-start | bytes 436
  36.9 14.4 %copy-start.1 = (bf16[2048,192]{0,1:T(8,128)(2,1)S(1)}, bf16[2048,192]{0,1:T(8,128)(2,1)}, u32[]{:S(2)}) copy-start(bf16[2048,192]{0,1:T(8,128)(2,1)} %param.5) | copy-start | bytes 2359300
  40.1 14.2 %collective-permute-start.3 = (bf16[4,2048,192]{1,2,0:T(8,128)(2,1)}, bf16[4,2048,192]{1,2,0:T(8,128)(2,1)}, u32[]{:S(2)}, u32[]{:S(2)}) collective-permute-start(bf16[4,2048,192]{1,2,0:T(8,128)(2,1)} %pad_maximum_fusion), channel_id=1, source_target_pairs={{64,0},{65,1},{66,2},{67,3},{68,4},{69,5},{70,6},{71,7},{72,8},{73... | collective-permute-start | bytes 9437192 | tf_op jit(solution)/shard_map/ppermute | solution.py:91
  51.1 1.5 copy-start.3
  51.4 46.3 %copy-start.5 = (f32[128,32]{0,1:T(8,128)}, f32[128,32]{0,1:T(8,128)S(1)}, u32[]{:S(2)}) copy-start(f32[128,32]{0,1:T(8,128)S(1)} %get-tuple-element.28) | copy-start | bytes 49156
  61.5 6.3 %collective-permute-start.4 = (bf16[1,64,512]{2,1,0:T(8,128)(2,1)S(1)}, bf16[1,64,512]{2,1,0:T(8,128)(2,1)S(1)}, u32[]{:S(2)}, u32[]{:S(2)}) collective-permute-start(bf16[1,64,512]{2,1,0:T(8,128)(2,1)S(1)} %bitcast.132), channel_id=1, source_target_pairs={{0,1},{1,2},{2,3},{3,4},{4,5},{5,6},{6,7},{7,8},{8,9},{9,10},{10,1... | collective-permute-start | bytes 196616 | tf_op jit(solution)/shard_map/ppermute | solution.py:47
  65.0 9.7 %copy-start.4 = (bf16[64,512]{1,0:T(8,128)(2,1)}, bf16[64,512]{1,0:T(8,128)(2,1)S(1)}, u32[]{:S(2)}) copy-start(bf16[64,512]{1,0:T(8,128)(2,1)S(1)} %copy.44) | copy-start | bytes 196612
  67.8 6.9 %collective-permute-start.7 = (bf16[1,2,64,512]{3,2,1,0:T(8,128)(2,1)S(1)}, bf16[1,2,64,512]{3,2,1,0:T(8,128)(2,1)S(1)}, u32[]{:S(2)}, u32[]{:S(2)}) collective-permute-start(bf16[1,2,64,512]{3,2,1,0:T(8,128)(2,1)S(1)} %get-tuple-element.25), channel_id=1, source_target_pairs={{1,0},{2,1},{3,2},{4,3},{5,4},{6,5},{7,6},{8,7},{9,8},{10,9},{11,1... | collective-permute-start | bytes 393224 | tf_op jit(solution)/shard_map/ppermute | solution.py:47
  74.7 11.0 %collective-permute-start.8 = (bf16[2,2,64,512]{3,2,1,0:T(8,128)(2,1)S(1)}, bf16[2,2,64,512]{3,2,1,0:T(8,128)(2,1)S(1)}, u32[]{:S(2)}, u32[]{:S(2)}) collective-permute-start(bf16[2,2,64,512]{3,2,1,0:T(8,128)(2,1)S(1)} %pad_maximum_fusion.7), channel_id=1, source_target_pairs={{2,0},{3,1},{4,2},{5,3},{6,4},{7,5},{8,6},{9,7},{10,8},{11,9},{12,... | collective-permute-start | bytes 786440 | tf_op jit(solution)/shard_map/ppermute | solution.py:47
  80.0 9.2 %collective-permute-start.5 = (bf16[2,64,512]{2,1,0:T(8,128)(2,1)S(1)}, bf16[2,64,512]{2,1,0:T(8,128)(2,1)S(1)}, u32[]{:S(2)}, u32[]{:S(2)}) collective-permute-start(bf16[2,64,512]{2,1,0:T(8,128)(2,1)S(1)} %get-tuple-element.26), channel_id=1, source_target_pairs={{0,2},{1,3},{2,4},{3,5},{4,6},{5,7},{6,8},{7,9},{8,10},{9,11},{10,... | collective-permute-start | bytes 393224 | tf_op jit(solution)/shard_map/ppermute | solution.py:47
  85.7 13.1 %collective-permute-start.9 = (bf16[4,2,64,512]{3,2,1,0:T(8,128)(2,1)S(1)}, bf16[4,2,64,512]{3,2,1,0:T(8,128)(2,1)S(1)}, u32[]{:S(2)}, u32[]{:S(2)}) collective-permute-start(bf16[4,2,64,512]{3,2,1,0:T(8,128)(2,1)S(1)} %pad_maximum_fusion.4), channel_id=1, source_target_pairs={{4,0},{5,1},{6,2},{7,3},{8,4},{9,5},{10,6},{11,7},{12,8},{13,9},{1... | collective-permute-start | bytes 1572872 | tf_op jit(solution)/shard_map/ppermute | solution.py:47
  89.3 8.4 %collective-permute-start.6 = (bf16[4,64,512]{2,1,0:T(8,128)(2,1)S(1)}, bf16[4,64,512]{2,1,0:T(8,128)(2,1)S(1)}, u32[]{:S(2)}, u32[]{:S(2)}) collective-permute-start(bf16[4,64,512]{2,1,0:T(8,128)(2,1)S(1)} %pad_maximum_fusion.6), channel_id=1, source_target_pairs={{0,4},{1,5},{2,6},{3,7},{4,8},{5,9},{6,10},{7,11},{8,12},{9,13},{1... | collective-permute-start | bytes 786440 | tf_op jit(solution)/shard_map/ppermute | solution.py:47
  98.8 11.5 %copy-start.6 = (f32[128,32]{0,1:T(8,128)S(1)}, f32[128,32]{0,1:T(8,128)}, u32[]{:S(2)}) copy-start(f32[128,32]{0,1:T(8,128)} %copy-done.5) | copy-start | bytes 49156
  100.0 77.4 %collective-permute-start.13 = (bf16[8,64,512]{2,1,0:T(8,128)(2,1)}, bf16[8,64,512]{2,1,0:T(8,128)(2,1)S(1)}, u32[]{:S(2)}, u32[]{:S(2)}) collective-permute-start(bf16[8,64,512]{2,1,0:T(8,128)(2,1)} %get-tuple-element.16), channel_id=1, source_target_pairs={{8,0},{9,1},{10,2},{11,3},{12,4},{13,5},{14,6},{15,7},{16,8},{17,9... | collective-permute-start | bytes 1572872 | tf_op jit(solution)/shard_map/ppermute | solution.py:47
  106.6 70.8 %collective-permute-start.12 = (bf16[8,64,512]{2,1,0:T(8,128)(2,1)}, bf16[8,64,512]{2,1,0:T(8,128)(2,1)}, u32[]{:S(2)}, u32[]{:S(2)}) collective-permute-start(bf16[8,64,512]{2,1,0:T(8,128)(2,1)} %get-tuple-element.15), channel_id=1, source_target_pairs={{56,48},{57,49},{58,50},{59,51},{60,52},{61,53},{62,54},{63,55},{1... | collective-permute-start | bytes 1572872 | tf_op jit(solution)/shard_map/ppermute | solution.py:47
  110.4 68.2 %collective-permute-start.10 = (bf16[8,64,512]{2,1,0:T(8,128)(2,1)S(1)}, bf16[8,64,512]{2,1,0:T(8,128)(2,1)S(1)}, u32[]{:S(2)}, u32[]{:S(2)}) collective-permute-start(bf16[8,64,512]{2,1,0:T(8,128)(2,1)S(1)} %pad_maximum_fusion.3), channel_id=1, source_target_pairs={{0,8},{1,9},{2,10},{3,11},{4,12},{5,13},{6,14},{7,15},{8,16},{9,17... | collective-permute-start | bytes 1572872 | tf_op jit(solution)/shard_map/ppermute | solution.py:47
  151.3 28.2 %collective-permute-start.11 = (bf16[1,64,512]{2,1,0:T(8,128)(2,1)S(1)}, bf16[1,64,512]{2,1,0:T(8,128)(2,1)S(1)}, u32[]{:S(2)}, u32[]{:S(2)}) collective-permute-start(bf16[1,64,512]{2,1,0:T(8,128)(2,1)S(1)} %bitcast.136), channel_id=1, source_target_pairs={{0,16},{1,17},{2,18},{3,19},{4,20},{5,21},{6,22},{7,23},{8,24},{9,... | collective-permute-start | bytes 196616 | tf_op jit(solution)/shard_map/ppermute | solution.py:47
  161.6 15.8 %collective-permute-start.14 = (bf16[1,64,512]{2,1,0:T(8,128)(2,1)}, bf16[1,64,512]{2,1,0:T(8,128)(2,1)S(1)}, u32[]{:S(2)}, u32[]{:S(2)}) collective-permute-start(bf16[1,64,512]{2,1,0:T(8,128)(2,1)} %bitcast.139), channel_id=1, source_target_pairs={{16,0},{17,1},{18,2},{19,3},{20,4},{21,5},{22,6},{23,7},{24,8},{25... | collective-permute-start | bytes 196616 | tf_op jit(solution)/shard_map/ppermute | solution.py:47
  180.1 4.9 %copy-start.7 = (pred[1088]{0:T(1024)(128)(4,1)S(1)}, pred[1088]{0:T(1024)(128)(4,1)}, u32[]{:S(2)}) copy-start(pred[1088]{0:T(1024)(128)(4,1)} %broadcast_in_dim.71) | copy-start | bytes 3268

commit v8 on v5

--- a/solution.py
+++ b/solution.py
@@ -206,25 +206,29 @@
         row = offset if span == 0 else SPAN - offset
         row = pl.multiple_of(row, SPAN)
         live = (qdoc_ref[span] == kdoc_ref[span]) & (kpos_ref[span] <= qpos_ref[span])
+        live = jnp.concatenate([live] * QUERY_PER_KV, axis=0)
         for group in range(KEY_VALUE_HEADS):
             key = kv_ref[:, group * HEAD_SIZE : (group + 1) * HEAD_SIZE]
             base = KEY_VALUE_HEADS * HEAD_SIZE + group * HEAD_SIZE
             value = kv_ref[:, base : base + HEAD_SIZE]
-            for member in range(QUERY_PER_KV):
-                head = group * QUERY_PER_KV + member
-                cols = slice(head * HEAD_SIZE, (head + 1) * HEAD_SIZE)
-                query = q_ref[pl.ds(row, SPAN), cols]
-                scores = lax.dot_general(
-                    query, key, (((1,), (1,)), ((), ())), preferred_element_type=jnp.float32
-                ) * 0.125
-                scores = jnp.where(live, scores, -1e30)
-                top = jnp.max(scores, axis=1, keepdims=True)
-                weights = jnp.where(live, jnp.exp(scores - top), 0.0)
-                total = jnp.sum(weights, axis=1, keepdims=True)
-                summed = jnp.dot(
-                    weights.astype(jnp.bfloat16), value, preferred_element_type=jnp.float32
-                )
-                o_ref[pl.ds(row, SPAN), cols] = (summed / total).astype(o_ref.dtype)
+            heads = range(group * QUERY_PER_KV, (group + 1) * QUERY_PER_KV)
+            query = jnp.concatenate(
+                [q_ref[pl.ds(row, SPAN), head * HEAD_SIZE : (head + 1) * HEAD_SIZE] for head in heads],
+                axis=0,
+            )
+            scores = lax.dot_general(
+                query, key, (((1,), (1,)), ((), ())), preferred_element_type=jnp.float32
+            ) * 0.125
+            scores = jnp.where(live, scores, -1e30)
+            top = jnp.max(scores, axis=1, keepdims=True)
+            weights = jnp.exp(scores - top)
+            total = jnp.sum(weights, axis=1, keepdims=True)
+            summed = jnp.dot(weights.astype(jnp.bfloat16), value, preferred_element_type=jnp.float32)
+            result = (summed / total).astype(o_ref.dtype)
+            for member, head in enumerate(heads):
+                o_ref[pl.ds(row, SPAN), head * HEAD_SIZE : (head + 1) * HEAD_SIZE] = result[
+                    member * SPAN : (member + 1) * SPAN
+                ]
 
 
 def attend(offset, query_rows, early_keys, late_keys, qpos, qdoc, kpos, kdoc):

time: 195 us -> 188 us (0.964)
  Pallas kernels: 14.3 us -> 7.8 us
    pallas_call x1, Pallas kernels: 14.3 us -> 7.8 us  [attend(): pl.pallas_call(attend_kernel, out_shape=jax.ShapeDtypeStruct(query_rows.s...]
where the time goes in v8:
time: 188 us
  waiting for transfers between devices  75 us (40%)
  starting transfers between devices  72.1 us (38%)
  local copies, waits for them, and re-layouts  16.8 us (9%)
  other arithmetic  11.8 us (6%)
  Pallas kernels  7.8 us (4%)
  matrix products  3.08 us (2%)
    ppermute x11, starting transfers between devices, moved(): return lax.ppermute(value, 'ctx', pairs)  50.6 us
    ppermute x11, waiting for transfers between devices, moved(): return lax.ppermute(value, 'ctx', pairs)  50.6 us
    ppermute x3, waiting for transfers between devices, project(): lax.ppermute(weight, both, pairs_for(f))  22.6 us
    ppermute x3, starting transfers between devices, project(): lax.ppermute(weight, both, pairs_for(f))  16.9 us
    pallas_call x1, Pallas kernels, attend(): pl.pallas_call(attend_kernel, out_shape=jax.ShapeDtypeStruct(query_rows.s...  7.8 us
    unnamed x14, local copies, waits for them, and re-layouts  6.71 us
    ppermute x1, starting transfers between devices, project(): mate = lax.ppermute(jnp.stack(mine), both, mate_pairs())  4.6 us
  transfers between devices with their start and end apart: 15, of which 6 were waited for; matrix products, arithmetic and copies ran while one was open for 11% of the time, Pallas kernels for 0%

profile of v8, /device:TPU:56, one launch (start us, length us, event | category | flops | bytes accessed | tf_op | source)
XLA Modules:
  0.0 187.7 jit_solution(14386270802055133505)
XLA Ops:
  0.0 11.1 %collective-permute-start = (bf16[2048,192]{0,1:T(8,128)(2,1)}, bf16[2048,192]{0,1:T(8,128)(2,1)S(1)}, u32[]{:S(2)}, u32[]{:S(2)}) collective-permute-start(bf16[2048,192]{0,1:T(8,128)(2,1)} %param.5), channel_id=1, source_target_pairs={{128,0},{129,1},{130,2},{131,3},{132,4},{133,5},{134,6},{135,7},{1... | collective-permute-start | bytes 2359304 | tf_op jit(solution)/shard_map/ppermute | solution.py:90
  11.1 2.5 %collective-permute-start.1 = (bf16[2048,192]{0,1:T(8,128)(2,1)}, bf16[2048,192]{0,1:T(8,128)(2,1)S(1)}, u32[]{:S(2)}, u32[]{:S(2)}) collective-permute-start(bf16[2048,192]{0,1:T(8,128)(2,1)} %param.5), channel_id=1, source_target_pairs={{256,0},{257,1},{258,2},{259,3},{260,4},{261,5},{262,6},{263,7},{2... | collective-permute-start | bytes 2359304 | tf_op jit(solution)/shard_map/ppermute | solution.py:90
  13.5 3.4 %collective-permute-start.2 = (bf16[2048,192]{0,1:T(8,128)(2,1)}, bf16[2048,192]{0,1:T(8,128)(2,1)S(1)}, u32[]{:S(2)}, u32[]{:S(2)}) collective-permute-start(bf16[2048,192]{0,1:T(8,128)(2,1)} %param.5), channel_id=1, source_target_pairs={{416,0},{417,1},{418,2},{419,3},{420,4},{421,5},{422,6},{423,7},{4... | collective-permute-start | bytes 2359304 | tf_op jit(solution)/shard_map/ppermute | solution.py:90
  17.3 0.7 multiply_bitcast_fusion
  18.0 1.2 fusion.45
  20.2 0.8 copy.73
  21.3 0.7 copy.78.qdoc_ref
  22.4 14.2 %collective-permute-done = bf16[2048,192]{0,1:T(8,128)(2,1)S(1)} collective-permute-done((bf16[2048,192]{0,1:T(8,128)(2,1)}, bf16[2048,192]{0,1:T(8,128)(2,1)S(1)}, u32[]{:S(2)}, u32[]{:S(2)}) %collective-permute-start) | collective-permute-done | bytes 786464 | tf_op jit(solution)/shard_map/ppermute | solution.py:90
  36.6 8.4 %collective-permute-done.1 = bf16[2048,192]{0,1:T(8,128)(2,1)S(1)} collective-permute-done((bf16[2048,192]{0,1:T(8,128)(2,1)}, bf16[2048,192]{0,1:T(8,128)(2,1)S(1)}, u32[]{:S(2)}, u32[]{:S(2)}) %collective-permute-start.1) | collective-permute-done | bytes 786464 | tf_op jit(solution)/shard_map/ppermute | solution.py:90
  45.0 1.5 pad_maximum_fusion
  46.5 4.6 %collective-permute-start.3 = (bf16[4,2048,192]{1,2,0:T(8,128)(2,1)S(1)}, bf16[4,2048,192]{1,2,0:T(8,128)(2,1)S(1)}, u32[]{:S(2)}, u32[]{:S(2)}) collective-permute-start(bf16[4,2048,192]{1,2,0:T(8,128)(2,1)S(1)} %pad_maximum_fusion), channel_id=1, source_target_pairs={{64,0},{65,1},{66,2},{67,3},{68,4},{69,5},{70,6},{71,7},{72,8},{73... | collective-permute-start | bytes 9437192 | tf_op jit(solution)/shard_map/ppermute | solution.py:91
  51.7 0.7 iota_add_fusion.qpos_ref
  52.8 0.6 reshape_select_fusion
  54.6 1.8 collective-permute-done.3
  56.8 0.4 fusion.11
  58.0 0.6 gather_fusion
  59.1 3.4 %collective-permute-start.4 = (bf16[1,64,512]{2,1,0:T(8,128)(2,1)S(1)}, bf16[1,64,512]{2,1,0:T(8,128)(2,1)S(1)}, u32[]{:S(2)}, u32[]{:S(2)}) collective-permute-start(bf16[1,64,512]{2,1,0:T(8,128)(2,1)S(1)} %bitcast.138), channel_id=1, source_target_pairs={{0,1},{1,2},{2,3},{3,4},{4,5},{5,6},{6,7},{7,8},{8,9},{9,10},{10,1... | collective-permute-start | bytes 196616 | tf_op jit(solution)/shard_map/ppermute | solution.py:47
  62.5 0.7 constant_dynamic-update-slice_fusion.13
  63.2 7.9 %collective-permute-start.8 = (bf16[1,64,512]{2,1,0:T(8,128)(2,1)S(1)}, bf16[1,64,512]{2,1,0:T(8,128)(2,1)}, u32[]{:S(2)}, u32[]{:S(2)}) collective-permute-start(bf16[1,64,512]{2,1,0:T(8,128)(2,1)S(1)} %bitcast.139), channel_id=1, source_target_pairs={{0,16},{1,17},{2,18},{3,19},{4,20},{5,21},{6,22},{7,23},{8,24},{9,... | collective-permute-start | bytes 196616 | tf_op jit(solution)/shard_map/ppermute | solution.py:47
  71.1 0.7 copy.64
  71.9 2.4 %collective-permute-start.14 = (bf16[1,64,512]{2,1,0:T(8,128)(2,1)}, bf16[1,64,512]{2,1,0:T(8,128)(2,1)}, u32[]{:S(2)}, u32[]{:S(2)}) collective-permute-start(bf16[1,64,512]{2,1,0:T(8,128)(2,1)} %bitcast.36), channel_id=1, source_target_pairs={{16,0},{17,1},{18,2},{19,3},{20,4},{21,5},{22,6},{23,7},{24,8},{25... | collective-permute-start | bytes 196616 | tf_op jit(solution)/shard_map/ppermute | solution.py:47
  74.3 1.6 fusion.30
  75.9 4.5 %collective-permute-start.9 = (bf16[1,2,64,512]{3,2,0,1:T(8,128)(2,1)S(1)}, bf16[1,2,64,512]{3,2,0,1:T(8,128)(2,1)S(1)}, u32[]{:S(2)}, u32[]{:S(2)}) collective-permute-start(bf16[1,2,64,512]{3,2,0,1:T(8,128)(2,1)S(1)} %get-tuple-element.20), channel_id=1, source_target_pairs={{1,0},{2,1},{3,2},{4,3},{5,4},{6,5},{7,6},{8,7},{9,8},{10,9},{11,1... | collective-permute-start | bytes 393224 | tf_op jit(solution)/shard_map/ppermute | solution.py:47
  80.5 0.8 constant_dynamic-update-slice_fusion.7
  81.4 2.8 %collective-permute-start.5 = (bf16[2,64,512]{2,1,0:T(8,128)(2,1)}, bf16[2,64,512]{2,1,0:T(8,128)(2,1)S(1)}, u32[]{:S(2)}, u32[]{:S(2)}) collective-permute-start(bf16[2,64,512]{2,1,0:T(8,128)(2,1)} %get-tuple-element.25), channel_id=1, source_target_pairs={{0,2},{1,3},{2,4},{3,5},{4,6},{5,7},{6,8},{7,9},{8,10},{9,11},{10,... | collective-permute-start | bytes 393224 | tf_op jit(solution)/shard_map/ppermute | solution.py:47
  84.2 0.8 pad_maximum_fusion.6
  84.9 5.4 %collective-permute-start.10 = (bf16[2,2,64,512]{3,2,1,0:T(8,128)(2,1)}, bf16[2,2,64,512]{3,2,1,0:T(8,128)(2,1)S(1)}, u32[]{:S(2)}, u32[]{:S(2)}) collective-permute-start(bf16[2,2,64,512]{3,2,1,0:T(8,128)(2,1)} %pad_maximum_fusion.6), channel_id=1, source_target_pairs={{2,0},{3,1},{4,2},{5,3},{6,4},{7,5},{8,6},{9,7},{10,8},{11,9},{12,... | collective-permute-start | bytes 786440 | tf_op jit(solution)/shard_map/ppermute | solution.py:47
  90.4 0.7 pad_maximum_fusion.4
  91.1 1.8 copy.77.q_ref
  92.9 0.7 constant_dynamic-update-slice_fusion.12
  93.6 16.9 %collective-permute-start.6 = (bf16[4,64,512]{2,1,0:T(8,128)(2,1)S(1)}, bf16[4,64,512]{2,1,0:T(8,128)(2,1)S(1)}, u32[]{:S(2)}, u32[]{:S(2)}) collective-permute-start(bf16[4,64,512]{2,1,0:T(8,128)(2,1)S(1)} %pad_maximum_fusion.5), channel_id=1, source_target_pairs={{0,4},{1,5},{2,6},{3,7},{4,8},{5,9},{6,10},{7,11},{8,12},{9,13},{1... | collective-permute-start | bytes 786440 | tf_op jit(solution)/shard_map/ppermute | solution.py:47
  110.6 1.9 %collective-permute-start.11 = (bf16[4,2,64,512]{3,2,1,0:T(8,128)(2,1)S(1)}, bf16[4,2,64,512]{3,2,1,0:T(8,128)(2,1)S(1)}, u32[]{:S(2)}, u32[]{:S(2)}) collective-permute-start(bf16[4,2,64,512]{3,2,1,0:T(8,128)(2,1)S(1)} %pad_maximum_fusion.3), channel_id=1, source_target_pairs={{4,0},{5,1},{6,2},{7,3},{8,4},{9,5},{10,6},{11,7},{12,8},{13,9},{1... | collective-permute-start | bytes 1572872 | tf_op jit(solution)/shard_map/ppermute | solution.py:47
  112.5 0.7 constant_dynamic-update-slice_fusion.11
  113.3 3.3 %collective-permute-done.6 = bf16[4,64,512]{2,1,0:T(8,128)(2,1)S(1)} collective-permute-done((bf16[4,64,512]{2,1,0:T(8,128)(2,1)S(1)}, bf16[4,64,512]{2,1,0:T(8,128)(2,1)S(1)}, u32[]{:S(2)}, u32[]{:S(2)}) %collective-permute-start.6) | collective-permute-done | bytes 262176 | tf_op jit(solution)/shard_map/ppermute | solution.py:47
  116.6 2.5 %collective-permute-start.7 = (bf16[8,64,512]{2,1,0:T(8,128)(2,1)S(1)}, bf16[8,64,512]{2,1,0:T(8,128)(2,1)S(1)}, u32[]{:S(2)}, u32[]{:S(2)}) collective-permute-start(bf16[8,64,512]{2,1,0:T(8,128)(2,1)S(1)} %pad_maximum_fusion.2), channel_id=1, source_target_pairs={{0,8},{1,9},{2,10},{3,11},{4,12},{5,13},{6,14},{7,15},{8,16},{9,17... | collective-permute-start | bytes 1572872 | tf_op jit(solution)/shard_map/ppermute | solution.py:47
  119.1 22.2 %collective-permute-done.11 = bf16[4,2,64,512]{3,2,1,0:T(8,128)(2,1)S(1)} collective-permute-done((bf16[4,2,64,512]{3,2,1,0:T(8,128)(2,1)S(1)}, bf16[4,2,64,512]{3,2,1,0:T(8,128)(2,1)S(1)}, u32[]{:S(2)}, u32[]{:S(2)}) %collective-permute-start.11) | collective-permute-done | bytes 524320 | tf_op jit(solution)/shard_map/ppermute | solution.py:47
  141.5 1.9 %collective-permute-start.13 = (bf16[8,64,512]{2,1,0:T(8,128)(2,1)S(1)}, bf16[8,64,512]{2,1,0:T(8,128)(2,1)S(1)}, u32[]{:S(2)}, u32[]{:S(2)}) collective-permute-start(bf16[8,64,512]{2,1,0:T(8,128)(2,1)S(1)} %get-tuple-element.8), channel_id=1, source_target_pairs={{8,0},{9,1},{10,2},{11,3},{12,4},{13,5},{14,6},{15,7},{16,8},{17,9... | collective-permute-start | bytes 1572872 | tf_op jit(solution)/shard_map/ppermute | solution.py:47
  143.4 0.9 collective-permute-start.12
  144.3 0.8 constant_dynamic-update-slice_fusion.10
  145.2 1.1 constant_dynamic-update-slice_fusion.9
  146.3 1.5 constant_dynamic-update-slice_fusion.8
  147.8 25.1 %collective-permute-done.13 = bf16[8,64,512]{2,1,0:T(8,128)(2,1)S(1)} collective-permute-done((bf16[8,64,512]{2,1,0:T(8,128)(2,1)S(1)}, bf16[8,64,512]{2,1,0:T(8,128)(2,1)S(1)}, u32[]{:S(2)}, u32[]{:S(2)}) %collective-permute-start.13) | collective-permute-done | bytes 524320 | tf_op jit(solution)/shard_map/ppermute | solution.py:47
  173.0 0.8 pad_dynamic-update-slice_fusion
  173.9 1.1 fusion.17
  174.9 1.1 fusion.16
  176.1 2.6 %gather_fusion.1 = bf16[17,64,512]{2,1,0:T(8,128)(2,1)S(1)} fusion(bf16[51,64,512]{2,1,0:T(8,128)(2,1)} %fusion.16, s32[1024]{0:T(1024)S(1)} %pad_clamp_fusion), kind=kCustom, calls=%fused_computation.1 | custom fusion | bytes 2228292 | tf_op jit(solution)/shard_map/jit(_take)/gather | solution.py:172
  178.6 1.2 bitcast_select_fusion.late_ref
  179.9 7.8 %shard_map.46 = bf16[128,1024]{1,0:T(8,128)(2,1)} custom-call(s32[1]{0:T(128)} %bitcast.offset_ref, bf16[128,1024]{1,0:T(8,128)(2,1)} %copy.77.q_ref, bf16[1088,512]{1,0:T(8,128)(2,1)} %bitcast.149, bf16[1088,512]{1,0:T(8,128)(2,1)} %bitcast_select_fusion.late_ref, s32[2,64,1]{2,1,0:T(8,128)} %iota_add_fusion.qpos_ref, s32[2,64,1]{2,1,0:T(8,128)} %copy.78.qdoc_ref, ...), custom_call_target="tpu_custom_call" | custom-call | tf_op jit(solution)/shard_map/pallas_call | solution.py:236
  (68 shorter events, 5.6 us)
Async XLA Ops:
  0.0 52.4 %copy-start = (bf16[1,128,2048]{2,1,0:T(8,128)(2,1)S(1)}, bf16[1,128,2048]{2,1,0:T(8,128)(2,1)}, u32[]{:S(2)}) copy-start(bf16[1,128,2048]{2,1,0:T(8,128)(2,1)} %param.4) | copy-start | bytes 1572868
  0.0 36.6 %collective-permute-start = (bf16[2048,192]{0,1:T(8,128)(2,1)}, bf16[2048,192]{0,1:T(8,128)(2,1)S(1)}, u32[]{:S(2)}, u32[]{:S(2)}) collective-permute-start(bf16[2048,192]{0,1:T(8,128)(2,1)} %param.5), channel_id=1, source_target_pairs={{128,0},{129,1},{130,2},{131,3},{132,4},{133,5},{134,6},{135,7},{1... | collective-permute-start | bytes 2359304 | tf_op jit(solution)/shard_map/ppermute | solution.py:90
  11.1 33.9 %collective-permute-start.1 = (bf16[2048,192]{0,1:T(8,128)(2,1)}, bf16[2048,192]{0,1:T(8,128)(2,1)S(1)}, u32[]{:S(2)}, u32[]{:S(2)}) collective-permute-start(bf16[2048,192]{0,1:T(8,128)(2,1)} %param.5), channel_id=1, source_target_pairs={{256,0},{257,1},{258,2},{259,3},{260,4},{261,5},{262,6},{263,7},{2... | collective-permute-start | bytes 2359304 | tf_op jit(solution)/shard_map/ppermute | solution.py:90
  13.5 31.5 %collective-permute-start.2 = (bf16[2048,192]{0,1:T(8,128)(2,1)}, bf16[2048,192]{0,1:T(8,128)(2,1)S(1)}, u32[]{:S(2)}, u32[]{:S(2)}) collective-permute-start(bf16[2048,192]{0,1:T(8,128)(2,1)} %param.5), channel_id=1, source_target_pairs={{416,0},{417,1},{418,2},{419,3},{420,4},{421,5},{422,6},{423,7},{4... | collective-permute-start | bytes 2359304 | tf_op jit(solution)/shard_map/ppermute | solution.py:90
  45.0 7.4 %copy-start.1 = (bf16[2048,192]{0,1:T(8,128)(2,1)S(1)}, bf16[2048,192]{0,1:T(8,128)(2,1)}, u32[]{:S(2)}) copy-start(bf16[2048,192]{0,1:T(8,128)(2,1)} %param.5) | copy-start | bytes 2359300
  46.5 9.9 %collective-permute-start.3 = (bf16[4,2048,192]{1,2,0:T(8,128)(2,1)S(1)}, bf16[4,2048,192]{1,2,0:T(8,128)(2,1)S(1)}, u32[]{:S(2)}, u32[]{:S(2)}) collective-permute-start(bf16[4,2048,192]{1,2,0:T(8,128)(2,1)S(1)} %pad_maximum_fusion), channel_id=1, source_target_pairs={{64,0},{65,1},{66,2},{67,3},{68,4},{69,5},{70,6},{71,7},{72,8},{73... | collective-permute-start | bytes 9437192 | tf_op jit(solution)/shard_map/ppermute | solution.py:91
  59.1 15.3 %collective-permute-start.4 = (bf16[1,64,512]{2,1,0:T(8,128)(2,1)S(1)}, bf16[1,64,512]{2,1,0:T(8,128)(2,1)S(1)}, u32[]{:S(2)}, u32[]{:S(2)}) collective-permute-start(bf16[1,64,512]{2,1,0:T(8,128)(2,1)S(1)} %bitcast.138), channel_id=1, source_target_pairs={{0,1},{1,2},{2,3},{3,4},{4,5},{5,6},{6,7},{7,8},{8,9},{9,10},{10,1... | collective-permute-start | bytes 196616 | tf_op jit(solution)/shard_map/ppermute | solution.py:47
  63.2 83.1 %collective-permute-start.8 = (bf16[1,64,512]{2,1,0:T(8,128)(2,1)S(1)}, bf16[1,64,512]{2,1,0:T(8,128)(2,1)}, u32[]{:S(2)}, u32[]{:S(2)}) collective-permute-start(bf16[1,64,512]{2,1,0:T(8,128)(2,1)S(1)} %bitcast.139), channel_id=1, source_target_pairs={{0,16},{1,17},{2,18},{3,19},{4,20},{5,21},{6,22},{7,23},{8,24},{9,... | collective-permute-start | bytes 196616 | tf_op jit(solution)/shard_map/ppermute | solution.py:47
  71.9 101.1 %collective-permute-start.14 = (bf16[1,64,512]{2,1,0:T(8,128)(2,1)}, bf16[1,64,512]{2,1,0:T(8,128)(2,1)}, u32[]{:S(2)}, u32[]{:S(2)}) collective-permute-start(bf16[1,64,512]{2,1,0:T(8,128)(2,1)} %bitcast.36), channel_id=1, source_target_pairs={{16,0},{17,1},{18,2},{19,3},{20,4},{21,5},{22,6},{23,7},{24,8},{25... | collective-permute-start | bytes 196616 | tf_op jit(solution)/shard_map/ppermute | solution.py:47
  75.9 8.3 %collective-permute-start.9 = (bf16[1,2,64,512]{3,2,0,1:T(8,128)(2,1)S(1)}, bf16[1,2,64,512]{3,2,0,1:T(8,128)(2,1)S(1)}, u32[]{:S(2)}, u32[]{:S(2)}) collective-permute-start(bf16[1,2,64,512]{3,2,0,1:T(8,128)(2,1)S(1)} %get-tuple-element.20), channel_id=1, source_target_pairs={{1,0},{2,1},{3,2},{4,3},{5,4},{6,5},{7,6},{8,7},{9,8},{10,9},{11,1... | collective-permute-start | bytes 393224 | tf_op jit(solution)/shard_map/ppermute | solution.py:47
  81.4 12.2 %collective-permute-start.5 = (bf16[2,64,512]{2,1,0:T(8,128)(2,1)}, bf16[2,64,512]{2,1,0:T(8,128)(2,1)S(1)}, u32[]{:S(2)}, u32[]{:S(2)}) collective-permute-start(bf16[2,64,512]{2,1,0:T(8,128)(2,1)} %get-tuple-element.25), channel_id=1, source_target_pairs={{0,2},{1,3},{2,4},{3,5},{4,6},{5,7},{6,8},{7,9},{8,10},{9,11},{10,... | collective-permute-start | bytes 393224 | tf_op jit(solution)/shard_map/ppermute | solution.py:47
  84.9 25.6 %collective-permute-start.10 = (bf16[2,2,64,512]{3,2,1,0:T(8,128)(2,1)}, bf16[2,2,64,512]{3,2,1,0:T(8,128)(2,1)S(1)}, u32[]{:S(2)}, u32[]{:S(2)}) collective-permute-start(bf16[2,2,64,512]{3,2,1,0:T(8,128)(2,1)} %pad_maximum_fusion.6), channel_id=1, source_target_pairs={{2,0},{3,1},{4,2},{5,3},{6,4},{7,5},{8,6},{9,7},{10,8},{11,9},{12,... | collective-permute-start | bytes 786440 | tf_op jit(solution)/shard_map/ppermute | solution.py:47
  93.6 22.9 %collective-permute-start.6 = (bf16[4,64,512]{2,1,0:T(8,128)(2,1)S(1)}, bf16[4,64,512]{2,1,0:T(8,128)(2,1)S(1)}, u32[]{:S(2)}, u32[]{:S(2)}) collective-permute-start(bf16[4,64,512]{2,1,0:T(8,128)(2,1)S(1)} %pad_maximum_fusion.5), channel_id=1, source_target_pairs={{0,4},{1,5},{2,6},{3,7},{4,8},{5,9},{6,10},{7,11},{8,12},{9,13},{1... | collective-permute-start | bytes 786440 | tf_op jit(solution)/shard_map/ppermute | solution.py:47
  110.6 30.7 %collective-permute-start.11 = (bf16[4,2,64,512]{3,2,1,0:T(8,128)(2,1)S(1)}, bf16[4,2,64,512]{3,2,1,0:T(8,128)(2,1)S(1)}, u32[]{:S(2)}, u32[]{:S(2)}) collective-permute-start(bf16[4,2,64,512]{3,2,1,0:T(8,128)(2,1)S(1)} %pad_maximum_fusion.3), channel_id=1, source_target_pairs={{4,0},{5,1},{6,2},{7,3},{8,4},{9,5},{10,6},{11,7},{12,8},{13,9},{1... | collective-permute-start | bytes 1572872 | tf_op jit(solution)/shard_map/ppermute | solution.py:47
  116.6 28.5 %collective-permute-start.7 = (bf16[8,64,512]{2,1,0:T(8,128)(2,1)S(1)}, bf16[8,64,512]{2,1,0:T(8,128)(2,1)S(1)}, u32[]{:S(2)}, u32[]{:S(2)}) collective-permute-start(bf16[8,64,512]{2,1,0:T(8,128)(2,1)S(1)} %pad_maximum_fusion.2), channel_id=1, source_target_pairs={{0,8},{1,9},{2,10},{3,11},{4,12},{5,13},{6,14},{7,15},{8,16},{9,17... | collective-permute-start | bytes 1572872 | tf_op jit(solution)/shard_map/ppermute | solution.py:47
  141.5 31.4 %collective-permute-start.13 = (bf16[8,64,512]{2,1,0:T(8,128)(2,1)S(1)}, bf16[8,64,512]{2,1,0:T(8,128)(2,1)S(1)}, u32[]{:S(2)}, u32[]{:S(2)}) collective-permute-start(bf16[8,64,512]{2,1,0:T(8,128)(2,1)S(1)} %get-tuple-element.8), channel_id=1, source_target_pairs={{8,0},{9,1},{10,2},{11,3},{12,4},{13,5},{14,6},{15,7},{16,8},{17,9... | collective-permute-start | bytes 1572872 | tf_op jit(solution)/shard_map/ppermute | solution.py:47
  143.4 29.5 %collective-permute-start.12 = (bf16[8,64,512]{2,1,0:T(8,128)(2,1)S(1)}, bf16[8,64,512]{2,1,0:T(8,128)(2,1)S(1)}, u32[]{:S(2)}, u32[]{:S(2)}) collective-permute-start(bf16[8,64,512]{2,1,0:T(8,128)(2,1)S(1)} %get-tuple-element.7), channel_id=1, source_target_pairs={{56,48},{57,49},{58,50},{59,51},{60,52},{61,53},{62,54},{63,55},{1... | collective-permute-start | bytes 1572872 | tf_op jit(solution)/shard_map/ppermute | solution.py:47

commit v9 on v8

--- a/solution.py
+++ b/solution.py
@@ -134,26 +134,31 @@
     late_queries = lax.dynamic_slice_in_dim(query_rows, SPAN - offset, SPAN, 0)
 
     count = devices
+    radix = 4
     up = early_rows[None]
     down = jnp.stack([early_rows, late_rows])[None]
+    tail = range(count - WINDOW // 2, count)
     reach = 1
     while reach < WINDOW:
-        up = jnp.concatenate(
-            [up, moved(up, count, [(d, d + reach) for d in range(count)])], axis=0
-        )
-        if 2 * reach < WINDOW:
-            got = moved(down, count, [(d, d - reach) for d in range(count)])
-        else:
-            tail = range(count - reach, count)
-            got = jnp.stack(
-                [
-                    moved(down[:, 0], count, [(d, d - reach) for d in tail]),
-                    moved(down[:, 1], count, [(d, d - reach) for d in range(count)]),
-                ],
-                axis=1,
-            )
-        down = jnp.concatenate([down, got], axis=0)
-        reach *= 2
+        ups, downs = [up], [down]
+        for times in range(1, radix):
+            shift = reach * times
+            ups.append(moved(up, count, [(d, d + shift) for d in range(count)]))
+            if shift < WINDOW // 2:
+                downs.append(moved(down, count, [(d, d - shift) for d in range(count)]))
+            else:
+                downs.append(
+                    jnp.stack(
+                        [
+                            moved(down[:, 0], count, [(d, d - shift) for d in tail]),
+                            moved(down[:, 1], count, [(d, d - shift) for d in range(count)]),
+                        ],
+                        axis=1,
+                    )
+                )
+        up = jnp.concatenate(ups, axis=0)
+        down = jnp.concatenate(downs, axis=0)
+        reach *= radix
     up = jnp.concatenate(
         [up, moved(early_rows[None], count, [(d, d + WINDOW) for d in range(count)])], axis=0
     )

time: 188 us -> 191 us (1.016)
  the two profiles are of different devices: /device:TPU:56 before, /device:TPU:122 now
where the time goes in v9:
time: 191 us
  waiting for transfers between devices  78.3 us (41%)
  starting transfers between devices  78.1 us (41%)
  local copies, waits for them, and re-layouts  14.1 us (7%)
  other arithmetic  7.93 us (4%)
  Pallas kernels  7.8 us (4%)
  matrix products  3.08 us (2%)
    ppermute x16, waiting for transfers between devices, moved(): return lax.ppermute(value, 'ctx', pairs)  55.9 us
    ppermute x16, starting transfers between devices, moved(): return lax.ppermute(value, 'ctx', pairs)  55.6 us
    ppermute x3, waiting for transfers between devices, project(): lax.ppermute(weight, both, pairs_for(f))  20.6 us
    ppermute x3, starting transfers between devices, project(): lax.ppermute(weight, both, pairs_for(f))  16 us
    pallas_call x1, Pallas kernels, attend(): pl.pallas_call(attend_kernel, out_shape=jax.ShapeDtypeStruct(query_rows.s...  7.8 us
    ppermute x1, starting transfers between devices, project(): mate = lax.ppermute(jnp.stack(mine), both, mate_pairs())  6.54 us
    unnamed x19, local copies, waits for them, and re-layouts  6.53 us
  transfers between devices with their start and end apart: 20, of which 8 were waited for; matrix products, arithmetic and copies ran while one was open for 8% of the time, Pallas kernels for 0%

profile of v9, /device:TPU:122, one launch (start us, length us, event | category | flops | bytes accessed | tf_op | source)
XLA Modules:
  0.0 190.5 jit_solution(7189359772485775086)
XLA Ops:
  0.0 2.0 %collective-permute-start = (bf16[2048,192]{0,1:T(8,128)(2,1)}, bf16[2048,192]{0,1:T(8,128)(2,1)S(1)}, u32[]{:S(2)}, u32[]{:S(2)}) collective-permute-start(bf16[2048,192]{0,1:T(8,128)(2,1)} %param.5), channel_id=1, source_target_pairs={{128,0},{129,1},{130,2},{131,3},{132,4},{133,5},{134,6},{135,7},{1... | collective-permute-start | bytes 2359304 | tf_op jit(solution)/shard_map/ppermute | solution.py:90
  2.1 10.6 %collective-permute-start.1 = (bf16[2048,192]{0,1:T(8,128)(2,1)}, bf16[2048,192]{0,1:T(8,128)(2,1)S(1)}, u32[]{:S(2)}, u32[]{:S(2)}) collective-permute-start(bf16[2048,192]{0,1:T(8,128)(2,1)} %param.5), channel_id=1, source_target_pairs={{256,0},{257,1},{258,2},{259,3},{260,4},{261,5},{262,6},{263,7},{2... | collective-permute-start | bytes 2359304 | tf_op jit(solution)/shard_map/ppermute | solution.py:90
  12.6 3.4 %collective-permute-start.2 = (bf16[2048,192]{0,1:T(8,128)(2,1)}, bf16[2048,192]{0,1:T(8,128)(2,1)S(1)}, u32[]{:S(2)}, u32[]{:S(2)}) collective-permute-start(bf16[2048,192]{0,1:T(8,128)(2,1)} %param.5), channel_id=1, source_target_pairs={{416,0},{417,1},{418,2},{419,3},{420,4},{421,5},{422,6},{423,7},{4... | collective-permute-start | bytes 2359304 | tf_op jit(solution)/shard_map/ppermute | solution.py:90
  16.4 0.7 multiply_bitcast_fusion
  17.1 1.3 fusion.45
  19.4 0.8 copy.78
  20.5 0.7 copy.83.qdoc_ref
  22.1 12.6 %collective-permute-done.1 = bf16[2048,192]{0,1:T(8,128)(2,1)S(1)} collective-permute-done((bf16[2048,192]{0,1:T(8,128)(2,1)}, bf16[2048,192]{0,1:T(8,128)(2,1)S(1)}, u32[]{:S(2)}, u32[]{:S(2)}) %collective-permute-start.1) | collective-permute-done | bytes 786464 | tf_op jit(solution)/shard_map/ppermute | solution.py:90
  34.7 7.4 %collective-permute-done.2 = bf16[2048,192]{0,1:T(8,128)(2,1)S(1)} collective-permute-done((bf16[2048,192]{0,1:T(8,128)(2,1)}, bf16[2048,192]{0,1:T(8,128)(2,1)S(1)}, u32[]{:S(2)}, u32[]{:S(2)}) %collective-permute-start.2) | collective-permute-done | bytes 786464 | tf_op jit(solution)/shard_map/ppermute | solution.py:90
  42.1 1.5 pad_maximum_fusion
  43.6 6.5 %collective-permute-start.3 = (bf16[4,2048,192]{1,2,0:T(8,128)(2,1)S(1)}, bf16[4,2048,192]{1,2,0:T(8,128)(2,1)S(1)}, u32[]{:S(2)}, u32[]{:S(2)}) collective-permute-start(bf16[4,2048,192]{1,2,0:T(8,128)(2,1)S(1)} %pad_maximum_fusion), channel_id=1, source_target_pairs={{64,0},{65,1},{66,2},{67,3},{68,4},{69,5},{70,6},{71,7},{72,8},{73... | collective-permute-start | bytes 9437192 | tf_op jit(solution)/shard_map/ppermute | solution.py:91
  50.8 0.7 iota_add_fusion.qpos_ref
  51.8 0.6 reshape_select_fusion
  53.6 1.8 collective-permute-done.3
  57.0 0.6 gather_fusion
  58.1 0.6 constant_dynamic-update-slice_fusion.20
  58.8 3.4 %collective-permute-start.4 = (bf16[1,64,512]{2,1,0:T(8,128)(2,1)S(1)}, bf16[1,64,512]{2,1,0:T(8,128)(2,1)S(1)}, u32[]{:S(2)}, u32[]{:S(2)}) collective-permute-start(bf16[1,64,512]{2,1,0:T(8,128)(2,1)S(1)} %bitcast.140), channel_id=1, source_target_pairs={{0,1},{1,2},{2,3},{3,4},{4,5},{5,6},{6,7},{7,8},{8,9},{9,10},{10,1... | collective-permute-start | bytes 196616 | tf_op jit(solution)/shard_map/ppermute | solution.py:47
  62.2 4.3 %collective-permute-start.5 = (bf16[1,64,512]{2,1,0:T(8,128)(2,1)S(1)}, bf16[1,64,512]{2,1,0:T(8,128)(2,1)S(1)}, u32[]{:S(2)}, u32[]{:S(2)}) collective-permute-start(bf16[1,64,512]{2,1,0:T(8,128)(2,1)S(1)} %bitcast.141), channel_id=1, source_target_pairs={{0,2},{1,3},{2,4},{3,5},{4,6},{5,7},{6,8},{7,9},{8,10},{9,11},{10,... | collective-permute-start | bytes 196616 | tf_op jit(solution)/shard_map/ppermute | solution.py:47
  66.5 4.1 %collective-permute-start.6 = (bf16[1,64,512]{2,1,0:T(8,128)(2,1)S(1)}, bf16[1,64,512]{2,1,0:T(8,128)(2,1)S(1)}, u32[]{:S(2)}, u32[]{:S(2)}) collective-permute-start(bf16[1,64,512]{2,1,0:T(8,128)(2,1)S(1)} %bitcast.142), channel_id=1, source_target_pairs={{0,3},{1,4},{2,5},{3,6},{4,7},{5,8},{6,9},{7,10},{8,11},{9,12},{10... | collective-permute-start | bytes 196616 | tf_op jit(solution)/shard_map/ppermute | solution.py:47
  70.5 7.7 %collective-permute-start.10 = (bf16[1,64,512]{2,1,0:T(8,128)(2,1)S(1)}, bf16[1,64,512]{2,1,0:T(8,128)(2,1)S(1)}, u32[]{:S(2)}, u32[]{:S(2)}) collective-permute-start(bf16[1,64,512]{2,1,0:T(8,128)(2,1)S(1)} %bitcast.143), channel_id=1, source_target_pairs={{0,16},{1,17},{2,18},{3,19},{4,20},{5,21},{6,22},{7,23},{8,24},{9,... | collective-permute-start | bytes 196616 | tf_op jit(solution)/shard_map/ppermute | solution.py:47
  78.4 0.9 copy.82.q_ref
  79.4 3.3 %collective-permute-start.11 = (bf16[1,2,64,512]{3,2,0,1:T(8,128)(2,1)S(1)}, bf16[1,2,64,512]{3,2,0,1:T(8,128)(2,1)S(1)}, u32[]{:S(2)}, u32[]{:S(2)}) collective-permute-start(bf16[1,2,64,512]{3,2,0,1:T(8,128)(2,1)S(1)} %get-tuple-element.20), channel_id=1, source_target_pairs={{1,0},{2,1},{3,2},{4,3},{5,4},{6,5},{7,6},{8,7},{9,8},{10,9},{11,1... | collective-permute-start | bytes 393224 | tf_op jit(solution)/shard_map/ppermute | solution.py:47
  82.8 2.7 %collective-permute-start.12 = (bf16[1,2,64,512]{3,2,0,1:T(8,128)(2,1)S(1)}, bf16[1,2,64,512]{3,2,0,1:T(8,128)(2,1)S(1)}, u32[]{:S(2)}, u32[]{:S(2)}) collective-permute-start(bf16[1,2,64,512]{3,2,0,1:T(8,128)(2,1)S(1)} %get-tuple-element.20), channel_id=1, source_target_pairs={{2,0},{3,1},{4,2},{5,3},{6,4},{7,5},{8,6},{9,7},{10,8},{11,9},{12,... | collective-permute-start | bytes 393224 | tf_op jit(solution)/shard_map/ppermute | solution.py:47
  85.5 2.1 %collective-permute-start.13 = (bf16[1,2,64,512]{3,2,0,1:T(8,128)(2,1)S(1)}, bf16[1,2,64,512]{3,2,0,1:T(8,128)(2,1)S(1)}, u32[]{:S(2)}, u32[]{:S(2)}) collective-permute-start(bf16[1,2,64,512]{3,2,0,1:T(8,128)(2,1)S(1)} %get-tuple-element.20), channel_id=1, source_target_pairs={{3,0},{4,1},{5,2},{6,3},{7,4},{8,5},{9,6},{10,7},{11,8},{12,9},{13... | collective-permute-start | bytes 393224 | tf_op jit(solution)/shard_map/ppermute | solution.py:47
  87.7 10.7 %collective-permute-start.7 = (bf16[4,64,512]{2,1,0:T(8,128)(2,1)S(1)}, bf16[4,64,512]{2,1,0:T(8,128)(2,1)S(1)}, u32[]{:S(2)}, u32[]{:S(2)}) collective-permute-start(bf16[4,64,512]{2,1,0:T(8,128)(2,1)S(1)} %pad_maximum_fusion.3), channel_id=1, source_target_pairs={{0,4},{1,5},{2,6},{3,7},{4,8},{5,9},{6,10},{7,11},{8,12},{9,13},{1... | collective-permute-start | bytes 786440 | tf_op jit(solution)/shard_map/ppermute | solution.py:47
  98.4 0.6 constant_dynamic-update-slice_fusion.19
  99.0 0.6 constant_dynamic-update-slice_fusion.18
  99.6 0.6 constant_dynamic-update-slice_fusion.17
  100.3 2.0 %collective-permute-start.8 = (bf16[4,64,512]{2,1,0:T(8,128)(2,1)S(1)}, bf16[4,64,512]{2,1,0:T(8,128)(2,1)S(1)}, u32[]{:S(2)}, u32[]{:S(2)}) collective-permute-start(bf16[4,64,512]{2,1,0:T(8,128)(2,1)S(1)} %pad_maximum_fusion.3), channel_id=1, source_target_pairs={{0,8},{1,9},{2,10},{3,11},{4,12},{5,13},{6,14},{7,15},{8,16},{9,17... | collective-permute-start | bytes 786440 | tf_op jit(solution)/shard_map/ppermute | solution.py:47
  102.3 1.9 %collective-permute-start.9 = (bf16[4,64,512]{2,1,0:T(8,128)(2,1)S(1)}, bf16[4,64,512]{2,1,0:T(8,128)(2,1)S(1)}, u32[]{:S(2)}, u32[]{:S(2)}) collective-permute-start(bf16[4,64,512]{2,1,0:T(8,128)(2,1)S(1)} %pad_maximum_fusion.3), channel_id=1, source_target_pairs={{0,12},{1,13},{2,14},{3,15},{4,16},{5,17},{6,18},{7,19},{8,20},{9,... | collective-permute-start | bytes 786440 | tf_op jit(solution)/shard_map/ppermute | solution.py:47
  104.6 3.7 %collective-permute-start.14 = (bf16[4,2,64,512]{3,2,0,1:T(8,128)(2,1)S(1)}, bf16[4,2,64,512]{3,2,0,1:T(8,128)(2,1)S(1)}, u32[]{:S(2)}, u32[]{:S(2)}) collective-permute-start(bf16[4,2,64,512]{3,2,0,1:T(8,128)(2,1)S(1)} %copy.75), channel_id=1, source_target_pairs={{4,0},{5,1},{6,2},{7,3},{8,4},{9,5},{10,6},{11,7},{12,8},{13,9},{1... | collective-permute-start | bytes 1572872 | tf_op jit(solution)/shard_map/ppermute | solution.py:47
  108.4 4.3 %collective-permute-start.16 = (bf16[4,64,512]{2,1,0:T(8,128)(2,1)S(1)}, bf16[4,64,512]{2,1,0:T(8,128)(2,1)S(1)}, u32[]{:S(2)}, u32[]{:S(2)}) collective-permute-start(bf16[4,64,512]{2,1,0:T(8,128)(2,1)S(1)} %slice_bitcast_fusion.10), channel_id=1, source_target_pairs={{8,0},{9,1},{10,2},{11,3},{12,4},{13,5},{14,6},{15,7},{16,8},{17,9... | collective-permute-start | bytes 786440 | tf_op jit(solution)/shard_map/ppermute | solution.py:47
  112.7 0.7 constant_dynamic-update-slice_fusion.16
  113.4 9.7 %collective-permute-done.8 = bf16[4,64,512]{2,1,0:T(8,128)(2,1)S(1)} collective-permute-done((bf16[4,64,512]{2,1,0:T(8,128)(2,1)S(1)}, bf16[4,64,512]{2,1,0:T(8,128)(2,1)S(1)}, u32[]{:S(2)}, u32[]{:S(2)}) %collective-permute-start.8) | collective-permute-done | bytes 262176 | tf_op jit(solution)/shard_map/ppermute | solution.py:47
  123.1 1.9 %collective-permute-start.18 = (bf16[4,64,512]{2,1,0:T(8,128)(2,1)S(1)}, bf16[4,64,512]{2,1,0:T(8,128)(2,1)S(1)}, u32[]{:S(2)}, u32[]{:S(2)}) collective-permute-start(bf16[4,64,512]{2,1,0:T(8,128)(2,1)S(1)} %slice_bitcast_fusion.10), channel_id=1, source_target_pairs={{12,0},{13,1},{14,2},{15,3},{16,4},{17,5},{18,6},{19,7},{20,8},{21... | collective-permute-start | bytes 786440 | tf_op jit(solution)/shard_map/ppermute | solution.py:47
  125.1 0.7 constant_dynamic-update-slice_fusion.15
  125.8 0.7 collective-permute-start.15
  126.5 0.8 constant_dynamic-update-slice_fusion.14
  127.2 0.7 collective-permute-start.17
  127.9 0.6 constant_dynamic-update-slice_fusion.13
  128.5 33.4 %collective-permute-done.14 = bf16[4,2,64,512]{3,2,0,1:T(8,128)(2,1)S(1)} collective-permute-done((bf16[4,2,64,512]{3,2,0,1:T(8,128)(2,1)S(1)}, bf16[4,2,64,512]{3,2,0,1:T(8,128)(2,1)S(1)}, u32[]{:S(2)}, u32[]{:S(2)}) %collective-permute-start.14) | collective-permute-done | bytes 524320 | tf_op jit(solution)/shard_map/ppermute | solution.py:47
  161.9 2.1 %collective-permute-start.19 = (bf16[1,64,512]{2,1,0:T(8,128)(2,1)S(1)}, bf16[1,64,512]{2,1,0:T(8,128)(2,1)S(1)}, u32[]{:S(2)}, u32[]{:S(2)}) collective-permute-start(bf16[1,64,512]{2,1,0:T(8,128)(2,1)S(1)} %bitcast.160), channel_id=1, source_target_pairs={{16,0},{17,1},{18,2},{19,3},{20,4},{21,5},{22,6},{23,7},{24,8},{25... | collective-permute-start | bytes 196616 | tf_op jit(solution)/shard_map/ppermute | solution.py:47
  164.2 12.6 %collective-permute-done.19 = bf16[1,64,512]{2,1,0:T(8,128)(2,1)S(1)} collective-permute-done((bf16[1,64,512]{2,1,0:T(8,128)(2,1)S(1)}, bf16[1,64,512]{2,1,0:T(8,128)(2,1)S(1)}, u32[]{:S(2)}, u32[]{:S(2)}) %collective-permute-start.19) | collective-permute-done | bytes 65568 | tf_op jit(solution)/shard_map/ppermute | solution.py:47
  176.8 1.1 fusion.17
  177.8 1.1 fusion.16
  178.9 2.6 %gather_fusion.1 = bf16[17,64,512]{2,1,0:T(8,128)(2,1)S(1)} fusion(bf16[51,64,512]{2,1,0:T(8,128)(2,1)} %fusion.16, s32[1024]{0:T(1024)S(1)} %pad_clamp_fusion), kind=kCustom, calls=%fused_computation.1 | custom fusion | bytes 2228292 | tf_op jit(solution)/shard_map/jit(_take)/gather | solution.py:177
  181.5 1.2 bitcast_select_fusion.late_ref
  182.7 7.8 %shard_map.46 = bf16[128,1024]{1,0:T(8,128)(2,1)} custom-call(s32[1]{0:T(128)} %bitcast.offset_ref, bf16[128,1024]{1,0:T(8,128)(2,1)} %copy.82.q_ref, bf16[1088,512]{1,0:T(8,128)(2,1)} %bitcast.149, bf16[1088,512]{1,0:T(8,128)(2,1)} %bitcast_select_fusion.late_ref, s32[2,64,1]{2,1,0:T(8,128)} %iota_add_fusion.qpos_ref, s32[2,64,1]{2,1,0:T(8,128)} %copy.83.qdoc_ref, ...), custom_call_target="tpu_custom_call" | custom-call | tf_op jit(solution)/shard_map/pallas_call | solution.py:241
  (83 shorter events, 6.9 us)
Async XLA Ops:
  0.0 51.5 %copy-start = (bf16[1,128,2048]{2,1,0:T(8,128)(2,1)S(1)}, bf16[1,128,2048]{2,1,0:T(8,128)(2,1)}, u32[]{:S(2)}) copy-start(bf16[1,128,2048]{2,1,0:T(8,128)(2,1)} %param.4) | copy-start | bytes 1572868
  0.0 22.1 %collective-permute-start = (bf16[2048,192]{0,1:T(8,128)(2,1)}, bf16[2048,192]{0,1:T(8,128)(2,1)S(1)}, u32[]{:S(2)}, u32[]{:S(2)}) collective-permute-start(bf16[2048,192]{0,1:T(8,128)(2,1)} %param.5), channel_id=1, source_target_pairs={{128,0},{129,1},{130,2},{131,3},{132,4},{133,5},{134,6},{135,7},{1... | collective-permute-start | bytes 2359304 | tf_op jit(solution)/shard_map/ppermute | solution.py:90
  2.1 32.7 %collective-permute-start.1 = (bf16[2048,192]{0,1:T(8,128)(2,1)}, bf16[2048,192]{0,1:T(8,128)(2,1)S(1)}, u32[]{:S(2)}, u32[]{:S(2)}) collective-permute-start(bf16[2048,192]{0,1:T(8,128)(2,1)} %param.5), channel_id=1, source_target_pairs={{256,0},{257,1},{258,2},{259,3},{260,4},{261,5},{262,6},{263,7},{2... | collective-permute-start | bytes 2359304 | tf_op jit(solution)/shard_map/ppermute | solution.py:90
  12.6 29.5 %collective-permute-start.2 = (bf16[2048,192]{0,1:T(8,128)(2,1)}, bf16[2048,192]{0,1:T(8,128)(2,1)S(1)}, u32[]{:S(2)}, u32[]{:S(2)}) collective-permute-start(bf16[2048,192]{0,1:T(8,128)(2,1)} %param.5), channel_id=1, source_target_pairs={{416,0},{417,1},{418,2},{419,3},{420,4},{421,5},{422,6},{423,7},{4... | collective-permute-start | bytes 2359304 | tf_op jit(solution)/shard_map/ppermute | solution.py:90
  42.1 9.3 %copy-start.1 = (bf16[2048,192]{0,1:T(8,128)(2,1)S(1)}, bf16[2048,192]{0,1:T(8,128)(2,1)}, u32[]{:S(2)}) copy-start(bf16[2048,192]{0,1:T(8,128)(2,1)} %param.5) | copy-start | bytes 2359300
  43.6 11.8 %collective-permute-start.3 = (bf16[4,2048,192]{1,2,0:T(8,128)(2,1)S(1)}, bf16[4,2048,192]{1,2,0:T(8,128)(2,1)S(1)}, u32[]{:S(2)}, u32[]{:S(2)}) collective-permute-start(bf16[4,2048,192]{1,2,0:T(8,128)(2,1)S(1)} %pad_maximum_fusion), channel_id=1, source_target_pairs={{64,0},{65,1},{66,2},{67,3},{68,4},{69,5},{70,6},{71,7},{72,8},{73... | collective-permute-start | bytes 9437192 | tf_op jit(solution)/shard_map/ppermute | solution.py:91
  58.8 24.0 %collective-permute-start.4 = (bf16[1,64,512]{2,1,0:T(8,128)(2,1)S(1)}, bf16[1,64,512]{2,1,0:T(8,128)(2,1)S(1)}, u32[]{:S(2)}, u32[]{:S(2)}) collective-permute-start(bf16[1,64,512]{2,1,0:T(8,128)(2,1)S(1)} %bitcast.140), channel_id=1, source_target_pairs={{0,1},{1,2},{2,3},{3,4},{4,5},{5,6},{6,7},{7,8},{8,9},{9,10},{10,1... | collective-permute-start | bytes 196616 | tf_op jit(solution)/shard_map/ppermute | solution.py:47
  62.2 23.4 %collective-permute-start.5 = (bf16[1,64,512]{2,1,0:T(8,128)(2,1)S(1)}, bf16[1,64,512]{2,1,0:T(8,128)(2,1)S(1)}, u32[]{:S(2)}, u32[]{:S(2)}) collective-permute-start(bf16[1,64,512]{2,1,0:T(8,128)(2,1)S(1)} %bitcast.141), channel_id=1, source_target_pairs={{0,2},{1,3},{2,4},{3,5},{4,6},{5,7},{6,8},{7,9},{8,10},{9,11},{10,... | collective-permute-start | bytes 196616 | tf_op jit(solution)/shard_map/ppermute | solution.py:47
  66.5 21.1 %collective-permute-start.6 = (bf16[1,64,512]{2,1,0:T(8,128)(2,1)S(1)}, bf16[1,64,512]{2,1,0:T(8,128)(2,1)S(1)}, u32[]{:S(2)}, u32[]{:S(2)}) collective-permute-start(bf16[1,64,512]{2,1,0:T(8,128)(2,1)S(1)} %bitcast.142), channel_id=1, source_target_pairs={{0,3},{1,4},{2,5},{3,6},{4,7},{5,8},{6,9},{7,10},{8,11},{9,12},{10... | collective-permute-start | bytes 196616 | tf_op jit(solution)/shard_map/ppermute | solution.py:47
  70.5 56.7 %collective-permute-start.10 = (bf16[1,64,512]{2,1,0:T(8,128)(2,1)S(1)}, bf16[1,64,512]{2,1,0:T(8,128)(2,1)S(1)}, u32[]{:S(2)}, u32[]{:S(2)}) collective-permute-start(bf16[1,64,512]{2,1,0:T(8,128)(2,1)S(1)} %bitcast.143), channel_id=1, source_target_pairs={{0,16},{1,17},{2,18},{3,19},{4,20},{5,21},{6,22},{7,23},{8,24},{9,... | collective-permute-start | bytes 196616 | tf_op jit(solution)/shard_map/ppermute | solution.py:47
  79.4 20.9 %collective-permute-start.11 = (bf16[1,2,64,512]{3,2,0,1:T(8,128)(2,1)S(1)}, bf16[1,2,64,512]{3,2,0,1:T(8,128)(2,1)S(1)}, u32[]{:S(2)}, u32[]{:S(2)}) collective-permute-start(bf16[1,2,64,512]{3,2,0,1:T(8,128)(2,1)S(1)} %get-tuple-element.20), channel_id=1, source_target_pairs={{1,0},{2,1},{3,2},{4,3},{5,4},{6,5},{7,6},{8,7},{9,8},{10,9},{11,1... | collective-permute-start | bytes 393224 | tf_op jit(solution)/shard_map/ppermute | solution.py:47
  82.8 19.5 %collective-permute-start.12 = (bf16[1,2,64,512]{3,2,0,1:T(8,128)(2,1)S(1)}, bf16[1,2,64,512]{3,2,0,1:T(8,128)(2,1)S(1)}, u32[]{:S(2)}, u32[]{:S(2)}) collective-permute-start(bf16[1,2,64,512]{3,2,0,1:T(8,128)(2,1)S(1)} %get-tuple-element.20), channel_id=1, source_target_pairs={{2,0},{3,1},{4,2},{5,3},{6,4},{7,5},{8,6},{9,7},{10,8},{11,9},{12,... | collective-permute-start | bytes 393224 | tf_op jit(solution)/shard_map/ppermute | solution.py:47
  85.5 18.9 %collective-permute-start.13 = (bf16[1,2,64,512]{3,2,0,1:T(8,128)(2,1)S(1)}, bf16[1,2,64,512]{3,2,0,1:T(8,128)(2,1)S(1)}, u32[]{:S(2)}, u32[]{:S(2)}) collective-permute-start(bf16[1,2,64,512]{3,2,0,1:T(8,128)(2,1)S(1)} %get-tuple-element.20), channel_id=1, source_target_pairs={{3,0},{4,1},{5,2},{6,3},{7,4},{8,5},{9,6},{10,7},{11,8},{12,9},{13... | collective-permute-start | bytes 393224 | tf_op jit(solution)/shard_map/ppermute | solution.py:47
  87.7 20.8 %collective-permute-start.7 = (bf16[4,64,512]{2,1,0:T(8,128)(2,1)S(1)}, bf16[4,64,512]{2,1,0:T(8,128)(2,1)S(1)}, u32[]{:S(2)}, u32[]{:S(2)}) collective-permute-start(bf16[4,64,512]{2,1,0:T(8,128)(2,1)S(1)} %pad_maximum_fusion.3), channel_id=1, source_target_pairs={{0,4},{1,5},{2,6},{3,7},{4,8},{5,9},{6,10},{7,11},{8,12},{9,13},{1... | collective-permute-start | bytes 786440 | tf_op jit(solution)/shard_map/ppermute | solution.py:47
  100.3 22.9 %collective-permute-start.8 = (bf16[4,64,512]{2,1,0:T(8,128)(2,1)S(1)}, bf16[4,64,512]{2,1,0:T(8,128)(2,1)S(1)}, u32[]{:S(2)}, u32[]{:S(2)}) collective-permute-start(bf16[4,64,512]{2,1,0:T(8,128)(2,1)S(1)} %pad_maximum_fusion.3), channel_id=1, source_target_pairs={{0,8},{1,9},{2,10},{3,11},{4,12},{5,13},{6,14},{7,15},{8,16},{9,17... | collective-permute-start | bytes 786440 | tf_op jit(solution)/shard_map/ppermute | solution.py:47
  102.3 23.5 %collective-permute-start.9 = (bf16[4,64,512]{2,1,0:T(8,128)(2,1)S(1)}, bf16[4,64,512]{2,1,0:T(8,128)(2,1)S(1)}, u32[]{:S(2)}, u32[]{:S(2)}) collective-permute-start(bf16[4,64,512]{2,1,0:T(8,128)(2,1)S(1)} %pad_maximum_fusion.3), channel_id=1, source_target_pairs={{0,12},{1,13},{2,14},{3,15},{4,16},{5,17},{6,18},{7,19},{8,20},{9,... | collective-permute-start | bytes 786440 | tf_op jit(solution)/shard_map/ppermute | solution.py:47
  104.6 57.3 %collective-permute-start.14 = (bf16[4,2,64,512]{3,2,0,1:T(8,128)(2,1)S(1)}, bf16[4,2,64,512]{3,2,0,1:T(8,128)(2,1)S(1)}, u32[]{:S(2)}, u32[]{:S(2)}) collective-permute-start(bf16[4,2,64,512]{3,2,0,1:T(8,128)(2,1)S(1)} %copy.75), channel_id=1, source_target_pairs={{4,0},{5,1},{6,2},{7,3},{8,4},{9,5},{10,6},{11,7},{12,8},{13,9},{1... | collective-permute-start | bytes 1572872 | tf_op jit(solution)/shard_map/ppermute | solution.py:47
  108.4 55.6 %collective-permute-start.16 = (bf16[4,64,512]{2,1,0:T(8,128)(2,1)S(1)}, bf16[4,64,512]{2,1,0:T(8,128)(2,1)S(1)}, u32[]{:S(2)}, u32[]{:S(2)}) collective-permute-start(bf16[4,64,512]{2,1,0:T(8,128)(2,1)S(1)} %slice_bitcast_fusion.10), channel_id=1, source_target_pairs={{8,0},{9,1},{10,2},{11,3},{12,4},{13,5},{14,6},{15,7},{16,8},{17,9... | collective-permute-start | bytes 786440 | tf_op jit(solution)/shard_map/ppermute | solution.py:47
  123.1 41.0 %collective-permute-start.18 = (bf16[4,64,512]{2,1,0:T(8,128)(2,1)S(1)}, bf16[4,64,512]{2,1,0:T(8,128)(2,1)S(1)}, u32[]{:S(2)}, u32[]{:S(2)}) collective-permute-start(bf16[4,64,512]{2,1,0:T(8,128)(2,1)S(1)} %slice_bitcast_fusion.10), channel_id=1, source_target_pairs={{12,0},{13,1},{14,2},{15,3},{16,4},{17,5},{18,6},{19,7},{20,8},{21... | collective-permute-start | bytes 786440 | tf_op jit(solution)/shard_map/ppermute | solution.py:47
  125.8 38.3 %collective-permute-start.15 = (bf16[4,64,512]{2,1,0:T(8,128)(2,1)S(1)}, bf16[4,64,512]{2,1,0:T(8,128)(2,1)S(1)}, u32[]{:S(2)}, u32[]{:S(2)}) collective-permute-start(bf16[4,64,512]{2,1,0:T(8,128)(2,1)S(1)} %slice_bitcast_fusion.11), channel_id=1, source_target_pairs={{56,48},{57,49},{58,50},{59,51},{60,52},{61,53},{62,54},{63,55},{1... | collective-permute-start | bytes 786440 | tf_op jit(solution)/shard_map/ppermute | solution.py:47
  127.2 36.9 %collective-permute-start.17 = (bf16[4,64,512]{2,1,0:T(8,128)(2,1)S(1)}, bf16[4,64,512]{2,1,0:T(8,128)(2,1)S(1)}, u32[]{:S(2)}, u32[]{:S(2)}) collective-permute-start(bf16[4,64,512]{2,1,0:T(8,128)(2,1)S(1)} %slice_bitcast_fusion.11), channel_id=1, source_target_pairs={{56,44},{57,45},{58,46},{59,47},{60,48},{61,49},{62,50},{63,51},{1... | collective-permute-start | bytes 786440 | tf_op jit(solution)/shard_map/ppermute | solution.py:47
  128.5 49.3 %copy-start.2 = (bf16[17,64,512]{2,1,0:T(8,128)(2,1)}, bf16[17,64,512]{2,1,0:T(8,128)(2,1)S(1)}, u32[]{:S(2)}) copy-start(bf16[17,64,512]{2,1,0:T(8,128)(2,1)S(1)} %get-tuple-element.24) | copy-start | bytes 3342340
  161.9 14.9 %collective-permute-start.19 = (bf16[1,64,512]{2,1,0:T(8,128)(2,1)S(1)}, bf16[1,64,512]{2,1,0:T(8,128)(2,1)S(1)}, u32[]{:S(2)}, u32[]{:S(2)}) collective-permute-start(bf16[1,64,512]{2,1,0:T(8,128)(2,1)S(1)} %bitcast.160), channel_id=1, source_target_pairs={{16,0},{17,1},{18,2},{19,3},{20,4},{21,5},{22,6},{23,7},{24,8},{25... | collective-permute-start | bytes 196616 | tf_op jit(solution)/shard_map/ppermute | solution.py:47

commit v10 on v8

--- a/solution.py
+++ b/solution.py
@@ -87,13 +87,12 @@
             step.append(lambda core, s=shift: s)
         else:
             step.append(lambda core, s=shift: s - lines)
-    mine = [weight] + [lax.ppermute(weight, both, pairs_for(f)) for f in step[1:]]
-    mate = lax.ppermute(jnp.stack(mine), both, mate_pairs())
-    parts = [jnp.dot(rows, block, preferred_element_type=jnp.float32) for block in mine]
-    parts += [
-        jnp.dot(rows, mate[index], preferred_element_type=jnp.float32) for index in range(len(mine))
-    ]
-    parts = jnp.stack(parts).astype(jnp.bfloat16)
+    partner = lax.ppermute(rows, both, mate_pairs())
+    mine = jnp.stack([weight] + [lax.ppermute(weight, both, pairs_for(f)) for f in step[1:]])
+    own = jnp.einsum("td,bdn->btn", rows, mine, preferred_element_type=jnp.float32)
+    theirs = jnp.einsum("td,bdn->btn", partner, mine, preferred_element_type=jnp.float32)
+    mate = lax.ppermute(theirs.astype(jnp.bfloat16), both, mate_pairs())
+    parts = jnp.concatenate([own.astype(jnp.bfloat16), mate], axis=0)
     seq_index = lax.axis_index("seq")
     line, core = seq_index // 2, seq_index % 2
     wanted = jnp.arange(2 * lines, dtype=jnp.int32)

time: 188 us -> 181 us (0.963); the launches traced: 188 us -> 179 us
  other arithmetic: 11.8 us -> 7.26 us
  local copies, waits for them, and re-layouts: 16.8 us -> 14.3 us
  waiting for transfers between devices: 75 us -> 72.6 us
    ppermute x1 -> x2, starting transfers between devices: 4.6 us -> 3.84 us  [the longest x1 1.92 us: project(): partner = lax.ppermute(rows, both, mate_pairs())]
  transfers between devices with their start and end apart: 15 -> 16, of which waited for: 6 -> 7; matrix products, arithmetic and copies ran while one was open for 11% -> 9% of each run, Pallas kernels for 0% -> 0%
where the time goes in v10:
time: 181 us; the launch traced here: 179 us
  waiting for transfers between devices  72.6 us (40%)
  starting transfers between devices  72.2 us (40%)
  local copies, waits for them, and re-layouts  14.3 us (8%)
  Pallas kernels  7.81 us (4%)
  other arithmetic  7.26 us (4%)
  matrix products  3.42 us (2%)
    ppermute x11, starting transfers between devices, moved(): return lax.ppermute(value, 'ctx', pairs)  51.6 us
    ppermute x11, waiting for transfers between devices, moved(): return lax.ppermute(value, 'ctx', pairs)  49.8 us
    ppermute x3, waiting for transfers between devices, project(): lax.ppermute(weight, both, pairs_for(f))  22.6 us
    ppermute x3, starting transfers between devices, project(): lax.ppermute(weight, both, pairs_for(f))  16.8 us
    pallas_call x1, Pallas kernels, attend(): pl.pallas_call(attend_kernel, out_shape=jax.ShapeDtypeStruct(query_rows.s...  7.81 us
    unnamed x14, local copies, waits for them, and re-layouts  6.66 us
  transfers between devices with their start and end apart: 16, of which 7 were waited for; matrix products, arithmetic and copies ran while one was open for 9% of the time, Pallas kernels for 0%

profile of v10, /device:TPU:56, one launch (start us, length us, event | category | flops | bytes accessed | tf_op | source)
XLA Modules:
  0.0 178.8 jit_solution(4580175554688626959)
XLA Ops:
  0.0 4.3 %collective-permute-start.2 = (bf16[2048,192]{0,1:T(8,128)(2,1)}, bf16[2048,192]{0,1:T(8,128)(2,1)S(1)}, u32[]{:S(2)}, u32[]{:S(2)}) collective-permute-start(bf16[2048,192]{0,1:T(8,128)(2,1)} %param.5), channel_id=1, source_target_pairs={{416,0},{417,1},{418,2},{419,3},{420,4},{421,5},{422,6},{423,7},{4... | collective-permute-start | bytes 2359304 | tf_op jit(solution)/shard_map/ppermute | solution.py:91
  4.3 10.0 %collective-permute-start.1 = (bf16[2048,192]{0,1:T(8,128)(2,1)}, bf16[2048,192]{0,1:T(8,128)(2,1)S(1)}, u32[]{:S(2)}, u32[]{:S(2)}) collective-permute-start(bf16[2048,192]{0,1:T(8,128)(2,1)} %param.5), channel_id=1, source_target_pairs={{256,0},{257,1},{258,2},{259,3},{260,4},{261,5},{262,6},{263,7},{2... | collective-permute-start | bytes 2359304 | tf_op jit(solution)/shard_map/ppermute | solution.py:91
  14.3 2.5 %collective-permute-start = (bf16[2048,192]{0,1:T(8,128)(2,1)}, bf16[2048,192]{0,1:T(8,128)(2,1)S(1)}, u32[]{:S(2)}, u32[]{:S(2)}) collective-permute-start(bf16[2048,192]{0,1:T(8,128)(2,1)} %param.5), channel_id=1, source_target_pairs={{128,0},{129,1},{130,2},{131,3},{132,4},{133,5},{134,6},{135,7},{1... | collective-permute-start | bytes 2359304 | tf_op jit(solution)/shard_map/ppermute | solution.py:91
  16.8 1.9 %collective-permute-start.3 = (bf16[128,2048]{1,0:T(8,128)(2,1)}, bf16[128,2048]{1,0:T(8,128)(2,1)S(1)}, u32[]{:S(2)}, u32[]{:S(2)}) collective-permute-start(bf16[128,2048]{1,0:T(8,128)(2,1)} %bitcast.104), channel_id=1, source_target_pairs={{64,0},{65,1},{66,2},{67,3},{68,4},{69,5},{70,6},{71,7},{72,8},{73... | collective-permute-start | bytes 1572872 | tf_op jit(solution)/shard_map/ppermute | solution.py:90
  18.9 0.7 iota_add_fusion.qpos_ref
  20.0 0.7 multiply_bitcast_fusion
  20.7 1.2 fusion.27
  22.9 0.8 copy.73
  24.0 0.7 copy.78.qdoc_ref
  25.0 0.3 fusion.6
  25.3 0.1 multiply_cosine_fusion
  25.5 0.6 reshape_select_fusion
  26.1 3.9 %collective-permute-done.2 = bf16[2048,192]{0,1:T(8,128)(2,1)S(1)} collective-permute-done((bf16[2048,192]{0,1:T(8,128)(2,1)}, bf16[2048,192]{0,1:T(8,128)(2,1)S(1)}, u32[]{:S(2)}, u32[]{:S(2)}) %collective-permute-start.2) | collective-permute-done | bytes 786464 | tf_op jit(solution)/shard_map/ppermute | solution.py:91
  30.0 10.3 %collective-permute-done.1 = bf16[2048,192]{0,1:T(8,128)(2,1)S(1)} collective-permute-done((bf16[2048,192]{0,1:T(8,128)(2,1)}, bf16[2048,192]{0,1:T(8,128)(2,1)S(1)}, u32[]{:S(2)}, u32[]{:S(2)}) %collective-permute-start.1) | collective-permute-done | bytes 786464 | tf_op jit(solution)/shard_map/ppermute | solution.py:91
  40.3 8.4 %collective-permute-done = bf16[2048,192]{0,1:T(8,128)(2,1)S(1)} collective-permute-done((bf16[2048,192]{0,1:T(8,128)(2,1)}, bf16[2048,192]{0,1:T(8,128)(2,1)S(1)}, u32[]{:S(2)}, u32[]{:S(2)}) %collective-permute-start) | collective-permute-done | bytes 786464 | tf_op jit(solution)/shard_map/ppermute | solution.py:91
  48.8 2.2 %fusion.1 = bf16[4,128,192]{1,2,0:T(8,128)(2,1)S(1)} fusion(bf16[1,2048,192]{1,2,0:T(8,128)(2,1)S(1)} %bitcast.98, bf16[1,2048,192]{1,2,0:T(8,128)(2,1)S(1)} %bitcast.100, bf16[1,2048,192]{1,2,0:T(8,128)(2,1)S(1)} %bitcast.102, bf16[1,2048,192]{1,2,0:T(8,128)(2,1)} %bitcast.96, bf16[128,2048]{1,0:T(8,128)(2,1)S(1)} %collective-permute-done.3), kind=kOutput, calls=%fused_computation.6 | convolution fusion | flops 407470080 | bytes 3866624 | tf_op jit(solution)/shard_map/td,bdn->btn/dot_general | solution.py:93
  51.0 1.9 %collective-permute-start.4 = (bf16[4,128,192]{1,2,0:T(8,128)(2,1)S(1)}, bf16[4,128,192]{1,2,0:T(8,128)(2,1)S(1)}, u32[]{:S(2)}, u32[]{:S(2)}) collective-permute-start(bf16[4,128,192]{1,2,0:T(8,128)(2,1)S(1)} %fusion.1), channel_id=1, source_target_pairs={{64,0},{65,1},{66,2},{67,3},{68,4},{69,5},{70,6},{71,7},{72,8},{73... | collective-permute-start | bytes 589832 | tf_op jit(solution)/shard_map/ppermute | solution.py:94
  52.9 1.2 fusion
  54.1 0.2 collective-permute-done.4
  54.4 0.6 gather_fusion
  55.2 0.1 fusion.7
  55.5 3.4 %collective-permute-start.5 = (bf16[1,64,512]{2,1,0:T(8,128)(2,1)S(1)}, bf16[1,64,512]{2,1,0:T(8,128)(2,1)S(1)}, u32[]{:S(2)}, u32[]{:S(2)}) collective-permute-start(bf16[1,64,512]{2,1,0:T(8,128)(2,1)S(1)} %bitcast.72), channel_id=1, source_target_pairs={{0,1},{1,2},{2,3},{3,4},{4,5},{5,6},{6,7},{7,8},{8,9},{9,10},{10,1... | collective-permute-start | bytes 196616 | tf_op jit(solution)/shard_map/ppermute | solution.py:47
  58.9 0.7 constant_dynamic-update-slice_fusion.13
  59.5 8.1 %collective-permute-start.9 = (bf16[1,64,512]{2,1,0:T(8,128)(2,1)S(1)}, bf16[1,64,512]{2,1,0:T(8,128)(2,1)}, u32[]{:S(2)}, u32[]{:S(2)}) collective-permute-start(bf16[1,64,512]{2,1,0:T(8,128)(2,1)S(1)} %bitcast.73), channel_id=1, source_target_pairs={{0,16},{1,17},{2,18},{3,19},{4,20},{5,21},{6,22},{7,23},{8,24},{9,... | collective-permute-start | bytes 196616 | tf_op jit(solution)/shard_map/ppermute | solution.py:47
  67.8 2.3 %collective-permute-start.15 = (bf16[1,64,512]{2,1,0:T(8,128)(2,1)S(1)}, bf16[1,64,512]{2,1,0:T(8,128)(2,1)S(1)}, u32[]{:S(2)}, u32[]{:S(2)}) collective-permute-start(bf16[1,64,512]{2,1,0:T(8,128)(2,1)S(1)} %bitcast.86), channel_id=1, source_target_pairs={{16,0},{17,1},{18,2},{19,3},{20,4},{21,5},{22,6},{23,7},{24,8},{25... | collective-permute-start | bytes 196616 | tf_op jit(solution)/shard_map/ppermute | solution.py:47
  70.1 4.6 %collective-permute-start.10 = (bf16[1,2,64,512]{3,2,0,1:T(8,128)(2,1)S(1)}, bf16[1,2,64,512]{3,2,0,1:T(8,128)(2,1)S(1)}, u32[]{:S(2)}, u32[]{:S(2)}) collective-permute-start(bf16[1,2,64,512]{3,2,0,1:T(8,128)(2,1)S(1)} %get-tuple-element.20), channel_id=1, source_target_pairs={{1,0},{2,1},{3,2},{4,3},{5,4},{6,5},{7,6},{8,7},{9,8},{10,9},{11,1... | collective-permute-start | bytes 393224 | tf_op jit(solution)/shard_map/ppermute | solution.py:47
  74.8 2.8 %collective-permute-start.6 = (bf16[2,64,512]{2,1,0:T(8,128)(2,1)S(1)}, bf16[2,64,512]{2,1,0:T(8,128)(2,1)S(1)}, u32[]{:S(2)}, u32[]{:S(2)}) collective-permute-start(bf16[2,64,512]{2,1,0:T(8,128)(2,1)S(1)} %get-tuple-element.25), channel_id=1, source_target_pairs={{0,2},{1,3},{2,4},{3,5},{4,6},{5,7},{6,8},{7,9},{8,10},{9,11},{10,... | collective-permute-start | bytes 393224 | tf_op jit(solution)/shard_map/ppermute | solution.py:47
  77.6 0.7 pad_maximum_fusion.9
  78.3 5.4 %collective-permute-start.11 = (bf16[2,2,64,512]{3,2,1,0:T(8,128)(2,1)}, bf16[2,2,64,512]{3,2,1,0:T(8,128)(2,1)S(1)}, u32[]{:S(2)}, u32[]{:S(2)}) collective-permute-start(bf16[2,2,64,512]{3,2,1,0:T(8,128)(2,1)} %pad_maximum_fusion.9), channel_id=1, source_target_pairs={{2,0},{3,1},{4,2},{5,3},{6,4},{7,5},{8,6},{9,7},{10,8},{11,9},{12,... | collective-permute-start | bytes 786440 | tf_op jit(solution)/shard_map/ppermute | solution.py:47
  83.8 0.9 copy.77.q_ref
  84.7 0.7 constant_dynamic-update-slice_fusion.12
  85.4 17.3 %collective-permute-start.7 = (bf16[4,64,512]{2,1,0:T(8,128)(2,1)S(1)}, bf16[4,64,512]{2,1,0:T(8,128)(2,1)S(1)}, u32[]{:S(2)}, u32[]{:S(2)}) collective-permute-start(bf16[4,64,512]{2,1,0:T(8,128)(2,1)S(1)} %pad_maximum_fusion.8), channel_id=1, source_target_pairs={{0,4},{1,5},{2,6},{3,7},{4,8},{5,9},{6,10},{7,11},{8,12},{9,13},{1... | collective-permute-start | bytes 786440 | tf_op jit(solution)/shard_map/ppermute | solution.py:47
  102.8 1.9 %collective-permute-start.12 = (bf16[4,2,64,512]{3,2,1,0:T(8,128)(2,1)S(1)}, bf16[4,2,64,512]{3,2,1,0:T(8,128)(2,1)S(1)}, u32[]{:S(2)}, u32[]{:S(2)}) collective-permute-start(bf16[4,2,64,512]{3,2,1,0:T(8,128)(2,1)S(1)} %pad_maximum_fusion.5), channel_id=1, source_target_pairs={{4,0},{5,1},{6,2},{7,3},{8,4},{9,5},{10,6},{11,7},{12,8},{13,9},{1... | collective-permute-start | bytes 1572872 | tf_op jit(solution)/shard_map/ppermute | solution.py:47
  104.7 0.7 constant_dynamic-update-slice_fusion.11
  105.4 3.0 %collective-permute-done.7 = bf16[4,64,512]{2,1,0:T(8,128)(2,1)S(1)} collective-permute-done((bf16[4,64,512]{2,1,0:T(8,128)(2,1)S(1)}, bf16[4,64,512]{2,1,0:T(8,128)(2,1)S(1)}, u32[]{:S(2)}, u32[]{:S(2)}) %collective-permute-start.7) | collective-permute-done | bytes 262176 | tf_op jit(solution)/shard_map/ppermute | solution.py:47
  108.5 3.2 %collective-permute-start.8 = (bf16[8,64,512]{2,1,0:T(8,128)(2,1)S(1)}, bf16[8,64,512]{2,1,0:T(8,128)(2,1)S(1)}, u32[]{:S(2)}, u32[]{:S(2)}) collective-permute-start(bf16[8,64,512]{2,1,0:T(8,128)(2,1)S(1)} %pad_maximum_fusion.4), channel_id=1, source_target_pairs={{0,8},{1,9},{2,10},{3,11},{4,12},{5,13},{6,14},{7,15},{8,16},{9,17... | collective-permute-start | bytes 1572872 | tf_op jit(solution)/shard_map/ppermute | solution.py:47
  111.7 21.3 %collective-permute-done.12 = bf16[4,2,64,512]{3,2,1,0:T(8,128)(2,1)S(1)} collective-permute-done((bf16[4,2,64,512]{3,2,1,0:T(8,128)(2,1)S(1)}, bf16[4,2,64,512]{3,2,1,0:T(8,128)(2,1)S(1)}, u32[]{:S(2)}, u32[]{:S(2)}) %collective-permute-start.12) | collective-permute-done | bytes 524320 | tf_op jit(solution)/shard_map/ppermute | solution.py:47
  133.1 1.9 %collective-permute-start.14 = (bf16[8,64,512]{2,1,0:T(8,128)(2,1)S(1)}, bf16[8,64,512]{2,1,0:T(8,128)(2,1)S(1)}, u32[]{:S(2)}, u32[]{:S(2)}) collective-permute-start(bf16[8,64,512]{2,1,0:T(8,128)(2,1)S(1)} %get-tuple-element.8), channel_id=1, source_target_pairs={{8,0},{9,1},{10,2},{11,3},{12,4},{13,5},{14,6},{15,7},{16,8},{17,9... | collective-permute-start | bytes 1572872 | tf_op jit(solution)/shard_map/ppermute | solution.py:47
  135.0 0.7 collective-permute-start.13
  135.7 0.8 constant_dynamic-update-slice_fusion.10
  136.6 1.1 constant_dynamic-update-slice_fusion.9
  137.7 1.5 constant_dynamic-update-slice_fusion.8
  139.2 25.6 %collective-permute-done.14 = bf16[8,64,512]{2,1,0:T(8,128)(2,1)S(1)} collective-permute-done((bf16[8,64,512]{2,1,0:T(8,128)(2,1)S(1)}, bf16[8,64,512]{2,1,0:T(8,128)(2,1)S(1)}, u32[]{:S(2)}, u32[]{:S(2)}) %collective-permute-start.14) | collective-permute-done | bytes 524320 | tf_op jit(solution)/shard_map/ppermute | solution.py:47
  164.9 1.1 fusion.3
  166.0 1.1 fusion.2
  167.1 2.6 %gather_fusion.1 = bf16[17,64,512]{2,1,0:T(8,128)(2,1)S(1)} fusion(bf16[51,64,512]{2,1,0:T(8,128)(2,1)} %fusion.2, s32[1024]{0:T(1024)S(1)} %pad_clamp_fusion), kind=kCustom, calls=%fused_computation.1 | custom fusion | bytes 2228292 | tf_op jit(solution)/shard_map/jit(_take)/gather | solution.py:171
  169.7 1.3 bitcast_select_fusion.late_ref
  170.9 7.8 %shard_map.46 = bf16[128,1024]{1,0:T(8,128)(2,1)} custom-call(s32[1]{0:T(128)} %bitcast.offset_ref, bf16[128,1024]{1,0:T(8,128)(2,1)} %copy.77.q_ref, bf16[1088,512]{1,0:T(8,128)(2,1)} %bitcast.83, bf16[1088,512]{1,0:T(8,128)(2,1)} %bitcast_select_fusion.late_ref, s32[2,64,1]{2,1,0:T(8,128)} %iota_add_fusion.qpos_ref, s32[2,64,1]{2,1,0:T(8,128)} %copy.78.qdoc_ref, ...), custom_call_target="tpu_custom_call" | custom-call | tf_op jit(solution)/shard_map/pallas_call | solution.py:235
  (64 shorter events, 2.6 us)
Async XLA Ops:
  0.0 30.0 %collective-permute-start.2 = (bf16[2048,192]{0,1:T(8,128)(2,1)}, bf16[2048,192]{0,1:T(8,128)(2,1)S(1)}, u32[]{:S(2)}, u32[]{:S(2)}) collective-permute-start(bf16[2048,192]{0,1:T(8,128)(2,1)} %param.5), channel_id=1, source_target_pairs={{416,0},{417,1},{418,2},{419,3},{420,4},{421,5},{422,6},{423,7},{4... | collective-permute-start | bytes 2359304 | tf_op jit(solution)/shard_map/ppermute | solution.py:91
  4.3 36.0 %collective-permute-start.1 = (bf16[2048,192]{0,1:T(8,128)(2,1)}, bf16[2048,192]{0,1:T(8,128)(2,1)S(1)}, u32[]{:S(2)}, u32[]{:S(2)}) collective-permute-start(bf16[2048,192]{0,1:T(8,128)(2,1)} %param.5), channel_id=1, source_target_pairs={{256,0},{257,1},{258,2},{259,3},{260,4},{261,5},{262,6},{263,7},{2... | collective-permute-start | bytes 2359304 | tf_op jit(solution)/shard_map/ppermute | solution.py:91
  14.3 34.4 %collective-permute-start = (bf16[2048,192]{0,1:T(8,128)(2,1)}, bf16[2048,192]{0,1:T(8,128)(2,1)S(1)}, u32[]{:S(2)}, u32[]{:S(2)}) collective-permute-start(bf16[2048,192]{0,1:T(8,128)(2,1)} %param.5), channel_id=1, source_target_pairs={{128,0},{129,1},{130,2},{131,3},{132,4},{133,5},{134,6},{135,7},{1... | collective-permute-start | bytes 2359304 | tf_op jit(solution)/shard_map/ppermute | solution.py:91
  16.8 9.3 %collective-permute-start.3 = (bf16[128,2048]{1,0:T(8,128)(2,1)}, bf16[128,2048]{1,0:T(8,128)(2,1)S(1)}, u32[]{:S(2)}, u32[]{:S(2)}) collective-permute-start(bf16[128,2048]{1,0:T(8,128)(2,1)} %bitcast.104), channel_id=1, source_target_pairs={{64,0},{65,1},{66,2},{67,3},{68,4},{69,5},{70,6},{71,7},{72,8},{73... | collective-permute-start | bytes 1572872 | tf_op jit(solution)/shard_map/ppermute | solution.py:90
  48.8 4.2 %copy-start = (bf16[2048,192]{0,1:T(8,128)(2,1)S(1)}, bf16[2048,192]{0,1:T(8,128)(2,1)}, u32[]{:S(2)}) copy-start(bf16[2048,192]{0,1:T(8,128)(2,1)} %param.5) | copy-start | bytes 2359300
  48.8 4.2 %copy-start.1 = (bf16[1,128,2048]{2,1,0:T(8,128)(2,1)S(1)}, bf16[1,128,2048]{2,1,0:T(8,128)(2,1)}, u32[]{:S(2)}) copy-start(bf16[1,128,2048]{2,1,0:T(8,128)(2,1)} %param.4) | copy-start | bytes 1572868
  51.0 3.3 %collective-permute-start.4 = (bf16[4,128,192]{1,2,0:T(8,128)(2,1)S(1)}, bf16[4,128,192]{1,2,0:T(8,128)(2,1)S(1)}, u32[]{:S(2)}, u32[]{:S(2)}) collective-permute-start(bf16[4,128,192]{1,2,0:T(8,128)(2,1)S(1)} %fusion.1), channel_id=1, source_target_pairs={{64,0},{65,1},{66,2},{67,3},{68,4},{69,5},{70,6},{71,7},{72,8},{73... | collective-permute-start | bytes 589832 | tf_op jit(solution)/shard_map/ppermute | solution.py:94
  55.5 14.6 %collective-permute-start.5 = (bf16[1,64,512]{2,1,0:T(8,128)(2,1)S(1)}, bf16[1,64,512]{2,1,0:T(8,128)(2,1)S(1)}, u32[]{:S(2)}, u32[]{:S(2)}) collective-permute-start(bf16[1,64,512]{2,1,0:T(8,128)(2,1)S(1)} %bitcast.72), channel_id=1, source_target_pairs={{0,1},{1,2},{2,3},{3,4},{4,5},{5,6},{6,7},{7,8},{8,9},{9,10},{10,1... | collective-permute-start | bytes 196616 | tf_op jit(solution)/shard_map/ppermute | solution.py:47
  59.5 78.2 %collective-permute-start.9 = (bf16[1,64,512]{2,1,0:T(8,128)(2,1)S(1)}, bf16[1,64,512]{2,1,0:T(8,128)(2,1)}, u32[]{:S(2)}, u32[]{:S(2)}) collective-permute-start(bf16[1,64,512]{2,1,0:T(8,128)(2,1)S(1)} %bitcast.73), channel_id=1, source_target_pairs={{0,16},{1,17},{2,18},{3,19},{4,20},{5,21},{6,22},{7,23},{8,24},{9,... | collective-permute-start | bytes 196616 | tf_op jit(solution)/shard_map/ppermute | solution.py:47
  67.8 97.1 %collective-permute-start.15 = (bf16[1,64,512]{2,1,0:T(8,128)(2,1)S(1)}, bf16[1,64,512]{2,1,0:T(8,128)(2,1)S(1)}, u32[]{:S(2)}, u32[]{:S(2)}) collective-permute-start(bf16[1,64,512]{2,1,0:T(8,128)(2,1)S(1)} %bitcast.86), channel_id=1, source_target_pairs={{16,0},{17,1},{18,2},{19,3},{20,4},{21,5},{22,6},{23,7},{24,8},{25... | collective-permute-start | bytes 196616 | tf_op jit(solution)/shard_map/ppermute | solution.py:47
  70.1 7.5 %collective-permute-start.10 = (bf16[1,2,64,512]{3,2,0,1:T(8,128)(2,1)S(1)}, bf16[1,2,64,512]{3,2,0,1:T(8,128)(2,1)S(1)}, u32[]{:S(2)}, u32[]{:S(2)}) collective-permute-start(bf16[1,2,64,512]{3,2,0,1:T(8,128)(2,1)S(1)} %get-tuple-element.20), channel_id=1, source_target_pairs={{1,0},{2,1},{3,2},{4,3},{5,4},{6,5},{7,6},{8,7},{9,8},{10,9},{11,1... | collective-permute-start | bytes 393224 | tf_op jit(solution)/shard_map/ppermute | solution.py:47
  74.8 10.5 %collective-permute-start.6 = (bf16[2,64,512]{2,1,0:T(8,128)(2,1)S(1)}, bf16[2,64,512]{2,1,0:T(8,128)(2,1)S(1)}, u32[]{:S(2)}, u32[]{:S(2)}) collective-permute-start(bf16[2,64,512]{2,1,0:T(8,128)(2,1)S(1)} %get-tuple-element.25), channel_id=1, source_target_pairs={{0,2},{1,3},{2,4},{3,5},{4,6},{5,7},{6,8},{7,9},{8,10},{9,11},{10,... | collective-permute-start | bytes 393224 | tf_op jit(solution)/shard_map/ppermute | solution.py:47
  78.3 24.3 %collective-permute-start.11 = (bf16[2,2,64,512]{3,2,1,0:T(8,128)(2,1)}, bf16[2,2,64,512]{3,2,1,0:T(8,128)(2,1)S(1)}, u32[]{:S(2)}, u32[]{:S(2)}) collective-permute-start(bf16[2,2,64,512]{3,2,1,0:T(8,128)(2,1)} %pad_maximum_fusion.9), channel_id=1, source_target_pairs={{2,0},{3,1},{4,2},{5,3},{6,4},{7,5},{8,6},{9,7},{10,8},{11,9},{12,... | collective-permute-start | bytes 786440 | tf_op jit(solution)/shard_map/ppermute | solution.py:47
  85.4 23.0 %collective-permute-start.7 = (bf16[4,64,512]{2,1,0:T(8,128)(2,1)S(1)}, bf16[4,64,512]{2,1,0:T(8,128)(2,1)S(1)}, u32[]{:S(2)}, u32[]{:S(2)}) collective-permute-start(bf16[4,64,512]{2,1,0:T(8,128)(2,1)S(1)} %pad_maximum_fusion.8), channel_id=1, source_target_pairs={{0,4},{1,5},{2,6},{3,7},{4,8},{5,9},{6,10},{7,11},{8,12},{9,13},{1... | collective-permute-start | bytes 786440 | tf_op jit(solution)/shard_map/ppermute | solution.py:47
  102.8 30.2 %collective-permute-start.12 = (bf16[4,2,64,512]{3,2,1,0:T(8,128)(2,1)S(1)}, bf16[4,2,64,512]{3,2,1,0:T(8,128)(2,1)S(1)}, u32[]{:S(2)}, u32[]{:S(2)}) collective-permute-start(bf16[4,2,64,512]{3,2,1,0:T(8,128)(2,1)S(1)} %pad_maximum_fusion.5), channel_id=1, source_target_pairs={{4,0},{5,1},{6,2},{7,3},{8,4},{9,5},{10,6},{11,7},{12,8},{13,9},{1... | collective-permute-start | bytes 1572872 | tf_op jit(solution)/shard_map/ppermute | solution.py:47
  108.5 28.1 %collective-permute-start.8 = (bf16[8,64,512]{2,1,0:T(8,128)(2,1)S(1)}, bf16[8,64,512]{2,1,0:T(8,128)(2,1)S(1)}, u32[]{:S(2)}, u32[]{:S(2)}) collective-permute-start(bf16[8,64,512]{2,1,0:T(8,128)(2,1)S(1)} %pad_maximum_fusion.4), channel_id=1, source_target_pairs={{0,8},{1,9},{2,10},{3,11},{4,12},{5,13},{6,14},{7,15},{8,16},{9,17... | collective-permute-start | bytes 1572872 | tf_op jit(solution)/shard_map/ppermute | solution.py:47
  133.1 31.7 %collective-permute-start.14 = (bf16[8,64,512]{2,1,0:T(8,128)(2,1)S(1)}, bf16[8,64,512]{2,1,0:T(8,128)(2,1)S(1)}, u32[]{:S(2)}, u32[]{:S(2)}) collective-permute-start(bf16[8,64,512]{2,1,0:T(8,128)(2,1)S(1)} %get-tuple-element.8), channel_id=1, source_target_pairs={{8,0},{9,1},{10,2},{11,3},{12,4},{13,5},{14,6},{15,7},{16,8},{17,9... | collective-permute-start | bytes 1572872 | tf_op jit(solution)/shard_map/ppermute | solution.py:47
  135.0 29.7 %collective-permute-start.13 = (bf16[8,64,512]{2,1,0:T(8,128)(2,1)S(1)}, bf16[8,64,512]{2,1,0:T(8,128)(2,1)S(1)}, u32[]{:S(2)}, u32[]{:S(2)}) collective-permute-start(bf16[8,64,512]{2,1,0:T(8,128)(2,1)S(1)} %get-tuple-element.7), channel_id=1, source_target_pairs={{56,48},{57,49},{58,50},{59,51},{60,52},{61,53},{62,54},{63,55},{1... | collective-permute-start | bytes 1572872 | tf_op jit(solution)/shard_map/ppermute | solution.py:47

commit v11 on v10

--- a/solution.py
+++ b/solution.py
@@ -159,17 +159,15 @@
     far = moved(late_rows[None], count, [(d, d - WINDOW) for d in range(count)])
     down = jnp.concatenate([down, jnp.stack([jnp.zeros_like(far), far], axis=1)], axis=0)
     early_keys = up.reshape(-1, up.shape[-1])
-    around = jnp.concatenate([up, down[:, 0], down[:, 1]], axis=0)
     steps = jnp.arange(WINDOW + 1, dtype=jnp.int32)
     source = 2 * count - 1 - my_index - steps
-    pick = jnp.where(
-        my_index + steps <= count - 1,
-        2 * (WINDOW + 1) + steps,
-        jnp.where(source <= my_index, my_index - source, WINDOW + 1 + source - my_index),
-    )
-    pick = jnp.clip(pick, 0, around.shape[0] - 1)
-    late_keys = jnp.take(around, pick, axis=0).reshape(-1, up.shape[-1])
-    key_blocks = jnp.stack([early_keys, late_keys])
+    from_up = (my_index + steps > count - 1) & (source <= my_index)
+    up_row = jnp.where(from_up, my_index - source, 0)
+    down_block = jnp.where(my_index + steps <= count - 1, 2 * steps + 1, 2 * (source - my_index))
+    down_row = jnp.where(from_up, 0, down_block)
+    up_row = jnp.clip(up_row, 0, WINDOW) * SPAN
+    down_row = jnp.clip(down_row, 0, 2 * WINDOW + 1) * SPAN
+    down_keys = down.reshape(-1, down.shape[-1])
 
     steps = jnp.arange(WINDOW + 1, dtype=jnp.int32)
     query_spans = jnp.stack([my_index, 2 * devices - 1 - my_index])
@@ -187,11 +185,14 @@
     )
 
     key_docs = jnp.where(key_ok, key_docs, -1)
+    meta = jnp.concatenate(
+        [offset.reshape(1), from_up.astype(jnp.int32), up_row, down_row]
+    ).astype(jnp.int32)
     return attend(
-        offset.reshape(1),
+        meta,
         query_rows,
         early_keys,
-        late_keys,
+        down_keys,
         query_places[:, :, None],
         query_docs[:, :, None],
         key_places[:, None, :],
@@ -199,8 +200,19 @@
     )[None]
 
 
-def attend_kernel(offset_ref, q_ref, early_ref, late_ref, qpos_ref, qdoc_ref, kpos_ref, kdoc_ref, o_ref):
-    offset = pl.multiple_of(offset_ref[0], SPAN)
+def attend_kernel(
+    meta_ref, q_ref, early_ref, down_ref, qpos_ref, qdoc_ref, kpos_ref, kdoc_ref, o_ref, late_ref
+):
+    offset = pl.multiple_of(meta_ref[0], SPAN)
+    blocks = WINDOW + 1
+    for step in range(blocks):
+        up_row = pl.multiple_of(meta_ref[1 + blocks + step], SPAN)
+        down_row = pl.multiple_of(meta_ref[1 + 2 * blocks + step], SPAN)
+        late_ref[step * SPAN : (step + 1) * SPAN, :] = jnp.where(
+            meta_ref[1 + step] > 0,
+            early_ref[pl.ds(up_row, SPAN), :],
+            down_ref[pl.ds(down_row, SPAN), :],
+        )
     for span, kv_ref in ((0, early_ref), (1, late_ref)):
         row = offset if span == 0 else SPAN - offset
         row = pl.multiple_of(row, SPAN)
@@ -230,15 +242,15 @@
                 ]
 
 
-def attend(offset, query_rows, early_keys, late_keys, qpos, qdoc, kpos, kdoc):
+def attend(meta, query_rows, early_keys, down_keys, qpos, qdoc, kpos, kdoc):
     vmem = pl.BlockSpec(memory_space=pltpu.VMEM)
     return pl.pallas_call(
         attend_kernel,
         out_shape=jax.ShapeDtypeStruct(query_rows.shape, query_rows.dtype),
         in_specs=[pl.BlockSpec(memory_space=pltpu.SMEM)] + [vmem] * 7,
         out_specs=vmem,
-    )(offset, query_rows, early_keys, late_keys, qpos, qdoc, kpos, kdoc)
-
+        scratch_shapes=[pltpu.VMEM(early_keys.shape, early_keys.dtype)],
+    )(meta, query_rows, early_keys, down_keys, qpos, qdoc, kpos, kdoc)
 
 def solution(mesh):
     placed = (P("seq", "ctx", None), P(None, "seq"), P("seq", None), P("seq", None))

time: 181 us -> 177 us (0.978)
  local copies, waits for them, and re-layouts: 14.3 us -> 10.4 us
    unnamed x14 -> x12, local copies, waits for them, and re-layouts: 6.66 us -> 3.55 us
    gather x1 -> x0, local copies, waits for them, and re-layouts: 2.56 us -> none  [body(): late_keys = jnp.take(around, pick, axis=0).reshape(-1, up.shape[-1])]
where the time goes in v11:
time: 177 us; the launch traced here: 175 us
  waiting for transfers between devices  72.7 us (41%)
  starting transfers between devices  72.2 us (41%)
  local copies, waits for them, and re-layouts  10.4 us (6%)
  Pallas kernels  8.24 us (5%)
  other arithmetic  6.64 us (4%)
  matrix products  3.42 us (2%)
    ppermute x11, starting transfers between devices, moved(): return lax.ppermute(value, 'ctx', pairs)  51.6 us
    ppermute x11, waiting for transfers between devices, moved(): return lax.ppermute(value, 'ctx', pairs)  50.4 us
    ppermute x3, waiting for transfers between devices, project(): lax.ppermute(weight, both, pairs_for(f))  22.2 us
    ppermute x3, starting transfers between devices, project(): lax.ppermute(weight, both, pairs_for(f))  16.8 us
    pallas_call x1, Pallas kernels, attend(): pl.pallas_call(attend_kernel, out_shape=jax.ShapeDtypeStruct(query_rows.s...  8.24 us
    unnamed x12, local copies, waits for them, and re-layouts  3.55 us
  transfers between devices with their start and end apart: 16, of which 7 were waited for; matrix products, arithmetic and copies ran while one was open for 9% of the time, Pallas kernels for 0%

profile of v11, /device:TPU:56, one launch (start us, length us, event | category | flops | bytes accessed | tf_op | source)
XLA Modules:
  0.0 174.8 jit_solution(1714946777760871546)
XLA Ops:
  0.0 4.3 %collective-permute-start.2 = (bf16[2048,192]{0,1:T(8,128)(2,1)}, bf16[2048,192]{0,1:T(8,128)(2,1)S(1)}, u32[]{:S(2)}, u32[]{:S(2)}) collective-permute-start(bf16[2048,192]{0,1:T(8,128)(2,1)} %param.5), channel_id=1, source_target_pairs={{416,0},{417,1},{418,2},{419,3},{420,4},{421,5},{422,6},{423,7},{4... | collective-permute-start | bytes 2359304 | tf_op jit(solution)/shard_map/ppermute | solution.py:91
  4.3 10.0 %collective-permute-start.1 = (bf16[2048,192]{0,1:T(8,128)(2,1)}, bf16[2048,192]{0,1:T(8,128)(2,1)S(1)}, u32[]{:S(2)}, u32[]{:S(2)}) collective-permute-start(bf16[2048,192]{0,1:T(8,128)(2,1)} %param.5), channel_id=1, source_target_pairs={{256,0},{257,1},{258,2},{259,3},{260,4},{261,5},{262,6},{263,7},{2... | collective-permute-start | bytes 2359304 | tf_op jit(solution)/shard_map/ppermute | solution.py:91
  14.3 2.5 %collective-permute-start = (bf16[2048,192]{0,1:T(8,128)(2,1)}, bf16[2048,192]{0,1:T(8,128)(2,1)S(1)}, u32[]{:S(2)}, u32[]{:S(2)}) collective-permute-start(bf16[2048,192]{0,1:T(8,128)(2,1)} %param.5), channel_id=1, source_target_pairs={{128,0},{129,1},{130,2},{131,3},{132,4},{133,5},{134,6},{135,7},{1... | collective-permute-start | bytes 2359304 | tf_op jit(solution)/shard_map/ppermute | solution.py:91
  16.8 1.9 %collective-permute-start.3 = (bf16[128,2048]{1,0:T(8,128)(2,1)}, bf16[128,2048]{1,0:T(8,128)(2,1)S(1)}, u32[]{:S(2)}, u32[]{:S(2)}) collective-permute-start(bf16[128,2048]{1,0:T(8,128)(2,1)} %bitcast.93), channel_id=1, source_target_pairs={{64,0},{65,1},{66,2},{67,3},{68,4},{69,5},{70,6},{71,7},{72,8},{73... | collective-permute-start | bytes 1572872 | tf_op jit(solution)/shard_map/ppermute | solution.py:90
  18.9 0.7 iota_add_fusion.qpos_ref
  20.1 0.7 multiply_bitcast_fusion
  20.7 1.2 fusion.24
  22.8 0.8 copy.64
  23.6 0.1 reduce
  23.7 0.1 fusion.9
  23.8 0.7 copy.69.qdoc_ref
  24.8 0.3 fusion.4
  25.2 0.1 multiply_cosine_fusion
  25.3 0.6 pad_add_fusion.meta_ref
  26.0 0.6 reshape_select_fusion
  26.6 3.4 %collective-permute-done.2 = bf16[2048,192]{0,1:T(8,128)(2,1)S(1)} collective-permute-done((bf16[2048,192]{0,1:T(8,128)(2,1)}, bf16[2048,192]{0,1:T(8,128)(2,1)S(1)}, u32[]{:S(2)}, u32[]{:S(2)}) %collective-permute-start.2) | collective-permute-done | bytes 786464 | tf_op jit(solution)/shard_map/ppermute | solution.py:91
  30.0 10.3 %collective-permute-done.1 = bf16[2048,192]{0,1:T(8,128)(2,1)S(1)} collective-permute-done((bf16[2048,192]{0,1:T(8,128)(2,1)}, bf16[2048,192]{0,1:T(8,128)(2,1)S(1)}, u32[]{:S(2)}, u32[]{:S(2)}) %collective-permute-start.1) | collective-permute-done | bytes 786464 | tf_op jit(solution)/shard_map/ppermute | solution.py:91
  40.3 8.4 %collective-permute-done = bf16[2048,192]{0,1:T(8,128)(2,1)S(1)} collective-permute-done((bf16[2048,192]{0,1:T(8,128)(2,1)}, bf16[2048,192]{0,1:T(8,128)(2,1)S(1)}, u32[]{:S(2)}, u32[]{:S(2)}) %collective-permute-start) | collective-permute-done | bytes 786464 | tf_op jit(solution)/shard_map/ppermute | solution.py:91
  48.8 2.2 %fusion.1 = bf16[4,128,192]{1,2,0:T(8,128)(2,1)S(1)} fusion(bf16[1,2048,192]{1,2,0:T(8,128)(2,1)S(1)} %bitcast.87, bf16[1,2048,192]{1,2,0:T(8,128)(2,1)S(1)} %bitcast.89, bf16[1,2048,192]{1,2,0:T(8,128)(2,1)S(1)} %bitcast.91, bf16[1,2048,192]{1,2,0:T(8,128)(2,1)} %bitcast.85, bf16[128,2048]{1,0:T(8,128)(2,1)S(1)} %collective-permute-done.3), kind=kOutput, calls=%fused_computation.5 | convolution fusion | flops 407470080 | bytes 3866624 | tf_op jit(solution)/shard_map/td,bdn->btn/dot_general | solution.py:93
  51.0 1.9 %collective-permute-start.4 = (bf16[4,128,192]{1,2,0:T(8,128)(2,1)S(1)}, bf16[4,128,192]{1,2,0:T(8,128)(2,1)S(1)}, u32[]{:S(2)}, u32[]{:S(2)}) collective-permute-start(bf16[4,128,192]{1,2,0:T(8,128)(2,1)S(1)} %fusion.1), channel_id=1, source_target_pairs={{64,0},{65,1},{66,2},{67,3},{68,4},{69,5},{70,6},{71,7},{72,8},{73... | collective-permute-start | bytes 589832 | tf_op jit(solution)/shard_map/ppermute | solution.py:94
  52.9 1.2 fusion
  54.1 0.2 collective-permute-done.4
  54.4 0.6 gather_fusion
  55.2 0.1 fusion.5
  55.4 3.4 %collective-permute-start.5 = (bf16[1,64,512]{2,1,0:T(8,128)(2,1)S(1)}, bf16[1,64,512]{2,1,0:T(8,128)(2,1)S(1)}, u32[]{:S(2)}, u32[]{:S(2)}) collective-permute-start(bf16[1,64,512]{2,1,0:T(8,128)(2,1)S(1)} %bitcast.61), channel_id=1, source_target_pairs={{0,1},{1,2},{2,3},{3,4},{4,5},{5,6},{6,7},{7,8},{8,9},{9,10},{10,1... | collective-permute-start | bytes 196616 | tf_op jit(solution)/shard_map/ppermute | solution.py:47
  58.8 0.6 constant_dynamic-update-slice_fusion.5
  59.5 8.1 %collective-permute-start.9 = (bf16[1,64,512]{2,1,0:T(8,128)(2,1)S(1)}, bf16[1,64,512]{2,1,0:T(8,128)(2,1)}, u32[]{:S(2)}, u32[]{:S(2)}) collective-permute-start(bf16[1,64,512]{2,1,0:T(8,128)(2,1)S(1)} %bitcast.62), channel_id=1, source_target_pairs={{0,16},{1,17},{2,18},{3,19},{4,20},{5,21},{6,22},{7,23},{8,24},{9,... | collective-permute-start | bytes 196616 | tf_op jit(solution)/shard_map/ppermute | solution.py:47
  67.7 2.3 %collective-permute-start.15 = (bf16[1,64,512]{2,1,0:T(8,128)(2,1)S(1)}, bf16[1,64,512]{2,1,0:T(8,128)(2,1)S(1)}, u32[]{:S(2)}, u32[]{:S(2)}) collective-permute-start(bf16[1,64,512]{2,1,0:T(8,128)(2,1)S(1)} %bitcast.75), channel_id=1, source_target_pairs={{16,0},{17,1},{18,2},{19,3},{20,4},{21,5},{22,6},{23,7},{24,8},{25... | collective-permute-start | bytes 196616 | tf_op jit(solution)/shard_map/ppermute | solution.py:47
  70.1 4.5 %collective-permute-start.10 = (bf16[1,2,64,512]{3,2,0,1:T(8,128)(2,1)S(1)}, bf16[1,2,64,512]{3,2,0,1:T(8,128)(2,1)S(1)}, u32[]{:S(2)}, u32[]{:S(2)}) collective-permute-start(bf16[1,2,64,512]{3,2,0,1:T(8,128)(2,1)S(1)} %get-tuple-element.16), channel_id=1, source_target_pairs={{1,0},{2,1},{3,2},{4,3},{5,4},{6,5},{7,6},{8,7},{9,8},{10,9},{11,1... | collective-permute-start | bytes 393224 | tf_op jit(solution)/shard_map/ppermute | solution.py:47
  74.7 2.8 %collective-permute-start.6 = (bf16[2,64,512]{2,1,0:T(8,128)(2,1)S(1)}, bf16[2,64,512]{2,1,0:T(8,128)(2,1)S(1)}, u32[]{:S(2)}, u32[]{:S(2)}) collective-permute-start(bf16[2,64,512]{2,1,0:T(8,128)(2,1)S(1)} %get-tuple-element.19), channel_id=1, source_target_pairs={{0,2},{1,3},{2,4},{3,5},{4,6},{5,7},{6,8},{7,9},{8,10},{9,11},{10,... | collective-permute-start | bytes 393224 | tf_op jit(solution)/shard_map/ppermute | solution.py:47
  77.6 0.7 pad_maximum_fusion.9
  78.3 5.4 %collective-permute-start.11 = (bf16[2,2,64,512]{3,2,1,0:T(8,128)(2,1)}, bf16[2,2,64,512]{3,2,1,0:T(8,128)(2,1)S(1)}, u32[]{:S(2)}, u32[]{:S(2)}) collective-permute-start(bf16[2,2,64,512]{3,2,1,0:T(8,128)(2,1)} %pad_maximum_fusion.9), channel_id=1, source_target_pairs={{2,0},{3,1},{4,2},{5,3},{6,4},{7,5},{8,6},{9,7},{10,8},{11,9},{12,... | collective-permute-start | bytes 786440 | tf_op jit(solution)/shard_map/ppermute | solution.py:47
  83.8 0.9 copy.68.q_ref
  84.6 0.6 constant_dynamic-update-slice_fusion.4
  85.3 17.4 %collective-permute-start.7 = (bf16[4,64,512]{2,1,0:T(8,128)(2,1)S(1)}, bf16[4,64,512]{2,1,0:T(8,128)(2,1)S(1)}, u32[]{:S(2)}, u32[]{:S(2)}) collective-permute-start(bf16[4,64,512]{2,1,0:T(8,128)(2,1)S(1)} %pad_maximum_fusion.8), channel_id=1, source_target_pairs={{0,4},{1,5},{2,6},{3,7},{4,8},{5,9},{6,10},{7,11},{8,12},{9,13},{1... | collective-permute-start | bytes 786440 | tf_op jit(solution)/shard_map/ppermute | solution.py:47
  102.8 1.9 %collective-permute-start.12 = (bf16[4,2,64,512]{3,2,1,0:T(8,128)(2,1)S(1)}, bf16[4,2,64,512]{3,2,1,0:T(8,128)(2,1)S(1)}, u32[]{:S(2)}, u32[]{:S(2)}) collective-permute-start(bf16[4,2,64,512]{3,2,1,0:T(8,128)(2,1)S(1)} %pad_maximum_fusion.5), channel_id=1, source_target_pairs={{4,0},{5,1},{6,2},{7,3},{8,4},{9,5},{10,6},{11,7},{12,8},{13,9},{1... | collective-permute-start | bytes 1572872 | tf_op jit(solution)/shard_map/ppermute | solution.py:47
  104.7 0.7 constant_dynamic-update-slice_fusion.3
  105.3 3.0 %collective-permute-done.7 = bf16[4,64,512]{2,1,0:T(8,128)(2,1)S(1)} collective-permute-done((bf16[4,64,512]{2,1,0:T(8,128)(2,1)S(1)}, bf16[4,64,512]{2,1,0:T(8,128)(2,1)S(1)}, u32[]{:S(2)}, u32[]{:S(2)}) %collective-permute-start.7) | collective-permute-done | bytes 262176 | tf_op jit(solution)/shard_map/ppermute | solution.py:47
  108.4 3.2 %collective-permute-start.8 = (bf16[8,64,512]{2,1,0:T(8,128)(2,1)S(1)}, bf16[8,64,512]{2,1,0:T(8,128)(2,1)S(1)}, u32[]{:S(2)}, u32[]{:S(2)}) collective-permute-start(bf16[8,64,512]{2,1,0:T(8,128)(2,1)S(1)} %pad_maximum_fusion.4), channel_id=1, source_target_pairs={{0,8},{1,9},{2,10},{3,11},{4,12},{5,13},{6,14},{7,15},{8,16},{9,17... | collective-permute-start | bytes 1572872 | tf_op jit(solution)/shard_map/ppermute | solution.py:47
  111.6 21.3 %collective-permute-done.12 = bf16[4,2,64,512]{3,2,1,0:T(8,128)(2,1)S(1)} collective-permute-done((bf16[4,2,64,512]{3,2,1,0:T(8,128)(2,1)S(1)}, bf16[4,2,64,512]{3,2,1,0:T(8,128)(2,1)S(1)}, u32[]{:S(2)}, u32[]{:S(2)}) %collective-permute-start.12) | collective-permute-done | bytes 524320 | tf_op jit(solution)/shard_map/ppermute | solution.py:47
  133.1 1.9 %collective-permute-start.14 = (bf16[8,64,512]{2,1,0:T(8,128)(2,1)S(1)}, bf16[8,64,512]{2,1,0:T(8,128)(2,1)S(1)}, u32[]{:S(2)}, u32[]{:S(2)}) collective-permute-start(bf16[8,64,512]{2,1,0:T(8,128)(2,1)S(1)} %get-tuple-element.8), channel_id=1, source_target_pairs={{8,0},{9,1},{10,2},{11,3},{12,4},{13,5},{14,6},{15,7},{16,8},{17,9... | collective-permute-start | bytes 1572872 | tf_op jit(solution)/shard_map/ppermute | solution.py:47
  135.0 0.7 collective-permute-start.13
  135.7 0.7 constant_dynamic-update-slice_fusion.2
  136.4 0.8 constant_dynamic-update-slice_fusion.1
  137.3 1.5 constant_dynamic-update-slice_fusion
  138.8 26.1 %collective-permute-done.14 = bf16[8,64,512]{2,1,0:T(8,128)(2,1)S(1)} collective-permute-done((bf16[8,64,512]{2,1,0:T(8,128)(2,1)S(1)}, bf16[8,64,512]{2,1,0:T(8,128)(2,1)S(1)}, u32[]{:S(2)}, u32[]{:S(2)}) %collective-permute-start.14) | collective-permute-done | bytes 524320 | tf_op jit(solution)/shard_map/ppermute | solution.py:47
  165.0 1.6 copy.63
  166.5 8.2 %shard_map.46 = bf16[128,1024]{1,0:T(8,128)(2,1)} custom-call(s32[52]{0:T(128)} %pad_add_fusion.meta_ref, bf16[128,1024]{1,0:T(8,128)(2,1)} %copy.68.q_ref, bf16[1088,512]{1,0:T(8,128)(2,1)} %bitcast.72, bf16[2176,512]{1,0:T(8,128)(2,1)} %bitcast.60, s32[2,64,1]{2,1,0:T(8,128)} %iota_add_fusion.qpos_ref, s32[2,64,1]{2,1,0:T(8,128)} %copy.69.qdoc_ref, ...), custom_call_target="tpu_custom_call" | custom-call | tf_op jit(solution)/shard_map/pallas_call | solution.py:247
  (59 shorter events, 2.2 us)
Async XLA Ops:
  0.0 30.0 %collective-permute-start.2 = (bf16[2048,192]{0,1:T(8,128)(2,1)}, bf16[2048,192]{0,1:T(8,128)(2,1)S(1)}, u32[]{:S(2)}, u32[]{:S(2)}) collective-permute-start(bf16[2048,192]{0,1:T(8,128)(2,1)} %param.5), channel_id=1, source_target_pairs={{416,0},{417,1},{418,2},{419,3},{420,4},{421,5},{422,6},{423,7},{4... | collective-permute-start | bytes 2359304 | tf_op jit(solution)/shard_map/ppermute | solution.py:91
  4.3 36.0 %collective-permute-start.1 = (bf16[2048,192]{0,1:T(8,128)(2,1)}, bf16[2048,192]{0,1:T(8,128)(2,1)S(1)}, u32[]{:S(2)}, u32[]{:S(2)}) collective-permute-start(bf16[2048,192]{0,1:T(8,128)(2,1)} %param.5), channel_id=1, source_target_pairs={{256,0},{257,1},{258,2},{259,3},{260,4},{261,5},{262,6},{263,7},{2... | collective-permute-start | bytes 2359304 | tf_op jit(solution)/shard_map/ppermute | solution.py:91
  14.3 34.4 %collective-permute-start = (bf16[2048,192]{0,1:T(8,128)(2,1)}, bf16[2048,192]{0,1:T(8,128)(2,1)S(1)}, u32[]{:S(2)}, u32[]{:S(2)}) collective-permute-start(bf16[2048,192]{0,1:T(8,128)(2,1)} %param.5), channel_id=1, source_target_pairs={{128,0},{129,1},{130,2},{131,3},{132,4},{133,5},{134,6},{135,7},{1... | collective-permute-start | bytes 2359304 | tf_op jit(solution)/shard_map/ppermute | solution.py:91
  16.8 9.8 %collective-permute-start.3 = (bf16[128,2048]{1,0:T(8,128)(2,1)}, bf16[128,2048]{1,0:T(8,128)(2,1)S(1)}, u32[]{:S(2)}, u32[]{:S(2)}) collective-permute-start(bf16[128,2048]{1,0:T(8,128)(2,1)} %bitcast.93), channel_id=1, source_target_pairs={{64,0},{65,1},{66,2},{67,3},{68,4},{69,5},{70,6},{71,7},{72,8},{73... | collective-permute-start | bytes 1572872 | tf_op jit(solution)/shard_map/ppermute | solution.py:90
  48.8 4.2 %copy-start = (bf16[2048,192]{0,1:T(8,128)(2,1)S(1)}, bf16[2048,192]{0,1:T(8,128)(2,1)}, u32[]{:S(2)}) copy-start(bf16[2048,192]{0,1:T(8,128)(2,1)} %param.5) | copy-start | bytes 2359300
  48.8 4.2 %copy-start.1 = (bf16[1,128,2048]{2,1,0:T(8,128)(2,1)S(1)}, bf16[1,128,2048]{2,1,0:T(8,128)(2,1)}, u32[]{:S(2)}) copy-start(bf16[1,128,2048]{2,1,0:T(8,128)(2,1)} %param.4) | copy-start | bytes 1572868
  51.0 3.3 %collective-permute-start.4 = (bf16[4,128,192]{1,2,0:T(8,128)(2,1)S(1)}, bf16[4,128,192]{1,2,0:T(8,128)(2,1)S(1)}, u32[]{:S(2)}, u32[]{:S(2)}) collective-permute-start(bf16[4,128,192]{1,2,0:T(8,128)(2,1)S(1)} %fusion.1), channel_id=1, source_target_pairs={{64,0},{65,1},{66,2},{67,3},{68,4},{69,5},{70,6},{71,7},{72,8},{73... | collective-permute-start | bytes 589832 | tf_op jit(solution)/shard_map/ppermute | solution.py:94
  55.4 14.6 %collective-permute-start.5 = (bf16[1,64,512]{2,1,0:T(8,128)(2,1)S(1)}, bf16[1,64,512]{2,1,0:T(8,128)(2,1)S(1)}, u32[]{:S(2)}, u32[]{:S(2)}) collective-permute-start(bf16[1,64,512]{2,1,0:T(8,128)(2,1)S(1)} %bitcast.61), channel_id=1, source_target_pairs={{0,1},{1,2},{2,3},{3,4},{4,5},{5,6},{6,7},{7,8},{8,9},{9,10},{10,1... | collective-permute-start | bytes 196616 | tf_op jit(solution)/shard_map/ppermute | solution.py:47
  59.5 77.8 %collective-permute-start.9 = (bf16[1,64,512]{2,1,0:T(8,128)(2,1)S(1)}, bf16[1,64,512]{2,1,0:T(8,128)(2,1)}, u32[]{:S(2)}, u32[]{:S(2)}) collective-permute-start(bf16[1,64,512]{2,1,0:T(8,128)(2,1)S(1)} %bitcast.62), channel_id=1, source_target_pairs={{0,16},{1,17},{2,18},{3,19},{4,20},{5,21},{6,22},{7,23},{8,24},{9,... | collective-permute-start | bytes 196616 | tf_op jit(solution)/shard_map/ppermute | solution.py:47
  67.7 97.2 %collective-permute-start.15 = (bf16[1,64,512]{2,1,0:T(8,128)(2,1)S(1)}, bf16[1,64,512]{2,1,0:T(8,128)(2,1)S(1)}, u32[]{:S(2)}, u32[]{:S(2)}) collective-permute-start(bf16[1,64,512]{2,1,0:T(8,128)(2,1)S(1)} %bitcast.75), channel_id=1, source_target_pairs={{16,0},{17,1},{18,2},{19,3},{20,4},{21,5},{22,6},{23,7},{24,8},{25... | collective-permute-start | bytes 196616 | tf_op jit(solution)/shard_map/ppermute | solution.py:47
  70.1 7.5 %collective-permute-start.10 = (bf16[1,2,64,512]{3,2,0,1:T(8,128)(2,1)S(1)}, bf16[1,2,64,512]{3,2,0,1:T(8,128)(2,1)S(1)}, u32[]{:S(2)}, u32[]{:S(2)}) collective-permute-start(bf16[1,2,64,512]{3,2,0,1:T(8,128)(2,1)S(1)} %get-tuple-element.16), channel_id=1, source_target_pairs={{1,0},{2,1},{3,2},{4,3},{5,4},{6,5},{7,6},{8,7},{9,8},{10,9},{11,1... | collective-permute-start | bytes 393224 | tf_op jit(solution)/shard_map/ppermute | solution.py:47
  74.7 10.5 %collective-permute-start.6 = (bf16[2,64,512]{2,1,0:T(8,128)(2,1)S(1)}, bf16[2,64,512]{2,1,0:T(8,128)(2,1)S(1)}, u32[]{:S(2)}, u32[]{:S(2)}) collective-permute-start(bf16[2,64,512]{2,1,0:T(8,128)(2,1)S(1)} %get-tuple-element.19), channel_id=1, source_target_pairs={{0,2},{1,3},{2,4},{3,5},{4,6},{5,7},{6,8},{7,9},{8,10},{9,11},{10,... | collective-permute-start | bytes 393224 | tf_op jit(solution)/shard_map/ppermute | solution.py:47
  78.3 24.4 %collective-permute-start.11 = (bf16[2,2,64,512]{3,2,1,0:T(8,128)(2,1)}, bf16[2,2,64,512]{3,2,1,0:T(8,128)(2,1)S(1)}, u32[]{:S(2)}, u32[]{:S(2)}) collective-permute-start(bf16[2,2,64,512]{3,2,1,0:T(8,128)(2,1)} %pad_maximum_fusion.9), channel_id=1, source_target_pairs={{2,0},{3,1},{4,2},{5,3},{6,4},{7,5},{8,6},{9,7},{10,8},{11,9},{12,... | collective-permute-start | bytes 786440 | tf_op jit(solution)/shard_map/ppermute | solution.py:47
  85.3 23.1 %collective-permute-start.7 = (bf16[4,64,512]{2,1,0:T(8,128)(2,1)S(1)}, bf16[4,64,512]{2,1,0:T(8,128)(2,1)S(1)}, u32[]{:S(2)}, u32[]{:S(2)}) collective-permute-start(bf16[4,64,512]{2,1,0:T(8,128)(2,1)S(1)} %pad_maximum_fusion.8), channel_id=1, source_target_pairs={{0,4},{1,5},{2,6},{3,7},{4,8},{5,9},{6,10},{7,11},{8,12},{9,13},{1... | collective-permute-start | bytes 786440 | tf_op jit(solution)/shard_map/ppermute | solution.py:47
  102.8 30.1 %collective-permute-start.12 = (bf16[4,2,64,512]{3,2,1,0:T(8,128)(2,1)S(1)}, bf16[4,2,64,512]{3,2,1,0:T(8,128)(2,1)S(1)}, u32[]{:S(2)}, u32[]{:S(2)}) collective-permute-start(bf16[4,2,64,512]{3,2,1,0:T(8,128)(2,1)S(1)} %pad_maximum_fusion.5), channel_id=1, source_target_pairs={{4,0},{5,1},{6,2},{7,3},{8,4},{9,5},{10,6},{11,7},{12,8},{13,9},{1... | collective-permute-start | bytes 1572872 | tf_op jit(solution)/shard_map/ppermute | solution.py:47
  108.4 28.0 %collective-permute-start.8 = (bf16[8,64,512]{2,1,0:T(8,128)(2,1)S(1)}, bf16[8,64,512]{2,1,0:T(8,128)(2,1)S(1)}, u32[]{:S(2)}, u32[]{:S(2)}) collective-permute-start(bf16[8,64,512]{2,1,0:T(8,128)(2,1)S(1)} %pad_maximum_fusion.4), channel_id=1, source_target_pairs={{0,8},{1,9},{2,10},{3,11},{4,12},{5,13},{6,14},{7,15},{8,16},{9,17... | collective-permute-start | bytes 1572872 | tf_op jit(solution)/shard_map/ppermute | solution.py:47
  133.1 31.8 %collective-permute-start.14 = (bf16[8,64,512]{2,1,0:T(8,128)(2,1)S(1)}, bf16[8,64,512]{2,1,0:T(8,128)(2,1)S(1)}, u32[]{:S(2)}, u32[]{:S(2)}) collective-permute-start(bf16[8,64,512]{2,1,0:T(8,128)(2,1)S(1)} %get-tuple-element.8), channel_id=1, source_target_pairs={{8,0},{9,1},{10,2},{11,3},{12,4},{13,5},{14,6},{15,7},{16,8},{17,9... | collective-permute-start | bytes 1572872 | tf_op jit(solution)/shard_map/ppermute | solution.py:47
  135.0 29.9 %collective-permute-start.13 = (bf16[8,64,512]{2,1,0:T(8,128)(2,1)S(1)}, bf16[8,64,512]{2,1,0:T(8,128)(2,1)S(1)}, u32[]{:S(2)}, u32[]{:S(2)}) collective-permute-start(bf16[8,64,512]{2,1,0:T(8,128)(2,1)S(1)} %get-tuple-element.7), channel_id=1, source_target_pairs={{56,48},{57,49},{58,50},{59,51},{60,52},{61,53},{62,54},{63,55},{1... | collective-permute-start | bytes 1572872 | tf_op jit(solution)/shard_map/ppermute | solution.py:47

commit v12 on v11

--- a/solution.py
+++ b/solution.py
@@ -99,6 +99,24 @@
     slot = (wanted // 2 - line) % lines + lines * (wanted % 2 != core).astype(jnp.int32)
     ordered = jnp.take(parts, slot, axis=0)
     return jnp.transpose(ordered, (1, 0, 2)).reshape(rows.shape[0], -1)
+
+
+def tip_pairs(count, half, base):
+    window = 2 * half
+    wanted = {}
+    for dest in range(count - window, count - half):
+        wanted[dest] = set(range(max(2 * count - 1 - window - dest, dest + half), count))
+    pairs, used = [], set()
+    for dest in sorted(wanted, key=lambda d: -len(wanted[d])):
+        for src in range(count - half, count):
+            held = set(range(src, count))
+            if src not in used and wanted[dest] <= held and wanted[dest] <= set(range(base, count)):
+                pairs.append((src, dest))
+                used.add(src)
+                break
+        else:
+            raise ValueError("no source")
+    return pairs
 
 
 def body(tokens, qkv_weight, doc_lengths, span_order):
@@ -133,6 +151,8 @@
     late_queries = lax.dynamic_slice_in_dim(query_rows, SPAN - offset, SPAN, 0)
 
     count = devices
+    half = WINDOW // 2
+    base = count - half // 2
     up = early_rows[None]
     down = jnp.stack([early_rows, late_rows])[None]
     reach = 1
@@ -143,14 +163,12 @@
         if 2 * reach < WINDOW:
             got = moved(down, count, [(d, d - reach) for d in range(count)])
         else:
-            tail = range(count - reach, count)
-            got = jnp.stack(
-                [
-                    moved(down[:, 0], count, [(d, d - reach) for d in tail]),
-                    moved(down[:, 1], count, [(d, d - reach) for d in range(count)]),
-                ],
-                axis=1,
-            )
+            padded = jnp.concatenate([jnp.zeros_like(down[: count - base, 0]), down[:, 0]], axis=0)
+            start = jnp.clip(count - my_index, 0, padded.shape[0] - (count - base))
+            tail_rows = lax.dynamic_slice_in_dim(padded, start, count - base, 0)
+            tip = moved(tail_rows, count, tip_pairs(count, half, base))
+            late = moved(down[:, 1], count, [(d, d - reach) for d in range(count)])
+            got = jnp.stack([jnp.zeros_like(late), late], axis=1)
         down = jnp.concatenate([down, got], axis=0)
         reach *= 2
     up = jnp.concatenate(
@@ -161,13 +179,16 @@
     early_keys = up.reshape(-1, up.shape[-1])
     steps = jnp.arange(WINDOW + 1, dtype=jnp.int32)
     source = 2 * count - 1 - my_index - steps
-    from_up = (my_index + steps > count - 1) & (source <= my_index)
-    up_row = jnp.where(from_up, my_index - source, 0)
-    down_block = jnp.where(my_index + steps <= count - 1, 2 * steps + 1, 2 * (source - my_index))
-    down_row = jnp.where(from_up, 0, down_block)
-    up_row = jnp.clip(up_row, 0, WINDOW) * SPAN
-    down_row = jnp.clip(down_row, 0, 2 * WINDOW + 1) * SPAN
+    own_late = my_index + steps <= count - 1
+    from_up = ~own_late & (source <= my_index)
+    from_tip = ~own_late & (source - my_index >= half)
+    kind = jnp.where(from_up, 1, jnp.where(from_tip, 2, 0)).astype(jnp.int32)
+    up_row = jnp.clip(jnp.where(from_up, my_index - source, 0), 0, WINDOW) * SPAN
+    down_block = jnp.where(own_late, 2 * steps + 1, 2 * (source - my_index))
+    down_row = jnp.clip(jnp.where(from_up | from_tip, 0, down_block), 0, 2 * WINDOW + 1) * SPAN
+    tip_row = jnp.clip(jnp.where(from_tip, source - base, 0), 0, count - base - 1) * SPAN
     down_keys = down.reshape(-1, down.shape[-1])
+    tip_keys = tip.reshape(-1, tip.shape[-1])
 
     steps = jnp.arange(WINDOW + 1, dtype=jnp.int32)
     query_spans = jnp.stack([my_index, 2 * devices - 1 - my_index])
@@ -186,13 +207,14 @@
 
     key_docs = jnp.where(key_ok, key_docs, -1)
     meta = jnp.concatenate(
-        [offset.reshape(1), from_up.astype(jnp.int32), up_row, down_row]
+        [offset.reshape(1), kind, up_row, down_row, tip_row]
     ).astype(jnp.int32)
     return attend(
         meta,
         query_rows,
         early_keys,
         down_keys,
+        tip_keys,
         query_places[:, :, None],
         query_docs[:, :, None],
         key_places[:, None, :],
@@ -201,17 +223,19 @@
 
 
 def attend_kernel(
-    meta_ref, q_ref, early_ref, down_ref, qpos_ref, qdoc_ref, kpos_ref, kdoc_ref, o_ref, late_ref
+    meta_ref, q_ref, early_ref, down_ref, tip_ref, qpos_ref, qdoc_ref, kpos_ref, kdoc_ref, o_ref, late_ref
 ):
     offset = pl.multiple_of(meta_ref[0], SPAN)
     blocks = WINDOW + 1
     for step in range(blocks):
+        kind = meta_ref[1 + step]
         up_row = pl.multiple_of(meta_ref[1 + blocks + step], SPAN)
         down_row = pl.multiple_of(meta_ref[1 + 2 * blocks + step], SPAN)
+        tip_row = pl.multiple_of(meta_ref[1 + 3 * blocks + step], SPAN)
         late_ref[step * SPAN : (step + 1) * SPAN, :] = jnp.where(
-            meta_ref[1 + step] > 0,
+            kind == 1,
             early_ref[pl.ds(up_row, SPAN), :],
-            down_ref[pl.ds(down_row, SPAN), :],
+            jnp.where(kind == 2, tip_ref[pl.ds(tip_row, SPAN), :], down_ref[pl.ds(down_row, SPAN), :]),
         )
     for span, kv_ref in ((0, early_ref), (1, late_ref)):
         row = offset if span == 0 else SPAN - offset
@@ -242,15 +266,15 @@
                 ]
 
 
-def attend(meta, query_rows, early_keys, down_keys, qpos, qdoc, kpos, kdoc):
+def attend(meta, query_rows, early_keys, down_keys, tip_keys, qpos, qdoc, kpos, kdoc):
     vmem = pl.BlockSpec(memory_space=pltpu.VMEM)
     return pl.pallas_call(
         attend_kernel,
         out_shape=jax.ShapeDtypeStruct(query_rows.shape, query_rows.dtype),
-        in_specs=[pl.BlockSpec(memory_space=pltpu.SMEM)] + [vmem] * 7,
+        in_specs=[pl.BlockSpec(memory_space=pltpu.SMEM)] + [vmem] * 8,
         out_specs=vmem,
         scratch_shapes=[pltpu.VMEM(early_keys.shape, early_keys.dtype)],
-    )(meta, query_rows, early_keys, down_keys, qpos, qdoc, kpos, kdoc)
+    )(meta, query_rows, early_keys, down_keys, tip_keys, qpos, qdoc, kpos, kdoc)
 
 def solution(mesh):
     placed = (P("seq", "ctx", None), P(None, "seq"), P("seq", None), P("seq", None))

time: 177 us -> 176 us (level)
  local copies, waits for them, and re-layouts: 10.4 us -> 6.93 us
  waiting for transfers between devices: 72.7 us -> 75.4 us
    ppermute x11, waiting for transfers between devices: 50.4 us -> 53.1 us  [moved(): return lax.ppermute(value, 'ctx', pairs)]
    unnamed x12 -> x17, local copies, waits for them, and re-layouts: 3.55 us -> 0.95 us
  transfers between devices with their start and end apart: 16 -> 16, of which waited for: 7 -> 8; matrix products, arithmetic and copies ran while one was open for 9% -> 7% of each run, Pallas kernels for 0% -> 0%
where the time goes in v12:
time: 176 us; the launch traced here: 174 us
  waiting for transfers between devices  75.4 us (43%)
  starting transfers between devices  73.2 us (42%)
  Pallas kernels  8.34 us (5%)
  local copies, waits for them, and re-layouts  6.93 us (4%)
  other arithmetic  5.31 us (3%)
  matrix products  3.42 us (2%)
    ppermute x11, waiting for transfers between devices, moved(): return lax.ppermute(value, 'ctx', pairs)  53.1 us
    ppermute x11, starting transfers between devices, moved(): return lax.ppermute(value, 'ctx', pairs)  52.6 us
    ppermute x3, waiting for transfers between devices, project(): lax.ppermute(weight, both, pairs_for(f))  22.1 us
    ppermute x3, starting transfers between devices, project(): lax.ppermute(weight, both, pairs_for(f))  16.8 us
    pallas_call x1, Pallas kernels, attend(): pl.pallas_call(attend_kernel, out_shape=jax.ShapeDtypeStruct(query_rows.s...  8.34 us
  transfers between devices with their start and end apart: 16, of which 8 were waited for; matrix products, arithmetic and copies ran while one was open for 7% of the time, Pallas kernels for 0%

profile of v12, /device:TPU:56, one launch (start us, length us, event | category | flops | bytes accessed | tf_op | source)
XLA Modules:
  0.0 173.8 jit_solution(10241477457933514449)
XLA Ops:
  0.0 4.3 %collective-permute-start.2 = (bf16[2048,192]{0,1:T(8,128)(2,1)}, bf16[2048,192]{0,1:T(8,128)(2,1)S(1)}, u32[]{:S(2)}, u32[]{:S(2)}) collective-permute-start(bf16[2048,192]{0,1:T(8,128)(2,1)} %param.5), channel_id=1, source_target_pairs={{416,0},{417,1},{418,2},{419,3},{420,4},{421,5},{422,6},{423,7},{4... | collective-permute-start | bytes 2359304 | tf_op jit(solution)/shard_map/ppermute | solution.py:91
  4.3 10.0 %collective-permute-start.1 = (bf16[2048,192]{0,1:T(8,128)(2,1)}, bf16[2048,192]{0,1:T(8,128)(2,1)S(1)}, u32[]{:S(2)}, u32[]{:S(2)}) collective-permute-start(bf16[2048,192]{0,1:T(8,128)(2,1)} %param.5), channel_id=1, source_target_pairs={{256,0},{257,1},{258,2},{259,3},{260,4},{261,5},{262,6},{263,7},{2... | collective-permute-start | bytes 2359304 | tf_op jit(solution)/shard_map/ppermute | solution.py:91
  14.3 2.5 %collective-permute-start = (bf16[2048,192]{0,1:T(8,128)(2,1)}, bf16[2048,192]{0,1:T(8,128)(2,1)S(1)}, u32[]{:S(2)}, u32[]{:S(2)}) collective-permute-start(bf16[2048,192]{0,1:T(8,128)(2,1)} %param.5), channel_id=1, source_target_pairs={{128,0},{129,1},{130,2},{131,3},{132,4},{133,5},{134,6},{135,7},{1... | collective-permute-start | bytes 2359304 | tf_op jit(solution)/shard_map/ppermute | solution.py:91
  16.8 1.9 %collective-permute-start.3 = (bf16[128,2048]{1,0:T(8,128)(2,1)}, bf16[128,2048]{1,0:T(8,128)(2,1)S(1)}, u32[]{:S(2)}, u32[]{:S(2)}) collective-permute-start(bf16[128,2048]{1,0:T(8,128)(2,1)} %bitcast.91), channel_id=1, source_target_pairs={{64,0},{65,1},{66,2},{67,3},{68,4},{69,5},{70,6},{71,7},{72,8},{73... | collective-permute-start | bytes 1572872 | tf_op jit(solution)/shard_map/ppermute | solution.py:90
  18.9 0.7 iota_add_fusion.qpos_ref
  20.0 0.7 multiply_bitcast_fusion
  20.7 1.3 fusion.25
  22.9 0.8 copy.75
  23.7 0.1 reduce
  23.8 0.1 fusion.9
  24.0 0.7 copy.80.qdoc_ref
  24.8 0.1 reshape.402
  24.9 0.3 fusion.4
  25.3 0.6 concatenate.54.meta_ref
  25.9 0.1 multiply_cosine_fusion
  26.0 0.6 reshape_select_fusion
  26.7 3.4 %collective-permute-done.2 = bf16[2048,192]{0,1:T(8,128)(2,1)S(1)} collective-permute-done((bf16[2048,192]{0,1:T(8,128)(2,1)}, bf16[2048,192]{0,1:T(8,128)(2,1)S(1)}, u32[]{:S(2)}, u32[]{:S(2)}) %collective-permute-start.2) | collective-permute-done | bytes 786464 | tf_op jit(solution)/shard_map/ppermute | solution.py:91
  30.0 10.3 %collective-permute-done.1 = bf16[2048,192]{0,1:T(8,128)(2,1)S(1)} collective-permute-done((bf16[2048,192]{0,1:T(8,128)(2,1)}, bf16[2048,192]{0,1:T(8,128)(2,1)S(1)}, u32[]{:S(2)}, u32[]{:S(2)}) %collective-permute-start.1) | collective-permute-done | bytes 786464 | tf_op jit(solution)/shard_map/ppermute | solution.py:91
  40.3 8.4 %collective-permute-done = bf16[2048,192]{0,1:T(8,128)(2,1)S(1)} collective-permute-done((bf16[2048,192]{0,1:T(8,128)(2,1)}, bf16[2048,192]{0,1:T(8,128)(2,1)S(1)}, u32[]{:S(2)}, u32[]{:S(2)}) %collective-permute-start) | collective-permute-done | bytes 786464 | tf_op jit(solution)/shard_map/ppermute | solution.py:91
  48.8 2.2 %fusion.1 = bf16[4,128,192]{1,2,0:T(8,128)(2,1)S(1)} fusion(bf16[1,2048,192]{1,2,0:T(8,128)(2,1)S(1)} %bitcast.85, bf16[1,2048,192]{1,2,0:T(8,128)(2,1)S(1)} %bitcast.87, bf16[1,2048,192]{1,2,0:T(8,128)(2,1)S(1)} %bitcast.89, bf16[1,2048,192]{1,2,0:T(8,128)(2,1)} %bitcast.83, bf16[128,2048]{1,0:T(8,128)(2,1)S(1)} %collective-permute-done.3), kind=kOutput, calls=%fused_computation.5 | convolution fusion | flops 407470080 | bytes 3866624 | tf_op jit(solution)/shard_map/td,bdn->btn/dot_general | solution.py:93
  51.0 1.9 %collective-permute-start.4 = (bf16[4,128,192]{1,2,0:T(8,128)(2,1)S(1)}, bf16[4,128,192]{1,2,0:T(8,128)(2,1)S(1)}, u32[]{:S(2)}, u32[]{:S(2)}) collective-permute-start(bf16[4,128,192]{1,2,0:T(8,128)(2,1)S(1)} %fusion.1), channel_id=1, source_target_pairs={{64,0},{65,1},{66,2},{67,3},{68,4},{69,5},{70,6},{71,7},{72,8},{73... | collective-permute-start | bytes 589832 | tf_op jit(solution)/shard_map/ppermute | solution.py:94
  52.9 1.2 fusion
  54.1 0.2 collective-permute-done.4
  54.4 0.6 gather_fusion
  55.0 0.1 broadcast_select_fusion
  55.2 0.1 fusion.5
  55.4 0.1 copy.65
  55.5 3.4 %collective-permute-start.5 = (bf16[1,64,512]{2,1,0:T(8,128)(2,1)S(1)}, bf16[1,64,512]{2,1,0:T(8,128)(2,1)S(1)}, u32[]{:S(2)}, u32[]{:S(2)}) collective-permute-start(bf16[1,64,512]{2,1,0:T(8,128)(2,1)S(1)} %bitcast.59), channel_id=1, source_target_pairs={{0,1},{1,2},{2,3},{3,4},{4,5},{5,6},{6,7},{7,8},{8,9},{9,10},{10,1... | collective-permute-start | bytes 196616 | tf_op jit(solution)/shard_map/ppermute | solution.py:47
  58.9 8.1 %collective-permute-start.9 = (bf16[1,64,512]{2,1,0:T(8,128)(2,1)S(1)}, bf16[1,64,512]{2,1,0:T(8,128)(2,1)S(1)}, u32[]{:S(2)}, u32[]{:S(2)}) collective-permute-start(bf16[1,64,512]{2,1,0:T(8,128)(2,1)S(1)} %bitcast.60), channel_id=1, source_target_pairs={{0,16},{1,17},{2,18},{3,19},{4,20},{5,21},{6,22},{7,23},{8,24},{9,... | collective-permute-start | bytes 196616 | tf_op jit(solution)/shard_map/ppermute | solution.py:47
  67.1 0.1 copy.66
  67.2 1.9 %collective-permute-start.14 = (bf16[1,64,512]{2,1,0:T(8,128)(2,1)S(1)}, bf16[1,64,512]{2,1,0:T(8,128)(2,1)S(1)}, u32[]{:S(2)}, u32[]{:S(2)}) collective-permute-start(bf16[1,64,512]{2,1,0:T(8,128)(2,1)S(1)} %bitcast.73), channel_id=1, source_target_pairs={{16,0},{17,1},{18,2},{19,3},{20,4},{21,5},{22,6},{23,7},{24,8},{25... | collective-permute-start | bytes 196616 | tf_op jit(solution)/shard_map/ppermute | solution.py:47
  69.2 4.6 %collective-permute-start.10 = (bf16[1,2,64,512]{3,2,0,1:T(8,128)(2,1)S(1)}, bf16[1,2,64,512]{3,2,0,1:T(8,128)(2,1)S(1)}, u32[]{:S(2)}, u32[]{:S(2)}) collective-permute-start(bf16[1,2,64,512]{3,2,0,1:T(8,128)(2,1)S(1)} %get-tuple-element.16), channel_id=1, source_target_pairs={{1,0},{2,1},{3,2},{4,3},{5,4},{6,5},{7,6},{8,7},{9,8},{10,9},{11,1... | collective-permute-start | bytes 393224 | tf_op jit(solution)/shard_map/ppermute | solution.py:47
  73.8 0.8 copy.79.q_ref
  74.6 2.8 %collective-permute-start.6 = (bf16[2,64,512]{2,1,0:T(8,128)(2,1)S(1)}, bf16[2,64,512]{2,1,0:T(8,128)(2,1)S(1)}, u32[]{:S(2)}, u32[]{:S(2)}) collective-permute-start(bf16[2,64,512]{2,1,0:T(8,128)(2,1)S(1)} %get-tuple-element.19), channel_id=1, source_target_pairs={{0,2},{1,3},{2,4},{3,5},{4,6},{5,7},{6,8},{7,9},{8,10},{9,11},{10,... | collective-permute-start | bytes 393224 | tf_op jit(solution)/shard_map/ppermute | solution.py:47
  77.5 5.4 %collective-permute-start.11 = (bf16[2,2,64,512]{3,2,1,0:T(8,128)(2,1)S(1)}, bf16[2,2,64,512]{3,2,1,0:T(8,128)(2,1)S(1)}, u32[]{:S(2)}, u32[]{:S(2)}) collective-permute-start(bf16[2,2,64,512]{3,2,1,0:T(8,128)(2,1)S(1)} %pad_maximum_fusion.9), channel_id=1, source_target_pairs={{2,0},{3,1},{4,2},{5,3},{6,4},{7,5},{8,6},{9,7},{10,8},{11,9},{12,... | collective-permute-start | bytes 786440 | tf_op jit(solution)/shard_map/ppermute | solution.py:47
  82.9 0.9 collective-permute-done.6
  83.9 18.6 %collective-permute-start.7 = (bf16[4,64,512]{2,1,0:T(8,128)(2,1)S(1)}, bf16[4,64,512]{2,1,0:T(8,128)(2,1)S(1)}, u32[]{:S(2)}, u32[]{:S(2)}) collective-permute-start(bf16[4,64,512]{2,1,0:T(8,128)(2,1)S(1)} %pad_maximum_fusion.8), channel_id=1, source_target_pairs={{0,4},{1,5},{2,6},{3,7},{4,8},{5,9},{6,10},{7,11},{8,12},{9,13},{1... | collective-permute-start | bytes 786440 | tf_op jit(solution)/shard_map/ppermute | solution.py:47
  102.6 1.9 %collective-permute-start.12 = (bf16[4,2,64,512]{3,2,1,0:T(8,128)(2,1)S(1)}, bf16[4,2,64,512]{3,2,1,0:T(8,128)(2,1)S(1)}, u32[]{:S(2)}, u32[]{:S(2)}) collective-permute-start(bf16[4,2,64,512]{3,2,1,0:T(8,128)(2,1)S(1)} %pad_maximum_fusion.5), channel_id=1, source_target_pairs={{4,0},{5,1},{6,2},{7,3},{8,4},{9,5},{10,6},{11,7},{12,8},{13,9},{1... | collective-permute-start | bytes 1572872 | tf_op jit(solution)/shard_map/ppermute | solution.py:47
  104.5 2.4 %collective-permute-done.7 = bf16[4,64,512]{2,1,0:T(8,128)(2,1)S(1)} collective-permute-done((bf16[4,64,512]{2,1,0:T(8,128)(2,1)S(1)}, bf16[4,64,512]{2,1,0:T(8,128)(2,1)S(1)}, u32[]{:S(2)}, u32[]{:S(2)}) %collective-permute-start.7) | collective-permute-done | bytes 262176 | tf_op jit(solution)/shard_map/ppermute | solution.py:47
  107.0 3.3 %collective-permute-start.8 = (bf16[8,64,512]{2,1,0:T(8,128)(2,1)S(1)}, bf16[8,64,512]{2,1,0:T(8,128)(2,1)S(1)}, u32[]{:S(2)}, u32[]{:S(2)}) collective-permute-start(bf16[8,64,512]{2,1,0:T(8,128)(2,1)S(1)} %pad_maximum_fusion.4), channel_id=1, source_target_pairs={{0,8},{1,9},{2,10},{3,11},{4,12},{5,13},{6,14},{7,15},{8,16},{9,17... | collective-permute-start | bytes 1572872 | tf_op jit(solution)/shard_map/ppermute | solution.py:47
  110.4 21.0 %collective-permute-done.12 = bf16[4,2,64,512]{3,2,1,0:T(8,128)(2,1)S(1)} collective-permute-done((bf16[4,2,64,512]{3,2,1,0:T(8,128)(2,1)S(1)}, bf16[4,2,64,512]{3,2,1,0:T(8,128)(2,1)S(1)}, u32[]{:S(2)}, u32[]{:S(2)}) %collective-permute-start.12) | collective-permute-done | bytes 524320 | tf_op jit(solution)/shard_map/ppermute | solution.py:47
  131.4 0.1 pad_maximum_fusion.1
  131.6 1.9 %collective-permute-start.13 = (bf16[8,64,512]{2,1,0:T(8,128)(2,1)S(1)}, bf16[8,64,512]{2,1,0:T(8,128)(2,1)S(1)}, u32[]{:S(2)}, u32[]{:S(2)}) collective-permute-start(bf16[8,64,512]{2,1,0:T(8,128)(2,1)S(1)} %get-tuple-element.8), channel_id=1, source_target_pairs={{8,0},{9,1},{10,2},{11,3},{12,4},{13,5},{14,6},{15,7},{16,8},{17,9... | collective-permute-start | bytes 1572872 | tf_op jit(solution)/shard_map/ppermute | solution.py:47
  133.6 0.7 collective-permute-start.15
  134.4 28.7 %collective-permute-done.13 = bf16[8,64,512]{2,1,0:T(8,128)(2,1)S(1)} collective-permute-done((bf16[8,64,512]{2,1,0:T(8,128)(2,1)S(1)}, bf16[8,64,512]{2,1,0:T(8,128)(2,1)S(1)}, u32[]{:S(2)}, u32[]{:S(2)}) %collective-permute-start.13) | collective-permute-done | bytes 524320 | tf_op jit(solution)/shard_map/ppermute | solution.py:47
  163.2 1.5 copy.74
  164.8 0.7 copy-done.1
  165.5 8.3 %shard_map.46 = bf16[128,1024]{1,0:T(8,128)(2,1)} custom-call(s32[69]{0:T(128)} %concatenate.54.meta_ref, bf16[128,1024]{1,0:T(8,128)(2,1)} %copy.79.q_ref, bf16[1088,512]{1,0:T(8,128)(2,1)} %bitcast.70, bf16[2176,512]{1,0:T(8,128)(2,1)} %bitcast.58, bf16[256,512]{1,0:T(8,128)(2,1)} %bitcast.77, s32[2,64,1]{2,1,0:T(8,128)} %iota_add_fusion.qpos_ref, ...), custom_call_target="tpu_custom_call" | custom-call | tf_op jit(solution)/shard_map/pallas_call | solution.py:271
  (64 shorter events, 1.9 us)
Async XLA Ops:
  0.0 30.0 %collective-permute-start.2 = (bf16[2048,192]{0,1:T(8,128)(2,1)}, bf16[2048,192]{0,1:T(8,128)(2,1)S(1)}, u32[]{:S(2)}, u32[]{:S(2)}) collective-permute-start(bf16[2048,192]{0,1:T(8,128)(2,1)} %param.5), channel_id=1, source_target_pairs={{416,0},{417,1},{418,2},{419,3},{420,4},{421,5},{422,6},{423,7},{4... | collective-permute-start | bytes 2359304 | tf_op jit(solution)/shard_map/ppermute | solution.py:91
  4.3 36.0 %collective-permute-start.1 = (bf16[2048,192]{0,1:T(8,128)(2,1)}, bf16[2048,192]{0,1:T(8,128)(2,1)S(1)}, u32[]{:S(2)}, u32[]{:S(2)}) collective-permute-start(bf16[2048,192]{0,1:T(8,128)(2,1)} %param.5), channel_id=1, source_target_pairs={{256,0},{257,1},{258,2},{259,3},{260,4},{261,5},{262,6},{263,7},{2... | collective-permute-start | bytes 2359304 | tf_op jit(solution)/shard_map/ppermute | solution.py:91
  14.3 34.4 %collective-permute-start = (bf16[2048,192]{0,1:T(8,128)(2,1)}, bf16[2048,192]{0,1:T(8,128)(2,1)S(1)}, u32[]{:S(2)}, u32[]{:S(2)}) collective-permute-start(bf16[2048,192]{0,1:T(8,128)(2,1)} %param.5), channel_id=1, source_target_pairs={{128,0},{129,1},{130,2},{131,3},{132,4},{133,5},{134,6},{135,7},{1... | collective-permute-start | bytes 2359304 | tf_op jit(solution)/shard_map/ppermute | solution.py:91
  16.8 9.9 %collective-permute-start.3 = (bf16[128,2048]{1,0:T(8,128)(2,1)}, bf16[128,2048]{1,0:T(8,128)(2,1)S(1)}, u32[]{:S(2)}, u32[]{:S(2)}) collective-permute-start(bf16[128,2048]{1,0:T(8,128)(2,1)} %bitcast.91), channel_id=1, source_target_pairs={{64,0},{65,1},{66,2},{67,3},{68,4},{69,5},{70,6},{71,7},{72,8},{73... | collective-permute-start | bytes 1572872 | tf_op jit(solution)/shard_map/ppermute | solution.py:90
  48.8 4.2 %copy-start.2 = (bf16[2048,192]{0,1:T(8,128)(2,1)S(1)}, bf16[2048,192]{0,1:T(8,128)(2,1)}, u32[]{:S(2)}) copy-start(bf16[2048,192]{0,1:T(8,128)(2,1)} %param.5) | copy-start | bytes 2359300
  48.8 4.2 %copy-start.3 = (bf16[1,128,2048]{2,1,0:T(8,128)(2,1)S(1)}, bf16[1,128,2048]{2,1,0:T(8,128)(2,1)}, u32[]{:S(2)}) copy-start(bf16[1,128,2048]{2,1,0:T(8,128)(2,1)} %param.4) | copy-start | bytes 1572868
  51.0 3.3 %collective-permute-start.4 = (bf16[4,128,192]{1,2,0:T(8,128)(2,1)S(1)}, bf16[4,128,192]{1,2,0:T(8,128)(2,1)S(1)}, u32[]{:S(2)}, u32[]{:S(2)}) collective-permute-start(bf16[4,128,192]{1,2,0:T(8,128)(2,1)S(1)} %fusion.1), channel_id=1, source_target_pairs={{64,0},{65,1},{66,2},{67,3},{68,4},{69,5},{70,6},{71,7},{72,8},{73... | collective-permute-start | bytes 589832 | tf_op jit(solution)/shard_map/ppermute | solution.py:94
  55.5 13.7 %collective-permute-start.5 = (bf16[1,64,512]{2,1,0:T(8,128)(2,1)S(1)}, bf16[1,64,512]{2,1,0:T(8,128)(2,1)S(1)}, u32[]{:S(2)}, u32[]{:S(2)}) collective-permute-start(bf16[1,64,512]{2,1,0:T(8,128)(2,1)S(1)} %bitcast.59), channel_id=1, source_target_pairs={{0,1},{1,2},{2,3},{3,4},{4,5},{5,6},{6,7},{7,8},{8,9},{9,10},{10,1... | collective-permute-start | bytes 196616 | tf_op jit(solution)/shard_map/ppermute | solution.py:47
  58.9 75.5 %collective-permute-start.9 = (bf16[1,64,512]{2,1,0:T(8,128)(2,1)S(1)}, bf16[1,64,512]{2,1,0:T(8,128)(2,1)S(1)}, u32[]{:S(2)}, u32[]{:S(2)}) collective-permute-start(bf16[1,64,512]{2,1,0:T(8,128)(2,1)S(1)} %bitcast.60), channel_id=1, source_target_pairs={{0,16},{1,17},{2,18},{3,19},{4,20},{5,21},{6,22},{7,23},{8,24},{9,... | collective-permute-start | bytes 196616 | tf_op jit(solution)/shard_map/ppermute | solution.py:47
  67.2 96.0 %collective-permute-start.14 = (bf16[1,64,512]{2,1,0:T(8,128)(2,1)S(1)}, bf16[1,64,512]{2,1,0:T(8,128)(2,1)S(1)}, u32[]{:S(2)}, u32[]{:S(2)}) collective-permute-start(bf16[1,64,512]{2,1,0:T(8,128)(2,1)S(1)} %bitcast.73), channel_id=1, source_target_pairs={{16,0},{17,1},{18,2},{19,3},{20,4},{21,5},{22,6},{23,7},{24,8},{25... | collective-permute-start | bytes 196616 | tf_op jit(solution)/shard_map/ppermute | solution.py:47
  69.2 8.3 %collective-permute-start.10 = (bf16[1,2,64,512]{3,2,0,1:T(8,128)(2,1)S(1)}, bf16[1,2,64,512]{3,2,0,1:T(8,128)(2,1)S(1)}, u32[]{:S(2)}, u32[]{:S(2)}) collective-permute-start(bf16[1,2,64,512]{3,2,0,1:T(8,128)(2,1)S(1)} %get-tuple-element.16), channel_id=1, source_target_pairs={{1,0},{2,1},{3,2},{4,3},{5,4},{6,5},{7,6},{8,7},{9,8},{10,9},{11,1... | collective-permute-start | bytes 393224 | tf_op jit(solution)/shard_map/ppermute | solution.py:47
  74.6 9.3 %collective-permute-start.6 = (bf16[2,64,512]{2,1,0:T(8,128)(2,1)S(1)}, bf16[2,64,512]{2,1,0:T(8,128)(2,1)S(1)}, u32[]{:S(2)}, u32[]{:S(2)}) collective-permute-start(bf16[2,64,512]{2,1,0:T(8,128)(2,1)S(1)} %get-tuple-element.19), channel_id=1, source_target_pairs={{0,2},{1,3},{2,4},{3,5},{4,6},{5,7},{6,8},{7,9},{8,10},{9,11},{10,... | collective-permute-start | bytes 393224 | tf_op jit(solution)/shard_map/ppermute | solution.py:47
  77.5 25.0 %collective-permute-start.11 = (bf16[2,2,64,512]{3,2,1,0:T(8,128)(2,1)S(1)}, bf16[2,2,64,512]{3,2,1,0:T(8,128)(2,1)S(1)}, u32[]{:S(2)}, u32[]{:S(2)}) collective-permute-start(bf16[2,2,64,512]{3,2,1,0:T(8,128)(2,1)S(1)} %pad_maximum_fusion.9), channel_id=1, source_target_pairs={{2,0},{3,1},{4,2},{5,3},{6,4},{7,5},{8,6},{9,7},{10,8},{11,9},{12,... | collective-permute-start | bytes 786440 | tf_op jit(solution)/shard_map/ppermute | solution.py:47
  83.9 23.1 %collective-permute-start.7 = (bf16[4,64,512]{2,1,0:T(8,128)(2,1)S(1)}, bf16[4,64,512]{2,1,0:T(8,128)(2,1)S(1)}, u32[]{:S(2)}, u32[]{:S(2)}) collective-permute-start(bf16[4,64,512]{2,1,0:T(8,128)(2,1)S(1)} %pad_maximum_fusion.8), channel_id=1, source_target_pairs={{0,4},{1,5},{2,6},{3,7},{4,8},{5,9},{6,10},{7,11},{8,12},{9,13},{1... | collective-permute-start | bytes 786440 | tf_op jit(solution)/shard_map/ppermute | solution.py:47
  102.6 28.8 %collective-permute-start.12 = (bf16[4,2,64,512]{3,2,1,0:T(8,128)(2,1)S(1)}, bf16[4,2,64,512]{3,2,1,0:T(8,128)(2,1)S(1)}, u32[]{:S(2)}, u32[]{:S(2)}) collective-permute-start(bf16[4,2,64,512]{3,2,1,0:T(8,128)(2,1)S(1)} %pad_maximum_fusion.5), channel_id=1, source_target_pairs={{4,0},{5,1},{6,2},{7,3},{8,4},{9,5},{10,6},{11,7},{12,8},{13,9},{1... | collective-permute-start | bytes 1572872 | tf_op jit(solution)/shard_map/ppermute | solution.py:47
  107.0 27.3 %collective-permute-start.8 = (bf16[8,64,512]{2,1,0:T(8,128)(2,1)S(1)}, bf16[8,64,512]{2,1,0:T(8,128)(2,1)S(1)}, u32[]{:S(2)}, u32[]{:S(2)}) collective-permute-start(bf16[8,64,512]{2,1,0:T(8,128)(2,1)S(1)} %pad_maximum_fusion.4), channel_id=1, source_target_pairs={{0,8},{1,9},{2,10},{3,11},{4,12},{5,13},{6,14},{7,15},{8,16},{9,17... | collective-permute-start | bytes 1572872 | tf_op jit(solution)/shard_map/ppermute | solution.py:47
  131.6 31.5 %collective-permute-start.13 = (bf16[8,64,512]{2,1,0:T(8,128)(2,1)S(1)}, bf16[8,64,512]{2,1,0:T(8,128)(2,1)S(1)}, u32[]{:S(2)}, u32[]{:S(2)}) collective-permute-start(bf16[8,64,512]{2,1,0:T(8,128)(2,1)S(1)} %get-tuple-element.8), channel_id=1, source_target_pairs={{8,0},{9,1},{10,2},{11,3},{12,4},{13,5},{14,6},{15,7},{16,8},{17,9... | collective-permute-start | bytes 1572872 | tf_op jit(solution)/shard_map/ppermute | solution.py:47
  133.6 31.2 %collective-permute-start.15 = (bf16[4,64,512]{2,1,0:T(8,128)(2,1)S(1)}, bf16[4,64,512]{2,1,0:T(8,128)(2,1)S(1)}, u32[]{:S(2)}, u32[]{:S(2)}) collective-permute-start(bf16[4,64,512]{2,1,0:T(8,128)(2,1)S(1)} %pad_dynamic-slice_fusion), channel_id=1, source_target_pairs={{56,51},{57,52},{58,50},{59,53},{60,49},{61,54},{62,48},{63,55},{1... | collective-permute-start | bytes 786440 | tf_op jit(solution)/shard_map/ppermute | solution.py:47
  134.4 30.3 %copy-start = (bf16[17,64,512]{2,1,0:T(8,128)(2,1)}, bf16[17,64,512]{2,1,0:T(8,128)(2,1)S(1)}, u32[]{:S(2)}) copy-start(bf16[17,64,512]{2,1,0:T(8,128)(2,1)S(1)} %constant_dynamic-update-slice_fusion) | copy-start | bytes 3342340
  164.8 0.7 copy-start.1

commit v13 on v12

--- a/solution.py
+++ b/solution.py
@@ -53,7 +53,7 @@
     return line, core, half, rest
 
 
-def device_of(line, core, half, rest, lanes, lines):
+def device_of(line, core, half, rest, lanes):
     return (2 * line + core) * lanes + half * (lanes // 2) + rest
 
 
@@ -69,14 +69,14 @@
             line, core, half, rest = chip_of(dest, lanes)
             level = half * lines + line + offset(core)
             level %= 2 * lines
-            found.append((device_of(level % lines, core, level // lines, rest, lanes, lines), dest))
+            found.append((device_of(level % lines, core, level // lines, rest, lanes), dest))
         return found
 
     def mate_pairs():
         found = []
         for dest in range(total):
             line, core, half, rest = chip_of(dest, lanes)
-            found.append((device_of(line, 1 - core, half, rest, lanes, lines), dest))
+            found.append((device_of(line, 1 - core, half, rest, lanes), dest))
         return found
 
     step = [lambda core: 0]
@@ -140,7 +140,6 @@
         token_positions,
     ).astype(jnp.bfloat16)
     value_rows = query_key_value[:, (QUERY_HEADS + KEY_VALUE_HEADS) * HEAD_SIZE :]
-    key_cols = key_rows.shape[1]
     stacked = jnp.concatenate([key_rows, value_rows], axis=1)
 
     early_first = order_row[2 * my_index] < devices
@@ -157,9 +156,7 @@
     down = jnp.stack([early_rows, late_rows])[None]
     reach = 1
     while reach < WINDOW:
-        up = jnp.concatenate(
-            [up, moved(up, count, [(d, d + reach) for d in range(count)])], axis=0
-        )
+        up = jnp.concatenate([up, moved(up, count, [(d, d + reach) for d in range(count)])], axis=0)
         if 2 * reach < WINDOW:
             got = moved(down, count, [(d, d - reach) for d in range(count)])
         else:
@@ -199,11 +196,6 @@
     query_places = query_spans[:, None] * SPAN + ramp[None, :]
     key_docs = documents(lengths_row, key_places)
     query_docs = documents(lengths_row, query_places)
-    live = (
-        (query_docs[:, :, None] == key_docs[:, None, :])
-        & (key_places[:, None, :] <= query_places[:, :, None])
-        & key_ok[:, None, :]
-    )
 
     key_docs = jnp.where(key_ok, key_docs, -1)
     meta = jnp.concatenate(
@@ -276,6 +268,7 @@
         scratch_shapes=[pltpu.VMEM(early_keys.shape, early_keys.dtype)],
     )(meta, query_rows, early_keys, down_keys, tip_keys, qpos, qdoc, kpos, kdoc)
 
+
 def solution(mesh):
     placed = (P("seq", "ctx", None), P(None, "seq"), P("seq", None), P("seq", None))
     return jax.shard_map(

time: 176 us -> 176 us (level)
  no operation moved by 1% of the time
where the time goes in v13:
time: 176 us; the launch traced here: 174 us
  waiting for transfers between devices  75.4 us (43%)
  starting transfers between devices  73.2 us (42%)
  Pallas kernels  8.34 us (5%)
  local copies, waits for them, and re-layouts  6.93 us (4%)
  other arithmetic  5.31 us (3%)
  matrix products  3.42 us (2%)
    ppermute x11, waiting for transfers between devices, moved(): return lax.ppermute(value, 'ctx', pairs)  53.1 us
    ppermute x11, starting transfers between devices, moved(): return lax.ppermute(value, 'ctx', pairs)  52.6 us
    ppermute x3, waiting for transfers between devices, project(): lax.ppermute(weight, both, pairs_for(f))  22.1 us
    ppermute x3, starting transfers between devices, project(): lax.ppermute(weight, both, pairs_for(f))  16.8 us
    pallas_call x1, Pallas kernels, attend(): pl.pallas_call(attend_kernel, out_shape=jax.ShapeDtypeStruct(query_rows.s...  8.34 us
  transfers between devices with their start and end apart: 16, of which 8 were waited for; matrix products, arithmetic and copies ran while one was open for 7% of the time, Pallas kernels for 0%

profile of v13, /device:TPU:56, one launch (start us, length us, event | category | flops | bytes accessed | tf_op | source)
XLA Modules:
  0.0 173.8 jit_solution(10241477457933514449)
XLA Ops:
  0.0 4.3 %collective-permute-start.2 = (bf16[2048,192]{0,1:T(8,128)(2,1)}, bf16[2048,192]{0,1:T(8,128)(2,1)S(1)}, u32[]{:S(2)}, u32[]{:S(2)}) collective-permute-start(bf16[2048,192]{0,1:T(8,128)(2,1)} %param.5), channel_id=1, source_target_pairs={{416,0},{417,1},{418,2},{419,3},{420,4},{421,5},{422,6},{423,7},{4... | collective-permute-start | bytes 2359304 | tf_op jit(solution)/shard_map/ppermute | solution.py:91
  4.3 10.0 %collective-permute-start.1 = (bf16[2048,192]{0,1:T(8,128)(2,1)}, bf16[2048,192]{0,1:T(8,128)(2,1)S(1)}, u32[]{:S(2)}, u32[]{:S(2)}) collective-permute-start(bf16[2048,192]{0,1:T(8,128)(2,1)} %param.5), channel_id=1, source_target_pairs={{256,0},{257,1},{258,2},{259,3},{260,4},{261,5},{262,6},{263,7},{2... | collective-permute-start | bytes 2359304 | tf_op jit(solution)/shard_map/ppermute | solution.py:91
  14.3 2.5 %collective-permute-start = (bf16[2048,192]{0,1:T(8,128)(2,1)}, bf16[2048,192]{0,1:T(8,128)(2,1)S(1)}, u32[]{:S(2)}, u32[]{:S(2)}) collective-permute-start(bf16[2048,192]{0,1:T(8,128)(2,1)} %param.5), channel_id=1, source_target_pairs={{128,0},{129,1},{130,2},{131,3},{132,4},{133,5},{134,6},{135,7},{1... | collective-permute-start | bytes 2359304 | tf_op jit(solution)/shard_map/ppermute | solution.py:91
  16.8 1.9 %collective-permute-start.3 = (bf16[128,2048]{1,0:T(8,128)(2,1)}, bf16[128,2048]{1,0:T(8,128)(2,1)S(1)}, u32[]{:S(2)}, u32[]{:S(2)}) collective-permute-start(bf16[128,2048]{1,0:T(8,128)(2,1)} %bitcast.91), channel_id=1, source_target_pairs={{64,0},{65,1},{66,2},{67,3},{68,4},{69,5},{70,6},{71,7},{72,8},{73... | collective-permute-start | bytes 1572872 | tf_op jit(solution)/shard_map/ppermute | solution.py:90
  18.9 0.7 iota_add_fusion.qpos_ref
  20.0 0.7 multiply_bitcast_fusion
  20.7 1.3 fusion.25
  22.9 0.8 copy.75
  23.7 0.1 reduce
  23.8 0.1 fusion.9
  24.0 0.7 copy.80.qdoc_ref
  24.8 0.1 reshape.402
  24.9 0.3 fusion.4
  25.3 0.6 concatenate.54.meta_ref
  25.9 0.1 multiply_cosine_fusion
  26.0 0.6 reshape_select_fusion
  26.7 3.4 %collective-permute-done.2 = bf16[2048,192]{0,1:T(8,128)(2,1)S(1)} collective-permute-done((bf16[2048,192]{0,1:T(8,128)(2,1)}, bf16[2048,192]{0,1:T(8,128)(2,1)S(1)}, u32[]{:S(2)}, u32[]{:S(2)}) %collective-permute-start.2) | collective-permute-done | bytes 786464 | tf_op jit(solution)/shard_map/ppermute | solution.py:91
  30.0 10.3 %collective-permute-done.1 = bf16[2048,192]{0,1:T(8,128)(2,1)S(1)} collective-permute-done((bf16[2048,192]{0,1:T(8,128)(2,1)}, bf16[2048,192]{0,1:T(8,128)(2,1)S(1)}, u32[]{:S(2)}, u32[]{:S(2)}) %collective-permute-start.1) | collective-permute-done | bytes 786464 | tf_op jit(solution)/shard_map/ppermute | solution.py:91
  40.3 8.4 %collective-permute-done = bf16[2048,192]{0,1:T(8,128)(2,1)S(1)} collective-permute-done((bf16[2048,192]{0,1:T(8,128)(2,1)}, bf16[2048,192]{0,1:T(8,128)(2,1)S(1)}, u32[]{:S(2)}, u32[]{:S(2)}) %collective-permute-start) | collective-permute-done | bytes 786464 | tf_op jit(solution)/shard_map/ppermute | solution.py:91
  48.8 2.2 %fusion.1 = bf16[4,128,192]{1,2,0:T(8,128)(2,1)S(1)} fusion(bf16[1,2048,192]{1,2,0:T(8,128)(2,1)S(1)} %bitcast.85, bf16[1,2048,192]{1,2,0:T(8,128)(2,1)S(1)} %bitcast.87, bf16[1,2048,192]{1,2,0:T(8,128)(2,1)S(1)} %bitcast.89, bf16[1,2048,192]{1,2,0:T(8,128)(2,1)} %bitcast.83, bf16[128,2048]{1,0:T(8,128)(2,1)S(1)} %collective-permute-done.3), kind=kOutput, calls=%fused_computation.5 | convolution fusion | flops 407470080 | bytes 3866624 | tf_op jit(solution)/shard_map/td,bdn->btn/dot_general | solution.py:93
  51.0 1.9 %collective-permute-start.4 = (bf16[4,128,192]{1,2,0:T(8,128)(2,1)S(1)}, bf16[4,128,192]{1,2,0:T(8,128)(2,1)S(1)}, u32[]{:S(2)}, u32[]{:S(2)}) collective-permute-start(bf16[4,128,192]{1,2,0:T(8,128)(2,1)S(1)} %fusion.1), channel_id=1, source_target_pairs={{64,0},{65,1},{66,2},{67,3},{68,4},{69,5},{70,6},{71,7},{72,8},{73... | collective-permute-start | bytes 589832 | tf_op jit(solution)/shard_map/ppermute | solution.py:94
  52.9 1.2 fusion
  54.1 0.2 collective-permute-done.4
  54.4 0.6 gather_fusion
  55.0 0.1 broadcast_select_fusion
  55.2 0.1 fusion.5
  55.4 0.1 copy.65
  55.5 3.4 %collective-permute-start.5 = (bf16[1,64,512]{2,1,0:T(8,128)(2,1)S(1)}, bf16[1,64,512]{2,1,0:T(8,128)(2,1)S(1)}, u32[]{:S(2)}, u32[]{:S(2)}) collective-permute-start(bf16[1,64,512]{2,1,0:T(8,128)(2,1)S(1)} %bitcast.59), channel_id=1, source_target_pairs={{0,1},{1,2},{2,3},{3,4},{4,5},{5,6},{6,7},{7,8},{8,9},{9,10},{10,1... | collective-permute-start | bytes 196616 | tf_op jit(solution)/shard_map/ppermute | solution.py:47
  58.9 8.1 %collective-permute-start.9 = (bf16[1,64,512]{2,1,0:T(8,128)(2,1)S(1)}, bf16[1,64,512]{2,1,0:T(8,128)(2,1)S(1)}, u32[]{:S(2)}, u32[]{:S(2)}) collective-permute-start(bf16[1,64,512]{2,1,0:T(8,128)(2,1)S(1)} %bitcast.60), channel_id=1, source_target_pairs={{0,16},{1,17},{2,18},{3,19},{4,20},{5,21},{6,22},{7,23},{8,24},{9,... | collective-permute-start | bytes 196616 | tf_op jit(solution)/shard_map/ppermute | solution.py:47
  67.1 0.1 copy.66
  67.2 1.9 %collective-permute-start.14 = (bf16[1,64,512]{2,1,0:T(8,128)(2,1)S(1)}, bf16[1,64,512]{2,1,0:T(8,128)(2,1)S(1)}, u32[]{:S(2)}, u32[]{:S(2)}) collective-permute-start(bf16[1,64,512]{2,1,0:T(8,128)(2,1)S(1)} %bitcast.73), channel_id=1, source_target_pairs={{16,0},{17,1},{18,2},{19,3},{20,4},{21,5},{22,6},{23,7},{24,8},{25... | collective-permute-start | bytes 196616 | tf_op jit(solution)/shard_map/ppermute | solution.py:47
  69.2 4.6 %collective-permute-start.10 = (bf16[1,2,64,512]{3,2,0,1:T(8,128)(2,1)S(1)}, bf16[1,2,64,512]{3,2,0,1:T(8,128)(2,1)S(1)}, u32[]{:S(2)}, u32[]{:S(2)}) collective-permute-start(bf16[1,2,64,512]{3,2,0,1:T(8,128)(2,1)S(1)} %get-tuple-element.16), channel_id=1, source_target_pairs={{1,0},{2,1},{3,2},{4,3},{5,4},{6,5},{7,6},{8,7},{9,8},{10,9},{11,1... | collective-permute-start | bytes 393224 | tf_op jit(solution)/shard_map/ppermute | solution.py:47
  73.8 0.8 copy.79.q_ref
  74.6 2.8 %collective-permute-start.6 = (bf16[2,64,512]{2,1,0:T(8,128)(2,1)S(1)}, bf16[2,64,512]{2,1,0:T(8,128)(2,1)S(1)}, u32[]{:S(2)}, u32[]{:S(2)}) collective-permute-start(bf16[2,64,512]{2,1,0:T(8,128)(2,1)S(1)} %get-tuple-element.19), channel_id=1, source_target_pairs={{0,2},{1,3},{2,4},{3,5},{4,6},{5,7},{6,8},{7,9},{8,10},{9,11},{10,... | collective-permute-start | bytes 393224 | tf_op jit(solution)/shard_map/ppermute | solution.py:47
  77.5 5.4 %collective-permute-start.11 = (bf16[2,2,64,512]{3,2,1,0:T(8,128)(2,1)S(1)}, bf16[2,2,64,512]{3,2,1,0:T(8,128)(2,1)S(1)}, u32[]{:S(2)}, u32[]{:S(2)}) collective-permute-start(bf16[2,2,64,512]{3,2,1,0:T(8,128)(2,1)S(1)} %pad_maximum_fusion.9), channel_id=1, source_target_pairs={{2,0},{3,1},{4,2},{5,3},{6,4},{7,5},{8,6},{9,7},{10,8},{11,9},{12,... | collective-permute-start | bytes 786440 | tf_op jit(solution)/shard_map/ppermute | solution.py:47
  82.9 0.9 collective-permute-done.6
  83.9 18.6 %collective-permute-start.7 = (bf16[4,64,512]{2,1,0:T(8,128)(2,1)S(1)}, bf16[4,64,512]{2,1,0:T(8,128)(2,1)S(1)}, u32[]{:S(2)}, u32[]{:S(2)}) collective-permute-start(bf16[4,64,512]{2,1,0:T(8,128)(2,1)S(1)} %pad_maximum_fusion.8), channel_id=1, source_target_pairs={{0,4},{1,5},{2,6},{3,7},{4,8},{5,9},{6,10},{7,11},{8,12},{9,13},{1... | collective-permute-start | bytes 786440 | tf_op jit(solution)/shard_map/ppermute | solution.py:47
  102.6 1.9 %collective-permute-start.12 = (bf16[4,2,64,512]{3,2,1,0:T(8,128)(2,1)S(1)}, bf16[4,2,64,512]{3,2,1,0:T(8,128)(2,1)S(1)}, u32[]{:S(2)}, u32[]{:S(2)}) collective-permute-start(bf16[4,2,64,512]{3,2,1,0:T(8,128)(2,1)S(1)} %pad_maximum_fusion.5), channel_id=1, source_target_pairs={{4,0},{5,1},{6,2},{7,3},{8,4},{9,5},{10,6},{11,7},{12,8},{13,9},{1... | collective-permute-start | bytes 1572872 | tf_op jit(solution)/shard_map/ppermute | solution.py:47
  104.5 2.4 %collective-permute-done.7 = bf16[4,64,512]{2,1,0:T(8,128)(2,1)S(1)} collective-permute-done((bf16[4,64,512]{2,1,0:T(8,128)(2,1)S(1)}, bf16[4,64,512]{2,1,0:T(8,128)(2,1)S(1)}, u32[]{:S(2)}, u32[]{:S(2)}) %collective-permute-start.7) | collective-permute-done | bytes 262176 | tf_op jit(solution)/shard_map/ppermute | solution.py:47
  107.0 3.3 %collective-permute-start.8 = (bf16[8,64,512]{2,1,0:T(8,128)(2,1)S(1)}, bf16[8,64,512]{2,1,0:T(8,128)(2,1)S(1)}, u32[]{:S(2)}, u32[]{:S(2)}) collective-permute-start(bf16[8,64,512]{2,1,0:T(8,128)(2,1)S(1)} %pad_maximum_fusion.4), channel_id=1, source_target_pairs={{0,8},{1,9},{2,10},{3,11},{4,12},{5,13},{6,14},{7,15},{8,16},{9,17... | collective-permute-start | bytes 1572872 | tf_op jit(solution)/shard_map/ppermute | solution.py:47
  110.4 21.0 %collective-permute-done.12 = bf16[4,2,64,512]{3,2,1,0:T(8,128)(2,1)S(1)} collective-permute-done((bf16[4,2,64,512]{3,2,1,0:T(8,128)(2,1)S(1)}, bf16[4,2,64,512]{3,2,1,0:T(8,128)(2,1)S(1)}, u32[]{:S(2)}, u32[]{:S(2)}) %collective-permute-start.12) | collective-permute-done | bytes 524320 | tf_op jit(solution)/shard_map/ppermute | solution.py:47
  131.4 0.1 pad_maximum_fusion.1
  131.6 1.9 %collective-permute-start.13 = (bf16[8,64,512]{2,1,0:T(8,128)(2,1)S(1)}, bf16[8,64,512]{2,1,0:T(8,128)(2,1)S(1)}, u32[]{:S(2)}, u32[]{:S(2)}) collective-permute-start(bf16[8,64,512]{2,1,0:T(8,128)(2,1)S(1)} %get-tuple-element.8), channel_id=1, source_target_pairs={{8,0},{9,1},{10,2},{11,3},{12,4},{13,5},{14,6},{15,7},{16,8},{17,9... | collective-permute-start | bytes 1572872 | tf_op jit(solution)/shard_map/ppermute | solution.py:47
  133.6 0.7 collective-permute-start.15
  134.4 28.7 %collective-permute-done.13 = bf16[8,64,512]{2,1,0:T(8,128)(2,1)S(1)} collective-permute-done((bf16[8,64,512]{2,1,0:T(8,128)(2,1)S(1)}, bf16[8,64,512]{2,1,0:T(8,128)(2,1)S(1)}, u32[]{:S(2)}, u32[]{:S(2)}) %collective-permute-start.13) | collective-permute-done | bytes 524320 | tf_op jit(solution)/shard_map/ppermute | solution.py:47
  163.2 1.5 copy.74
  164.8 0.7 copy-done.1
  165.5 8.3 %shard_map.46 = bf16[128,1024]{1,0:T(8,128)(2,1)} custom-call(s32[69]{0:T(128)} %concatenate.54.meta_ref, bf16[128,1024]{1,0:T(8,128)(2,1)} %copy.79.q_ref, bf16[1088,512]{1,0:T(8,128)(2,1)} %bitcast.70, bf16[2176,512]{1,0:T(8,128)(2,1)} %bitcast.58, bf16[256,512]{1,0:T(8,128)(2,1)} %bitcast.77, s32[2,64,1]{2,1,0:T(8,128)} %iota_add_fusion.qpos_ref, ...), custom_call_target="tpu_custom_call" | custom-call | tf_op jit(solution)/shard_map/pallas_call | solution.py:263
  (64 shorter events, 1.9 us)
Async XLA Ops:
  0.0 30.0 %collective-permute-start.2 = (bf16[2048,192]{0,1:T(8,128)(2,1)}, bf16[2048,192]{0,1:T(8,128)(2,1)S(1)}, u32[]{:S(2)}, u32[]{:S(2)}) collective-permute-start(bf16[2048,192]{0,1:T(8,128)(2,1)} %param.5), channel_id=1, source_target_pairs={{416,0},{417,1},{418,2},{419,3},{420,4},{421,5},{422,6},{423,7},{4... | collective-permute-start | bytes 2359304 | tf_op jit(solution)/shard_map/ppermute | solution.py:91
  4.3 36.0 %collective-permute-start.1 = (bf16[2048,192]{0,1:T(8,128)(2,1)}, bf16[2048,192]{0,1:T(8,128)(2,1)S(1)}, u32[]{:S(2)}, u32[]{:S(2)}) collective-permute-start(bf16[2048,192]{0,1:T(8,128)(2,1)} %param.5), channel_id=1, source_target_pairs={{256,0},{257,1},{258,2},{259,3},{260,4},{261,5},{262,6},{263,7},{2... | collective-permute-start | bytes 2359304 | tf_op jit(solution)/shard_map/ppermute | solution.py:91
  14.3 34.4 %collective-permute-start = (bf16[2048,192]{0,1:T(8,128)(2,1)}, bf16[2048,192]{0,1:T(8,128)(2,1)S(1)}, u32[]{:S(2)}, u32[]{:S(2)}) collective-permute-start(bf16[2048,192]{0,1:T(8,128)(2,1)} %param.5), channel_id=1, source_target_pairs={{128,0},{129,1},{130,2},{131,3},{132,4},{133,5},{134,6},{135,7},{1... | collective-permute-start | bytes 2359304 | tf_op jit(solution)/shard_map/ppermute | solution.py:91
  16.8 9.9 %collective-permute-start.3 = (bf16[128,2048]{1,0:T(8,128)(2,1)}, bf16[128,2048]{1,0:T(8,128)(2,1)S(1)}, u32[]{:S(2)}, u32[]{:S(2)}) collective-permute-start(bf16[128,2048]{1,0:T(8,128)(2,1)} %bitcast.91), channel_id=1, source_target_pairs={{64,0},{65,1},{66,2},{67,3},{68,4},{69,5},{70,6},{71,7},{72,8},{73... | collective-permute-start | bytes 1572872 | tf_op jit(solution)/shard_map/ppermute | solution.py:90
  48.8 4.2 %copy-start.2 = (bf16[2048,192]{0,1:T(8,128)(2,1)S(1)}, bf16[2048,192]{0,1:T(8,128)(2,1)}, u32[]{:S(2)}) copy-start(bf16[2048,192]{0,1:T(8,128)(2,1)} %param.5) | copy-start | bytes 2359300
  48.8 4.2 %copy-start.3 = (bf16[1,128,2048]{2,1,0:T(8,128)(2,1)S(1)}, bf16[1,128,2048]{2,1,0:T(8,128)(2,1)}, u32[]{:S(2)}) copy-start(bf16[1,128,2048]{2,1,0:T(8,128)(2,1)} %param.4) | copy-start | bytes 1572868
  51.0 3.3 %collective-permute-start.4 = (bf16[4,128,192]{1,2,0:T(8,128)(2,1)S(1)}, bf16[4,128,192]{1,2,0:T(8,128)(2,1)S(1)}, u32[]{:S(2)}, u32[]{:S(2)}) collective-permute-start(bf16[4,128,192]{1,2,0:T(8,128)(2,1)S(1)} %fusion.1), channel_id=1, source_target_pairs={{64,0},{65,1},{66,2},{67,3},{68,4},{69,5},{70,6},{71,7},{72,8},{73... | collective-permute-start | bytes 589832 | tf_op jit(solution)/shard_map/ppermute | solution.py:94
  55.5 13.7 %collective-permute-start.5 = (bf16[1,64,512]{2,1,0:T(8,128)(2,1)S(1)}, bf16[1,64,512]{2,1,0:T(8,128)(2,1)S(1)}, u32[]{:S(2)}, u32[]{:S(2)}) collective-permute-start(bf16[1,64,512]{2,1,0:T(8,128)(2,1)S(1)} %bitcast.59), channel_id=1, source_target_pairs={{0,1},{1,2},{2,3},{3,4},{4,5},{5,6},{6,7},{7,8},{8,9},{9,10},{10,1... | collective-permute-start | bytes 196616 | tf_op jit(solution)/shard_map/ppermute | solution.py:47
  58.9 75.5 %collective-permute-start.9 = (bf16[1,64,512]{2,1,0:T(8,128)(2,1)S(1)}, bf16[1,64,512]{2,1,0:T(8,128)(2,1)S(1)}, u32[]{:S(2)}, u32[]{:S(2)}) collective-permute-start(bf16[1,64,512]{2,1,0:T(8,128)(2,1)S(1)} %bitcast.60), channel_id=1, source_target_pairs={{0,16},{1,17},{2,18},{3,19},{4,20},{5,21},{6,22},{7,23},{8,24},{9,... | collective-permute-start | bytes 196616 | tf_op jit(solution)/shard_map/ppermute | solution.py:47
  67.2 96.0 %collective-permute-start.14 = (bf16[1,64,512]{2,1,0:T(8,128)(2,1)S(1)}, bf16[1,64,512]{2,1,0:T(8,128)(2,1)S(1)}, u32[]{:S(2)}, u32[]{:S(2)}) collective-permute-start(bf16[1,64,512]{2,1,0:T(8,128)(2,1)S(1)} %bitcast.73), channel_id=1, source_target_pairs={{16,0},{17,1},{18,2},{19,3},{20,4},{21,5},{22,6},{23,7},{24,8},{25... | collective-permute-start | bytes 196616 | tf_op jit(solution)/shard_map/ppermute | solution.py:47
  69.2 8.3 %collective-permute-start.10 = (bf16[1,2,64,512]{3,2,0,1:T(8,128)(2,1)S(1)}, bf16[1,2,64,512]{3,2,0,1:T(8,128)(2,1)S(1)}, u32[]{:S(2)}, u32[]{:S(2)}) collective-permute-start(bf16[1,2,64,512]{3,2,0,1:T(8,128)(2,1)S(1)} %get-tuple-element.16), channel_id=1, source_target_pairs={{1,0},{2,1},{3,2},{4,3},{5,4},{6,5},{7,6},{8,7},{9,8},{10,9},{11,1... | collective-permute-start | bytes 393224 | tf_op jit(solution)/shard_map/ppermute | solution.py:47
  74.6 9.3 %collective-permute-start.6 = (bf16[2,64,512]{2,1,0:T(8,128)(2,1)S(1)}, bf16[2,64,512]{2,1,0:T(8,128)(2,1)S(1)}, u32[]{:S(2)}, u32[]{:S(2)}) collective-permute-start(bf16[2,64,512]{2,1,0:T(8,128)(2,1)S(1)} %get-tuple-element.19), channel_id=1, source_target_pairs={{0,2},{1,3},{2,4},{3,5},{4,6},{5,7},{6,8},{7,9},{8,10},{9,11},{10,... | collective-permute-start | bytes 393224 | tf_op jit(solution)/shard_map/ppermute | solution.py:47
  77.5 25.0 %collective-permute-start.11 = (bf16[2,2,64,512]{3,2,1,0:T(8,128)(2,1)S(1)}, bf16[2,2,64,512]{3,2,1,0:T(8,128)(2,1)S(1)}, u32[]{:S(2)}, u32[]{:S(2)}) collective-permute-start(bf16[2,2,64,512]{3,2,1,0:T(8,128)(2,1)S(1)} %pad_maximum_fusion.9), channel_id=1, source_target_pairs={{2,0},{3,1},{4,2},{5,3},{6,4},{7,5},{8,6},{9,7},{10,8},{11,9},{12,... | collective-permute-start | bytes 786440 | tf_op jit(solution)/shard_map/ppermute | solution.py:47
  83.9 23.1 %collective-permute-start.7 = (bf16[4,64,512]{2,1,0:T(8,128)(2,1)S(1)}, bf16[4,64,512]{2,1,0:T(8,128)(2,1)S(1)}, u32[]{:S(2)}, u32[]{:S(2)}) collective-permute-start(bf16[4,64,512]{2,1,0:T(8,128)(2,1)S(1)} %pad_maximum_fusion.8), channel_id=1, source_target_pairs={{0,4},{1,5},{2,6},{3,7},{4,8},{5,9},{6,10},{7,11},{8,12},{9,13},{1... | collective-permute-start | bytes 786440 | tf_op jit(solution)/shard_map/ppermute | solution.py:47
  102.6 28.8 %collective-permute-start.12 = (bf16[4,2,64,512]{3,2,1,0:T(8,128)(2,1)S(1)}, bf16[4,2,64,512]{3,2,1,0:T(8,128)(2,1)S(1)}, u32[]{:S(2)}, u32[]{:S(2)}) collective-permute-start(bf16[4,2,64,512]{3,2,1,0:T(8,128)(2,1)S(1)} %pad_maximum_fusion.5), channel_id=1, source_target_pairs={{4,0},{5,1},{6,2},{7,3},{8,4},{9,5},{10,6},{11,7},{12,8},{13,9},{1... | collective-permute-start | bytes 1572872 | tf_op jit(solution)/shard_map/ppermute | solution.py:47
  107.0 27.3 %collective-permute-start.8 = (bf16[8,64,512]{2,1,0:T(8,128)(2,1)S(1)}, bf16[8,64,512]{2,1,0:T(8,128)(2,1)S(1)}, u32[]{:S(2)}, u32[]{:S(2)}) collective-permute-start(bf16[8,64,512]{2,1,0:T(8,128)(2,1)S(1)} %pad_maximum_fusion.4), channel_id=1, source_target_pairs={{0,8},{1,9},{2,10},{3,11},{4,12},{5,13},{6,14},{7,15},{8,16},{9,17... | collective-permute-start | bytes 1572872 | tf_op jit(solution)/shard_map/ppermute | solution.py:47
  131.6 31.5 %collective-permute-start.13 = (bf16[8,64,512]{2,1,0:T(8,128)(2,1)S(1)}, bf16[8,64,512]{2,1,0:T(8,128)(2,1)S(1)}, u32[]{:S(2)}, u32[]{:S(2)}) collective-permute-start(bf16[8,64,512]{2,1,0:T(8,128)(2,1)S(1)} %get-tuple-element.8), channel_id=1, source_target_pairs={{8,0},{9,1},{10,2},{11,3},{12,4},{13,5},{14,6},{15,7},{16,8},{17,9... | collective-permute-start | bytes 1572872 | tf_op jit(solution)/shard_map/ppermute | solution.py:47
  133.6 31.2 %collective-permute-start.15 = (bf16[4,64,512]{2,1,0:T(8,128)(2,1)S(1)}, bf16[4,64,512]{2,1,0:T(8,128)(2,1)S(1)}, u32[]{:S(2)}, u32[]{:S(2)}) collective-permute-start(bf16[4,64,512]{2,1,0:T(8,128)(2,1)S(1)} %pad_dynamic-slice_fusion), channel_id=1, source_target_pairs={{56,51},{57,52},{58,50},{59,53},{60,49},{61,54},{62,48},{63,55},{1... | collective-permute-start | bytes 786440 | tf_op jit(solution)/shard_map/ppermute | solution.py:47
  134.4 30.3 %copy-start = (bf16[17,64,512]{2,1,0:T(8,128)(2,1)}, bf16[17,64,512]{2,1,0:T(8,128)(2,1)S(1)}, u32[]{:S(2)}) copy-start(bf16[17,64,512]{2,1,0:T(8,128)(2,1)S(1)} %constant_dynamic-update-slice_fusion) | copy-start | bytes 3342340
  164.8 0.7 copy-start.1
